TPU v7x, 32 devices: a whole 2x2x4 slice. The times are simulated.
32 devices in a mesh: dp: 32 (over z, y, x, core), mp: 1.
Axes of the slice: x: 2, y: 2, z: 4, core: 2. Of those that a mesh axis runs over, the one named last changes fastest.
Arguments:
- context: bfloat16 [16384, 6144], P('dp', 'mp'), may hold values from -6 to 6
- weight: float32 [6144, 6144], P(('mp', 'dp')), may hold values from -0.078125 to 0.078125
- moment_one: float32 [6144, 6144], P(('mp', 'dp')), may hold values from -4 to 4
- moment_two: float32 [6144, 6144], P(('mp', 'dp')), may hold values from 0.05 to 2
- grad_out: bfloat16 [16384, 6144], P(('dp', 'mp')), may hold values from -6 to 6
Outputs:
- output: bfloat16 [16384, 6144], P(('dp', 'mp'))
- d_context: bfloat16 [16384, 6144], P('dp', 'mp')
- new_weight: float32 [6144, 6144], P(('mp', 'dp'))
- new_moment_one: float32 [6144, 6144], P(('mp', 'dp'))
- new_moment_two: float32 [6144, 6144], P(('mp', 'dp'))
All inputs are finite; a program needn't handle non-finite values.
Results may differ from a plain program's by a relative error of at most 0.017.
Values may be sent and summed in bfloat16 or wider, within the bound.
No kernel may reach another device: no remote copies, remote signals or barrier semaphores. Data moves between devices by JAX's collectives and lax.ppermute only.
A program may use at most 192 MiB of HBM per device.

v0:
```python
import math

import jax
import jax.numpy as jnp
from jax import lax
from jax.sharding import PartitionSpec as P


def per_device(context, weight, moment_one, moment_two, grad_out):
    weight_bf = weight.astype(jnp.bfloat16)
    tok_rows = context.shape[0]
    full_weight = lax.all_gather(weight_bf, "dp", axis=0, tiled=True)
    partials = jnp.dot(context, full_weight, preferred_element_type=jnp.float32)
    summed = lax.psum_scatter(partials.astype(jnp.bfloat16), "mp", scatter_dimension=0, tiled=True)
    piece = lax.all_gather(grad_out, "mp", axis=0, tiled=True)
    back_rows = lax.dot_general(
        piece, full_weight, (((1,), (1,)), ((), ())), preferred_element_type=jnp.float32
    )
    ctx_grad = back_rows
    ctx_grad, full_cotangent = (ctx_grad, piece)
    weight_grad = lax.dot_general(
        context, full_cotangent, (((0,), (0,)), ((), ())), preferred_element_type=jnp.float32
    )
    grad_shard = lax.psum_scatter(
        weight_grad.astype(jnp.bfloat16), "dp", scatter_dimension=0, tiled=True
    ).astype(jnp.float32)
    d_context = ctx_grad.astype(jnp.bfloat16)
    tokens_all = tok_rows * lax.axis_size("dp")
    grad = grad_shard * (1.0 / math.sqrt(tokens_all))
    new_moment_one = 0.9 * moment_one + 0.1 * grad
    new_moment_two = 0.999 * moment_two + 0.001 * grad * grad
    first_fix = 1.0 - 0.9**10
    second_fix = 1.0 - 0.999**10
    update = (
        new_moment_one / first_fix / (jnp.sqrt(new_moment_two / second_fix) + 1e-08) + 0.1 * weight
    )
    new_weight = weight - 0.001 * update
    return (summed, d_context, new_weight, new_moment_one, new_moment_two)


def solution(mesh):
    placed = (
        P("dp", "mp"),
        P(("mp", "dp"), None),
        P(("mp", "dp"), None),
        P(("mp", "dp"), None),
        P(("dp", "mp"), None),
    )
    return jax.shard_map(
        per_device,
        mesh=mesh,
        in_specs=placed,
        out_specs=(
            P(("dp", "mp"), None),
            P("dp", "mp"),
            P(("mp", "dp"), None),
            P(("mp", "dp"), None),
            P(("mp", "dp"), None),
        ),
        check_vma=False,
    )
```

profile of v0, /device:TPU:0, one launch (start us, length us, event | category | flops | bytes accessed | tf_op | source)
XLA Modules:
  0.0 1225.9 jit_solution(6301845388372518640)
XLA Ops:
  7.2 0.0 reduce-scatter.2.cloned.1.call-start
  7.2 48.5 %convolution_convert_fusion = bf16[6144,6144]{1,0:T(8,128)(2,1)} fusion(bf16[512,6144]{1,0:T(8,128)(2,1)} %param.5, bf16[512,6144]{1,0:T(8,128)(2,1)} %param.9), kind=kOutput, calls=%fused_computation | convolution fusion | flops 38692454400 | bytes 88080384 | tf_op jit(solution)/shard_map/dot_general | solution.py:21
  55.8 0.0 reduce-scatter.2.cloned.1.call-update
  55.8 0.2 all-gather.2.cloned.1.call-start
  56.0 658.6 %reduce-scatter.2.cloned.1.call-done = bf16[192,6144]{1,0:T(8,128)(2,1)} async-done(((bf16[6144,6144]{1,0:T(8,128)(2,1)}), bf16[192,6144]{1,0:T(8,128)(2,1)}) %reduce-scatter.2.cloned.1.call-update) | async-done | bytes 2359312 | tf_op jit(solution)/shard_map/reduce_scatter | solution.py:24
  714.6 13.8 %multiply_subtract_fusion = (f32[192,6144]{1,0:T(8,128)}, f32[192,6144]{1,0:T(8,128)}, f32[192,6144]{1,0:T(8,128)}, bf16[192,6144]{1,0:T(8,128)(2,1)}) fusion(f32[192,6144]{1,0:T(8,128)} %param.6, bf16[192,6144]{1,0:T(8,128)(2,1)} %reduce-scatter.2.cloned.1.call-done, f32[192,6144]{1,0:T(8,128)} %param.7, f32[192,6144]{1,0:T(8,128)} %param.8), kind=kLoop, calls=%fused_computation.9 | loop fusion | flops 21233664 | bytes 33030144 | tf_op jit(solution)/shard_map/sub | solution.py:37
  728.4 0.0 all-gather.2.cloned.1.call-update
  728.5 395.8 %all-gather.2.cloned.1.call-done = bf16[6144,6144]{1,0:T(8,128)(2,1)} async-done(((bf16[192,6144]{1,0:T(8,128)(2,1)}), bf16[6144,6144]{1,0:T(8,128)(2,1)}) %all-gather.2.cloned.1.call-update) | async-done | bytes 75497488 | tf_op jit(solution)/shard_map/all_gather | solution.py:12
  1124.2 47.5 %convolution_convert_fusion.1 = bf16[512,6144]{1,0:T(8,128)(2,1)} fusion(bf16[512,6144]{1,0:T(8,128)(2,1)} %param.9, bf16[6144,6144]{1,0:T(8,128)(2,1)} %all-gather.2.cloned.1.call-done), kind=kOutput, calls=%fused_computation.1 | convolution fusion | flops 38657851392 | bytes 88080384 | tf_op jit(solution)/shard_map/dot_general | solution.py:16
  1171.7 47.3 %convolution_convert_fusion.2 = bf16[512,6144]{1,0:T(8,128)(2,1)} fusion(bf16[512,6144]{1,0:T(8,128)(2,1)} %param.5, bf16[6144,6144]{1,0:T(8,128)(2,1)} %all-gather.2.cloned.1.call-done), kind=kOutput, calls=%fused_computation.2 | convolution fusion | flops 38657851392 | bytes 88080384 | tf_op jit(solution)/shard_map/dot_general | solution.py:13
Async XLA Ops:
  7.2 707.4 %reduce-scatter.2.cloned.1.call-start = ((), (), s32[]{:S(2)}) async-start(), calls=%async_computation.2 | async-start | bytes 77856768 | tf_op jit(solution)/shard_map/reduce_scatter | solution.py:24
  55.8 1068.5 %all-gather.2.cloned.1.call-start = ((), (), s32[]{:S(2)}) async-start(), calls=%async_computation.1 | async-start | bytes 77856768 | tf_op jit(solution)/shard_map/all_gather | solution.py:12
Sparse Core Ops, SparseCore 0:
  55.9 658.6 reduce-scatter.1
  728.6 395.6 all-gather.1
where the time goes:
time: 1230 us
  waiting for transfers between devices  1050 us (85%)
  matrix products  143 us (12%)
  between operations  14 us (1%)
  other arithmetic  13.8 us (1%)
    reduce_scatter x1, waiting for transfers between devices, per_device(): lax.psum_scatter(weight_grad.astype(jnp.bfloat16), 'dp', scatter_dimensio...  659 us
    all_gather x1, waiting for transfers between devices, per_device(): full_weight = lax.all_gather(weight_bf, 'dp', axis=0, tiled=True)  396 us
    dot_general x1, matrix products, per_device(): lax.dot_general(context, full_cotangent, (((0,), (0,)), ((), ())), prefer...  48.5 us
    dot_general x1, matrix products, per_device(): lax.dot_general(piece, full_weight, (((1,), (1,)), ((), ())), preferred_e...  47.5 us
    dot_general x1, matrix products, per_device(): partials = jnp.dot(context, full_weight, preferred_element_type=jnp.float32)  47.3 us
  transfers between devices with their start and end apart: 2, of which 2 were waited for; matrix products, arithmetic and copies ran while one was open for 0% of the time, Pallas kernels for 0%

commit v1 on v0

--- a/solution.py
+++ b/solution.py
@@ -5,9 +5,11 @@
 from jax import lax
 from jax.sharding import PartitionSpec as P
 
+GRAD_CHUNKS = 4
+
 
 def per_device(context, weight, moment_one, moment_two, grad_out):
-    weight_bf = weight.astype(jnp.bfloat16)
+    weight_bf, weight = lax.optimization_barrier((weight.astype(jnp.bfloat16), weight))
     tok_rows = context.shape[0]
     full_weight = lax.all_gather(weight_bf, "dp", axis=0, tiled=True)
     partials = jnp.dot(context, full_weight, preferred_element_type=jnp.float32)
@@ -16,15 +18,23 @@
     back_rows = lax.dot_general(
         piece, full_weight, (((1,), (1,)), ((), ())), preferred_element_type=jnp.float32
     )
-    ctx_grad = back_rows
-    ctx_grad, full_cotangent = (ctx_grad, piece)
-    weight_grad = lax.dot_general(
-        context, full_cotangent, (((0,), (0,)), ((), ())), preferred_element_type=jnp.float32
-    )
-    grad_shard = lax.psum_scatter(
-        weight_grad.astype(jnp.bfloat16), "dp", scatter_dimension=0, tiled=True
-    ).astype(jnp.float32)
-    d_context = ctx_grad.astype(jnp.bfloat16)
+    d_context = back_rows.astype(jnp.bfloat16)
+    width = piece.shape[1] // GRAD_CHUNKS
+    ctx_in = context
+    shards = []
+    for c in range(GRAD_CHUNKS):
+        if c >= 2:
+            ctx_in, _ = lax.optimization_barrier((ctx_in, shards[c - 2]))
+        weight_grad = lax.dot_general(
+            ctx_in,
+            piece[:, c * width:(c + 1) * width],
+            (((0,), (0,)), ((), ())),
+            preferred_element_type=jnp.float32,
+        )
+        shards.append(
+            lax.psum_scatter(weight_grad.astype(jnp.bfloat16), "dp", scatter_dimension=0, tiled=True)
+        )
+    grad_shard = jnp.concatenate(shards, axis=1).astype(jnp.float32)
     tokens_all = tok_rows * lax.axis_size("dp")
     grad = grad_shard * (1.0 / math.sqrt(tokens_all))
     new_moment_one = 0.9 * moment_one + 0.1 * grad

time: 1230 us -> 1400 us (1.14)
  waiting for transfers between devices: 1050 us -> 1180 us
  matrix products: 143 us -> 161 us
  local copies, waits for them, and re-layouts: 0 us -> 17.2 us
    reduce_scatter x1 -> x4, waiting for transfers between devices: 659 us -> 790 us  [per_device(): lax.psum_scatter(weight_grad.astype(jnp.bfloat16), 'dp', scatter_dimensio...]
    dot_general x1 -> x4, matrix products: 48.5 us -> 66.1 us  [per_device(): lax.dot_general(ctx_in, piece[:, c * width:(c + 1) * width], (((0,), (0,)...]
    unnamed x0 -> x6, local copies, waits for them, and re-layouts: none -> 17.2 us
  transfers between devices with their start and end apart: 2 -> 5, of which waited for: 2 -> 5; matrix products, arithmetic and copies ran while one was open for 0% -> 5% of each run, Pallas kernels for 0% -> 0%
where the time goes in v1:
time: 1400 us; the launch traced here: 1390 us
  waiting for transfers between devices  1180 us (84%)
  matrix products  161 us (12%)
  local copies, waits for them, and re-layouts  17.2 us (1%)
  other arithmetic  15.8 us (1%)
  between operations  14.2 us (1%)
    reduce_scatter x4, waiting for transfers between devices, per_device(): lax.psum_scatter(weight_grad.astype(jnp.bfloat16), 'dp', scatter_dimensio...  790 us
    all_gather x1, waiting for transfers between devices, per_device(): full_weight = lax.all_gather(weight_bf, 'dp', axis=0, tiled=True)  388 us
    dot_general x4, matrix products, per_device(): lax.dot_general(ctx_in, piece[:, c * width:(c + 1) * width], (((0,), (0,)...  66.1 us
    dot_general x1, matrix products, per_device(): lax.dot_general(piece, full_weight, (((1,), (1,)), ((), ())), preferred_e...  47.7 us
    dot_general x1, matrix products, per_device(): partials = jnp.dot(context, full_weight, preferred_element_type=jnp.float32)  47.6 us
  transfers between devices with their start and end apart: 5, of which 5 were waited for; matrix products, arithmetic and copies ran while one was open for 5% of the time, Pallas kernels for 0%

profile of v1, /device:TPU:0, one launch (start us, length us, event | category | flops | bytes accessed | tf_op | source)
XLA Modules:
  0.0 1387.4 jit_solution(15919206330719589847)
XLA Ops:
  7.2 0.0 reduce-scatter.5.cloned.1.call-start
  7.2 16.3 %convolution_convert_fusion.3 = bf16[6144,1536]{1,0:T(8,128)(2,1)} fusion(bf16[512,6144]{1,0:T(8,128)(2,1)} %param.5, bf16[512,6144]{1,0:T(8,128)(2,1)} %param.9), kind=kOutput, calls=%fused_computation.3 | convolution fusion | flops 9673113600 | bytes 26738688 | tf_op jit(solution)/shard_map/dot_general | solution.py:28
  23.5 0.0 reduce-scatter.5.cloned.1.call-update
  23.5 0.0 reduce-scatter.7.cloned.1.call-start
  23.5 16.6 %convolution_convert_fusion.2 = bf16[6144,1536]{1,0:T(8,128)(2,1)} fusion(bf16[512,6144]{1,0:T(8,128)(2,1)} %param.5, bf16[512,6144]{1,0:T(8,128)(2,1)} %param.9), kind=kOutput, calls=%fused_computation.2 | convolution fusion | flops 9673113600 | bytes 26738688 | tf_op jit(solution)/shard_map/dot_general | solution.py:28
  40.1 0.0 reduce-scatter.7.cloned.1.call-update
  40.2 0.2 reduce-scatter.9.cloned.1.call-start
  40.4 192.6 %reduce-scatter.5.cloned.1.call-done = bf16[192,1536]{1,0:T(8,128)(2,1)} async-done(((bf16[6144,1536]{1,0:T(8,128)(2,1)}), bf16[192,1536]{1,0:T(8,128)(2,1)}) %reduce-scatter.5.cloned.1.call-update) | async-done | bytes 589840 | tf_op jit(solution)/shard_map/reduce_scatter | solution.py:35
  233.0 16.6 %convolution_convert_fusion.1 = bf16[6144,1536]{1,0:T(8,128)(2,1)} fusion(bf16[512,6144]{1,0:T(8,128)(2,1)} %param.5, bf16[512,6144]{1,0:T(8,128)(2,1)} %param.9), kind=kOutput, calls=%fused_computation.1 | convolution fusion | flops 9673113600 | bytes 26738688 | tf_op jit(solution)/shard_map/dot_general | solution.py:28
  249.7 0.0 reduce-scatter.9.cloned.1.call-update
  249.7 0.0 reduce-scatter.11.cloned.1.call-start
  249.7 195.3 %reduce-scatter.7.cloned.1.call-done = bf16[192,1536]{1,0:T(8,128)(2,1)} async-done(((bf16[6144,1536]{1,0:T(8,128)(2,1)}), bf16[192,1536]{1,0:T(8,128)(2,1)}) %reduce-scatter.7.cloned.1.call-update) | async-done | bytes 589840 | tf_op jit(solution)/shard_map/reduce_scatter | solution.py:35
  445.1 16.6 %convolution_convert_fusion = bf16[6144,1536]{1,0:T(8,128)(2,1)} fusion(bf16[512,6144]{1,0:T(8,128)(2,1)} %param.5, bf16[512,6144]{1,0:T(8,128)(2,1)} %param.9), kind=kOutput, calls=%fused_computation | convolution fusion | flops 9673113600 | bytes 26738688 | tf_op jit(solution)/shard_map/dot_general | solution.py:28
  461.7 0.0 reduce-scatter.11.cloned.1.call-update
  461.7 0.0 copy-start
  461.7 0.0 copy-start.1
  461.8 0.3 all-gather.2.cloned.1.call-start
  462.0 4.6 convert_element_type.30
  466.6 0.0 all-gather.2.cloned.1.call-update
  466.6 190.6 %reduce-scatter.9.cloned.1.call-done = bf16[192,1536]{1,0:T(8,128)(2,1)} async-done(((bf16[6144,1536]{1,0:T(8,128)(2,1)}), bf16[192,1536]{1,0:T(8,128)(2,1)}) %reduce-scatter.9.cloned.1.call-update) | async-done | bytes 589840 | tf_op jit(solution)/shard_map/reduce_scatter | solution.py:35
  657.2 212.0 %reduce-scatter.11.cloned.1.call-done = bf16[192,1536]{1,0:T(8,128)(2,1)} async-done(((bf16[6144,1536]{1,0:T(8,128)(2,1)}), bf16[192,1536]{1,0:T(8,128)(2,1)}) %reduce-scatter.11.cloned.1.call-update) | async-done | bytes 589840 | tf_op jit(solution)/shard_map/reduce_scatter | solution.py:35
  869.2 0.0 copy-done
  869.2 0.0 copy-done.1
  869.2 11.2 multiply_subtract_fusion
  880.4 387.5 %all-gather.2.cloned.1.call-done = bf16[6144,6144]{1,0:T(8,128)(2,1)} async-done(((bf16[192,6144]{1,0:T(8,128)(2,1)}), bf16[6144,6144]{1,0:T(8,128)(2,1)}) %all-gather.2.cloned.1.call-update) | async-done | bytes 75497488 | tf_op jit(solution)/shard_map/all_gather | solution.py:14
  1267.9 47.6 %fusion = bf16[512,6144]{0,1:T(8,128)(2,1)} fusion(bf16[6144,6144]{1,0:T(8,128)(2,1)} %all-gather.2.cloned.1.call-done, bf16[512,6144]{1,0:T(8,128)(2,1)} %param.5), kind=kOutput, calls=%fused_computation.6 | convolution fusion | flops 38657851392 | bytes 88080384 | tf_op jit(solution)/shard_map/dot_general | solution.py:15
  1315.5 8.6 copy.10
  1324.1 47.7 %fusion.1 = bf16[512,6144]{0,1:T(8,128)(2,1)} fusion(bf16[6144,6144]{1,0:T(8,128)(2,1)} %all-gather.2.cloned.1.call-done, bf16[512,6144]{1,0:T(8,128)(2,1)} %param.9), kind=kOutput, calls=%fused_computation.7 | convolution fusion | flops 38657851392 | bytes 88080384 | tf_op jit(solution)/shard_map/dot_general | solution.py:18
  1371.8 8.6 copy.11
Async XLA Ops:
  7.2 225.9 %reduce-scatter.5.cloned.1.call-start = ((), (), s32[]{:S(2)}) async-start(), calls=%async_computation.5 | async-start | bytes 19464192 | tf_op jit(solution)/shard_map/reduce_scatter | solution.py:35
  23.5 421.6 %reduce-scatter.7.cloned.1.call-start = ((), (), s32[]{:S(2)}) async-start(), calls=%async_computation.6 | async-start | bytes 19464192 | tf_op jit(solution)/shard_map/reduce_scatter | solution.py:35
  40.2 617.0 %reduce-scatter.9.cloned.1.call-start = ((), (), s32[]{:S(2)}) async-start(), calls=%async_computation.7 | async-start | bytes 19464192 | tf_op jit(solution)/shard_map/reduce_scatter | solution.py:35
  249.7 619.5 %reduce-scatter.11.cloned.1.call-start = ((), (), s32[]{:S(2)}) async-start(), calls=%async_computation.8 | async-start | bytes 19464192 | tf_op jit(solution)/shard_map/reduce_scatter | solution.py:35
  461.7 407.4 %copy-start = (bf16[192,1536]{1,0:T(8,128)(2,1)S(1)}, bf16[192,1536]{1,0:T(8,128)(2,1)}, u32[]{:S(2)}) copy-start(bf16[192,1536]{1,0:T(8,128)(2,1)} %reduce-scatter.5.cloned.1.call-done) | copy-start | bytes 1769476
  461.7 407.4 %copy-start.1 = (bf16[192,1536]{1,0:T(8,128)(2,1)S(1)}, bf16[192,1536]{1,0:T(8,128)(2,1)}, u32[]{:S(2)}) copy-start(bf16[192,1536]{1,0:T(8,128)(2,1)} %reduce-scatter.7.cloned.1.call-done) | copy-start | bytes 1769476
  461.8 806.1 %all-gather.2.cloned.1.call-start = ((), (), s32[]{:S(2)}) async-start(), calls=%async_computation.4 | async-start | bytes 77856768 | tf_op jit(solution)/shard_map/all_gather | solution.py:14
Sparse Core Ops, SparseCore 0:
  23.6 209.3 reduce-scatter.4
  239.4 205.5 reduce-scatter.6
  451.5 205.6 reduce-scatter.8
  663.5 205.6 reduce-scatter.10
  872.5 395.3 all-gather.1

commit v2 on v0

v2 whole, which is shorter than its diff:
```python
import math

import jax
import jax.numpy as jnp
import numpy as np
from jax import lax
from jax.sharding import PartitionSpec as P


def ring_order(n_dp, n_mp):
    if n_dp != 32 or n_mp != 1:
        return list(range(n_dp))
    order = []
    for i, (x, y) in enumerate(((0, 0), (1, 0), (1, 1), (0, 1))):
        for z in range(4) if i % 2 == 0 else range(3, -1, -1):
            chip = (z * 2 + y) * 2 + x
            order += [chip * 2, chip * 2 + 1]
    return order


def make_per_device(order):
    n = len(order)
    position = [0] * n
    for i, d in enumerate(order):
        position[d] = i
    forward = [(order[i], order[(i + 1) % n]) for i in range(n)]
    backward = [(order[(i + 1) % n], order[i]) for i in range(n)]

    def per_device(context, weight, moment_one, moment_two, grad_out):
        weight_bf, weight = lax.optimization_barrier((weight.astype(jnp.bfloat16), weight))
        rows = weight_bf.shape[0]
        tok_rows = context.shape[0]
        piece = lax.all_gather(grad_out, "mp", axis=0, tiled=True)
        weight_grad = lax.dot_general(
            context, piece, (((0,), (0,)), ((), ())), preferred_element_type=jnp.float32
        )
        grad_shard = lax.psum_scatter(
            weight_grad.astype(jnp.bfloat16), "dp", scatter_dimension=0, tiled=True
        ).astype(jnp.float32)

        width = piece.shape[1]
        half = width // 2
        ctx_t = context.T
        order_arr = jnp.asarray(np.array(order, np.int32))
        me = jnp.asarray(np.array(position, np.int32))[lax.axis_index("dp")]
        cw = weight_bf[:, :half]
        ccw = weight_bf[:, half:]
        out_cw = jnp.zeros((tok_rows, half), jnp.float32)
        out_ccw = jnp.zeros((tok_rows, width - half), jnp.float32)
        dctx_t = jnp.zeros((ctx_t.shape[0], tok_rows), jnp.float32)
        dims_fwd = (((0,), (0,)), ((), ()))
        dims_bwd = (((1,), (1,)), ((), ()))
        def consume(step, cw, ccw, out_cw, out_ccw, dctx_t):
            src_cw = order_arr[(me - step) % n] * rows
            src_ccw = order_arr[(me + step) % n] * rows
            ctx_cw = lax.dynamic_slice_in_dim(ctx_t, src_cw, rows, 0)
            ctx_ccw = lax.dynamic_slice_in_dim(ctx_t, src_ccw, rows, 0)
            out_cw = out_cw + lax.dot_general(ctx_cw, cw, dims_fwd, preferred_element_type=jnp.float32)
            out_ccw = out_ccw + lax.dot_general(ctx_ccw, ccw, dims_fwd, preferred_element_type=jnp.float32)
            part_cw = lax.dot_general(cw, piece[:, :half], dims_bwd, preferred_element_type=jnp.float32)
            dctx_t = lax.dynamic_update_slice_in_dim(
                dctx_t, lax.dynamic_slice_in_dim(dctx_t, src_cw, rows, 0) + part_cw, src_cw, 0
            )
            part_ccw = lax.dot_general(ccw, piece[:, half:], dims_bwd, preferred_element_type=jnp.float32)
            dctx_t = lax.dynamic_update_slice_in_dim(
                dctx_t, lax.dynamic_slice_in_dim(dctx_t, src_ccw, rows, 0) + part_ccw, src_ccw, 0
            )
            return out_cw, out_ccw, dctx_t

        def ring_step(step, carry):
            cw, ccw, out_cw, out_ccw, dctx_t = carry
            cw_next = lax.ppermute(cw, "dp", forward)
            ccw_next = lax.ppermute(ccw, "dp", backward)
            out_cw, out_ccw, dctx_t = consume(step, cw, ccw, out_cw, out_ccw, dctx_t)
            return cw_next, ccw_next, out_cw, out_ccw, dctx_t

        cw, ccw, out_cw, out_ccw, dctx_t = lax.fori_loop(
            0, n - 1, ring_step, (cw, ccw, out_cw, out_ccw, dctx_t)
        )
        out_cw, out_ccw, dctx_t = consume(n - 1, cw, ccw, out_cw, out_ccw, dctx_t)
        partials = jnp.concatenate([out_cw, out_ccw], axis=1)
        summed = lax.psum_scatter(partials.astype(jnp.bfloat16), "mp", scatter_dimension=0, tiled=True)
        d_context = dctx_t.T.astype(jnp.bfloat16)

        tokens_all = tok_rows * lax.axis_size("dp")
        grad = grad_shard * (1.0 / math.sqrt(tokens_all))
        new_moment_one = 0.9 * moment_one + 0.1 * grad
        new_moment_two = 0.999 * moment_two + 0.001 * grad * grad
        first_fix = 1.0 - 0.9**10
        second_fix = 1.0 - 0.999**10
        update = (
            new_moment_one / first_fix / (jnp.sqrt(new_moment_two / second_fix) + 1e-08) + 0.1 * weight
        )
        new_weight = weight - 0.001 * update
        return (summed, d_context, new_weight, new_moment_one, new_moment_two)

    return per_device


def solution(mesh):
    placed = (
        P("dp", "mp"),
        P(("mp", "dp"), None),
        P(("mp", "dp"), None),
        P(("mp", "dp"), None),
        P(("dp", "mp"), None),
    )
    order = ring_order(mesh.shape["dp"], mesh.shape["mp"])
    return jax.shard_map(
        make_per_device(order),
        mesh=mesh,
        in_specs=placed,
        out_specs=(
            P(("dp", "mp"), None),
            P("dp", "mp"),
            P(("mp", "dp"), None),
            P(("mp", "dp"), None),
            P(("mp", "dp"), None),
        ),
        check_vma=False,
    )
```

time: 1230 us -> 1280 us (1.041)
  waiting for transfers between devices: 1050 us -> 19.8 us
  matrix products: 143 us -> 641 us
  starting transfers between devices: 0.26 us -> 254 us
  local copies, waits for them, and re-layouts: 0 us -> 231 us
  loops' own time: 0 us -> 80.9 us
    reduce_scatter x1, waiting for transfers between devices: 659 us -> 0.01 us  [per_device(): lax.psum_scatter(weight_grad.astype(jnp.bfloat16), 'dp', scatter_dimensio...]
    dot_general x3 -> x129, matrix products: 143 us -> 641 us  [the longest x32 217 us: consume(): lax.dot_general(ctx_cw, cw, dims_fwd, preferred_element_type=jnp.float32)]
    all_gather x1 -> x0, waiting for transfers between devices: 396 us -> none  [per_device(): full_weight = lax.all_gather(weight_bf, 'dp', axis=0, tiled=True)]
    ppermute x0 -> x62, starting transfers between devices: none -> 254 us  [the longest x31 220 us: ring_step(): cw_next = lax.ppermute(cw, 'dp', forward)]
    while x0 -> x248, local copies, waits for them, and re-layouts: none -> 182 us
    another operation x0 -> x1, loops' own time: none -> 80.9 us  [per_device(): lax.fori_loop(0, n - 1, ring_step, (cw, ccw, out_cw, out_ccw, dctx_t))]
    dynamic_slice x0 -> x33, local copies, waits for them, and re-layouts: none -> 21.4 us  [the longest x31 20.2 us: consume(): src_ccw = order_arr[(me + step) % n] * rows]
    ppermute x0 -> x62, waiting for transfers between devices: none -> 19.8 us  [the longest x31 10.1 us: ring_step(): ccw_next = lax.ppermute(ccw, 'dp', backward)]
  transfers between devices with their start and end apart: 2 -> 63, of which waited for: 2 -> 10; matrix products, arithmetic and copies ran while one was open for 0% -> 61% of each run, Pallas kernels for 0% -> 0%
where the time goes in v2:
time: 1280 us; the launch traced here: 1270 us
  matrix products  641 us (50%)
  starting transfers between devices  254 us (20%)
  local copies, waits for them, and re-layouts  231 us (18%)
  loops' own time  80.9 us (6%)
  other arithmetic  26 us (2%)
  waiting for transfers between devices  19.8 us (2%)
  between operations  16.7 us (1%)
    ppermute x31, starting transfers between devices, ring_step(): cw_next = lax.ppermute(cw, 'dp', forward)  220 us
    dot_general x32, matrix products, consume(): lax.dot_general(ctx_cw, cw, dims_fwd, preferred_element_type=jnp.float32)  217 us
    while x248, local copies, waits for them, and re-layouts  182 us
    dot_general x32, matrix products, consume(): lax.dot_general(ccw, piece[:, half:], dims_bwd, preferred_element_type=jn...  145 us
    dot_general x32, matrix products, consume(): lax.dot_general(cw, piece[:, :half], dims_bwd, preferred_element_type=jnp...  126 us
    dot_general x32, matrix products, consume(): lax.dot_general(ctx_ccw, ccw, dims_fwd, preferred_element_type=jnp.float32)  105 us
    another operation x1, loops' own time, per_device(): lax.fori_loop(0, n - 1, ring_step, (cw, ccw, out_cw, out_ccw, dctx_t))  80.9 us
    dot_general x1, matrix products, per_device(): lax.dot_general(context, piece, (((0,), (0,)), ((), ())), preferred_eleme...  48.4 us
  transfers between devices with their start and end apart: 63, of which 10 were waited for; matrix products, arithmetic and copies ran while one was open for 61% of the time, Pallas kernels for 0%

profile of v2, /device:TPU:0, one launch (start us, length us, event | category | flops | bytes accessed | tf_op | source)
XLA Modules:
  0.0 1269.9 jit_solution(5560190100446425829)
XLA Ops:
  7.2 48.4 %convolution_convert_fusion = bf16[6144,6144]{1,0:T(8,128)(2,1)} fusion(bf16[512,6144]{1,0:T(8,128)(2,1)} %param.9, bf16[512,6144]{1,0:T(8,128)(2,1)} %param.13), kind=kOutput, calls=%fused_computation.14 | convolution fusion | flops 38692454400 | bytes 88080384 | tf_op jit(solution)/shard_map/dot_general | solution.py:34
  60.1 8.9 copy.12
  74.0 8.1 broadcast_in_dim.3
  82.1 1132.6 %while.25 = (s32[]{:T(128)}, bf16[192,3072]{1,0:T(8,128)(2,1)}, bf16[192,3072]{1,0:T(8,128)(2,1)}, f32[512,3072]{1,0:T(8,128)}, f32[512,3072]{1,0:T(8,128)}, /*i...) while((s32[]{:T(128)}, bf16[192,3072]{1,0:T(8,128)(2,1)}, ...), condition=%wide.region_1.2_spmd.clone.clone, body=%wide.region_0.0_spmd.sunk.clone.clone.sunk | while | flops 2422407168 | bytes 96338680 | solution.py:77
  95.9 5.2 fusion.79
  101.1 5.4 select_add_fusion.4
  126.2 5.2 fusion.79
  131.5 8.4 select_add_fusion.4
  159.6 5.2 fusion.79
  164.8 8.4 select_add_fusion.4
  196.0 6.8 select_add_fusion.4
  209.9 35.7 %collective-permute-start = (bf16[192,3072]{1,0:T(8,128)(2,1)S(1)}, bf16[192,3072]{1,0:T(8,128)(2,1)}, u32[]{:S(2)}, u32[]{:S(2)}) collective-permute-start(bf16[192,3072]{1,0:T(8,128)(2,1)S(1)} %copy.23), channel_id=1, source_target_pairs={{0,1},{1,8},{8,9},{9,16},{16,17},{17,24},{24,25},{25,26},{26,27},{... | collective-permute-start | bytes 3538952 | tf_op jit(solution)/shard_map/while/body/eval_jaxpr/ppermute | solution.py:72
  255.3 4.5 fusion.79
  259.8 6.8 select_add_fusion.4
  273.7 30.4 %collective-permute-start = (bf16[192,3072]{1,0:T(8,128)(2,1)S(1)}, bf16[192,3072]{1,0:T(8,128)(2,1)}, u32[]{:S(2)}, u32[]{:S(2)}) collective-permute-start(bf16[192,3072]{1,0:T(8,128)(2,1)S(1)} %copy.23), channel_id=1, source_target_pairs={{0,1},{1,8},{8,9},{9,16},{16,17},{17,24},{24,25},{25,26},{26,27},{... | collective-permute-start | bytes 3538952 | tf_op jit(solution)/shard_map/while/body/eval_jaxpr/ppermute | solution.py:72
  313.7 4.7 fusion.79
  318.3 6.8 select_add_fusion.4
  332.3 32.6 %collective-permute-start = (bf16[192,3072]{1,0:T(8,128)(2,1)S(1)}, bf16[192,3072]{1,0:T(8,128)(2,1)}, u32[]{:S(2)}, u32[]{:S(2)}) collective-permute-start(bf16[192,3072]{1,0:T(8,128)(2,1)S(1)} %copy.23), channel_id=1, source_target_pairs={{0,1},{1,8},{8,9},{9,16},{16,17},{17,24},{24,25},{25,26},{26,27},{... | collective-permute-start | bytes 3538952 | tf_op jit(solution)/shard_map/while/body/eval_jaxpr/ppermute | solution.py:72
  374.4 4.5 fusion.79
  378.9 7.1 select_add_fusion.4
  393.1 31.3 %collective-permute-start = (bf16[192,3072]{1,0:T(8,128)(2,1)S(1)}, bf16[192,3072]{1,0:T(8,128)(2,1)}, u32[]{:S(2)}, u32[]{:S(2)}) collective-permute-start(bf16[192,3072]{1,0:T(8,128)(2,1)S(1)} %copy.23), channel_id=1, source_target_pairs={{0,1},{1,8},{8,9},{9,16},{16,17},{17,24},{24,25},{25,26},{26,27},{... | collective-permute-start | bytes 3538952 | tf_op jit(solution)/shard_map/while/body/eval_jaxpr/ppermute | solution.py:72
  433.9 4.4 fusion.79
  438.3 6.9 select_add_fusion.4
  468.3 6.8 select_add_fusion.4
  494.4 4.6 fusion.79
  499.1 6.8 select_add_fusion.4
  524.2 4.6 fusion.79
  528.9 6.8 select_add_fusion.4
  559.2 7.0 select_add_fusion.4
  584.9 4.5 fusion.79
  589.4 6.8 select_add_fusion.4
  603.3 15.4 %collective-permute-start = (bf16[192,3072]{1,0:T(8,128)(2,1)S(1)}, bf16[192,3072]{1,0:T(8,128)(2,1)}, u32[]{:S(2)}, u32[]{:S(2)}) collective-permute-start(bf16[192,3072]{1,0:T(8,128)(2,1)S(1)} %copy.23), channel_id=1, source_target_pairs={{0,1},{1,8},{8,9},{9,16},{16,17},{17,24},{24,25},{25,26},{26,27},{... | collective-permute-start | bytes 3538952 | tf_op jit(solution)/shard_map/while/body/eval_jaxpr/ppermute | solution.py:72
  628.2 4.5 fusion.79
  632.7 6.8 select_add_fusion.4
  646.6 25.6 %collective-permute-start = (bf16[192,3072]{1,0:T(8,128)(2,1)S(1)}, bf16[192,3072]{1,0:T(8,128)(2,1)}, u32[]{:S(2)}, u32[]{:S(2)}) collective-permute-start(bf16[192,3072]{1,0:T(8,128)(2,1)S(1)} %copy.23), channel_id=1, source_target_pairs={{0,1},{1,8},{8,9},{9,16},{16,17},{17,24},{24,25},{25,26},{26,27},{... | collective-permute-start | bytes 3538952 | tf_op jit(solution)/shard_map/while/body/eval_jaxpr/ppermute | solution.py:72
  681.8 4.6 fusion.79
  686.4 6.8 select_add_fusion.4
  700.3 20.3 %collective-permute-start = (bf16[192,3072]{1,0:T(8,128)(2,1)S(1)}, bf16[192,3072]{1,0:T(8,128)(2,1)}, u32[]{:S(2)}, u32[]{:S(2)}) collective-permute-start(bf16[192,3072]{1,0:T(8,128)(2,1)S(1)} %copy.23), channel_id=1, source_target_pairs={{0,1},{1,8},{8,9},{9,16},{16,17},{17,24},{24,25},{25,26},{26,27},{... | collective-permute-start | bytes 3538952 | tf_op jit(solution)/shard_map/while/body/eval_jaxpr/ppermute | solution.py:72
  730.1 4.5 fusion.79
  734.6 6.9 select_add_fusion.4
  764.3 6.8 select_add_fusion.4
  774.3 6.9 collective-permute-done
  798.1 6.8 select_add_fusion.4
  812.1 18.5 %collective-permute-start = (bf16[192,3072]{1,0:T(8,128)(2,1)S(1)}, bf16[192,3072]{1,0:T(8,128)(2,1)}, u32[]{:S(2)}, u32[]{:S(2)}) collective-permute-start(bf16[192,3072]{1,0:T(8,128)(2,1)S(1)} %copy.23), channel_id=1, source_target_pairs={{0,1},{1,8},{8,9},{9,16},{16,17},{17,24},{24,25},{25,26},{26,27},{... | collective-permute-start | bytes 3538952 | tf_op jit(solution)/shard_map/while/body/eval_jaxpr/ppermute | solution.py:72
  840.1 4.5 fusion.79
  844.6 6.8 select_add_fusion.4
  858.5 4.9 collective-permute-start
  877.4 6.8 select_add_fusion.4
  906.9 6.8 select_add_fusion.4
  936.4 6.8 select_add_fusion.4
  965.9 6.8 select_add_fusion.4
  995.4 6.8 select_add_fusion.4
  1024.9 6.8 select_add_fusion.4
  1054.4 6.8 select_add_fusion.4
  1079.6 4.4 fusion.79
  1084.0 6.8 select_add_fusion.4
  1113.5 6.8 select_add_fusion.4
  1138.6 4.4 fusion.79
  1143.1 6.8 select_add_fusion.4
  1172.6 6.8 select_add_fusion.4
  1202.1 6.8 select_add_fusion.4
  1223.2 8.1 convert_bitcast_fusion
  1231.3 8.6 copy.13
  1251.8 11.3 multiply_subtract_fusion
  (519 shorter events, 570.6 us)
Async XLA Ops:
  7.2 1244.6 %reduce-scatter.2.cloned.1.call-start = ((), (), s32[]{:S(2)}) async-start(), calls=%async_computation.1 | async-start | bytes 77856768 | tf_op jit(solution)/shard_map/reduce_scatter | solution.py:37
  83.5 26.5 %collective-permute-start = (bf16[192,3072]{1,0:T(8,128)(2,1)S(1)}, bf16[192,3072]{1,0:T(8,128)(2,1)}, u32[]{:S(2)}, u32[]{:S(2)}) collective-permute-start(bf16[192,3072]{1,0:T(8,128)(2,1)S(1)} %copy.23), channel_id=1, source_target_pairs={{0,1},{1,8},{8,9},{9,16},{16,17},{17,24},{24,25},{25,26},{26,27},{... | collective-permute-start | bytes 3538952 | tf_op jit(solution)/shard_map/while/body/eval_jaxpr/ppermute | solution.py:72
  86.4 23.6 %collective-permute-start.1 = (bf16[192,3072]{1,0:T(8,128)(2,1)}, bf16[192,3072]{1,0:T(8,128)(2,1)}, u32[]{:S(2)}, u32[]{:S(2)}) collective-permute-start(bf16[192,3072]{1,0:T(8,128)(2,1)} %copy.24), channel_id=1, source_target_pairs={{1,0},{8,1},{9,8},{16,9},{17,16},{24,17},{25,24},{26,25},{27,26},{... | collective-permute-start | bytes 3538952 | tf_op jit(solution)/shard_map/while/body/eval_jaxpr/ppermute | solution.py:73
  114.6 28.8 %collective-permute-start = (bf16[192,3072]{1,0:T(8,128)(2,1)S(1)}, bf16[192,3072]{1,0:T(8,128)(2,1)}, u32[]{:S(2)}, u32[]{:S(2)}) collective-permute-start(bf16[192,3072]{1,0:T(8,128)(2,1)S(1)} %copy.23), channel_id=1, source_target_pairs={{0,1},{1,8},{8,9},{9,16},{16,17},{17,24},{24,25},{25,26},{26,27},{... | collective-permute-start | bytes 3538952 | tf_op jit(solution)/shard_map/while/body/eval_jaxpr/ppermute | solution.py:72
  118.1 25.2 %collective-permute-start.1 = (bf16[192,3072]{1,0:T(8,128)(2,1)}, bf16[192,3072]{1,0:T(8,128)(2,1)}, u32[]{:S(2)}, u32[]{:S(2)}) collective-permute-start(bf16[192,3072]{1,0:T(8,128)(2,1)} %copy.24), channel_id=1, source_target_pairs={{1,0},{8,1},{9,8},{16,9},{17,16},{24,17},{25,24},{26,25},{27,26},{... | collective-permute-start | bytes 3538952 | tf_op jit(solution)/shard_map/while/body/eval_jaxpr/ppermute | solution.py:73
  126.2 13.6 %slice-start = ((s8[6291456]{0:T(1024)(128)(4,1)}), s8[2097152]{0:T(1024)(128)(4,1)S(1)}, s32[]{:S(2)}) async-start(s8[6291456]{0:T(1024)(128)(4,1)} %bitcast.30), calls=%async_computation.2 | async-start | bytes 4194304 | tf_op jit(solution)/shard_map/while
  148.0 28.5 %collective-permute-start = (bf16[192,3072]{1,0:T(8,128)(2,1)S(1)}, bf16[192,3072]{1,0:T(8,128)(2,1)}, u32[]{:S(2)}, u32[]{:S(2)}) collective-permute-start(bf16[192,3072]{1,0:T(8,128)(2,1)S(1)} %copy.23), channel_id=1, source_target_pairs={{0,1},{1,8},{8,9},{9,16},{16,17},{17,24},{24,25},{25,26},{26,27},{... | collective-permute-start | bytes 3538952 | tf_op jit(solution)/shard_map/while/body/eval_jaxpr/ppermute | solution.py:72
  151.6 24.9 %collective-permute-start.1 = (bf16[192,3072]{1,0:T(8,128)(2,1)}, bf16[192,3072]{1,0:T(8,128)(2,1)}, u32[]{:S(2)}, u32[]{:S(2)}) collective-permute-start(bf16[192,3072]{1,0:T(8,128)(2,1)} %copy.24), channel_id=1, source_target_pairs={{1,0},{8,1},{9,8},{16,9},{17,16},{24,17},{25,24},{26,25},{27,26},{... | collective-permute-start | bytes 3538952 | tf_op jit(solution)/shard_map/while/body/eval_jaxpr/ppermute | solution.py:73
  180.4 25.7 %collective-permute-start = (bf16[192,3072]{1,0:T(8,128)(2,1)S(1)}, bf16[192,3072]{1,0:T(8,128)(2,1)}, u32[]{:S(2)}, u32[]{:S(2)}) collective-permute-start(bf16[192,3072]{1,0:T(8,128)(2,1)S(1)} %copy.23), channel_id=1, source_target_pairs={{0,1},{1,8},{8,9},{9,16},{16,17},{17,24},{24,25},{25,26},{26,27},{... | collective-permute-start | bytes 3538952 | tf_op jit(solution)/shard_map/while/body/eval_jaxpr/ppermute | solution.py:72
  183.4 22.6 %collective-permute-start.1 = (bf16[192,3072]{1,0:T(8,128)(2,1)}, bf16[192,3072]{1,0:T(8,128)(2,1)}, u32[]{:S(2)}, u32[]{:S(2)}) collective-permute-start(bf16[192,3072]{1,0:T(8,128)(2,1)} %copy.24), channel_id=1, source_target_pairs={{1,0},{8,1},{9,8},{16,9},{17,16},{24,17},{25,24},{26,25},{27,26},{... | collective-permute-start | bytes 3538952 | tf_op jit(solution)/shard_map/while/body/eval_jaxpr/ppermute | solution.py:73
  209.9 59.9 %collective-permute-start = (bf16[192,3072]{1,0:T(8,128)(2,1)S(1)}, bf16[192,3072]{1,0:T(8,128)(2,1)}, u32[]{:S(2)}, u32[]{:S(2)}) collective-permute-start(bf16[192,3072]{1,0:T(8,128)(2,1)S(1)} %copy.23), channel_id=1, source_target_pairs={{0,1},{1,8},{8,9},{9,16},{16,17},{17,24},{24,25},{25,26},{26,27},{... | collective-permute-start | bytes 3538952 | tf_op jit(solution)/shard_map/while/body/eval_jaxpr/ppermute | solution.py:72
  248.2 21.7 %collective-permute-start.1 = (bf16[192,3072]{1,0:T(8,128)(2,1)}, bf16[192,3072]{1,0:T(8,128)(2,1)}, u32[]{:S(2)}, u32[]{:S(2)}) collective-permute-start(bf16[192,3072]{1,0:T(8,128)(2,1)} %copy.24), channel_id=1, source_target_pairs={{1,0},{8,1},{9,8},{16,9},{17,16},{24,17},{25,24},{26,25},{27,26},{... | collective-permute-start | bytes 3538952 | tf_op jit(solution)/shard_map/while/body/eval_jaxpr/ppermute | solution.py:73
  273.7 54.7 %collective-permute-start = (bf16[192,3072]{1,0:T(8,128)(2,1)S(1)}, bf16[192,3072]{1,0:T(8,128)(2,1)}, u32[]{:S(2)}, u32[]{:S(2)}) collective-permute-start(bf16[192,3072]{1,0:T(8,128)(2,1)S(1)} %copy.23), channel_id=1, source_target_pairs={{0,1},{1,8},{8,9},{9,16},{16,17},{17,24},{24,25},{25,26},{26,27},{... | collective-permute-start | bytes 3538952 | tf_op jit(solution)/shard_map/while/body/eval_jaxpr/ppermute | solution.py:72
  306.5 22.5 %collective-permute-start.1 = (bf16[192,3072]{1,0:T(8,128)(2,1)}, bf16[192,3072]{1,0:T(8,128)(2,1)}, u32[]{:S(2)}, u32[]{:S(2)}) collective-permute-start(bf16[192,3072]{1,0:T(8,128)(2,1)} %copy.24), channel_id=1, source_target_pairs={{1,0},{8,1},{9,8},{16,9},{17,16},{24,17},{25,24},{26,25},{27,26},{... | collective-permute-start | bytes 3538952 | tf_op jit(solution)/shard_map/while/body/eval_jaxpr/ppermute | solution.py:73
  332.3 57.0 %collective-permute-start = (bf16[192,3072]{1,0:T(8,128)(2,1)S(1)}, bf16[192,3072]{1,0:T(8,128)(2,1)}, u32[]{:S(2)}, u32[]{:S(2)}) collective-permute-start(bf16[192,3072]{1,0:T(8,128)(2,1)S(1)} %copy.23), channel_id=1, source_target_pairs={{0,1},{1,8},{8,9},{9,16},{16,17},{17,24},{24,25},{25,26},{26,27},{... | collective-permute-start | bytes 3538952 | tf_op jit(solution)/shard_map/while/body/eval_jaxpr/ppermute | solution.py:72
  367.2 22.5 %collective-permute-start.1 = (bf16[192,3072]{1,0:T(8,128)(2,1)}, bf16[192,3072]{1,0:T(8,128)(2,1)}, u32[]{:S(2)}, u32[]{:S(2)}) collective-permute-start(bf16[192,3072]{1,0:T(8,128)(2,1)} %copy.24), channel_id=1, source_target_pairs={{1,0},{8,1},{9,8},{16,9},{17,16},{24,17},{25,24},{26,25},{27,26},{... | collective-permute-start | bytes 3538952 | tf_op jit(solution)/shard_map/while/body/eval_jaxpr/ppermute | solution.py:73
  393.1 55.5 %collective-permute-start = (bf16[192,3072]{1,0:T(8,128)(2,1)S(1)}, bf16[192,3072]{1,0:T(8,128)(2,1)}, u32[]{:S(2)}, u32[]{:S(2)}) collective-permute-start(bf16[192,3072]{1,0:T(8,128)(2,1)S(1)} %copy.23), channel_id=1, source_target_pairs={{0,1},{1,8},{8,9},{9,16},{16,17},{17,24},{24,25},{25,26},{26,27},{... | collective-permute-start | bytes 3538952 | tf_op jit(solution)/shard_map/while/body/eval_jaxpr/ppermute | solution.py:72
  426.8 21.8 %collective-permute-start.1 = (bf16[192,3072]{1,0:T(8,128)(2,1)}, bf16[192,3072]{1,0:T(8,128)(2,1)}, u32[]{:S(2)}, u32[]{:S(2)}) collective-permute-start(bf16[192,3072]{1,0:T(8,128)(2,1)} %copy.24), channel_id=1, source_target_pairs={{1,0},{8,1},{9,8},{16,9},{17,16},{24,17},{25,24},{26,25},{27,26},{... | collective-permute-start | bytes 3538952 | tf_op jit(solution)/shard_map/while/body/eval_jaxpr/ppermute | solution.py:73
  452.5 25.9 %collective-permute-start = (bf16[192,3072]{1,0:T(8,128)(2,1)S(1)}, bf16[192,3072]{1,0:T(8,128)(2,1)}, u32[]{:S(2)}, u32[]{:S(2)}) collective-permute-start(bf16[192,3072]{1,0:T(8,128)(2,1)S(1)} %copy.23), channel_id=1, source_target_pairs={{0,1},{1,8},{8,9},{9,16},{16,17},{17,24},{24,25},{25,26},{26,27},{... | collective-permute-start | bytes 3538952 | tf_op jit(solution)/shard_map/while/body/eval_jaxpr/ppermute | solution.py:72
  455.6 25.8 %collective-permute-start.1 = (bf16[192,3072]{1,0:T(8,128)(2,1)}, bf16[192,3072]{1,0:T(8,128)(2,1)}, u32[]{:S(2)}, u32[]{:S(2)}) collective-permute-start(bf16[192,3072]{1,0:T(8,128)(2,1)} %copy.24), channel_id=1, source_target_pairs={{1,0},{8,1},{9,8},{16,9},{17,16},{24,17},{25,24},{26,25},{27,26},{... | collective-permute-start | bytes 3538952 | tf_op jit(solution)/shard_map/while/body/eval_jaxpr/ppermute | solution.py:73
  482.6 26.4 %collective-permute-start = (bf16[192,3072]{1,0:T(8,128)(2,1)S(1)}, bf16[192,3072]{1,0:T(8,128)(2,1)}, u32[]{:S(2)}, u32[]{:S(2)}) collective-permute-start(bf16[192,3072]{1,0:T(8,128)(2,1)S(1)} %copy.23), channel_id=1, source_target_pairs={{0,1},{1,8},{8,9},{9,16},{16,17},{17,24},{24,25},{25,26},{26,27},{... | collective-permute-start | bytes 3538952 | tf_op jit(solution)/shard_map/while/body/eval_jaxpr/ppermute | solution.py:72
  485.0 24.7 %collective-permute-start.1 = (bf16[192,3072]{1,0:T(8,128)(2,1)}, bf16[192,3072]{1,0:T(8,128)(2,1)}, u32[]{:S(2)}, u32[]{:S(2)}) collective-permute-start(bf16[192,3072]{1,0:T(8,128)(2,1)} %copy.24), channel_id=1, source_target_pairs={{1,0},{8,1},{9,8},{16,9},{17,16},{24,17},{25,24},{26,25},{27,26},{... | collective-permute-start | bytes 3538952 | tf_op jit(solution)/shard_map/while/body/eval_jaxpr/ppermute | solution.py:73
  513.0 25.9 %collective-permute-start = (bf16[192,3072]{1,0:T(8,128)(2,1)S(1)}, bf16[192,3072]{1,0:T(8,128)(2,1)}, u32[]{:S(2)}, u32[]{:S(2)}) collective-permute-start(bf16[192,3072]{1,0:T(8,128)(2,1)S(1)} %copy.23), channel_id=1, source_target_pairs={{0,1},{1,8},{8,9},{9,16},{16,17},{17,24},{24,25},{25,26},{26,27},{... | collective-permute-start | bytes 3538952 | tf_op jit(solution)/shard_map/while/body/eval_jaxpr/ppermute | solution.py:72
  515.4 26.6 %collective-permute-start.1 = (bf16[192,3072]{1,0:T(8,128)(2,1)}, bf16[192,3072]{1,0:T(8,128)(2,1)}, u32[]{:S(2)}, u32[]{:S(2)}) collective-permute-start(bf16[192,3072]{1,0:T(8,128)(2,1)} %copy.24), channel_id=1, source_target_pairs={{1,0},{8,1},{9,8},{16,9},{17,16},{24,17},{25,24},{26,25},{27,26},{... | collective-permute-start | bytes 3538952 | tf_op jit(solution)/shard_map/while/body/eval_jaxpr/ppermute | solution.py:73
  543.3 28.9 %collective-permute-start = (bf16[192,3072]{1,0:T(8,128)(2,1)S(1)}, bf16[192,3072]{1,0:T(8,128)(2,1)}, u32[]{:S(2)}, u32[]{:S(2)}) collective-permute-start(bf16[192,3072]{1,0:T(8,128)(2,1)S(1)} %copy.23), channel_id=1, source_target_pairs={{0,1},{1,8},{8,9},{9,16},{16,17},{17,24},{24,25},{25,26},{26,27},{... | collective-permute-start | bytes 3538952 | tf_op jit(solution)/shard_map/while/body/eval_jaxpr/ppermute | solution.py:72
  545.7 26.5 %collective-permute-start.1 = (bf16[192,3072]{1,0:T(8,128)(2,1)}, bf16[192,3072]{1,0:T(8,128)(2,1)}, u32[]{:S(2)}, u32[]{:S(2)}) collective-permute-start(bf16[192,3072]{1,0:T(8,128)(2,1)} %copy.24), channel_id=1, source_target_pairs={{1,0},{8,1},{9,8},{16,9},{17,16},{24,17},{25,24},{26,25},{27,26},{... | collective-permute-start | bytes 3538952 | tf_op jit(solution)/shard_map/while/body/eval_jaxpr/ppermute | solution.py:73
  573.5 25.9 %collective-permute-start = (bf16[192,3072]{1,0:T(8,128)(2,1)S(1)}, bf16[192,3072]{1,0:T(8,128)(2,1)}, u32[]{:S(2)}, u32[]{:S(2)}) collective-permute-start(bf16[192,3072]{1,0:T(8,128)(2,1)S(1)} %copy.23), channel_id=1, source_target_pairs={{0,1},{1,8},{8,9},{9,16},{16,17},{17,24},{24,25},{25,26},{26,27},{... | collective-permute-start | bytes 3538952 | tf_op jit(solution)/shard_map/while/body/eval_jaxpr/ppermute | solution.py:72
  575.9 24.4 %collective-permute-start.1 = (bf16[192,3072]{1,0:T(8,128)(2,1)}, bf16[192,3072]{1,0:T(8,128)(2,1)}, u32[]{:S(2)}, u32[]{:S(2)}) collective-permute-start(bf16[192,3072]{1,0:T(8,128)(2,1)} %copy.24), channel_id=1, source_target_pairs={{1,0},{8,1},{9,8},{16,9},{17,16},{24,17},{25,24},{26,25},{27,26},{... | collective-permute-start | bytes 3538952 | tf_op jit(solution)/shard_map/while/body/eval_jaxpr/ppermute | solution.py:73
  603.3 39.5 %collective-permute-start = (bf16[192,3072]{1,0:T(8,128)(2,1)S(1)}, bf16[192,3072]{1,0:T(8,128)(2,1)}, u32[]{:S(2)}, u32[]{:S(2)}) collective-permute-start(bf16[192,3072]{1,0:T(8,128)(2,1)S(1)} %copy.23), channel_id=1, source_target_pairs={{0,1},{1,8},{8,9},{9,16},{16,17},{17,24},{24,25},{25,26},{26,27},{... | collective-permute-start | bytes 3538952 | tf_op jit(solution)/shard_map/while/body/eval_jaxpr/ppermute | solution.py:72
  621.1 21.7 %collective-permute-start.1 = (bf16[192,3072]{1,0:T(8,128)(2,1)}, bf16[192,3072]{1,0:T(8,128)(2,1)}, u32[]{:S(2)}, u32[]{:S(2)}) collective-permute-start(bf16[192,3072]{1,0:T(8,128)(2,1)} %copy.24), channel_id=1, source_target_pairs={{1,0},{8,1},{9,8},{16,9},{17,16},{24,17},{25,24},{26,25},{27,26},{... | collective-permute-start | bytes 3538952 | tf_op jit(solution)/shard_map/while/body/eval_jaxpr/ppermute | solution.py:73
  646.6 49.8 %collective-permute-start = (bf16[192,3072]{1,0:T(8,128)(2,1)S(1)}, bf16[192,3072]{1,0:T(8,128)(2,1)}, u32[]{:S(2)}, u32[]{:S(2)}) collective-permute-start(bf16[192,3072]{1,0:T(8,128)(2,1)S(1)} %copy.23), channel_id=1, source_target_pairs={{0,1},{1,8},{8,9},{9,16},{16,17},{17,24},{24,25},{25,26},{26,27},{... | collective-permute-start | bytes 3538952 | tf_op jit(solution)/shard_map/while/body/eval_jaxpr/ppermute | solution.py:72
  674.7 22.5 %collective-permute-start.1 = (bf16[192,3072]{1,0:T(8,128)(2,1)}, bf16[192,3072]{1,0:T(8,128)(2,1)}, u32[]{:S(2)}, u32[]{:S(2)}) collective-permute-start(bf16[192,3072]{1,0:T(8,128)(2,1)} %copy.24), channel_id=1, source_target_pairs={{1,0},{8,1},{9,8},{16,9},{17,16},{24,17},{25,24},{26,25},{27,26},{... | collective-permute-start | bytes 3538952 | tf_op jit(solution)/shard_map/while/body/eval_jaxpr/ppermute | solution.py:73
  700.3 44.4 %collective-permute-start = (bf16[192,3072]{1,0:T(8,128)(2,1)S(1)}, bf16[192,3072]{1,0:T(8,128)(2,1)}, u32[]{:S(2)}, u32[]{:S(2)}) collective-permute-start(bf16[192,3072]{1,0:T(8,128)(2,1)S(1)} %copy.23), channel_id=1, source_target_pairs={{0,1},{1,8},{8,9},{9,16},{16,17},{17,24},{24,25},{25,26},{26,27},{... | collective-permute-start | bytes 3538952 | tf_op jit(solution)/shard_map/while/body/eval_jaxpr/ppermute | solution.py:72
  723.0 21.8 %collective-permute-start.1 = (bf16[192,3072]{1,0:T(8,128)(2,1)}, bf16[192,3072]{1,0:T(8,128)(2,1)}, u32[]{:S(2)}, u32[]{:S(2)}) collective-permute-start(bf16[192,3072]{1,0:T(8,128)(2,1)} %copy.24), channel_id=1, source_target_pairs={{1,0},{8,1},{9,8},{16,9},{17,16},{24,17},{25,24},{26,25},{27,26},{... | collective-permute-start | bytes 3538952 | tf_op jit(solution)/shard_map/while/body/eval_jaxpr/ppermute | solution.py:73
  748.6 32.6 %collective-permute-start = (bf16[192,3072]{1,0:T(8,128)(2,1)S(1)}, bf16[192,3072]{1,0:T(8,128)(2,1)}, u32[]{:S(2)}, u32[]{:S(2)}) collective-permute-start(bf16[192,3072]{1,0:T(8,128)(2,1)S(1)} %copy.23), channel_id=1, source_target_pairs={{0,1},{1,8},{8,9},{9,16},{16,17},{17,24},{24,25},{25,26},{26,27},{... | collective-permute-start | bytes 3538952 | tf_op jit(solution)/shard_map/while/body/eval_jaxpr/ppermute | solution.py:72
  751.4 29.8 %collective-permute-start.1 = (bf16[192,3072]{1,0:T(8,128)(2,1)}, bf16[192,3072]{1,0:T(8,128)(2,1)}, u32[]{:S(2)}, u32[]{:S(2)}) collective-permute-start(bf16[192,3072]{1,0:T(8,128)(2,1)} %copy.24), channel_id=1, source_target_pairs={{1,0},{8,1},{9,8},{16,9},{17,16},{24,17},{25,24},{26,25},{27,26},{... | collective-permute-start | bytes 3538952 | tf_op jit(solution)/shard_map/while/body/eval_jaxpr/ppermute | solution.py:73
  782.5 25.8 %collective-permute-start = (bf16[192,3072]{1,0:T(8,128)(2,1)S(1)}, bf16[192,3072]{1,0:T(8,128)(2,1)}, u32[]{:S(2)}, u32[]{:S(2)}) collective-permute-start(bf16[192,3072]{1,0:T(8,128)(2,1)S(1)} %copy.23), channel_id=1, source_target_pairs={{0,1},{1,8},{8,9},{9,16},{16,17},{17,24},{24,25},{25,26},{26,27},{... | collective-permute-start | bytes 3538952 | tf_op jit(solution)/shard_map/while/body/eval_jaxpr/ppermute | solution.py:72
  784.9 24.2 %collective-permute-start.1 = (bf16[192,3072]{1,0:T(8,128)(2,1)}, bf16[192,3072]{1,0:T(8,128)(2,1)}, u32[]{:S(2)}, u32[]{:S(2)}) collective-permute-start(bf16[192,3072]{1,0:T(8,128)(2,1)} %copy.24), channel_id=1, source_target_pairs={{1,0},{8,1},{9,8},{16,9},{17,16},{24,17},{25,24},{26,25},{27,26},{... | collective-permute-start | bytes 3538952 | tf_op jit(solution)/shard_map/while/body/eval_jaxpr/ppermute | solution.py:73
  812.1 42.5 %collective-permute-start = (bf16[192,3072]{1,0:T(8,128)(2,1)S(1)}, bf16[192,3072]{1,0:T(8,128)(2,1)}, u32[]{:S(2)}, u32[]{:S(2)}) collective-permute-start(bf16[192,3072]{1,0:T(8,128)(2,1)S(1)} %copy.23), channel_id=1, source_target_pairs={{0,1},{1,8},{8,9},{9,16},{16,17},{17,24},{24,25},{25,26},{26,27},{... | collective-permute-start | bytes 3538952 | tf_op jit(solution)/shard_map/while/body/eval_jaxpr/ppermute | solution.py:72
  833.0 21.6 %collective-permute-start.1 = (bf16[192,3072]{1,0:T(8,128)(2,1)}, bf16[192,3072]{1,0:T(8,128)(2,1)}, u32[]{:S(2)}, u32[]{:S(2)}) collective-permute-start(bf16[192,3072]{1,0:T(8,128)(2,1)} %copy.24), channel_id=1, source_target_pairs={{1,0},{8,1},{9,8},{16,9},{17,16},{24,17},{25,24},{26,25},{27,26},{... | collective-permute-start | bytes 3538952 | tf_op jit(solution)/shard_map/while/body/eval_jaxpr/ppermute | solution.py:73
  858.5 28.8 %collective-permute-start = (bf16[192,3072]{1,0:T(8,128)(2,1)S(1)}, bf16[192,3072]{1,0:T(8,128)(2,1)}, u32[]{:S(2)}, u32[]{:S(2)}) collective-permute-start(bf16[192,3072]{1,0:T(8,128)(2,1)S(1)} %copy.23), channel_id=1, source_target_pairs={{0,1},{1,8},{8,9},{9,16},{16,17},{17,24},{24,25},{25,26},{26,27},{... | collective-permute-start | bytes 3538952 | tf_op jit(solution)/shard_map/while/body/eval_jaxpr/ppermute | solution.py:72
  865.8 21.6 %collective-permute-start.1 = (bf16[192,3072]{1,0:T(8,128)(2,1)}, bf16[192,3072]{1,0:T(8,128)(2,1)}, u32[]{:S(2)}, u32[]{:S(2)}) collective-permute-start(bf16[192,3072]{1,0:T(8,128)(2,1)} %copy.24), channel_id=1, source_target_pairs={{1,0},{8,1},{9,8},{16,9},{17,16},{24,17},{25,24},{26,25},{27,26},{... | collective-permute-start | bytes 3538952 | tf_op jit(solution)/shard_map/while/body/eval_jaxpr/ppermute | solution.py:73
  891.2 25.7 %collective-permute-start = (bf16[192,3072]{1,0:T(8,128)(2,1)S(1)}, bf16[192,3072]{1,0:T(8,128)(2,1)}, u32[]{:S(2)}, u32[]{:S(2)}) collective-permute-start(bf16[192,3072]{1,0:T(8,128)(2,1)S(1)} %copy.23), channel_id=1, source_target_pairs={{0,1},{1,8},{8,9},{9,16},{16,17},{17,24},{24,25},{25,26},{26,27},{... | collective-permute-start | bytes 3538952 | tf_op jit(solution)/shard_map/while/body/eval_jaxpr/ppermute | solution.py:72
  894.1 22.9 %collective-permute-start.1 = (bf16[192,3072]{1,0:T(8,128)(2,1)}, bf16[192,3072]{1,0:T(8,128)(2,1)}, u32[]{:S(2)}, u32[]{:S(2)}) collective-permute-start(bf16[192,3072]{1,0:T(8,128)(2,1)} %copy.24), channel_id=1, source_target_pairs={{1,0},{8,1},{9,8},{16,9},{17,16},{24,17},{25,24},{26,25},{27,26},{... | collective-permute-start | bytes 3538952 | tf_op jit(solution)/shard_map/while/body/eval_jaxpr/ppermute | solution.py:73
  920.8 25.6 %collective-permute-start = (bf16[192,3072]{1,0:T(8,128)(2,1)S(1)}, bf16[192,3072]{1,0:T(8,128)(2,1)}, u32[]{:S(2)}, u32[]{:S(2)}) collective-permute-start(bf16[192,3072]{1,0:T(8,128)(2,1)S(1)} %copy.23), channel_id=1, source_target_pairs={{0,1},{1,8},{8,9},{9,16},{16,17},{17,24},{24,25},{25,26},{26,27},{... | collective-permute-start | bytes 3538952 | tf_op jit(solution)/shard_map/while/body/eval_jaxpr/ppermute | solution.py:72
  923.2 23.3 %collective-permute-start.1 = (bf16[192,3072]{1,0:T(8,128)(2,1)}, bf16[192,3072]{1,0:T(8,128)(2,1)}, u32[]{:S(2)}, u32[]{:S(2)}) collective-permute-start(bf16[192,3072]{1,0:T(8,128)(2,1)} %copy.24), channel_id=1, source_target_pairs={{1,0},{8,1},{9,8},{16,9},{17,16},{24,17},{25,24},{26,25},{27,26},{... | collective-permute-start | bytes 3538952 | tf_op jit(solution)/shard_map/while/body/eval_jaxpr/ppermute | solution.py:73
  950.3 25.6 %collective-permute-start = (bf16[192,3072]{1,0:T(8,128)(2,1)S(1)}, bf16[192,3072]{1,0:T(8,128)(2,1)}, u32[]{:S(2)}, u32[]{:S(2)}) collective-permute-start(bf16[192,3072]{1,0:T(8,128)(2,1)S(1)} %copy.23), channel_id=1, source_target_pairs={{0,1},{1,8},{8,9},{9,16},{16,17},{17,24},{24,25},{25,26},{26,27},{... | collective-permute-start | bytes 3538952 | tf_op jit(solution)/shard_map/while/body/eval_jaxpr/ppermute | solution.py:72
  952.7 23.3 %collective-permute-start.1 = (bf16[192,3072]{1,0:T(8,128)(2,1)}, bf16[192,3072]{1,0:T(8,128)(2,1)}, u32[]{:S(2)}, u32[]{:S(2)}) collective-permute-start(bf16[192,3072]{1,0:T(8,128)(2,1)} %copy.24), channel_id=1, source_target_pairs={{1,0},{8,1},{9,8},{16,9},{17,16},{24,17},{25,24},{26,25},{27,26},{... | collective-permute-start | bytes 3538952 | tf_op jit(solution)/shard_map/while/body/eval_jaxpr/ppermute | solution.py:73
  979.8 25.6 %collective-permute-start = (bf16[192,3072]{1,0:T(8,128)(2,1)S(1)}, bf16[192,3072]{1,0:T(8,128)(2,1)}, u32[]{:S(2)}, u32[]{:S(2)}) collective-permute-start(bf16[192,3072]{1,0:T(8,128)(2,1)S(1)} %copy.23), channel_id=1, source_target_pairs={{0,1},{1,8},{8,9},{9,16},{16,17},{17,24},{24,25},{25,26},{26,27},{... | collective-permute-start | bytes 3538952 | tf_op jit(solution)/shard_map/while/body/eval_jaxpr/ppermute | solution.py:72
  982.2 23.3 %collective-permute-start.1 = (bf16[192,3072]{1,0:T(8,128)(2,1)}, bf16[192,3072]{1,0:T(8,128)(2,1)}, u32[]{:S(2)}, u32[]{:S(2)}) collective-permute-start(bf16[192,3072]{1,0:T(8,128)(2,1)} %copy.24), channel_id=1, source_target_pairs={{1,0},{8,1},{9,8},{16,9},{17,16},{24,17},{25,24},{26,25},{27,26},{... | collective-permute-start | bytes 3538952 | tf_op jit(solution)/shard_map/while/body/eval_jaxpr/ppermute | solution.py:73
  1009.3 25.6 %collective-permute-start = (bf16[192,3072]{1,0:T(8,128)(2,1)S(1)}, bf16[192,3072]{1,0:T(8,128)(2,1)}, u32[]{:S(2)}, u32[]{:S(2)}) collective-permute-start(bf16[192,3072]{1,0:T(8,128)(2,1)S(1)} %copy.23), channel_id=1, source_target_pairs={{0,1},{1,8},{8,9},{9,16},{16,17},{17,24},{24,25},{25,26},{26,27},{... | collective-permute-start | bytes 3538952 | tf_op jit(solution)/shard_map/while/body/eval_jaxpr/ppermute | solution.py:72
  1011.7 23.3 %collective-permute-start.1 = (bf16[192,3072]{1,0:T(8,128)(2,1)}, bf16[192,3072]{1,0:T(8,128)(2,1)}, u32[]{:S(2)}, u32[]{:S(2)}) collective-permute-start(bf16[192,3072]{1,0:T(8,128)(2,1)} %copy.24), channel_id=1, source_target_pairs={{1,0},{8,1},{9,8},{16,9},{17,16},{24,17},{25,24},{26,25},{27,26},{... | collective-permute-start | bytes 3538952 | tf_op jit(solution)/shard_map/while/body/eval_jaxpr/ppermute | solution.py:73
  1038.8 25.6 %collective-permute-start = (bf16[192,3072]{1,0:T(8,128)(2,1)S(1)}, bf16[192,3072]{1,0:T(8,128)(2,1)}, u32[]{:S(2)}, u32[]{:S(2)}) collective-permute-start(bf16[192,3072]{1,0:T(8,128)(2,1)S(1)} %copy.23), channel_id=1, source_target_pairs={{0,1},{1,8},{8,9},{9,16},{16,17},{17,24},{24,25},{25,26},{26,27},{... | collective-permute-start | bytes 3538952 | tf_op jit(solution)/shard_map/while/body/eval_jaxpr/ppermute | solution.py:72
  1041.2 23.3 %collective-permute-start.1 = (bf16[192,3072]{1,0:T(8,128)(2,1)}, bf16[192,3072]{1,0:T(8,128)(2,1)}, u32[]{:S(2)}, u32[]{:S(2)}) collective-permute-start(bf16[192,3072]{1,0:T(8,128)(2,1)} %copy.24), channel_id=1, source_target_pairs={{1,0},{8,1},{9,8},{16,9},{17,16},{24,17},{25,24},{26,25},{27,26},{... | collective-permute-start | bytes 3538952 | tf_op jit(solution)/shard_map/while/body/eval_jaxpr/ppermute | solution.py:73
  1068.3 25.7 %collective-permute-start = (bf16[192,3072]{1,0:T(8,128)(2,1)S(1)}, bf16[192,3072]{1,0:T(8,128)(2,1)}, u32[]{:S(2)}, u32[]{:S(2)}) collective-permute-start(bf16[192,3072]{1,0:T(8,128)(2,1)S(1)} %copy.23), channel_id=1, source_target_pairs={{0,1},{1,8},{8,9},{9,16},{16,17},{17,24},{24,25},{25,26},{26,27},{... | collective-permute-start | bytes 3538952 | tf_op jit(solution)/shard_map/while/body/eval_jaxpr/ppermute | solution.py:72
  1070.7 23.3 %collective-permute-start.1 = (bf16[192,3072]{1,0:T(8,128)(2,1)}, bf16[192,3072]{1,0:T(8,128)(2,1)}, u32[]{:S(2)}, u32[]{:S(2)}) collective-permute-start(bf16[192,3072]{1,0:T(8,128)(2,1)} %copy.24), channel_id=1, source_target_pairs={{1,0},{8,1},{9,8},{16,9},{17,16},{24,17},{25,24},{26,25},{27,26},{... | collective-permute-start | bytes 3538952 | tf_op jit(solution)/shard_map/while/body/eval_jaxpr/ppermute | solution.py:73
  1097.9 25.7 %collective-permute-start = (bf16[192,3072]{1,0:T(8,128)(2,1)S(1)}, bf16[192,3072]{1,0:T(8,128)(2,1)}, u32[]{:S(2)}, u32[]{:S(2)}) collective-permute-start(bf16[192,3072]{1,0:T(8,128)(2,1)S(1)} %copy.23), channel_id=1, source_target_pairs={{0,1},{1,8},{8,9},{9,16},{16,17},{17,24},{24,25},{25,26},{26,27},{... | collective-permute-start | bytes 3538952 | tf_op jit(solution)/shard_map/while/body/eval_jaxpr/ppermute | solution.py:72
  1100.2 23.3 %collective-permute-start.1 = (bf16[192,3072]{1,0:T(8,128)(2,1)}, bf16[192,3072]{1,0:T(8,128)(2,1)}, u32[]{:S(2)}, u32[]{:S(2)}) collective-permute-start(bf16[192,3072]{1,0:T(8,128)(2,1)} %copy.24), channel_id=1, source_target_pairs={{1,0},{8,1},{9,8},{16,9},{17,16},{24,17},{25,24},{26,25},{27,26},{... | collective-permute-start | bytes 3538952 | tf_op jit(solution)/shard_map/while/body/eval_jaxpr/ppermute | solution.py:73
  1127.4 25.7 %collective-permute-start = (bf16[192,3072]{1,0:T(8,128)(2,1)S(1)}, bf16[192,3072]{1,0:T(8,128)(2,1)}, u32[]{:S(2)}, u32[]{:S(2)}) collective-permute-start(bf16[192,3072]{1,0:T(8,128)(2,1)S(1)} %copy.23), channel_id=1, source_target_pairs={{0,1},{1,8},{8,9},{9,16},{16,17},{17,24},{24,25},{25,26},{26,27},{... | collective-permute-start | bytes 3538952 | tf_op jit(solution)/shard_map/while/body/eval_jaxpr/ppermute | solution.py:72
  1129.7 23.3 %collective-permute-start.1 = (bf16[192,3072]{1,0:T(8,128)(2,1)}, bf16[192,3072]{1,0:T(8,128)(2,1)}, u32[]{:S(2)}, u32[]{:S(2)}) collective-permute-start(bf16[192,3072]{1,0:T(8,128)(2,1)} %copy.24), channel_id=1, source_target_pairs={{1,0},{8,1},{9,8},{16,9},{17,16},{24,17},{25,24},{26,25},{27,26},{... | collective-permute-start | bytes 3538952 | tf_op jit(solution)/shard_map/while/body/eval_jaxpr/ppermute | solution.py:73
  1156.9 25.6 %collective-permute-start = (bf16[192,3072]{1,0:T(8,128)(2,1)S(1)}, bf16[192,3072]{1,0:T(8,128)(2,1)}, u32[]{:S(2)}, u32[]{:S(2)}) collective-permute-start(bf16[192,3072]{1,0:T(8,128)(2,1)S(1)} %copy.23), channel_id=1, source_target_pairs={{0,1},{1,8},{8,9},{9,16},{16,17},{17,24},{24,25},{25,26},{26,27},{... | collective-permute-start | bytes 3538952 | tf_op jit(solution)/shard_map/while/body/eval_jaxpr/ppermute | solution.py:72
  1159.3 23.3 %collective-permute-start.1 = (bf16[192,3072]{1,0:T(8,128)(2,1)}, bf16[192,3072]{1,0:T(8,128)(2,1)}, u32[]{:S(2)}, u32[]{:S(2)}) collective-permute-start(bf16[192,3072]{1,0:T(8,128)(2,1)} %copy.24), channel_id=1, source_target_pairs={{1,0},{8,1},{9,8},{16,9},{17,16},{24,17},{25,24},{26,25},{27,26},{... | collective-permute-start | bytes 3538952 | tf_op jit(solution)/shard_map/while/body/eval_jaxpr/ppermute | solution.py:73
  1186.4 25.6 %collective-permute-start = (bf16[192,3072]{1,0:T(8,128)(2,1)S(1)}, bf16[192,3072]{1,0:T(8,128)(2,1)}, u32[]{:S(2)}, u32[]{:S(2)}) collective-permute-start(bf16[192,3072]{1,0:T(8,128)(2,1)S(1)} %copy.23), channel_id=1, source_target_pairs={{0,1},{1,8},{8,9},{9,16},{16,17},{17,24},{24,25},{25,26},{26,27},{... | collective-permute-start | bytes 3538952 | tf_op jit(solution)/shard_map/while/body/eval_jaxpr/ppermute | solution.py:72
  1188.8 23.3 %collective-permute-start.1 = (bf16[192,3072]{1,0:T(8,128)(2,1)}, bf16[192,3072]{1,0:T(8,128)(2,1)}, u32[]{:S(2)}, u32[]{:S(2)}) collective-permute-start(bf16[192,3072]{1,0:T(8,128)(2,1)} %copy.24), channel_id=1, source_target_pairs={{1,0},{8,1},{9,8},{16,9},{17,16},{24,17},{25,24},{26,25},{27,26},{... | collective-permute-start | bytes 3538952 | tf_op jit(solution)/shard_map/while/body/eval_jaxpr/ppermute | solution.py:73
  (94 other events, 642.7 us)
Sparse Core Ops, SparseCore 0:
  55.8 802.8 reduce-scatter.1

commit v3 on v2

--- a/solution.py
+++ b/solution.py
@@ -38,49 +38,46 @@
             weight_grad.astype(jnp.bfloat16), "dp", scatter_dimension=0, tiled=True
         ).astype(jnp.float32)
 
-        width = piece.shape[1]
-        half = width // 2
+        half = rows // 2
         ctx_t = context.T
         order_arr = jnp.asarray(np.array(order, np.int32))
         me = jnp.asarray(np.array(position, np.int32))[lax.axis_index("dp")]
-        cw = weight_bf[:, :half]
-        ccw = weight_bf[:, half:]
-        out_cw = jnp.zeros((tok_rows, half), jnp.float32)
-        out_ccw = jnp.zeros((tok_rows, width - half), jnp.float32)
-        dctx_t = jnp.zeros((ctx_t.shape[0], tok_rows), jnp.float32)
+        cw = weight_bf[:half]
+        ccw = weight_bf[half:]
+        out = jnp.zeros((tok_rows, piece.shape[1]), jnp.float32)
+        dctx_t = jnp.zeros((ctx_t.shape[0], tok_rows), jnp.bfloat16)
         dims_fwd = (((0,), (0,)), ((), ()))
         dims_bwd = (((1,), (1,)), ((), ()))
-        def consume(step, cw, ccw, out_cw, out_ccw, dctx_t):
+
+        def consume(step, cw, ccw, out, dctx_t):
             src_cw = order_arr[(me - step) % n] * rows
-            src_ccw = order_arr[(me + step) % n] * rows
-            ctx_cw = lax.dynamic_slice_in_dim(ctx_t, src_cw, rows, 0)
-            ctx_ccw = lax.dynamic_slice_in_dim(ctx_t, src_ccw, rows, 0)
-            out_cw = out_cw + lax.dot_general(ctx_cw, cw, dims_fwd, preferred_element_type=jnp.float32)
-            out_ccw = out_ccw + lax.dot_general(ctx_ccw, ccw, dims_fwd, preferred_element_type=jnp.float32)
-            part_cw = lax.dot_general(cw, piece[:, :half], dims_bwd, preferred_element_type=jnp.float32)
-            dctx_t = lax.dynamic_update_slice_in_dim(
-                dctx_t, lax.dynamic_slice_in_dim(dctx_t, src_cw, rows, 0) + part_cw, src_cw, 0
+            src_ccw = order_arr[(me + step) % n] * rows + half
+            ctx_blk = jnp.concatenate(
+                [
+                    lax.dynamic_slice_in_dim(ctx_t, src_cw, half, 0),
+                    lax.dynamic_slice_in_dim(ctx_t, src_ccw, rows - half, 0),
+                ],
+                axis=0,
             )
-            part_ccw = lax.dot_general(ccw, piece[:, half:], dims_bwd, preferred_element_type=jnp.float32)
-            dctx_t = lax.dynamic_update_slice_in_dim(
-                dctx_t, lax.dynamic_slice_in_dim(dctx_t, src_ccw, rows, 0) + part_ccw, src_ccw, 0
-            )
-            return out_cw, out_ccw, dctx_t
+            w_blk = jnp.concatenate([cw, ccw], axis=0)
+            out = out + lax.dot_general(ctx_blk, w_blk, dims_fwd, preferred_element_type=jnp.float32)
+            part_cw = lax.dot_general(cw, piece, dims_bwd, preferred_element_type=jnp.float32)
+            dctx_t = lax.dynamic_update_slice_in_dim(dctx_t, part_cw.astype(jnp.bfloat16), src_cw, 0)
+            part_ccw = lax.dot_general(ccw, piece, dims_bwd, preferred_element_type=jnp.float32)
+            dctx_t = lax.dynamic_update_slice_in_dim(dctx_t, part_ccw.astype(jnp.bfloat16), src_ccw, 0)
+            return out, dctx_t
 
         def ring_step(step, carry):
-            cw, ccw, out_cw, out_ccw, dctx_t = carry
+            cw, ccw, out, dctx_t = carry
             cw_next = lax.ppermute(cw, "dp", forward)
             ccw_next = lax.ppermute(ccw, "dp", backward)
-            out_cw, out_ccw, dctx_t = consume(step, cw, ccw, out_cw, out_ccw, dctx_t)
-            return cw_next, ccw_next, out_cw, out_ccw, dctx_t
+            out, dctx_t = consume(step, cw, ccw, out, dctx_t)
+            return cw_next, ccw_next, out, dctx_t
 
-        cw, ccw, out_cw, out_ccw, dctx_t = lax.fori_loop(
-            0, n - 1, ring_step, (cw, ccw, out_cw, out_ccw, dctx_t)
-        )
-        out_cw, out_ccw, dctx_t = consume(n - 1, cw, ccw, out_cw, out_ccw, dctx_t)
-        partials = jnp.concatenate([out_cw, out_ccw], axis=1)
-        summed = lax.psum_scatter(partials.astype(jnp.bfloat16), "mp", scatter_dimension=0, tiled=True)
-        d_context = dctx_t.T.astype(jnp.bfloat16)
+        cw, ccw, out, dctx_t = lax.fori_loop(0, n - 1, ring_step, (cw, ccw, out, dctx_t))
+        out, dctx_t = consume(n - 1, cw, ccw, out, dctx_t)
+        summed = lax.psum_scatter(out.astype(jnp.bfloat16), "mp", scatter_dimension=0, tiled=True)
+        d_context = dctx_t.T
 
         tokens_all = tok_rows * lax.axis_size("dp")
         grad = grad_shard * (1.0 / math.sqrt(tokens_all))

time: 1280 us -> 1320 us (1.031)
  matrix products: 641 us -> 731 us
  local copies, waits for them, and re-layouts: 231 us -> 200 us
  waiting for transfers between devices: 19.8 us -> 0.4 us
  starting transfers between devices: 254 us -> 269 us
    dot_general x128 -> x96, matrix products: 593 us -> 683 us  [the longest x32 369 us: consume(): lax.dot_general(ctx_blk, w_blk, dims_fwd, preferred_element_type=jnp.floa...]
    while x248 -> x187, local copies, waits for them, and re-layouts: 182 us -> 128 us
    dynamic_slice x1 -> x32, local copies, waits for them, and re-layouts: 0.59 us -> 21.4 us  [consume(): src_cw = order_arr[(me - step) % n] * rows]
    dynamic_slice x31 -> x32, local copies, waits for them, and re-layouts: 20.2 us -> 31.1 us  [consume(): lax.dynamic_slice_in_dim(ctx_t, src_cw, half, 0)]
  transfers between devices with their start and end apart: 63 -> 63, of which waited for: 10 -> 1; matrix products, arithmetic and copies ran while one was open for 61% -> 67% of each run, Pallas kernels for 0% -> 0%
where the time goes in v3:
time: 1320 us; the launch traced here: 1310 us
  matrix products  731 us (55%)
  starting transfers between devices  269 us (20%)
  local copies, waits for them, and re-layouts  200 us (15%)
  loops' own time  81.9 us (6%)
  between operations  16.8 us (1%)
  other arithmetic  14.8 us (1%)
    dot_general x32, matrix products, consume(): lax.dot_general(ctx_blk, w_blk, dims_fwd, preferred_element_type=jnp.floa...  369 us
    ppermute x31, starting transfers between devices, ring_step(): cw_next = lax.ppermute(cw, 'dp', forward)  231 us
    dot_general x32, matrix products, consume(): lax.dot_general(cw, piece, dims_bwd, preferred_element_type=jnp.float32)  184 us
    dot_general x32, matrix products, consume(): lax.dot_general(ccw, piece, dims_bwd, preferred_element_type=jnp.float32)  129 us
    while x186, local copies, waits for them, and re-layouts  119 us
    another operation x1, loops' own time, per_device(): lax.fori_loop(0, n - 1, ring_step, (cw, ccw, out, dctx_t))  81.9 us
    dot_general x1, matrix products, per_device(): lax.dot_general(context, piece, (((0,), (0,)), ((), ())), preferred_eleme...  48.4 us
    ppermute x31, starting transfers between devices, ring_step(): ccw_next = lax.ppermute(ccw, 'dp', backward)  38.3 us
  transfers between devices with their start and end apart: 63, of which 1 were waited for; matrix products, arithmetic and copies ran while one was open for 67% of the time, Pallas kernels for 0%

profile of v3, /device:TPU:0, one launch (start us, length us, event | category | flops | bytes accessed | tf_op | source)
XLA Modules:
  0.0 1314.2 jit_solution(9954740511264856666)
XLA Ops:
  7.2 48.4 %convolution_convert_fusion.2 = bf16[6144,6144]{1,0:T(8,128)(2,1)} fusion(bf16[512,6144]{1,0:T(8,128)(2,1)} %param.9, bf16[512,6144]{1,0:T(8,128)(2,1)} %param.13), kind=kOutput, calls=%fused_computation.14 | convolution fusion | flops 38692454400 | bytes 88080384 | tf_op jit(solution)/shard_map/dot_general | solution.py:34
  58.2 8.6 copy.12
  77.6 1183.7 %while.23 = (s32[]{:T(128)}, bf16[96,6144]{1,0:T(8,128)(2,1)}, bf16[96,6144]{1,0:T(8,128)(2,1)}, f32[512,6144]{1,0:T(8,128)}, bf16[6144,512]{1,0:T(8,128)(2,1)},...) while((s32[]{:T(128)}, bf16[96,6144]{1,0:T(8,128)(2,1)}, ...), condition=%wide.region_1.2_spmd.clone.clone, body=%wide.region_0.0_spmd.sunk.clone.clone.sunk | while | flops 2427420672 | bytes 76284656 | solution.py:77
  88.5 6.7 fusion.50
  99.4 9.8 select_add_fusion.2
  119.5 6.6 fusion.50
  130.2 15.3 %select_add_fusion.2 = f32[512,6144]{1,0:T(8,128)} fusion(f32[512,6144]{1,0:T(8,128)} %get-tuple-element.398, pred[]{:T(512)S(6)} %compare.7, bf16[96,6144]{1,0:T(8,128)(2,1)} %copy.25, bf16[96,6144]{1,0:T(8,128)(2,1)S(1)} %copy.24, bf16[96,512]{1,0:T(8,128)(2,1)S(1)} %get-tuple-element.376, bf16[96,512]{1,0:T(8,128)(2,1)S(1)} %get-tuple-element.377), kind=kOutput, calls=%fused_computation.clone.1 | convolution fusion | flops 1219362816 | bytes 27721728 | tf_op jit(solution)/shard_map/while/body/eval_jaxpr/dot_general | solution.py:63
  155.8 6.6 fusion.50
  166.5 13.5 %select_add_fusion.2 = f32[512,6144]{1,0:T(8,128)} fusion(f32[512,6144]{1,0:T(8,128)} %get-tuple-element.398, pred[]{:T(512)S(6)} %compare.7, bf16[96,6144]{1,0:T(8,128)(2,1)} %copy.25, bf16[96,6144]{1,0:T(8,128)(2,1)S(1)} %copy.24, bf16[96,512]{1,0:T(8,128)(2,1)S(1)} %get-tuple-element.376, bf16[96,512]{1,0:T(8,128)(2,1)S(1)} %get-tuple-element.377), kind=kOutput, calls=%fused_computation.clone.1 | convolution fusion | flops 1219362816 | bytes 27721728 | tf_op jit(solution)/shard_map/while/body/eval_jaxpr/dot_general | solution.py:63
  189.8 5.7 fusion.50
  199.5 11.5 select_add_fusion.2
  212.4 34.5 %collective-permute-start = (bf16[96,6144]{1,0:T(8,128)(2,1)S(1)}, bf16[96,6144]{1,0:T(8,128)(2,1)}, u32[]{:S(2)}, u32[]{:S(2)}) collective-permute-start(bf16[96,6144]{1,0:T(8,128)(2,1)S(1)} %copy.24), channel_id=1, source_target_pairs={{0,1},{1,8},{8,9},{9,16},{16,17},{17,24},{24,25},{25,26},{26,27},{... | collective-permute-start | bytes 3538952 | tf_op jit(solution)/shard_map/while/body/eval_jaxpr/ppermute | solution.py:72
  253.7 5.7 fusion.50
  263.4 11.5 select_add_fusion.2
  276.4 32.2 %collective-permute-start = (bf16[96,6144]{1,0:T(8,128)(2,1)S(1)}, bf16[96,6144]{1,0:T(8,128)(2,1)}, u32[]{:S(2)}, u32[]{:S(2)}) collective-permute-start(bf16[96,6144]{1,0:T(8,128)(2,1)S(1)} %copy.24), channel_id=1, source_target_pairs={{0,1},{1,8},{8,9},{9,16},{16,17},{17,24},{24,25},{25,26},{26,27},{... | collective-permute-start | bytes 3538952 | tf_op jit(solution)/shard_map/while/body/eval_jaxpr/ppermute | solution.py:72
  315.3 5.7 fusion.50
  325.0 11.5 select_add_fusion.2
  337.9 33.8 %collective-permute-start = (bf16[96,6144]{1,0:T(8,128)(2,1)S(1)}, bf16[96,6144]{1,0:T(8,128)(2,1)}, u32[]{:S(2)}, u32[]{:S(2)}) collective-permute-start(bf16[96,6144]{1,0:T(8,128)(2,1)S(1)} %copy.24), channel_id=1, source_target_pairs={{0,1},{1,8},{8,9},{9,16},{16,17},{17,24},{24,25},{25,26},{26,27},{... | collective-permute-start | bytes 3538952 | tf_op jit(solution)/shard_map/while/body/eval_jaxpr/ppermute | solution.py:72
  378.5 5.8 fusion.50
  388.3 11.5 select_add_fusion.2
  401.2 33.2 %collective-permute-start = (bf16[96,6144]{1,0:T(8,128)(2,1)S(1)}, bf16[96,6144]{1,0:T(8,128)(2,1)}, u32[]{:S(2)}, u32[]{:S(2)}) collective-permute-start(bf16[96,6144]{1,0:T(8,128)(2,1)S(1)} %copy.24), channel_id=1, source_target_pairs={{0,1},{1,8},{8,9},{9,16},{16,17},{17,24},{24,25},{25,26},{26,27},{... | collective-permute-start | bytes 3538952 | tf_op jit(solution)/shard_map/while/body/eval_jaxpr/ppermute | solution.py:72
  441.1 5.8 fusion.50
  450.9 11.8 select_add_fusion.2
  472.5 5.9 fusion.50
  482.4 11.5 select_add_fusion.2
  503.7 5.8 fusion.50
  513.6 11.3 select_add_fusion.2
  534.8 5.7 fusion.50
  544.4 11.5 select_add_fusion.2
  565.8 5.7 fusion.50
  575.5 12.0 select_add_fusion.2
  597.3 5.7 fusion.50
  607.1 11.6 select_add_fusion.2
  620.1 33.7 %collective-permute-start = (bf16[96,6144]{1,0:T(8,128)(2,1)S(1)}, bf16[96,6144]{1,0:T(8,128)(2,1)}, u32[]{:S(2)}, u32[]{:S(2)}) collective-permute-start(bf16[96,6144]{1,0:T(8,128)(2,1)S(1)} %copy.24), channel_id=1, source_target_pairs={{0,1},{1,8},{8,9},{9,16},{16,17},{17,24},{24,25},{25,26},{26,27},{... | collective-permute-start | bytes 3538952 | tf_op jit(solution)/shard_map/while/body/eval_jaxpr/ppermute | solution.py:72
  660.4 5.7 fusion.50
  670.1 11.6 select_add_fusion.2
  683.2 31.1 %collective-permute-start = (bf16[96,6144]{1,0:T(8,128)(2,1)S(1)}, bf16[96,6144]{1,0:T(8,128)(2,1)}, u32[]{:S(2)}, u32[]{:S(2)}) collective-permute-start(bf16[96,6144]{1,0:T(8,128)(2,1)S(1)} %copy.24), channel_id=1, source_target_pairs={{0,1},{1,8},{8,9},{9,16},{16,17},{17,24},{24,25},{25,26},{26,27},{... | collective-permute-start | bytes 3538952 | tf_op jit(solution)/shard_map/while/body/eval_jaxpr/ppermute | solution.py:72
  720.9 5.8 fusion.50
  730.7 11.4 select_add_fusion.2
  752.6 5.7 fusion.50
  762.3 11.4 select_add_fusion.2
  783.5 5.6 fusion.50
  793.1 11.4 select_add_fusion.2
  806.0 27.5 %collective-permute-start = (bf16[96,6144]{1,0:T(8,128)(2,1)S(1)}, bf16[96,6144]{1,0:T(8,128)(2,1)}, u32[]{:S(2)}, u32[]{:S(2)}) collective-permute-start(bf16[96,6144]{1,0:T(8,128)(2,1)S(1)} %copy.24), channel_id=1, source_target_pairs={{0,1},{1,8},{8,9},{9,16},{16,17},{17,24},{24,25},{25,26},{26,27},{... | collective-permute-start | bytes 3538952 | tf_op jit(solution)/shard_map/while/body/eval_jaxpr/ppermute | solution.py:72
  840.1 5.7 fusion.50
  849.7 11.3 select_add_fusion.2
  870.9 5.7 fusion.50
  880.5 11.3 select_add_fusion.2
  911.3 11.3 select_add_fusion.2
  942.1 11.3 select_add_fusion.2
  963.3 5.6 fusion.50
  972.9 11.3 select_add_fusion.2
  1003.7 11.3 select_add_fusion.2
  1034.5 11.3 select_add_fusion.2
  1065.3 11.3 select_add_fusion.2
  1096.1 11.3 select_add_fusion.2
  1126.8 11.3 select_add_fusion.2
  1157.6 11.3 select_add_fusion.2
  1188.4 11.3 select_add_fusion.2
  1219.2 11.3 select_add_fusion.2
  1250.0 11.3 select_add_fusion.2
  1261.3 8.6 copy.13
  1286.2 9.9 add_convert_fusion
  1296.1 11.3 multiply_subtract_fusion
  (458 shorter events, 426.9 us)
Async XLA Ops:
  7.2 1288.9 %reduce-scatter.2.cloned.1.call-start = ((), (), s32[]{:S(2)}) async-start(), calls=%async_computation.1 | async-start | bytes 77856768 | tf_op jit(solution)/shard_map/reduce_scatter | solution.py:37
  79.2 30.0 %collective-permute-start = (bf16[96,6144]{1,0:T(8,128)(2,1)S(1)}, bf16[96,6144]{1,0:T(8,128)(2,1)}, u32[]{:S(2)}, u32[]{:S(2)}) collective-permute-start(bf16[96,6144]{1,0:T(8,128)(2,1)S(1)} %copy.24), channel_id=1, source_target_pairs={{0,1},{1,8},{8,9},{9,16},{16,17},{17,24},{24,25},{25,26},{26,27},{... | collective-permute-start | bytes 3538952 | tf_op jit(solution)/shard_map/while/body/eval_jaxpr/ppermute | solution.py:72
  82.1 27.0 %collective-permute-start.1 = (bf16[96,6144]{1,0:T(8,128)(2,1)}, bf16[96,6144]{1,0:T(8,128)(2,1)}, u32[]{:S(2)}, u32[]{:S(2)}) collective-permute-start(bf16[96,6144]{1,0:T(8,128)(2,1)} %copy.25), channel_id=1, source_target_pairs={{1,0},{8,1},{9,8},{16,9},{17,16},{24,17},{25,24},{26,25},{27,26},{... | collective-permute-start | bytes 3538952 | tf_op jit(solution)/shard_map/while/body/eval_jaxpr/ppermute | solution.py:73
  110.7 34.8 %collective-permute-start = (bf16[96,6144]{1,0:T(8,128)(2,1)S(1)}, bf16[96,6144]{1,0:T(8,128)(2,1)}, u32[]{:S(2)}, u32[]{:S(2)}) collective-permute-start(bf16[96,6144]{1,0:T(8,128)(2,1)S(1)} %copy.24), channel_id=1, source_target_pairs={{0,1},{1,8},{8,9},{9,16},{16,17},{17,24},{24,25},{25,26},{26,27},{... | collective-permute-start | bytes 3538952 | tf_op jit(solution)/shard_map/while/body/eval_jaxpr/ppermute | solution.py:72
  114.2 31.3 %collective-permute-start.1 = (bf16[96,6144]{1,0:T(8,128)(2,1)}, bf16[96,6144]{1,0:T(8,128)(2,1)}, u32[]{:S(2)}, u32[]{:S(2)}) collective-permute-start(bf16[96,6144]{1,0:T(8,128)(2,1)} %copy.25), channel_id=1, source_target_pairs={{1,0},{8,1},{9,8},{16,9},{17,16},{24,17},{25,24},{26,25},{27,26},{... | collective-permute-start | bytes 3538952 | tf_op jit(solution)/shard_map/while/body/eval_jaxpr/ppermute | solution.py:73
  147.2 32.8 %collective-permute-start = (bf16[96,6144]{1,0:T(8,128)(2,1)S(1)}, bf16[96,6144]{1,0:T(8,128)(2,1)}, u32[]{:S(2)}, u32[]{:S(2)}) collective-permute-start(bf16[96,6144]{1,0:T(8,128)(2,1)S(1)} %copy.24), channel_id=1, source_target_pairs={{0,1},{1,8},{8,9},{9,16},{16,17},{17,24},{24,25},{25,26},{26,27},{... | collective-permute-start | bytes 3538952 | tf_op jit(solution)/shard_map/while/body/eval_jaxpr/ppermute | solution.py:72
  150.5 29.5 %collective-permute-start.1 = (bf16[96,6144]{1,0:T(8,128)(2,1)}, bf16[96,6144]{1,0:T(8,128)(2,1)}, u32[]{:S(2)}, u32[]{:S(2)}) collective-permute-start(bf16[96,6144]{1,0:T(8,128)(2,1)} %copy.25), channel_id=1, source_target_pairs={{1,0},{8,1},{9,8},{16,9},{17,16},{24,17},{25,24},{26,25},{27,26},{... | collective-permute-start | bytes 3538952 | tf_op jit(solution)/shard_map/while/body/eval_jaxpr/ppermute | solution.py:73
  181.4 29.5 %collective-permute-start = (bf16[96,6144]{1,0:T(8,128)(2,1)S(1)}, bf16[96,6144]{1,0:T(8,128)(2,1)}, u32[]{:S(2)}, u32[]{:S(2)}) collective-permute-start(bf16[96,6144]{1,0:T(8,128)(2,1)S(1)} %copy.24), channel_id=1, source_target_pairs={{0,1},{1,8},{8,9},{9,16},{16,17},{17,24},{24,25},{25,26},{26,27},{... | collective-permute-start | bytes 3538952 | tf_op jit(solution)/shard_map/while/body/eval_jaxpr/ppermute | solution.py:72
  184.2 26.8 %collective-permute-start.1 = (bf16[96,6144]{1,0:T(8,128)(2,1)}, bf16[96,6144]{1,0:T(8,128)(2,1)}, u32[]{:S(2)}, u32[]{:S(2)}) collective-permute-start(bf16[96,6144]{1,0:T(8,128)(2,1)} %copy.25), channel_id=1, source_target_pairs={{1,0},{8,1},{9,8},{16,9},{17,16},{24,17},{25,24},{26,25},{27,26},{... | collective-permute-start | bytes 3538952 | tf_op jit(solution)/shard_map/while/body/eval_jaxpr/ppermute | solution.py:73
  211.0 48.4 %slice-start = ((s8[6291456]{0:T(1024)(128)(4,1)}), s8[2097152]{0:T(1024)(128)(4,1)S(1)}, s32[]{:S(2)}) async-start(s8[6291456]{0:T(1024)(128)(4,1)} %bitcast.37), calls=%async_computation.2 | async-start | bytes 4194304 | tf_op jit(solution)/shard_map/while
  212.4 62.6 %collective-permute-start = (bf16[96,6144]{1,0:T(8,128)(2,1)S(1)}, bf16[96,6144]{1,0:T(8,128)(2,1)}, u32[]{:S(2)}, u32[]{:S(2)}) collective-permute-start(bf16[96,6144]{1,0:T(8,128)(2,1)S(1)} %copy.24), channel_id=1, source_target_pairs={{0,1},{1,8},{8,9},{9,16},{16,17},{17,24},{24,25},{25,26},{26,27},{... | collective-permute-start | bytes 3538952 | tf_op jit(solution)/shard_map/while/body/eval_jaxpr/ppermute | solution.py:72
  249.5 25.5 %collective-permute-start.1 = (bf16[96,6144]{1,0:T(8,128)(2,1)}, bf16[96,6144]{1,0:T(8,128)(2,1)}, u32[]{:S(2)}, u32[]{:S(2)}) collective-permute-start(bf16[96,6144]{1,0:T(8,128)(2,1)} %copy.25), channel_id=1, source_target_pairs={{1,0},{8,1},{9,8},{16,9},{17,16},{24,17},{25,24},{26,25},{27,26},{... | collective-permute-start | bytes 3538952 | tf_op jit(solution)/shard_map/while/body/eval_jaxpr/ppermute | solution.py:73
  276.4 60.1 %collective-permute-start = (bf16[96,6144]{1,0:T(8,128)(2,1)S(1)}, bf16[96,6144]{1,0:T(8,128)(2,1)}, u32[]{:S(2)}, u32[]{:S(2)}) collective-permute-start(bf16[96,6144]{1,0:T(8,128)(2,1)S(1)} %copy.24), channel_id=1, source_target_pairs={{0,1},{1,8},{8,9},{9,16},{16,17},{17,24},{24,25},{25,26},{26,27},{... | collective-permute-start | bytes 3538952 | tf_op jit(solution)/shard_map/while/body/eval_jaxpr/ppermute | solution.py:72
  311.1 25.4 %collective-permute-start.1 = (bf16[96,6144]{1,0:T(8,128)(2,1)}, bf16[96,6144]{1,0:T(8,128)(2,1)}, u32[]{:S(2)}, u32[]{:S(2)}) collective-permute-start(bf16[96,6144]{1,0:T(8,128)(2,1)} %copy.25), channel_id=1, source_target_pairs={{1,0},{8,1},{9,8},{16,9},{17,16},{24,17},{25,24},{26,25},{27,26},{... | collective-permute-start | bytes 3538952 | tf_op jit(solution)/shard_map/while/body/eval_jaxpr/ppermute | solution.py:73
  337.9 61.8 %collective-permute-start = (bf16[96,6144]{1,0:T(8,128)(2,1)S(1)}, bf16[96,6144]{1,0:T(8,128)(2,1)}, u32[]{:S(2)}, u32[]{:S(2)}) collective-permute-start(bf16[96,6144]{1,0:T(8,128)(2,1)S(1)} %copy.24), channel_id=1, source_target_pairs={{0,1},{1,8},{8,9},{9,16},{16,17},{17,24},{24,25},{25,26},{26,27},{... | collective-permute-start | bytes 3538952 | tf_op jit(solution)/shard_map/while/body/eval_jaxpr/ppermute | solution.py:72
  374.2 25.5 %collective-permute-start.1 = (bf16[96,6144]{1,0:T(8,128)(2,1)}, bf16[96,6144]{1,0:T(8,128)(2,1)}, u32[]{:S(2)}, u32[]{:S(2)}) collective-permute-start(bf16[96,6144]{1,0:T(8,128)(2,1)} %copy.25), channel_id=1, source_target_pairs={{1,0},{8,1},{9,8},{16,9},{17,16},{24,17},{25,24},{26,25},{27,26},{... | collective-permute-start | bytes 3538952 | tf_op jit(solution)/shard_map/while/body/eval_jaxpr/ppermute | solution.py:73
  401.2 61.5 %collective-permute-start = (bf16[96,6144]{1,0:T(8,128)(2,1)S(1)}, bf16[96,6144]{1,0:T(8,128)(2,1)}, u32[]{:S(2)}, u32[]{:S(2)}) collective-permute-start(bf16[96,6144]{1,0:T(8,128)(2,1)S(1)} %copy.24), channel_id=1, source_target_pairs={{0,1},{1,8},{8,9},{9,16},{16,17},{17,24},{24,25},{25,26},{26,27},{... | collective-permute-start | bytes 3538952 | tf_op jit(solution)/shard_map/while/body/eval_jaxpr/ppermute | solution.py:72
  436.8 25.8 %collective-permute-start.1 = (bf16[96,6144]{1,0:T(8,128)(2,1)}, bf16[96,6144]{1,0:T(8,128)(2,1)}, u32[]{:S(2)}, u32[]{:S(2)}) collective-permute-start(bf16[96,6144]{1,0:T(8,128)(2,1)} %copy.25), channel_id=1, source_target_pairs={{1,0},{8,1},{9,8},{16,9},{17,16},{24,17},{25,24},{26,25},{27,26},{... | collective-permute-start | bytes 3538952 | tf_op jit(solution)/shard_map/while/body/eval_jaxpr/ppermute | solution.py:73
  464.1 29.8 %collective-permute-start = (bf16[96,6144]{1,0:T(8,128)(2,1)S(1)}, bf16[96,6144]{1,0:T(8,128)(2,1)}, u32[]{:S(2)}, u32[]{:S(2)}) collective-permute-start(bf16[96,6144]{1,0:T(8,128)(2,1)S(1)} %copy.24), channel_id=1, source_target_pairs={{0,1},{1,8},{8,9},{9,16},{16,17},{17,24},{24,25},{25,26},{26,27},{... | collective-permute-start | bytes 3538952 | tf_op jit(solution)/shard_map/while/body/eval_jaxpr/ppermute | solution.py:72
  466.9 27.0 %collective-permute-start.1 = (bf16[96,6144]{1,0:T(8,128)(2,1)}, bf16[96,6144]{1,0:T(8,128)(2,1)}, u32[]{:S(2)}, u32[]{:S(2)}) collective-permute-start(bf16[96,6144]{1,0:T(8,128)(2,1)} %copy.25), channel_id=1, source_target_pairs={{1,0},{8,1},{9,8},{16,9},{17,16},{24,17},{25,24},{26,25},{27,26},{... | collective-permute-start | bytes 3538952 | tf_op jit(solution)/shard_map/while/body/eval_jaxpr/ppermute | solution.py:73
  495.3 29.6 %collective-permute-start = (bf16[96,6144]{1,0:T(8,128)(2,1)S(1)}, bf16[96,6144]{1,0:T(8,128)(2,1)}, u32[]{:S(2)}, u32[]{:S(2)}) collective-permute-start(bf16[96,6144]{1,0:T(8,128)(2,1)S(1)} %copy.24), channel_id=1, source_target_pairs={{0,1},{1,8},{8,9},{9,16},{16,17},{17,24},{24,25},{25,26},{26,27},{... | collective-permute-start | bytes 3538952 | tf_op jit(solution)/shard_map/while/body/eval_jaxpr/ppermute | solution.py:72
  497.7 27.2 %collective-permute-start.1 = (bf16[96,6144]{1,0:T(8,128)(2,1)}, bf16[96,6144]{1,0:T(8,128)(2,1)}, u32[]{:S(2)}, u32[]{:S(2)}) collective-permute-start(bf16[96,6144]{1,0:T(8,128)(2,1)} %copy.25), channel_id=1, source_target_pairs={{1,0},{8,1},{9,8},{16,9},{17,16},{24,17},{25,24},{26,25},{27,26},{... | collective-permute-start | bytes 3538952 | tf_op jit(solution)/shard_map/while/body/eval_jaxpr/ppermute | solution.py:73
  526.4 29.6 %collective-permute-start = (bf16[96,6144]{1,0:T(8,128)(2,1)S(1)}, bf16[96,6144]{1,0:T(8,128)(2,1)}, u32[]{:S(2)}, u32[]{:S(2)}) collective-permute-start(bf16[96,6144]{1,0:T(8,128)(2,1)S(1)} %copy.24), channel_id=1, source_target_pairs={{0,1},{1,8},{8,9},{9,16},{16,17},{17,24},{24,25},{25,26},{26,27},{... | collective-permute-start | bytes 3538952 | tf_op jit(solution)/shard_map/while/body/eval_jaxpr/ppermute | solution.py:72
  528.8 27.2 %collective-permute-start.1 = (bf16[96,6144]{1,0:T(8,128)(2,1)}, bf16[96,6144]{1,0:T(8,128)(2,1)}, u32[]{:S(2)}, u32[]{:S(2)}) collective-permute-start(bf16[96,6144]{1,0:T(8,128)(2,1)} %copy.25), channel_id=1, source_target_pairs={{1,0},{8,1},{9,8},{16,9},{17,16},{24,17},{25,24},{26,25},{27,26},{... | collective-permute-start | bytes 3538952 | tf_op jit(solution)/shard_map/while/body/eval_jaxpr/ppermute | solution.py:73
  557.4 30.1 %collective-permute-start = (bf16[96,6144]{1,0:T(8,128)(2,1)S(1)}, bf16[96,6144]{1,0:T(8,128)(2,1)}, u32[]{:S(2)}, u32[]{:S(2)}) collective-permute-start(bf16[96,6144]{1,0:T(8,128)(2,1)S(1)} %copy.24), channel_id=1, source_target_pairs={{0,1},{1,8},{8,9},{9,16},{16,17},{17,24},{24,25},{25,26},{26,27},{... | collective-permute-start | bytes 3538952 | tf_op jit(solution)/shard_map/while/body/eval_jaxpr/ppermute | solution.py:72
  559.9 27.7 %collective-permute-start.1 = (bf16[96,6144]{1,0:T(8,128)(2,1)}, bf16[96,6144]{1,0:T(8,128)(2,1)}, u32[]{:S(2)}, u32[]{:S(2)}) collective-permute-start(bf16[96,6144]{1,0:T(8,128)(2,1)} %copy.25), channel_id=1, source_target_pairs={{1,0},{8,1},{9,8},{16,9},{17,16},{24,17},{25,24},{26,25},{27,26},{... | collective-permute-start | bytes 3538952 | tf_op jit(solution)/shard_map/while/body/eval_jaxpr/ppermute | solution.py:73
  589.0 29.7 %collective-permute-start = (bf16[96,6144]{1,0:T(8,128)(2,1)S(1)}, bf16[96,6144]{1,0:T(8,128)(2,1)}, u32[]{:S(2)}, u32[]{:S(2)}) collective-permute-start(bf16[96,6144]{1,0:T(8,128)(2,1)S(1)} %copy.24), channel_id=1, source_target_pairs={{0,1},{1,8},{8,9},{9,16},{16,17},{17,24},{24,25},{25,26},{26,27},{... | collective-permute-start | bytes 3538952 | tf_op jit(solution)/shard_map/while/body/eval_jaxpr/ppermute | solution.py:72
  591.3 27.3 %collective-permute-start.1 = (bf16[96,6144]{1,0:T(8,128)(2,1)}, bf16[96,6144]{1,0:T(8,128)(2,1)}, u32[]{:S(2)}, u32[]{:S(2)}) collective-permute-start(bf16[96,6144]{1,0:T(8,128)(2,1)} %copy.25), channel_id=1, source_target_pairs={{1,0},{8,1},{9,8},{16,9},{17,16},{24,17},{25,24},{26,25},{27,26},{... | collective-permute-start | bytes 3538952 | tf_op jit(solution)/shard_map/while/body/eval_jaxpr/ppermute | solution.py:73
  620.1 61.7 %collective-permute-start = (bf16[96,6144]{1,0:T(8,128)(2,1)S(1)}, bf16[96,6144]{1,0:T(8,128)(2,1)}, u32[]{:S(2)}, u32[]{:S(2)}) collective-permute-start(bf16[96,6144]{1,0:T(8,128)(2,1)S(1)} %copy.24), channel_id=1, source_target_pairs={{0,1},{1,8},{8,9},{9,16},{16,17},{17,24},{24,25},{25,26},{26,27},{... | collective-permute-start | bytes 3538952 | tf_op jit(solution)/shard_map/while/body/eval_jaxpr/ppermute | solution.py:72
  656.2 25.6 %collective-permute-start.1 = (bf16[96,6144]{1,0:T(8,128)(2,1)}, bf16[96,6144]{1,0:T(8,128)(2,1)}, u32[]{:S(2)}, u32[]{:S(2)}) collective-permute-start(bf16[96,6144]{1,0:T(8,128)(2,1)} %copy.25), channel_id=1, source_target_pairs={{1,0},{8,1},{9,8},{16,9},{17,16},{24,17},{25,24},{26,25},{27,26},{... | collective-permute-start | bytes 3538952 | tf_op jit(solution)/shard_map/while/body/eval_jaxpr/ppermute | solution.py:73
  683.2 58.9 %collective-permute-start = (bf16[96,6144]{1,0:T(8,128)(2,1)S(1)}, bf16[96,6144]{1,0:T(8,128)(2,1)}, u32[]{:S(2)}, u32[]{:S(2)}) collective-permute-start(bf16[96,6144]{1,0:T(8,128)(2,1)S(1)} %copy.24), channel_id=1, source_target_pairs={{0,1},{1,8},{8,9},{9,16},{16,17},{17,24},{24,25},{25,26},{26,27},{... | collective-permute-start | bytes 3538952 | tf_op jit(solution)/shard_map/while/body/eval_jaxpr/ppermute | solution.py:72
  716.7 25.7 %collective-permute-start.1 = (bf16[96,6144]{1,0:T(8,128)(2,1)}, bf16[96,6144]{1,0:T(8,128)(2,1)}, u32[]{:S(2)}, u32[]{:S(2)}) collective-permute-start(bf16[96,6144]{1,0:T(8,128)(2,1)} %copy.25), channel_id=1, source_target_pairs={{1,0},{8,1},{9,8},{16,9},{17,16},{24,17},{25,24},{26,25},{27,26},{... | collective-permute-start | bytes 3538952 | tf_op jit(solution)/shard_map/while/body/eval_jaxpr/ppermute | solution.py:73
  743.8 29.9 %collective-permute-start = (bf16[96,6144]{1,0:T(8,128)(2,1)S(1)}, bf16[96,6144]{1,0:T(8,128)(2,1)}, u32[]{:S(2)}, u32[]{:S(2)}) collective-permute-start(bf16[96,6144]{1,0:T(8,128)(2,1)S(1)} %copy.24), channel_id=1, source_target_pairs={{0,1},{1,8},{8,9},{9,16},{16,17},{17,24},{24,25},{25,26},{26,27},{... | collective-permute-start | bytes 3538952 | tf_op jit(solution)/shard_map/while/body/eval_jaxpr/ppermute | solution.py:72
  746.4 27.2 %collective-permute-start.1 = (bf16[96,6144]{1,0:T(8,128)(2,1)}, bf16[96,6144]{1,0:T(8,128)(2,1)}, u32[]{:S(2)}, u32[]{:S(2)}) collective-permute-start(bf16[96,6144]{1,0:T(8,128)(2,1)} %copy.25), channel_id=1, source_target_pairs={{1,0},{8,1},{9,8},{16,9},{17,16},{24,17},{25,24},{26,25},{27,26},{... | collective-permute-start | bytes 3538952 | tf_op jit(solution)/shard_map/while/body/eval_jaxpr/ppermute | solution.py:73
  775.1 29.4 %collective-permute-start = (bf16[96,6144]{1,0:T(8,128)(2,1)S(1)}, bf16[96,6144]{1,0:T(8,128)(2,1)}, u32[]{:S(2)}, u32[]{:S(2)}) collective-permute-start(bf16[96,6144]{1,0:T(8,128)(2,1)S(1)} %copy.24), channel_id=1, source_target_pairs={{0,1},{1,8},{8,9},{9,16},{16,17},{17,24},{24,25},{25,26},{26,27},{... | collective-permute-start | bytes 3538952 | tf_op jit(solution)/shard_map/while/body/eval_jaxpr/ppermute | solution.py:72
  777.5 27.0 %collective-permute-start.1 = (bf16[96,6144]{1,0:T(8,128)(2,1)}, bf16[96,6144]{1,0:T(8,128)(2,1)}, u32[]{:S(2)}, u32[]{:S(2)}) collective-permute-start(bf16[96,6144]{1,0:T(8,128)(2,1)} %copy.25), channel_id=1, source_target_pairs={{1,0},{8,1},{9,8},{16,9},{17,16},{24,17},{25,24},{26,25},{27,26},{... | collective-permute-start | bytes 3538952 | tf_op jit(solution)/shard_map/while/body/eval_jaxpr/ppermute | solution.py:73
  806.0 55.1 %collective-permute-start = (bf16[96,6144]{1,0:T(8,128)(2,1)S(1)}, bf16[96,6144]{1,0:T(8,128)(2,1)}, u32[]{:S(2)}, u32[]{:S(2)}) collective-permute-start(bf16[96,6144]{1,0:T(8,128)(2,1)S(1)} %copy.24), channel_id=1, source_target_pairs={{0,1},{1,8},{8,9},{9,16},{16,17},{17,24},{24,25},{25,26},{26,27},{... | collective-permute-start | bytes 3538952 | tf_op jit(solution)/shard_map/while/body/eval_jaxpr/ppermute | solution.py:72
  835.8 25.3 %collective-permute-start.1 = (bf16[96,6144]{1,0:T(8,128)(2,1)}, bf16[96,6144]{1,0:T(8,128)(2,1)}, u32[]{:S(2)}, u32[]{:S(2)}) collective-permute-start(bf16[96,6144]{1,0:T(8,128)(2,1)} %copy.25), channel_id=1, source_target_pairs={{1,0},{8,1},{9,8},{16,9},{17,16},{24,17},{25,24},{26,25},{27,26},{... | collective-permute-start | bytes 3538952 | tf_op jit(solution)/shard_map/while/body/eval_jaxpr/ppermute | solution.py:73
  862.5 29.4 %collective-permute-start = (bf16[96,6144]{1,0:T(8,128)(2,1)S(1)}, bf16[96,6144]{1,0:T(8,128)(2,1)}, u32[]{:S(2)}, u32[]{:S(2)}) collective-permute-start(bf16[96,6144]{1,0:T(8,128)(2,1)S(1)} %copy.24), channel_id=1, source_target_pairs={{0,1},{1,8},{8,9},{9,16},{16,17},{17,24},{24,25},{25,26},{26,27},{... | collective-permute-start | bytes 3538952 | tf_op jit(solution)/shard_map/while/body/eval_jaxpr/ppermute | solution.py:72
  865.4 26.5 %collective-permute-start.1 = (bf16[96,6144]{1,0:T(8,128)(2,1)}, bf16[96,6144]{1,0:T(8,128)(2,1)}, u32[]{:S(2)}, u32[]{:S(2)}) collective-permute-start(bf16[96,6144]{1,0:T(8,128)(2,1)} %copy.25), channel_id=1, source_target_pairs={{1,0},{8,1},{9,8},{16,9},{17,16},{24,17},{25,24},{26,25},{27,26},{... | collective-permute-start | bytes 3538952 | tf_op jit(solution)/shard_map/while/body/eval_jaxpr/ppermute | solution.py:73
  893.3 29.4 %collective-permute-start = (bf16[96,6144]{1,0:T(8,128)(2,1)S(1)}, bf16[96,6144]{1,0:T(8,128)(2,1)}, u32[]{:S(2)}, u32[]{:S(2)}) collective-permute-start(bf16[96,6144]{1,0:T(8,128)(2,1)S(1)} %copy.24), channel_id=1, source_target_pairs={{0,1},{1,8},{8,9},{9,16},{16,17},{17,24},{24,25},{25,26},{26,27},{... | collective-permute-start | bytes 3538952 | tf_op jit(solution)/shard_map/while/body/eval_jaxpr/ppermute | solution.py:72
  895.8 26.9 %collective-permute-start.1 = (bf16[96,6144]{1,0:T(8,128)(2,1)}, bf16[96,6144]{1,0:T(8,128)(2,1)}, u32[]{:S(2)}, u32[]{:S(2)}) collective-permute-start(bf16[96,6144]{1,0:T(8,128)(2,1)} %copy.25), channel_id=1, source_target_pairs={{1,0},{8,1},{9,8},{16,9},{17,16},{24,17},{25,24},{26,25},{27,26},{... | collective-permute-start | bytes 3538952 | tf_op jit(solution)/shard_map/while/body/eval_jaxpr/ppermute | solution.py:73
  924.1 29.4 %collective-permute-start = (bf16[96,6144]{1,0:T(8,128)(2,1)S(1)}, bf16[96,6144]{1,0:T(8,128)(2,1)}, u32[]{:S(2)}, u32[]{:S(2)}) collective-permute-start(bf16[96,6144]{1,0:T(8,128)(2,1)S(1)} %copy.24), channel_id=1, source_target_pairs={{0,1},{1,8},{8,9},{9,16},{16,17},{17,24},{24,25},{25,26},{26,27},{... | collective-permute-start | bytes 3538952 | tf_op jit(solution)/shard_map/while/body/eval_jaxpr/ppermute | solution.py:72
  926.6 26.9 %collective-permute-start.1 = (bf16[96,6144]{1,0:T(8,128)(2,1)}, bf16[96,6144]{1,0:T(8,128)(2,1)}, u32[]{:S(2)}, u32[]{:S(2)}) collective-permute-start(bf16[96,6144]{1,0:T(8,128)(2,1)} %copy.25), channel_id=1, source_target_pairs={{1,0},{8,1},{9,8},{16,9},{17,16},{24,17},{25,24},{26,25},{27,26},{... | collective-permute-start | bytes 3538952 | tf_op jit(solution)/shard_map/while/body/eval_jaxpr/ppermute | solution.py:73
  954.9 29.4 %collective-permute-start = (bf16[96,6144]{1,0:T(8,128)(2,1)S(1)}, bf16[96,6144]{1,0:T(8,128)(2,1)}, u32[]{:S(2)}, u32[]{:S(2)}) collective-permute-start(bf16[96,6144]{1,0:T(8,128)(2,1)S(1)} %copy.24), channel_id=1, source_target_pairs={{0,1},{1,8},{8,9},{9,16},{16,17},{17,24},{24,25},{25,26},{26,27},{... | collective-permute-start | bytes 3538952 | tf_op jit(solution)/shard_map/while/body/eval_jaxpr/ppermute | solution.py:72
  957.3 26.9 %collective-permute-start.1 = (bf16[96,6144]{1,0:T(8,128)(2,1)}, bf16[96,6144]{1,0:T(8,128)(2,1)}, u32[]{:S(2)}, u32[]{:S(2)}) collective-permute-start(bf16[96,6144]{1,0:T(8,128)(2,1)} %copy.25), channel_id=1, source_target_pairs={{1,0},{8,1},{9,8},{16,9},{17,16},{24,17},{25,24},{26,25},{27,26},{... | collective-permute-start | bytes 3538952 | tf_op jit(solution)/shard_map/while/body/eval_jaxpr/ppermute | solution.py:73
  985.7 29.4 %collective-permute-start = (bf16[96,6144]{1,0:T(8,128)(2,1)S(1)}, bf16[96,6144]{1,0:T(8,128)(2,1)}, u32[]{:S(2)}, u32[]{:S(2)}) collective-permute-start(bf16[96,6144]{1,0:T(8,128)(2,1)S(1)} %copy.24), channel_id=1, source_target_pairs={{0,1},{1,8},{8,9},{9,16},{16,17},{17,24},{24,25},{25,26},{26,27},{... | collective-permute-start | bytes 3538952 | tf_op jit(solution)/shard_map/while/body/eval_jaxpr/ppermute | solution.py:72
  988.1 26.9 %collective-permute-start.1 = (bf16[96,6144]{1,0:T(8,128)(2,1)}, bf16[96,6144]{1,0:T(8,128)(2,1)}, u32[]{:S(2)}, u32[]{:S(2)}) collective-permute-start(bf16[96,6144]{1,0:T(8,128)(2,1)} %copy.25), channel_id=1, source_target_pairs={{1,0},{8,1},{9,8},{16,9},{17,16},{24,17},{25,24},{26,25},{27,26},{... | collective-permute-start | bytes 3538952 | tf_op jit(solution)/shard_map/while/body/eval_jaxpr/ppermute | solution.py:73
  1016.5 29.4 %collective-permute-start = (bf16[96,6144]{1,0:T(8,128)(2,1)S(1)}, bf16[96,6144]{1,0:T(8,128)(2,1)}, u32[]{:S(2)}, u32[]{:S(2)}) collective-permute-start(bf16[96,6144]{1,0:T(8,128)(2,1)S(1)} %copy.24), channel_id=1, source_target_pairs={{0,1},{1,8},{8,9},{9,16},{16,17},{17,24},{24,25},{25,26},{26,27},{... | collective-permute-start | bytes 3538952 | tf_op jit(solution)/shard_map/while/body/eval_jaxpr/ppermute | solution.py:72
  1018.9 26.9 %collective-permute-start.1 = (bf16[96,6144]{1,0:T(8,128)(2,1)}, bf16[96,6144]{1,0:T(8,128)(2,1)}, u32[]{:S(2)}, u32[]{:S(2)}) collective-permute-start(bf16[96,6144]{1,0:T(8,128)(2,1)} %copy.25), channel_id=1, source_target_pairs={{1,0},{8,1},{9,8},{16,9},{17,16},{24,17},{25,24},{26,25},{27,26},{... | collective-permute-start | bytes 3538952 | tf_op jit(solution)/shard_map/while/body/eval_jaxpr/ppermute | solution.py:73
  1047.3 29.4 %collective-permute-start = (bf16[96,6144]{1,0:T(8,128)(2,1)S(1)}, bf16[96,6144]{1,0:T(8,128)(2,1)}, u32[]{:S(2)}, u32[]{:S(2)}) collective-permute-start(bf16[96,6144]{1,0:T(8,128)(2,1)S(1)} %copy.24), channel_id=1, source_target_pairs={{0,1},{1,8},{8,9},{9,16},{16,17},{17,24},{24,25},{25,26},{26,27},{... | collective-permute-start | bytes 3538952 | tf_op jit(solution)/shard_map/while/body/eval_jaxpr/ppermute | solution.py:72
  1049.7 26.9 %collective-permute-start.1 = (bf16[96,6144]{1,0:T(8,128)(2,1)}, bf16[96,6144]{1,0:T(8,128)(2,1)}, u32[]{:S(2)}, u32[]{:S(2)}) collective-permute-start(bf16[96,6144]{1,0:T(8,128)(2,1)} %copy.25), channel_id=1, source_target_pairs={{1,0},{8,1},{9,8},{16,9},{17,16},{24,17},{25,24},{26,25},{27,26},{... | collective-permute-start | bytes 3538952 | tf_op jit(solution)/shard_map/while/body/eval_jaxpr/ppermute | solution.py:73
  1078.0 29.4 %collective-permute-start = (bf16[96,6144]{1,0:T(8,128)(2,1)S(1)}, bf16[96,6144]{1,0:T(8,128)(2,1)}, u32[]{:S(2)}, u32[]{:S(2)}) collective-permute-start(bf16[96,6144]{1,0:T(8,128)(2,1)S(1)} %copy.24), channel_id=1, source_target_pairs={{0,1},{1,8},{8,9},{9,16},{16,17},{17,24},{24,25},{25,26},{26,27},{... | collective-permute-start | bytes 3538952 | tf_op jit(solution)/shard_map/while/body/eval_jaxpr/ppermute | solution.py:72
  1080.5 26.9 %collective-permute-start.1 = (bf16[96,6144]{1,0:T(8,128)(2,1)}, bf16[96,6144]{1,0:T(8,128)(2,1)}, u32[]{:S(2)}, u32[]{:S(2)}) collective-permute-start(bf16[96,6144]{1,0:T(8,128)(2,1)} %copy.25), channel_id=1, source_target_pairs={{1,0},{8,1},{9,8},{16,9},{17,16},{24,17},{25,24},{26,25},{27,26},{... | collective-permute-start | bytes 3538952 | tf_op jit(solution)/shard_map/while/body/eval_jaxpr/ppermute | solution.py:73
  1108.8 29.4 %collective-permute-start = (bf16[96,6144]{1,0:T(8,128)(2,1)S(1)}, bf16[96,6144]{1,0:T(8,128)(2,1)}, u32[]{:S(2)}, u32[]{:S(2)}) collective-permute-start(bf16[96,6144]{1,0:T(8,128)(2,1)S(1)} %copy.24), channel_id=1, source_target_pairs={{0,1},{1,8},{8,9},{9,16},{16,17},{17,24},{24,25},{25,26},{26,27},{... | collective-permute-start | bytes 3538952 | tf_op jit(solution)/shard_map/while/body/eval_jaxpr/ppermute | solution.py:72
  1111.3 26.9 %collective-permute-start.1 = (bf16[96,6144]{1,0:T(8,128)(2,1)}, bf16[96,6144]{1,0:T(8,128)(2,1)}, u32[]{:S(2)}, u32[]{:S(2)}) collective-permute-start(bf16[96,6144]{1,0:T(8,128)(2,1)} %copy.25), channel_id=1, source_target_pairs={{1,0},{8,1},{9,8},{16,9},{17,16},{24,17},{25,24},{26,25},{27,26},{... | collective-permute-start | bytes 3538952 | tf_op jit(solution)/shard_map/while/body/eval_jaxpr/ppermute | solution.py:73
  1139.6 29.4 %collective-permute-start = (bf16[96,6144]{1,0:T(8,128)(2,1)S(1)}, bf16[96,6144]{1,0:T(8,128)(2,1)}, u32[]{:S(2)}, u32[]{:S(2)}) collective-permute-start(bf16[96,6144]{1,0:T(8,128)(2,1)S(1)} %copy.24), channel_id=1, source_target_pairs={{0,1},{1,8},{8,9},{9,16},{16,17},{17,24},{24,25},{25,26},{26,27},{... | collective-permute-start | bytes 3538952 | tf_op jit(solution)/shard_map/while/body/eval_jaxpr/ppermute | solution.py:72
  1142.1 26.9 %collective-permute-start.1 = (bf16[96,6144]{1,0:T(8,128)(2,1)}, bf16[96,6144]{1,0:T(8,128)(2,1)}, u32[]{:S(2)}, u32[]{:S(2)}) collective-permute-start(bf16[96,6144]{1,0:T(8,128)(2,1)} %copy.25), channel_id=1, source_target_pairs={{1,0},{8,1},{9,8},{16,9},{17,16},{24,17},{25,24},{26,25},{27,26},{... | collective-permute-start | bytes 3538952 | tf_op jit(solution)/shard_map/while/body/eval_jaxpr/ppermute | solution.py:73
  1170.4 29.4 %collective-permute-start = (bf16[96,6144]{1,0:T(8,128)(2,1)S(1)}, bf16[96,6144]{1,0:T(8,128)(2,1)}, u32[]{:S(2)}, u32[]{:S(2)}) collective-permute-start(bf16[96,6144]{1,0:T(8,128)(2,1)S(1)} %copy.24), channel_id=1, source_target_pairs={{0,1},{1,8},{8,9},{9,16},{16,17},{17,24},{24,25},{25,26},{26,27},{... | collective-permute-start | bytes 3538952 | tf_op jit(solution)/shard_map/while/body/eval_jaxpr/ppermute | solution.py:72
  1172.9 26.9 %collective-permute-start.1 = (bf16[96,6144]{1,0:T(8,128)(2,1)}, bf16[96,6144]{1,0:T(8,128)(2,1)}, u32[]{:S(2)}, u32[]{:S(2)}) collective-permute-start(bf16[96,6144]{1,0:T(8,128)(2,1)} %copy.25), channel_id=1, source_target_pairs={{1,0},{8,1},{9,8},{16,9},{17,16},{24,17},{25,24},{26,25},{27,26},{... | collective-permute-start | bytes 3538952 | tf_op jit(solution)/shard_map/while/body/eval_jaxpr/ppermute | solution.py:73
  1201.2 29.4 %collective-permute-start = (bf16[96,6144]{1,0:T(8,128)(2,1)S(1)}, bf16[96,6144]{1,0:T(8,128)(2,1)}, u32[]{:S(2)}, u32[]{:S(2)}) collective-permute-start(bf16[96,6144]{1,0:T(8,128)(2,1)S(1)} %copy.24), channel_id=1, source_target_pairs={{0,1},{1,8},{8,9},{9,16},{16,17},{17,24},{24,25},{25,26},{26,27},{... | collective-permute-start | bytes 3538952 | tf_op jit(solution)/shard_map/while/body/eval_jaxpr/ppermute | solution.py:72
  1203.6 26.9 %collective-permute-start.1 = (bf16[96,6144]{1,0:T(8,128)(2,1)}, bf16[96,6144]{1,0:T(8,128)(2,1)}, u32[]{:S(2)}, u32[]{:S(2)}) collective-permute-start(bf16[96,6144]{1,0:T(8,128)(2,1)} %copy.25), channel_id=1, source_target_pairs={{1,0},{8,1},{9,8},{16,9},{17,16},{24,17},{25,24},{26,25},{27,26},{... | collective-permute-start | bytes 3538952 | tf_op jit(solution)/shard_map/while/body/eval_jaxpr/ppermute | solution.py:73
  1232.0 29.4 %collective-permute-start = (bf16[96,6144]{1,0:T(8,128)(2,1)S(1)}, bf16[96,6144]{1,0:T(8,128)(2,1)}, u32[]{:S(2)}, u32[]{:S(2)}) collective-permute-start(bf16[96,6144]{1,0:T(8,128)(2,1)S(1)} %copy.24), channel_id=1, source_target_pairs={{0,1},{1,8},{8,9},{9,16},{16,17},{17,24},{24,25},{25,26},{26,27},{... | collective-permute-start | bytes 3538952 | tf_op jit(solution)/shard_map/while/body/eval_jaxpr/ppermute | solution.py:72
  1234.4 26.9 %collective-permute-start.1 = (bf16[96,6144]{1,0:T(8,128)(2,1)}, bf16[96,6144]{1,0:T(8,128)(2,1)}, u32[]{:S(2)}, u32[]{:S(2)}) collective-permute-start(bf16[96,6144]{1,0:T(8,128)(2,1)} %copy.25), channel_id=1, source_target_pairs={{1,0},{8,1},{9,8},{16,9},{17,16},{24,17},{25,24},{26,25},{27,26},{... | collective-permute-start | bytes 3538952 | tf_op jit(solution)/shard_map/while/body/eval_jaxpr/ppermute | solution.py:73
  (63 other events, 840.7 us)
Sparse Core Ops, SparseCore 0:
  55.8 793.5 reduce-scatter.1

commit v4 on v0

v4 whole, which is shorter than its diff:
```python
import math

import jax
import jax.numpy as jnp
from jax import lax
from jax.sharding import Mesh
from jax.sharding import PartitionSpec as P

DP = ("chip", "core")


def per_device(context, weight, moment_one, moment_two, grad_out):
    rows = weight.shape[0]
    tok_rows, local_cols = context.shape
    chips = lax.axis_size("chip")
    weight_bf = weight.astype(jnp.bfloat16)
    piece = lax.all_gather(grad_out, "mp", axis=0, tiled=True)
    width = piece.shape[1]
    swap = [(0, 1), (1, 0)]
    ctx_split = context.reshape(tok_rows, chips, 2, rows)
    me = lax.axis_index("core")
    ctx_own = jnp.where(me == 0, ctx_split[:, :, 0], ctx_split[:, :, 1]).reshape(tok_rows, chips * rows)
    ctx_other = jnp.where(me == 0, ctx_split[:, :, 1], ctx_split[:, :, 0]).reshape(tok_rows, chips * rows)
    dims_wgrad = (((0,), (0,)), ((), ()))

    grad_for_other = lax.dot_general(
        ctx_other, piece, dims_wgrad, preferred_element_type=jnp.float32
    ).astype(jnp.bfloat16)
    grad_from_other = lax.ppermute(grad_for_other, "core", swap)

    own_half = lax.all_gather(weight_bf, "chip", axis=0, tiled=True)
    grad_mine = lax.dot_general(ctx_own, piece, dims_wgrad, preferred_element_type=jnp.float32)
    chip_grad = (grad_mine + grad_from_other.astype(jnp.float32)).astype(jnp.bfloat16)
    chip_grad, own_half = lax.optimization_barrier((chip_grad, own_half))
    grad_shard = lax.psum_scatter(chip_grad, "chip", scatter_dimension=0, tiled=True).astype(jnp.float32)

    other_half = lax.ppermute(own_half, "core", swap)
    out = jnp.dot(ctx_own, own_half, preferred_element_type=jnp.float32)
    d_own = lax.dot_general(piece, own_half, (((1,), (1,)), ((), ())), preferred_element_type=jnp.float32)
    out = out + jnp.dot(ctx_other, other_half, preferred_element_type=jnp.float32)
    d_other = lax.dot_general(
        piece, other_half, (((1,), (1,)), ((), ())), preferred_element_type=jnp.float32
    )
    summed = lax.psum_scatter(out.astype(jnp.bfloat16), "mp", scatter_dimension=0, tiled=True)
    d_own = d_own.astype(jnp.bfloat16).reshape(tok_rows, chips, rows)
    d_other = d_other.astype(jnp.bfloat16).reshape(tok_rows, chips, rows)
    first = jnp.where(me == 0, d_own, d_other)
    second = jnp.where(me == 0, d_other, d_own)
    d_context = jnp.stack([first, second], axis=2).reshape(tok_rows, local_cols)

    tokens_all = tok_rows * chips * 2
    grad = grad_shard * (1.0 / math.sqrt(tokens_all))
    new_moment_one = 0.9 * moment_one + 0.1 * grad
    new_moment_two = 0.999 * moment_two + 0.001 * grad * grad
    first_fix = 1.0 - 0.9**10
    second_fix = 1.0 - 0.999**10
    update = (
        new_moment_one / first_fix / (jnp.sqrt(new_moment_two / second_fix) + 1e-08) + 0.1 * weight
    )
    new_weight = weight - 0.001 * update
    return (summed, d_context, new_weight, new_moment_one, new_moment_two)


def solution(mesh):
    names = mesh.axis_names
    devices = mesh.devices.transpose([names.index("dp"), names.index("mp")])
    n_dp, n_mp = devices.shape
    split = Mesh(devices.reshape(n_dp // 2, 2, n_mp), ("chip", "core", "mp"))
    placed = (
        P(DP, "mp"),
        P(("mp",) + DP, None),
        P(("mp",) + DP, None),
        P(("mp",) + DP, None),
        P(DP + ("mp",), None),
    )
    return jax.shard_map(
        per_device,
        mesh=split,
        in_specs=placed,
        out_specs=(
            P(DP + ("mp",), None),
            P(DP, "mp"),
            P(("mp",) + DP, None),
            P(("mp",) + DP, None),
            P(("mp",) + DP, None),
        ),
        check_vma=False,
    )
```

time: 1230 us -> 978 us (0.80)
  waiting for transfers between devices: 1050 us -> 734 us
  matrix products: 143 us -> 177 us
  local copies, waits for them, and re-layouts: 0 us -> 17.4 us
  other arithmetic: 13.8 us -> 27.3 us
    reduce_scatter x1, waiting for transfers between devices: 659 us -> 364 us  [per_device(): lax.psum_scatter(chip_grad, 'chip', scatter_dimension=0, tiled=True)]
    all_gather x1, waiting for transfers between devices: 396 us -> 259 us  [per_device(): own_half = lax.all_gather(weight_bf, 'chip', axis=0, tiled=True)]
    ppermute x0 -> x2, waiting for transfers between devices: none -> 111 us  [the longest x1 55.5 us: per_device(): other_half = lax.ppermute(own_half, 'core', swap)]
    dot_general x3 -> x6, matrix products: 143 us -> 177 us  [the longest x1 35.8 us: per_device(): lax.dot_general(ctx_own, piece, dims_wgrad, preferred_element_type=jnp.fl...]
    unnamed x0 -> x2, local copies, waits for them, and re-layouts: none -> 17.4 us
  transfers between devices with their start and end apart: 2 -> 4, of which waited for: 2 -> 4; matrix products, arithmetic and copies ran while one was open for 0% -> 21% of each run, Pallas kernels for 0% -> 0%
where the time goes in v4:
time: 978 us; the launch traced here: 971 us
  waiting for transfers between devices  734 us (75%)
  matrix products  177 us (18%)
  other arithmetic  27.3 us (3%)
  local copies, waits for them, and re-layouts  17.4 us (2%)
  between operations  14.3 us (1%)
    reduce_scatter x1, waiting for transfers between devices, per_device(): lax.psum_scatter(chip_grad, 'chip', scatter_dimension=0, tiled=True)  364 us
    all_gather x1, waiting for transfers between devices, per_device(): own_half = lax.all_gather(weight_bf, 'chip', axis=0, tiled=True)  259 us
    ppermute x1, waiting for transfers between devices, per_device(): other_half = lax.ppermute(own_half, 'core', swap)  55.5 us
    ppermute x1, waiting for transfers between devices, per_device(): grad_from_other = lax.ppermute(grad_for_other, 'core', swap)  55.1 us
    dot_general x1, matrix products, per_device(): lax.dot_general(ctx_own, piece, dims_wgrad, preferred_element_type=jnp.fl...  35.8 us
    dot_general x1, matrix products, per_device(): lax.dot_general(piece, own_half, (((1,), (1,)), ((), ())), preferred_elem...  28.6 us
    dot_general x1, matrix products, per_device(): lax.dot_general(ctx_other, piece, dims_wgrad, preferred_element_type=jnp....  28.3 us
    dot_general x1, matrix products, per_device(): lax.dot_general(piece, other_half, (((1,), (1,)), ((), ())), preferred_el...  28.2 us
  transfers between devices with their start and end apart: 4, of which 4 were waited for; matrix products, arithmetic and copies ran while one was open for 21% of the time, Pallas kernels for 0%

profile of v4, /device:TPU:0, one launch (start us, length us, event | category | flops | bytes accessed | tf_op | source)
XLA Modules:
  0.0 970.7 jit_solution(7771107328413126171)
XLA Ops:
  7.2 0.0 all-gather.2.cloned.1.call-start
  7.2 4.1 convert_element_type.29
  11.3 0.0 all-gather.2.cloned.1.call-update
  11.3 0.0 reduce-scatter.2.cloned.1.call-start
  11.3 8.6 copy.11
  20.0 5.5 broadcast_select_fusion.2
  25.5 28.3 %convolution_convert_fusion = bf16[3072,6144]{1,0:T(8,128)(2,1)} fusion(bf16[512,3072]{0,1:T(8,128)(2,1)} %bitcast.30, bf16[512,6144]{1,0:T(8,128)(2,1)} %param.9), kind=kOutput, calls=%fused_computation.1 | convolution fusion | flops 19346227200 | bytes 47185920 | tf_op jit(solution)/shard_map/dot_general | solution.py:26
  53.8 0.5 collective-permute-start
  54.3 55.1 %collective-permute-done = bf16[3072,6144]{1,0:T(8,128)(2,1)} collective-permute-done((bf16[3072,6144]{1,0:T(8,128)(2,1)}, bf16[3072,6144]{1,0:T(8,128)(2,1)}, u32[]{:S(2)}, u32[]{:S(2)}) %collective-permute-start) | collective-permute-done | bytes 37748768 | tf_op jit(solution)/shard_map/ppermute | solution.py:29
  109.4 35.8 %add_convert_fusion = bf16[3072,6144]{1,0:T(8,128)(2,1)} fusion(bf16[3072,6144]{1,0:T(8,128)(2,1)} %collective-permute-done, bf16[512,3072]{0,1:T(8,128)(2,1)S(1)} %bitcast.28, bf16[512,6144]{1,0:T(8,128)(2,1)} %param.9), kind=kOutput, calls=%fused_computation | convolution fusion | flops 19383975936 | bytes 84934656 | tf_op jit(solution)/shard_map/dot_general | solution.py:32
  145.3 259.3 %all-gather.2.cloned.1.call-done = bf16[3072,6144]{1,0:T(8,128)(2,1)} async-done(((bf16[192,6144]{1,0:T(8,128)(2,1)}), bf16[3072,6144]{1,0:T(8,128)(2,1)}) %all-gather.2.cloned.1.call-update) | async-done | bytes 37748752 | tf_op jit(solution)/shard_map/all_gather | solution.py:31
  404.6 0.0 reduce-scatter.2.cloned.1.call-update
  404.6 0.1 collective-permute-start.1
  404.7 55.5 %collective-permute-done.1 = bf16[3072,6144]{1,0:T(8,128)(2,1)} collective-permute-done((bf16[3072,6144]{1,0:T(8,128)(2,1)}, bf16[3072,6144]{1,0:T(8,128)(2,1)}, u32[]{:S(2)}, u32[]{:S(2)}) %collective-permute-start.1) | collective-permute-done | bytes 37748768 | tf_op jit(solution)/shard_map/ppermute | solution.py:37
  460.2 28.2 %convolution_convert_fusion.1 = bf16[3072,512]{1,0:T(8,128)(2,1)} fusion(bf16[3072,6144]{1,0:T(8,128)(2,1)} %collective-permute-done.1, bf16[512,6144]{1,0:T(8,128)(2,1)} %param.9), kind=kOutput, calls=%fused_computation.11 | convolution fusion | flops 19328925696 | bytes 47185920 | tf_op jit(solution)/shard_map/dot_general | solution.py:41
  488.4 28.6 %broadcast_select_fusion.1 = (bf16[3072,512]{1,0:T(8,128)(2,1)}, bf16[3072,512]{1,0:T(8,128)(2,1)}) fusion(bf16[3072,512]{1,0:T(8,128)(2,1)} %convolution_convert_fusion.1, pred[]{:T(512)S(6)} %eq.2, bf16[3072,6144]{1,0:T(8,128)(2,1)} %all-gather.2.cloned.1.call-done, bf16[512,6144]{1,0:T(8,128)(2,1)} %param.9), kind=kOutput, calls=%fused_computation.14 | convolution fusion | flops 19332071424 | bytes 53477376 | tf_op jit(solution)/shard_map/dot_general | solution.py:39
  517.0 6.4 pad_maximum_fusion
  523.4 8.8 copy.14
  532.1 28.1 %fusion.5 = f32[512,6144]{1,0:T(8,128)} fusion(bf16[512,3072]{0,1:T(8,128)(2,1)} %bitcast.31, bf16[3072,6144]{1,0:T(8,128)(2,1)} %collective-permute-done.1), kind=kOutput, calls=%fused_computation.17 | convolution fusion | flops 19327352832 | bytes 53477376 | tf_op jit(solution)/shard_map/dot_general | solution.py:40
  560.2 27.8 %add_convert_fusion.1 = bf16[512,6144]{1,0:T(8,128)(2,1)} fusion(f32[512,6144]{1,0:T(8,128)} %fusion.5, bf16[512,3072]{0,1:T(8,128)(2,1)S(1)} %bitcast.29, bf16[3072,6144]{1,0:T(8,128)(2,1)} %all-gather.2.cloned.1.call-done), kind=kOutput, calls=%fused_computation.2 | convolution fusion | flops 19333644288 | bytes 59768832 | tf_op jit(solution)/shard_map/dot_general | solution.py:38
  588.1 364.2 %reduce-scatter.2.cloned.1.call-done = bf16[192,6144]{1,0:T(8,128)(2,1)} async-done(((bf16[3072,6144]{1,0:T(8,128)(2,1)}), bf16[192,6144]{1,0:T(8,128)(2,1)}) %reduce-scatter.2.cloned.1.call-update) | async-done | bytes 2359312 | tf_op jit(solution)/shard_map/reduce_scatter | solution.py:35
  952.3 11.3 %multiply_subtract_fusion = (f32[192,6144]{1,0:T(8,128)}, f32[192,6144]{1,0:T(8,128)}, f32[192,6144]{1,0:T(8,128)}) fusion(f32[192,6144]{1,0:T(8,128)} %param.6, bf16[192,6144]{1,0:T(8,128)(2,1)} %reduce-scatter.2.cloned.1.call-done, f32[192,6144]{1,0:T(8,128)} %param.7, f32[192,6144]{1,0:T(8,128)} %param.8), kind=kLoop, calls=%fused_computation.10 | loop fusion | flops 20054016 | bytes 30670848 | tf_op jit(solution)/shard_map/sub | solution.py:60
Async XLA Ops:
  7.2 397.5 %all-gather.2.cloned.1.call-start = ((), (), s32[]{:S(2)}) async-start(), calls=%async_computation.1 | async-start | bytes 40108032 | tf_op jit(solution)/shard_map/all_gather | solution.py:31
  11.3 941.0 %reduce-scatter.2.cloned.1.call-start = ((), (), s32[]{:S(2)}) async-start(), calls=%async_computation.2 | async-start | bytes 40108032 | tf_op jit(solution)/shard_map/reduce_scatter | solution.py:35
  53.8 55.6 %collective-permute-start = (bf16[3072,6144]{1,0:T(8,128)(2,1)}, bf16[3072,6144]{1,0:T(8,128)(2,1)}, u32[]{:S(2)}, u32[]{:S(2)}) collective-permute-start(bf16[3072,6144]{1,0:T(8,128)(2,1)} %convolution_convert_fusion), channel_id=1, source_target_pairs={{0,1},{1,0},{2,3},{3,2},{4,5},{5,4},{6,7},{7,6},{8,9},{9,8},{10,11... | collective-permute-start | bytes 113246216 | tf_op jit(solution)/shard_map/ppermute | solution.py:29
  404.6 55.6 %collective-permute-start.1 = (bf16[3072,6144]{1,0:T(8,128)(2,1)}, bf16[3072,6144]{1,0:T(8,128)(2,1)}, u32[]{:S(2)}, u32[]{:S(2)}) collective-permute-start(bf16[3072,6144]{1,0:T(8,128)(2,1)} %all-gather.2.cloned.1.call-done), channel_id=1, source_target_pairs={{0,1},{1,0},{2,3},{3,2},{4,5},{5,4},{6,7},{7,6},{8,9},{9,8},{10,11... | collective-permute-start | bytes 113246216 | tf_op jit(solution)/shard_map/ppermute | solution.py:37
Sparse Core Ops, SparseCore 0:
  11.4 393.1 all-gather.1
  410.6 541.6 reduce-scatter.1

commit v5 on v4

--- a/solution.py
+++ b/solution.py
@@ -2,11 +2,22 @@
 
 import jax
 import jax.numpy as jnp
+import numpy as np
 from jax import lax
 from jax.sharding import Mesh
 from jax.sharding import PartitionSpec as P
 
 DP = ("chip", "core")
+
+
+def chip_cycle(n):
+    if n != 16:
+        return list(range(n))
+    order = []
+    for i, (x, y) in enumerate(((0, 0), (1, 0), (1, 1), (0, 1))):
+        for z in range(4) if i % 2 == 0 else range(3, -1, -1):
+            order.append((z * 2 + y) * 2 + x)
+    return order
 
 
 def per_device(context, weight, moment_one, moment_two, grad_out):
@@ -28,25 +39,47 @@
     ).astype(jnp.bfloat16)
     grad_from_other = lax.ppermute(grad_for_other, "core", swap)
 
-    own_half = lax.all_gather(weight_bf, "chip", axis=0, tiled=True)
     grad_mine = lax.dot_general(ctx_own, piece, dims_wgrad, preferred_element_type=jnp.float32)
     chip_grad = (grad_mine + grad_from_other.astype(jnp.float32)).astype(jnp.bfloat16)
-    chip_grad, own_half = lax.optimization_barrier((chip_grad, own_half))
-    grad_shard = lax.psum_scatter(chip_grad, "chip", scatter_dimension=0, tiled=True).astype(jnp.float32)
+    weight_bf, chip_grad = lax.optimization_barrier((weight_bf, chip_grad))
+    full_weight = lax.all_gather(weight_bf, DP, axis=0, tiled=True)
 
-    other_half = lax.ppermute(own_half, "core", swap)
-    out = jnp.dot(ctx_own, own_half, preferred_element_type=jnp.float32)
-    d_own = lax.dot_general(piece, own_half, (((1,), (1,)), ((), ())), preferred_element_type=jnp.float32)
-    out = out + jnp.dot(ctx_other, other_half, preferred_element_type=jnp.float32)
-    d_other = lax.dot_general(
-        piece, other_half, (((1,), (1,)), ((), ())), preferred_element_type=jnp.float32
-    )
+    n = chips
+    order = chip_cycle(n)
+    position = [0] * n
+    for i, c in enumerate(order):
+        position[c] = i
+    forward = [(order[i], order[(i + 1) % n]) for i in range(n)]
+    backward = [(order[(i + 1) % n], order[i]) for i in range(n)]
+    order_arr = jnp.asarray(np.array(order, np.int32))
+    pos = jnp.asarray(np.array(position, np.int32))[lax.axis_index("chip")]
+    half = width // 2
+
+    def own_block(block):
+        return lax.dynamic_slice_in_dim(chip_grad, block * rows, rows, 0).astype(jnp.float32)
+
+    def ring_step(step, carry):
+        send_cw, send_ccw = carry
+        recv_cw = lax.ppermute(send_cw, "chip", forward)
+        recv_ccw = lax.ppermute(send_ccw, "chip", backward)
+        mine_cw = own_block(order_arr[(pos - step - 2) % n])[:, :half]
+        mine_ccw = own_block(order_arr[(pos + step + 2) % n])[:, half:]
+        return (
+            (recv_cw.astype(jnp.float32) + mine_cw).astype(jnp.bfloat16),
+            (recv_ccw.astype(jnp.float32) + mine_ccw).astype(jnp.bfloat16),
+        )
+
+    start_cw = own_block(order_arr[(pos - 1) % n])[:, :half].astype(jnp.bfloat16)
+    start_ccw = own_block(order_arr[(pos + 1) % n])[:, half:].astype(jnp.bfloat16)
+    done_cw, done_ccw = lax.fori_loop(0, n - 1, ring_step, (start_cw, start_ccw))
+    grad_shard = jnp.concatenate([done_cw, done_ccw], axis=1).astype(jnp.float32)
+    full_weight, grad_shard = lax.optimization_barrier((full_weight, grad_shard))
+
+    out = jnp.dot(context, full_weight, preferred_element_type=jnp.float32)
     summed = lax.psum_scatter(out.astype(jnp.bfloat16), "mp", scatter_dimension=0, tiled=True)
-    d_own = d_own.astype(jnp.bfloat16).reshape(tok_rows, chips, rows)
-    d_other = d_other.astype(jnp.bfloat16).reshape(tok_rows, chips, rows)
-    first = jnp.where(me == 0, d_own, d_other)
-    second = jnp.where(me == 0, d_other, d_own)
-    d_context = jnp.stack([first, second], axis=2).reshape(tok_rows, local_cols)
+    d_context = lax.dot_general(
+        piece, full_weight, (((1,), (1,)), ((), ())), preferred_element_type=jnp.float32
+    ).astype(jnp.bfloat16)
 
     tokens_all = tok_rows * chips * 2
     grad = grad_shard * (1.0 / math.sqrt(tokens_all))

time: 978 us -> 1040 us (1.063)
  waiting for transfers between devices: 734 us -> 638 us
  starting transfers between devices: 0.64 us -> 64.6 us
  other arithmetic: 27.3 us -> 78.1 us
  loops' own time: 0 us -> 40.4 us
  local copies, waits for them, and re-layouts: 17.4 us -> 39.9 us
  matrix products: 177 us -> 159 us
    ppermute x1 -> x30, waiting for transfers between devices: 55.5 us -> 587 us  [the longest x15 580 us: ring_step(): recv_ccw = lax.ppermute(send_ccw, 'chip', backward)]
    reduce_scatter x1 -> x0, waiting for transfers between devices: 364 us -> none  [per_device(): lax.psum_scatter(chip_grad, 'chip', scatter_dimension=0, tiled=True)]
    all_gather x1, waiting for transfers between devices: 259 us -> 0.01 us  [per_device(): full_weight = lax.all_gather(weight_bf, DP, axis=0, tiled=True)]
    ppermute x1 -> x30, starting transfers between devices: 0.07 us -> 64.1 us  [the longest x15 44.8 us: ring_step(): recv_ccw = lax.ppermute(send_ccw, 'chip', backward)]
    convert_element_type x0 -> x16, other arithmetic: none -> 57.1 us  [the longest x15 53.1 us: ring_step(): (recv_ccw.astype(jnp.float32) + mine_ccw).astype(jnp.bfloat16)]
    another operation x0 -> x1, loops' own time: none -> 40.4 us  [per_device(): lax.fori_loop(0, n - 1, ring_step, (start_cw, start_ccw))]
    dot_general x4 -> x2, matrix products: 113 us -> 95.1 us  [the longest x1 47.6 us: per_device(): out = jnp.dot(context, full_weight, preferred_element_type=jnp.float32)]
    dynamic_slice x0 -> x17, local copies, waits for them, and re-layouts: none -> 11.2 us  [the longest x15 10 us: ring_step(): mine_ccw = own_block(order_arr[(pos + step + 2) % n])[:, half:]]
  transfers between devices with their start and end apart: 4 -> 32, of which waited for: 4 -> 24; matrix products, arithmetic and copies ran while one was open for 21% -> 7% of each run, Pallas kernels for 0% -> 0%
where the time goes in v5:
time: 1040 us
  waiting for transfers between devices  638 us (61%)
  matrix products  159 us (15%)
  other arithmetic  78.1 us (8%)
  starting transfers between devices  64.6 us (6%)
  loops' own time  40.4 us (4%)
  local copies, waits for them, and re-layouts  39.9 us (4%)
  between operations  16.7 us (2%)
    ppermute x15, waiting for transfers between devices, ring_step(): recv_ccw = lax.ppermute(send_ccw, 'chip', backward)  580 us
    convert_element_type x15, other arithmetic, ring_step(): (recv_ccw.astype(jnp.float32) + mine_ccw).astype(jnp.bfloat16)  53.1 us
    ppermute x1, waiting for transfers between devices, per_device(): grad_from_other = lax.ppermute(grad_for_other, 'core', swap)  51.1 us
    dot_general x1, matrix products, per_device(): out = jnp.dot(context, full_weight, preferred_element_type=jnp.float32)  47.6 us
    dot_general x1, matrix products, per_device(): lax.dot_general(piece, full_weight, (((1,), (1,)), ((), ())), preferred_e...  47.4 us
    ppermute x15, starting transfers between devices, ring_step(): recv_ccw = lax.ppermute(send_ccw, 'chip', backward)  44.8 us
    another operation x1, loops' own time, per_device(): lax.fori_loop(0, n - 1, ring_step, (start_cw, start_ccw))  40.4 us
    dot_general x1, matrix products, per_device(): lax.dot_general(ctx_own, piece, dims_wgrad, preferred_element_type=jnp.fl...  35.8 us
  transfers between devices with their start and end apart: 32, of which 24 were waited for; matrix products, arithmetic and copies ran while one was open for 7% of the time, Pallas kernels for 0%

profile of v5, /device:TPU:0, one launch (start us, length us, event | category | flops | bytes accessed | tf_op | source)
XLA Modules:
  0.0 1036.5 jit_solution(13480498033877441387)
XLA Ops:
  7.2 8.6 copy.14
  15.8 4.2 broadcast_select_fusion
  20.0 27.7 %convolution_convert_fusion = bf16[3072,6144]{1,0:T(8,128)(2,1)} fusion(bf16[512,3072]{0,1:T(8,128)(2,1)} %bitcast.26, bf16[512,6144]{1,0:T(8,128)(2,1)} %param.13), kind=kOutput, calls=%fused_computation.3 | convolution fusion | flops 19346227200 | bytes 47185920 | tf_op jit(solution)/shard_map/dot_general | solution.py:37
  48.2 4.1 convert_element_type.87
  52.2 51.1 %collective-permute-done.2 = bf16[3072,6144]{1,0:T(8,128)(2,1)} collective-permute-done((bf16[3072,6144]{1,0:T(8,128)(2,1)}, bf16[3072,6144]{1,0:T(8,128)(2,1)}, u32[]{:S(2)}, u32[]{:S(2)}) %collective-permute-start.2) | collective-permute-done | bytes 37748768 | tf_op jit(solution)/shard_map/ppermute | solution.py:40
  103.3 35.8 %add_convert_fusion.2 = bf16[3072,6144]{1,0:T(8,128)(2,1)} fusion(bf16[3072,6144]{1,0:T(8,128)(2,1)} %collective-permute-done.2, bf16[512,3072]{0,1:T(8,128)(2,1)S(1)} %bitcast.25, bf16[512,6144]{1,0:T(8,128)(2,1)} %param.13), kind=kOutput, calls=%fused_computation.2 | convolution fusion | flops 19383975936 | bytes 84934656 | tf_op jit(solution)/shard_map/dot_general | solution.py:42
  142.9 2.8 fusion.3
  145.7 754.8 %while.18 = (s32[]{:T(128)}, bf16[192,3072]{1,0:T(8,128)(2,1)}, bf16[192,3072]{1,0:T(8,128)(2,1)S(1)}, s32[]{:T(128)}, bf16[3072,6144]{1,0:T(8,128)(2,1)}, /*ind...) while((s32[]{:T(128)}, bf16[192,3072]{1,0:T(8,128)(2,1)}, ...), condition=%wide.region_1.2_spmd.clone, body=%wide.region_0.1_spmd.sunk.clone.sunk | while | flops 4718635 | bytes 16515767 | solution.py:74
  145.7 2.9 collective-permute-start
  152.1 61.5 %collective-permute-done = bf16[192,3072]{1,0:T(8,128)(2,1)S(1)} collective-permute-done((bf16[192,3072]{1,0:T(8,128)(2,1)S(1)}, bf16[192,3072]{1,0:T(8,128)(2,1)S(1)}, u32[]{:S(2)}, u32[]{:S(2)}) %collective-permute-start) | collective-permute-done | bytes 1179680 | tf_op jit(solution)/shard_map/while/body/eval_jaxpr/ppermute | solution.py:64
  213.6 3.5 add_convert_fusion.4
  217.1 8.3 collective-permute-start
  228.8 48.2 %collective-permute-done = bf16[192,3072]{1,0:T(8,128)(2,1)S(1)} collective-permute-done((bf16[192,3072]{1,0:T(8,128)(2,1)S(1)}, bf16[192,3072]{1,0:T(8,128)(2,1)S(1)}, u32[]{:S(2)}, u32[]{:S(2)}) %collective-permute-start) | collective-permute-done | bytes 1179680 | tf_op jit(solution)/shard_map/while/body/eval_jaxpr/ppermute | solution.py:64
  277.0 3.5 add_convert_fusion.4
  280.5 6.6 collective-permute-start
  287.2 2.1 collective-permute-start.1
  292.6 72.3 %collective-permute-done = bf16[192,3072]{1,0:T(8,128)(2,1)S(1)} collective-permute-done((bf16[192,3072]{1,0:T(8,128)(2,1)S(1)}, bf16[192,3072]{1,0:T(8,128)(2,1)S(1)}, u32[]{:S(2)}, u32[]{:S(2)}) %collective-permute-start) | collective-permute-done | bytes 1179680 | tf_op jit(solution)/shard_map/while/body/eval_jaxpr/ppermute | solution.py:64
  364.9 3.5 add_convert_fusion.4
  368.4 4.3 collective-permute-start
  376.0 36.2 %collective-permute-done = bf16[192,3072]{1,0:T(8,128)(2,1)S(1)} collective-permute-done((bf16[192,3072]{1,0:T(8,128)(2,1)S(1)}, bf16[192,3072]{1,0:T(8,128)(2,1)S(1)}, u32[]{:S(2)}, u32[]{:S(2)}) %collective-permute-start) | collective-permute-done | bytes 1179680 | tf_op jit(solution)/shard_map/while/body/eval_jaxpr/ppermute | solution.py:64
  412.3 3.5 add_convert_fusion.4
  415.8 4.3 collective-permute-start
  420.1 4.0 collective-permute-start.1
  427.4 72.9 %collective-permute-done = bf16[192,3072]{1,0:T(8,128)(2,1)S(1)} collective-permute-done((bf16[192,3072]{1,0:T(8,128)(2,1)S(1)}, bf16[192,3072]{1,0:T(8,128)(2,1)S(1)}, u32[]{:S(2)}, u32[]{:S(2)}) %collective-permute-start) | collective-permute-done | bytes 1179680 | tf_op jit(solution)/shard_map/while/body/eval_jaxpr/ppermute | solution.py:64
  500.3 3.5 add_convert_fusion.4
  503.9 4.3 collective-permute-start
  508.2 2.8 collective-permute-start.1
  514.3 71.1 %collective-permute-done = bf16[192,3072]{1,0:T(8,128)(2,1)S(1)} collective-permute-done((bf16[192,3072]{1,0:T(8,128)(2,1)S(1)}, bf16[192,3072]{1,0:T(8,128)(2,1)S(1)}, u32[]{:S(2)}, u32[]{:S(2)}) %collective-permute-start) | collective-permute-done | bytes 1179680 | tf_op jit(solution)/shard_map/while/body/eval_jaxpr/ppermute | solution.py:64
  585.5 3.7 add_convert_fusion.4
  589.2 3.0 collective-permute-start
  596.8 73.0 %collective-permute-done = bf16[192,3072]{1,0:T(8,128)(2,1)S(1)} collective-permute-done((bf16[192,3072]{1,0:T(8,128)(2,1)S(1)}, bf16[192,3072]{1,0:T(8,128)(2,1)S(1)}, u32[]{:S(2)}, u32[]{:S(2)}) %collective-permute-start) | collective-permute-done | bytes 1179680 | tf_op jit(solution)/shard_map/while/body/eval_jaxpr/ppermute | solution.py:64
  669.7 3.5 add_convert_fusion.4
  673.3 5.1 collective-permute-start
  681.8 24.1 %collective-permute-done = bf16[192,3072]{1,0:T(8,128)(2,1)S(1)} collective-permute-done((bf16[192,3072]{1,0:T(8,128)(2,1)S(1)}, bf16[192,3072]{1,0:T(8,128)(2,1)S(1)}, u32[]{:S(2)}, u32[]{:S(2)}) %collective-permute-start) | collective-permute-done | bytes 1179680 | tf_op jit(solution)/shard_map/while/body/eval_jaxpr/ppermute | solution.py:64
  706.1 3.5 add_convert_fusion.4
  709.6 3.0 collective-permute-start
  715.9 19.0 %collective-permute-done = bf16[192,3072]{1,0:T(8,128)(2,1)S(1)} collective-permute-done((bf16[192,3072]{1,0:T(8,128)(2,1)S(1)}, bf16[192,3072]{1,0:T(8,128)(2,1)S(1)}, u32[]{:S(2)}, u32[]{:S(2)}) %collective-permute-start) | collective-permute-done | bytes 1179680 | tf_op jit(solution)/shard_map/while/body/eval_jaxpr/ppermute | solution.py:64
  734.9 3.3 collective-permute-done.1
  738.2 3.5 add_convert_fusion.4
  741.7 1.7 collective-permute-start
  747.1 19.1 %collective-permute-done = bf16[192,3072]{1,0:T(8,128)(2,1)S(1)} collective-permute-done((bf16[192,3072]{1,0:T(8,128)(2,1)S(1)}, bf16[192,3072]{1,0:T(8,128)(2,1)S(1)}, u32[]{:S(2)}, u32[]{:S(2)}) %collective-permute-start) | collective-permute-done | bytes 1179680 | tf_op jit(solution)/shard_map/while/body/eval_jaxpr/ppermute | solution.py:64
  766.2 1.7 collective-permute-done.1
  767.9 3.5 add_convert_fusion.4
  771.9 1.5 collective-permute-start.1
  776.8 17.9 %collective-permute-done = bf16[192,3072]{1,0:T(8,128)(2,1)S(1)} collective-permute-done((bf16[192,3072]{1,0:T(8,128)(2,1)S(1)}, bf16[192,3072]{1,0:T(8,128)(2,1)S(1)}, u32[]{:S(2)}, u32[]{:S(2)}) %collective-permute-start) | collective-permute-done | bytes 1179680 | tf_op jit(solution)/shard_map/while/body/eval_jaxpr/ppermute | solution.py:64
  795.2 3.5 add_convert_fusion.4
  799.0 1.7 collective-permute-start.1
  804.1 17.1 %collective-permute-done = bf16[192,3072]{1,0:T(8,128)(2,1)S(1)} collective-permute-done((bf16[192,3072]{1,0:T(8,128)(2,1)S(1)}, bf16[192,3072]{1,0:T(8,128)(2,1)S(1)}, u32[]{:S(2)}, u32[]{:S(2)}) %collective-permute-start) | collective-permute-done | bytes 1179680 | tf_op jit(solution)/shard_map/while/body/eval_jaxpr/ppermute | solution.py:64
  821.4 3.5 add_convert_fusion.4
  825.1 1.8 collective-permute-start.1
  830.3 17.0 %collective-permute-done = bf16[192,3072]{1,0:T(8,128)(2,1)S(1)} collective-permute-done((bf16[192,3072]{1,0:T(8,128)(2,1)S(1)}, bf16[192,3072]{1,0:T(8,128)(2,1)S(1)}, u32[]{:S(2)}, u32[]{:S(2)}) %collective-permute-start) | collective-permute-done | bytes 1179680 | tf_op jit(solution)/shard_map/while/body/eval_jaxpr/ppermute | solution.py:64
  847.6 3.5 add_convert_fusion.4
  851.2 2.0 collective-permute-start.1
  856.5 16.8 %collective-permute-done = bf16[192,3072]{1,0:T(8,128)(2,1)S(1)} collective-permute-done((bf16[192,3072]{1,0:T(8,128)(2,1)S(1)}, bf16[192,3072]{1,0:T(8,128)(2,1)S(1)}, u32[]{:S(2)}, u32[]{:S(2)}) %collective-permute-start) | collective-permute-done | bytes 1179680 | tf_op jit(solution)/shard_map/while/body/eval_jaxpr/ppermute | solution.py:64
  873.8 3.5 add_convert_fusion.4
  877.4 2.0 collective-permute-start.1
  882.7 14.0 %collective-permute-done = bf16[192,3072]{1,0:T(8,128)(2,1)S(1)} collective-permute-done((bf16[192,3072]{1,0:T(8,128)(2,1)S(1)}, bf16[192,3072]{1,0:T(8,128)(2,1)S(1)}, u32[]{:S(2)}, u32[]{:S(2)}) %collective-permute-start) | collective-permute-done | bytes 1179680 | tf_op jit(solution)/shard_map/while/body/eval_jaxpr/ppermute | solution.py:64
  897.0 3.5 add_convert_fusion.4
  900.5 4.0 maximum_convert_fusion
  904.5 47.6 %fusion = bf16[512,6144]{0,1:T(8,128)(2,1)} fusion(bf16[6144,6144]{1,0:T(8,128)(2,1)} %all-gather.2.cloned.1.call-done, bf16[512,6144]{1,0:T(8,128)(2,1)} %param.9), kind=kOutput, calls=%fused_computation.6 | convolution fusion | flops 38657851392 | bytes 88080384 | tf_op jit(solution)/shard_map/dot_general | solution.py:78
  952.1 47.4 %fusion.1 = bf16[512,6144]{0,1:T(8,128)(2,1)} fusion(bf16[6144,6144]{1,0:T(8,128)(2,1)} %all-gather.2.cloned.1.call-done, bf16[512,6144]{1,0:T(8,128)(2,1)} %param.13), kind=kOutput, calls=%fused_computation.7 | convolution fusion | flops 38657851392 | bytes 88080384 | tf_op jit(solution)/shard_map/dot_general | solution.py:80
  999.6 8.6 copy.15
  1008.2 8.6 copy.16
  1016.8 12.8 %multiply_subtract_fusion = (f32[192,6144]{1,0:T(8,128)}, f32[192,6144]{1,0:T(8,128)}, f32[192,6144]{1,0:T(8,128)}) fusion(f32[192,6144]{1,0:T(8,128)} %param.10, f32[192,6144]{1,0:T(8,128)} %maximum_convert_fusion, f32[192,6144]{1,0:T(8,128)} %param.11, f32[192,6144]{1,0:T(8,128)} %param.12), kind=kLoop, calls=%fused_computation.8 | loop fusion | flops 18874368 | bytes 33030144 | tf_op jit(solution)/shard_map/sub | solution.py:93
  (52 shorter events, 16.7 us)
Async XLA Ops:
  7.2 897.3 %all-gather.2.cloned.1.call-start = ((), (), s32[]{:S(2)}) async-start(), calls=%async_computation | async-start | bytes 77856768 | tf_op jit(solution)/shard_map/all_gather | solution.py:45
  47.7 55.6 %collective-permute-start.2 = (bf16[3072,6144]{1,0:T(8,128)(2,1)}, bf16[3072,6144]{1,0:T(8,128)(2,1)}, u32[]{:S(2)}, u32[]{:S(2)}) collective-permute-start(bf16[3072,6144]{1,0:T(8,128)(2,1)} %convolution_convert_fusion), channel_id=1, source_target_pairs={{0,1},{1,0},{2,3},{3,2},{4,5},{5,4},{6,7},{7,6},{8,9},{9,8},{10,11... | collective-permute-start | bytes 113246216 | tf_op jit(solution)/shard_map/ppermute | solution.py:40
  103.3 35.8 %copy-start.2 = (s32[16]{0:T(128)S(1)}, s32[16]{0:T(128)}, u32[]{:S(2)}) copy-start(s32[16]{0:T(128)} %constant.142.clone) | copy-start | bytes 196
  103.3 37.7 %copy-start.1 = (s32[16]{0:T(128)S(1)}, s32[16]{0:T(128)}, u32[]{:S(2)}) copy-start(s32[16]{0:T(128)} %constant.141.clone) | copy-start | bytes 196
  139.1 6.7 copy-start
  145.7 67.9 %collective-permute-start = (bf16[192,3072]{1,0:T(8,128)(2,1)S(1)}, bf16[192,3072]{1,0:T(8,128)(2,1)S(1)}, u32[]{:S(2)}, u32[]{:S(2)}) collective-permute-start(bf16[192,3072]{1,0:T(8,128)(2,1)S(1)} %get-tuple-element.279), channel_id=1, source_target_pairs={{8,0},{16,8},{24,16},{26,24},{18,26},{10,18},{2,10},{6,2},{14,6},{... | collective-permute-start | bytes 3538952 | tf_op jit(solution)/shard_map/while/body/eval_jaxpr/ppermute | solution.py:64
  148.6 65.0 %collective-permute-start.1 = (bf16[192,3072]{1,0:T(8,128)(2,1)}, bf16[192,3072]{1,0:T(8,128)(2,1)S(1)}, u32[]{:S(2)}, u32[]{:S(2)}) collective-permute-start(bf16[192,3072]{1,0:T(8,128)(2,1)} %get-tuple-element.278), channel_id=1, source_target_pairs={{0,8},{8,16},{16,24},{24,26},{26,18},{18,10},{10,2},{2,6},{6,14},{... | collective-permute-start | bytes 3538952 | tf_op jit(solution)/shard_map/while/body/eval_jaxpr/ppermute | solution.py:63
  217.1 59.8 %collective-permute-start = (bf16[192,3072]{1,0:T(8,128)(2,1)S(1)}, bf16[192,3072]{1,0:T(8,128)(2,1)S(1)}, u32[]{:S(2)}, u32[]{:S(2)}) collective-permute-start(bf16[192,3072]{1,0:T(8,128)(2,1)S(1)} %get-tuple-element.279), channel_id=1, source_target_pairs={{8,0},{16,8},{24,16},{26,24},{18,26},{10,18},{2,10},{6,2},{14,6},{... | collective-permute-start | bytes 3538952 | tf_op jit(solution)/shard_map/while/body/eval_jaxpr/ppermute | solution.py:64
  225.4 51.6 %collective-permute-start.1 = (bf16[192,3072]{1,0:T(8,128)(2,1)}, bf16[192,3072]{1,0:T(8,128)(2,1)S(1)}, u32[]{:S(2)}, u32[]{:S(2)}) collective-permute-start(bf16[192,3072]{1,0:T(8,128)(2,1)} %get-tuple-element.278), channel_id=1, source_target_pairs={{0,8},{8,16},{16,24},{24,26},{26,18},{18,10},{10,2},{2,6},{6,14},{... | collective-permute-start | bytes 3538952 | tf_op jit(solution)/shard_map/while/body/eval_jaxpr/ppermute | solution.py:63
  280.5 84.3 %collective-permute-start = (bf16[192,3072]{1,0:T(8,128)(2,1)S(1)}, bf16[192,3072]{1,0:T(8,128)(2,1)S(1)}, u32[]{:S(2)}, u32[]{:S(2)}) collective-permute-start(bf16[192,3072]{1,0:T(8,128)(2,1)S(1)} %get-tuple-element.279), channel_id=1, source_target_pairs={{8,0},{16,8},{24,16},{26,24},{18,26},{10,18},{2,10},{6,2},{14,6},{... | collective-permute-start | bytes 3538952 | tf_op jit(solution)/shard_map/while/body/eval_jaxpr/ppermute | solution.py:64
  287.2 77.7 %collective-permute-start.1 = (bf16[192,3072]{1,0:T(8,128)(2,1)}, bf16[192,3072]{1,0:T(8,128)(2,1)S(1)}, u32[]{:S(2)}, u32[]{:S(2)}) collective-permute-start(bf16[192,3072]{1,0:T(8,128)(2,1)} %get-tuple-element.278), channel_id=1, source_target_pairs={{0,8},{8,16},{16,24},{24,26},{26,18},{18,10},{10,2},{2,6},{6,14},{... | collective-permute-start | bytes 3538952 | tf_op jit(solution)/shard_map/while/body/eval_jaxpr/ppermute | solution.py:63
  368.4 43.9 %collective-permute-start = (bf16[192,3072]{1,0:T(8,128)(2,1)S(1)}, bf16[192,3072]{1,0:T(8,128)(2,1)S(1)}, u32[]{:S(2)}, u32[]{:S(2)}) collective-permute-start(bf16[192,3072]{1,0:T(8,128)(2,1)S(1)} %get-tuple-element.279), channel_id=1, source_target_pairs={{8,0},{16,8},{24,16},{26,24},{18,26},{10,18},{2,10},{6,2},{14,6},{... | collective-permute-start | bytes 3538952 | tf_op jit(solution)/shard_map/while/body/eval_jaxpr/ppermute | solution.py:64
  372.7 39.6 %collective-permute-start.1 = (bf16[192,3072]{1,0:T(8,128)(2,1)}, bf16[192,3072]{1,0:T(8,128)(2,1)S(1)}, u32[]{:S(2)}, u32[]{:S(2)}) collective-permute-start(bf16[192,3072]{1,0:T(8,128)(2,1)} %get-tuple-element.278), channel_id=1, source_target_pairs={{0,8},{8,16},{16,24},{24,26},{26,18},{18,10},{10,2},{2,6},{6,14},{... | collective-permute-start | bytes 3538952 | tf_op jit(solution)/shard_map/while/body/eval_jaxpr/ppermute | solution.py:63
  415.8 84.5 %collective-permute-start = (bf16[192,3072]{1,0:T(8,128)(2,1)S(1)}, bf16[192,3072]{1,0:T(8,128)(2,1)S(1)}, u32[]{:S(2)}, u32[]{:S(2)}) collective-permute-start(bf16[192,3072]{1,0:T(8,128)(2,1)S(1)} %get-tuple-element.279), channel_id=1, source_target_pairs={{8,0},{16,8},{24,16},{26,24},{18,26},{10,18},{2,10},{6,2},{14,6},{... | collective-permute-start | bytes 3538952 | tf_op jit(solution)/shard_map/while/body/eval_jaxpr/ppermute | solution.py:64
  420.1 80.2 %collective-permute-start.1 = (bf16[192,3072]{1,0:T(8,128)(2,1)}, bf16[192,3072]{1,0:T(8,128)(2,1)S(1)}, u32[]{:S(2)}, u32[]{:S(2)}) collective-permute-start(bf16[192,3072]{1,0:T(8,128)(2,1)} %get-tuple-element.278), channel_id=1, source_target_pairs={{0,8},{8,16},{16,24},{24,26},{26,18},{18,10},{10,2},{2,6},{6,14},{... | collective-permute-start | bytes 3538952 | tf_op jit(solution)/shard_map/while/body/eval_jaxpr/ppermute | solution.py:63
  503.9 81.6 %collective-permute-start = (bf16[192,3072]{1,0:T(8,128)(2,1)S(1)}, bf16[192,3072]{1,0:T(8,128)(2,1)S(1)}, u32[]{:S(2)}, u32[]{:S(2)}) collective-permute-start(bf16[192,3072]{1,0:T(8,128)(2,1)S(1)} %get-tuple-element.279), channel_id=1, source_target_pairs={{8,0},{16,8},{24,16},{26,24},{18,26},{10,18},{2,10},{6,2},{14,6},{... | collective-permute-start | bytes 3538952 | tf_op jit(solution)/shard_map/while/body/eval_jaxpr/ppermute | solution.py:64
  508.2 77.3 %collective-permute-start.1 = (bf16[192,3072]{1,0:T(8,128)(2,1)}, bf16[192,3072]{1,0:T(8,128)(2,1)S(1)}, u32[]{:S(2)}, u32[]{:S(2)}) collective-permute-start(bf16[192,3072]{1,0:T(8,128)(2,1)} %get-tuple-element.278), channel_id=1, source_target_pairs={{0,8},{8,16},{16,24},{24,26},{26,18},{18,10},{10,2},{2,6},{6,14},{... | collective-permute-start | bytes 3538952 | tf_op jit(solution)/shard_map/while/body/eval_jaxpr/ppermute | solution.py:63
  589.2 80.5 %collective-permute-start = (bf16[192,3072]{1,0:T(8,128)(2,1)S(1)}, bf16[192,3072]{1,0:T(8,128)(2,1)S(1)}, u32[]{:S(2)}, u32[]{:S(2)}) collective-permute-start(bf16[192,3072]{1,0:T(8,128)(2,1)S(1)} %get-tuple-element.279), channel_id=1, source_target_pairs={{8,0},{16,8},{24,16},{26,24},{18,26},{10,18},{2,10},{6,2},{14,6},{... | collective-permute-start | bytes 3538952 | tf_op jit(solution)/shard_map/while/body/eval_jaxpr/ppermute | solution.py:64
  592.2 77.6 %collective-permute-start.1 = (bf16[192,3072]{1,0:T(8,128)(2,1)}, bf16[192,3072]{1,0:T(8,128)(2,1)S(1)}, u32[]{:S(2)}, u32[]{:S(2)}) collective-permute-start(bf16[192,3072]{1,0:T(8,128)(2,1)} %get-tuple-element.278), channel_id=1, source_target_pairs={{0,8},{8,16},{16,24},{24,26},{26,18},{18,10},{10,2},{2,6},{6,14},{... | collective-permute-start | bytes 3538952 | tf_op jit(solution)/shard_map/while/body/eval_jaxpr/ppermute | solution.py:63
  673.3 32.6 %collective-permute-start = (bf16[192,3072]{1,0:T(8,128)(2,1)S(1)}, bf16[192,3072]{1,0:T(8,128)(2,1)S(1)}, u32[]{:S(2)}, u32[]{:S(2)}) collective-permute-start(bf16[192,3072]{1,0:T(8,128)(2,1)S(1)} %get-tuple-element.279), channel_id=1, source_target_pairs={{8,0},{16,8},{24,16},{26,24},{18,26},{10,18},{2,10},{6,2},{14,6},{... | collective-permute-start | bytes 3538952 | tf_op jit(solution)/shard_map/while/body/eval_jaxpr/ppermute | solution.py:64
  678.4 27.7 %collective-permute-start.1 = (bf16[192,3072]{1,0:T(8,128)(2,1)}, bf16[192,3072]{1,0:T(8,128)(2,1)S(1)}, u32[]{:S(2)}, u32[]{:S(2)}) collective-permute-start(bf16[192,3072]{1,0:T(8,128)(2,1)} %get-tuple-element.278), channel_id=1, source_target_pairs={{0,8},{8,16},{16,24},{24,26},{26,18},{18,10},{10,2},{2,6},{6,14},{... | collective-permute-start | bytes 3538952 | tf_op jit(solution)/shard_map/while/body/eval_jaxpr/ppermute | solution.py:63
  709.6 25.3 %collective-permute-start = (bf16[192,3072]{1,0:T(8,128)(2,1)S(1)}, bf16[192,3072]{1,0:T(8,128)(2,1)S(1)}, u32[]{:S(2)}, u32[]{:S(2)}) collective-permute-start(bf16[192,3072]{1,0:T(8,128)(2,1)S(1)} %get-tuple-element.279), channel_id=1, source_target_pairs={{8,0},{16,8},{24,16},{26,24},{18,26},{10,18},{2,10},{6,2},{14,6},{... | collective-permute-start | bytes 3538952 | tf_op jit(solution)/shard_map/while/body/eval_jaxpr/ppermute | solution.py:64
  712.6 25.6 %collective-permute-start.1 = (bf16[192,3072]{1,0:T(8,128)(2,1)}, bf16[192,3072]{1,0:T(8,128)(2,1)S(1)}, u32[]{:S(2)}, u32[]{:S(2)}) collective-permute-start(bf16[192,3072]{1,0:T(8,128)(2,1)} %get-tuple-element.278), channel_id=1, source_target_pairs={{0,8},{8,16},{16,24},{24,26},{26,18},{18,10},{10,2},{2,6},{6,14},{... | collective-permute-start | bytes 3538952 | tf_op jit(solution)/shard_map/while/body/eval_jaxpr/ppermute | solution.py:63
  741.7 24.5 %collective-permute-start = (bf16[192,3072]{1,0:T(8,128)(2,1)S(1)}, bf16[192,3072]{1,0:T(8,128)(2,1)S(1)}, u32[]{:S(2)}, u32[]{:S(2)}) collective-permute-start(bf16[192,3072]{1,0:T(8,128)(2,1)S(1)} %get-tuple-element.279), channel_id=1, source_target_pairs={{8,0},{16,8},{24,16},{26,24},{18,26},{10,18},{2,10},{6,2},{14,6},{... | collective-permute-start | bytes 3538952 | tf_op jit(solution)/shard_map/while/body/eval_jaxpr/ppermute | solution.py:64
  743.5 24.4 %collective-permute-start.1 = (bf16[192,3072]{1,0:T(8,128)(2,1)}, bf16[192,3072]{1,0:T(8,128)(2,1)S(1)}, u32[]{:S(2)}, u32[]{:S(2)}) collective-permute-start(bf16[192,3072]{1,0:T(8,128)(2,1)} %get-tuple-element.278), channel_id=1, source_target_pairs={{0,8},{8,16},{16,24},{24,26},{26,18},{18,10},{10,2},{2,6},{6,14},{... | collective-permute-start | bytes 3538952 | tf_op jit(solution)/shard_map/while/body/eval_jaxpr/ppermute | solution.py:63
  771.4 23.3 %collective-permute-start = (bf16[192,3072]{1,0:T(8,128)(2,1)S(1)}, bf16[192,3072]{1,0:T(8,128)(2,1)S(1)}, u32[]{:S(2)}, u32[]{:S(2)}) collective-permute-start(bf16[192,3072]{1,0:T(8,128)(2,1)S(1)} %get-tuple-element.279), channel_id=1, source_target_pairs={{8,0},{16,8},{24,16},{26,24},{18,26},{10,18},{2,10},{6,2},{14,6},{... | collective-permute-start | bytes 3538952 | tf_op jit(solution)/shard_map/while/body/eval_jaxpr/ppermute | solution.py:64
  771.9 23.2 %collective-permute-start.1 = (bf16[192,3072]{1,0:T(8,128)(2,1)}, bf16[192,3072]{1,0:T(8,128)(2,1)S(1)}, u32[]{:S(2)}, u32[]{:S(2)}) collective-permute-start(bf16[192,3072]{1,0:T(8,128)(2,1)} %get-tuple-element.278), channel_id=1, source_target_pairs={{0,8},{8,16},{16,24},{24,26},{26,18},{18,10},{10,2},{2,6},{6,14},{... | collective-permute-start | bytes 3538952 | tf_op jit(solution)/shard_map/while/body/eval_jaxpr/ppermute | solution.py:63
  798.7 22.5 %collective-permute-start = (bf16[192,3072]{1,0:T(8,128)(2,1)S(1)}, bf16[192,3072]{1,0:T(8,128)(2,1)S(1)}, u32[]{:S(2)}, u32[]{:S(2)}) collective-permute-start(bf16[192,3072]{1,0:T(8,128)(2,1)S(1)} %get-tuple-element.279), channel_id=1, source_target_pairs={{8,0},{16,8},{24,16},{26,24},{18,26},{10,18},{2,10},{6,2},{14,6},{... | collective-permute-start | bytes 3538952 | tf_op jit(solution)/shard_map/while/body/eval_jaxpr/ppermute | solution.py:64
  799.0 22.3 %collective-permute-start.1 = (bf16[192,3072]{1,0:T(8,128)(2,1)}, bf16[192,3072]{1,0:T(8,128)(2,1)S(1)}, u32[]{:S(2)}, u32[]{:S(2)}) collective-permute-start(bf16[192,3072]{1,0:T(8,128)(2,1)} %get-tuple-element.278), channel_id=1, source_target_pairs={{0,8},{8,16},{16,24},{24,26},{26,18},{18,10},{10,2},{2,6},{6,14},{... | collective-permute-start | bytes 3538952 | tf_op jit(solution)/shard_map/while/body/eval_jaxpr/ppermute | solution.py:63
  824.9 22.3 %collective-permute-start = (bf16[192,3072]{1,0:T(8,128)(2,1)S(1)}, bf16[192,3072]{1,0:T(8,128)(2,1)S(1)}, u32[]{:S(2)}, u32[]{:S(2)}) collective-permute-start(bf16[192,3072]{1,0:T(8,128)(2,1)S(1)} %get-tuple-element.279), channel_id=1, source_target_pairs={{8,0},{16,8},{24,16},{26,24},{18,26},{10,18},{2,10},{6,2},{14,6},{... | collective-permute-start | bytes 3538952 | tf_op jit(solution)/shard_map/while/body/eval_jaxpr/ppermute | solution.py:64
  825.1 22.5 %collective-permute-start.1 = (bf16[192,3072]{1,0:T(8,128)(2,1)}, bf16[192,3072]{1,0:T(8,128)(2,1)S(1)}, u32[]{:S(2)}, u32[]{:S(2)}) collective-permute-start(bf16[192,3072]{1,0:T(8,128)(2,1)} %get-tuple-element.278), channel_id=1, source_target_pairs={{0,8},{8,16},{16,24},{24,26},{26,18},{18,10},{10,2},{2,6},{6,14},{... | collective-permute-start | bytes 3538952 | tf_op jit(solution)/shard_map/while/body/eval_jaxpr/ppermute | solution.py:63
  851.2 22.2 %collective-permute-start = (bf16[192,3072]{1,0:T(8,128)(2,1)S(1)}, bf16[192,3072]{1,0:T(8,128)(2,1)S(1)}, u32[]{:S(2)}, u32[]{:S(2)}) collective-permute-start(bf16[192,3072]{1,0:T(8,128)(2,1)S(1)} %get-tuple-element.279), channel_id=1, source_target_pairs={{8,0},{16,8},{24,16},{26,24},{18,26},{10,18},{2,10},{6,2},{14,6},{... | collective-permute-start | bytes 3538952 | tf_op jit(solution)/shard_map/while/body/eval_jaxpr/ppermute | solution.py:64
  851.2 22.5 %collective-permute-start.1 = (bf16[192,3072]{1,0:T(8,128)(2,1)}, bf16[192,3072]{1,0:T(8,128)(2,1)S(1)}, u32[]{:S(2)}, u32[]{:S(2)}) collective-permute-start(bf16[192,3072]{1,0:T(8,128)(2,1)} %get-tuple-element.278), channel_id=1, source_target_pairs={{0,8},{8,16},{16,24},{24,26},{26,18},{18,10},{10,2},{2,6},{6,14},{... | collective-permute-start | bytes 3538952 | tf_op jit(solution)/shard_map/while/body/eval_jaxpr/ppermute | solution.py:63
  877.3 19.3 %collective-permute-start = (bf16[192,3072]{1,0:T(8,128)(2,1)S(1)}, bf16[192,3072]{1,0:T(8,128)(2,1)S(1)}, u32[]{:S(2)}, u32[]{:S(2)}) collective-permute-start(bf16[192,3072]{1,0:T(8,128)(2,1)S(1)} %get-tuple-element.279), channel_id=1, source_target_pairs={{8,0},{16,8},{24,16},{26,24},{18,26},{10,18},{2,10},{6,2},{14,6},{... | collective-permute-start | bytes 3538952 | tf_op jit(solution)/shard_map/while/body/eval_jaxpr/ppermute | solution.py:64
  877.4 19.6 %collective-permute-start.1 = (bf16[192,3072]{1,0:T(8,128)(2,1)}, bf16[192,3072]{1,0:T(8,128)(2,1)S(1)}, u32[]{:S(2)}, u32[]{:S(2)}) collective-permute-start(bf16[192,3072]{1,0:T(8,128)(2,1)} %get-tuple-element.278), channel_id=1, source_target_pairs={{0,8},{8,16},{16,24},{24,26},{26,18},{18,10},{10,2},{2,6},{6,14},{... | collective-permute-start | bytes 3538952 | tf_op jit(solution)/shard_map/while/body/eval_jaxpr/ppermute | solution.py:63
Sparse Core Ops, SparseCore 0:
  139.2 556.0 all-gather.1

commit v6 on v5

--- a/solution.py
+++ b/solution.py
@@ -34,15 +34,20 @@
     ctx_other = jnp.where(me == 0, ctx_split[:, :, 1], ctx_split[:, :, 0]).reshape(tok_rows, chips * rows)
     dims_wgrad = (((0,), (0,)), ((), ()))
 
-    grad_for_other = lax.dot_general(
-        ctx_other, piece, dims_wgrad, preferred_element_type=jnp.float32
-    ).astype(jnp.bfloat16)
-    grad_from_other = lax.ppermute(grad_for_other, "core", swap)
-
-    grad_mine = lax.dot_general(ctx_own, piece, dims_wgrad, preferred_element_type=jnp.float32)
-    chip_grad = (grad_mine + grad_from_other.astype(jnp.float32)).astype(jnp.bfloat16)
-    weight_bf, chip_grad = lax.optimization_barrier((weight_bf, chip_grad))
     full_weight = lax.all_gather(weight_bf, DP, axis=0, tiled=True)
+    quarter = chips * rows // 4
+    sums = []
+    for q in range(4):
+        cols = slice(q * quarter, (q + 1) * quarter)
+        ctx_q = ctx_other[:, cols]
+        if sums:
+            ctx_q, _ = lax.optimization_barrier((ctx_q, sums[-1]))
+        grad_for_other = lax.dot_general(
+            ctx_q, piece, dims_wgrad, preferred_element_type=jnp.float32
+        ).astype(jnp.bfloat16)
+        grad_from_other = lax.ppermute(grad_for_other, "core", swap)
+        grad_mine = lax.dot_general(ctx_own[:, cols], piece, dims_wgrad, preferred_element_type=jnp.float32)
+        sums.append((grad_mine + grad_from_other.astype(jnp.float32)).astype(jnp.bfloat16))
 
     n = chips
     order = chip_cycle(n)
@@ -55,31 +60,54 @@
     pos = jnp.asarray(np.array(position, np.int32))[lax.axis_index("chip")]
     half = width // 2
 
+    per_quarter = quarter // rows
+
     def own_block(block):
-        return lax.dynamic_slice_in_dim(chip_grad, block * rows, rows, 0).astype(jnp.float32)
+        within = (block % per_quarter) * rows
+        which = block // per_quarter
+        picked = lax.dynamic_slice_in_dim(sums[0], within, rows, 0)
+        for q in range(1, 4):
+            picked = jnp.where(which == q, lax.dynamic_slice_in_dim(sums[q], within, rows, 0), picked)
+        return picked.astype(jnp.float32)
 
-    def ring_step(step, carry):
-        send_cw, send_ccw = carry
+    n_pieces = 3
+    out_cols = width // n_pieces
+    d_rows = local_cols // n_pieces
+
+    def product(j, w):
+        if j < n_pieces:
+            return jnp.dot(
+                context, w[:, j * out_cols:(j + 1) * out_cols], preferred_element_type=jnp.float32
+            ).astype(jnp.bfloat16)
+        k = j - n_pieces
+        return lax.dot_general(
+            piece, w[k * d_rows:(k + 1) * d_rows], (((1,), (1,)), ((), ())),
+            preferred_element_type=jnp.float32,
+        ).astype(jnp.bfloat16)
+
+    send_cw = own_block(order_arr[(pos - 1) % n])[:, :half].astype(jnp.bfloat16)
+    send_ccw = own_block(order_arr[(pos + 1) % n])[:, half:].astype(jnp.bfloat16)
+    products = []
+    first_piece = max(0, n - 1 - 2 * n_pieces)
+    for step in range(n - 1):
         recv_cw = lax.ppermute(send_cw, "chip", forward)
         recv_ccw = lax.ppermute(send_ccw, "chip", backward)
+        j = step - first_piece
+        if 0 <= j < 2 * n_pieces:
+            w_now, _ = lax.optimization_barrier((full_weight, send_cw))
+            products.append(product(j, w_now))
         mine_cw = own_block(order_arr[(pos - step - 2) % n])[:, :half]
         mine_ccw = own_block(order_arr[(pos + step + 2) % n])[:, half:]
-        return (
-            (recv_cw.astype(jnp.float32) + mine_cw).astype(jnp.bfloat16),
-            (recv_ccw.astype(jnp.float32) + mine_ccw).astype(jnp.bfloat16),
-        )
-
-    start_cw = own_block(order_arr[(pos - 1) % n])[:, :half].astype(jnp.bfloat16)
-    start_ccw = own_block(order_arr[(pos + 1) % n])[:, half:].astype(jnp.bfloat16)
-    done_cw, done_ccw = lax.fori_loop(0, n - 1, ring_step, (start_cw, start_ccw))
-    grad_shard = jnp.concatenate([done_cw, done_ccw], axis=1).astype(jnp.float32)
-    full_weight, grad_shard = lax.optimization_barrier((full_weight, grad_shard))
-
-    out = jnp.dot(context, full_weight, preferred_element_type=jnp.float32)
-    summed = lax.psum_scatter(out.astype(jnp.bfloat16), "mp", scatter_dimension=0, tiled=True)
-    d_context = lax.dot_general(
-        piece, full_weight, (((1,), (1,)), ((), ())), preferred_element_type=jnp.float32
-    ).astype(jnp.bfloat16)
+        send_cw = (recv_cw.astype(jnp.float32) + mine_cw).astype(jnp.bfloat16)
+        send_ccw = (recv_ccw.astype(jnp.float32) + mine_ccw).astype(jnp.bfloat16)
+        if 0 <= j < 2 * n_pieces:
+            send_cw, send_ccw, products[-1] = lax.optimization_barrier((send_cw, send_ccw, products[-1]))
+    for j in range(len(products), 2 * n_pieces):
+        products.append(product(j, full_weight))
+    grad_shard = jnp.concatenate([send_cw, send_ccw], axis=1).astype(jnp.float32)
+    out = jnp.concatenate(products[:n_pieces], axis=1)
+    summed = lax.psum_scatter(out, "mp", scatter_dimension=0, tiled=True)
+    d_context = jnp.concatenate(products[n_pieces:], axis=1)
 
     tokens_all = tok_rows * chips * 2
     grad = grad_shard * (1.0 / math.sqrt(tokens_all))

time: 1040 us -> 940 us (0.904)
  waiting for transfers between devices: 638 us -> 377 us
  between operations: 16.7 us -> 117 us
  other arithmetic: 78.1 us -> 155 us
  matrix products: 159 us -> 203 us
  loops' own time: 40.4 us -> 0 us
  starting transfers between devices: 64.6 us -> 47.5 us
  local copies, waits for them, and re-layouts: 39.9 us -> 29.1 us
    ppermute x30, waiting for transfers between devices: 587 us -> 334 us  [the longest x15 333 us: per_device(): recv_ccw = lax.ppermute(send_ccw, 'chip', backward)]
    convert_element_type x16 -> x15, other arithmetic: 57.1 us -> 106 us  [per_device(): send_ccw = (recv_ccw.astype(jnp.float32) + mine_ccw).astype(jnp.bfloat16)]
    dot_general x4 -> x14, matrix products: 159 us -> 203 us  [the longest x3 62.1 us: product(): lax.dot_general(piece, w[k * d_rows:(k + 1) * d_rows], (((1,), (1,)), (()...]
    another operation x1 -> x0, loops' own time: 40.4 us -> none  [per_device(): lax.fori_loop(0, n - 1, ring_step, (start_cw, start_ccw))]
    concatenate x0 -> x2, other arithmetic: none -> 23.2 us  [the longest x1 17.8 us: per_device(): d_context = jnp.concatenate(products[n_pieces:], axis=1)]
    ppermute x30, starting transfers between devices: 64.1 us -> 45.5 us  [the longest x15 30.2 us: per_device(): recv_cw = lax.ppermute(send_cw, 'chip', forward)]
    ppermute x1 -> x4, waiting for transfers between devices: 51.1 us -> 42.9 us  [per_device(): grad_from_other = lax.ppermute(grad_for_other, 'core', swap)]
    unnamed x9 -> x19, local copies, waits for them, and re-layouts: 25.9 us -> 26.9 us
  transfers between devices with their start and end apart: 32 -> 35, of which waited for: 24 -> 17; matrix products, arithmetic and copies ran while one was open for 7% -> 31% of each run, Pallas kernels for 0% -> 0%
where the time goes in v6:
time: 940 us; the launch traced here: 929 us
  waiting for transfers between devices  377 us (40%)
  matrix products  203 us (22%)
  other arithmetic  155 us (16%)
  between operations  117 us (12%)
  starting transfers between devices  47.5 us (5%)
  local copies, waits for them, and re-layouts  29.1 us (3%)
    ppermute x15, waiting for transfers between devices, per_device(): recv_ccw = lax.ppermute(send_ccw, 'chip', backward)  333 us
    convert_element_type x15, other arithmetic, per_device(): send_ccw = (recv_ccw.astype(jnp.float32) + mine_ccw).astype(jnp.bfloat16)  106 us
    dot_general x3, matrix products, product(): lax.dot_general(piece, w[k * d_rows:(k + 1) * d_rows], (((1,), (1,)), (()...  62.1 us
    dot_general x3, matrix products, product(): jnp.dot(context, w[:, j * out_cols:(j + 1) * out_cols], preferred_element...  61.4 us
    ppermute x4, waiting for transfers between devices, per_device(): grad_from_other = lax.ppermute(grad_for_other, 'core', swap)  42.9 us
    dot_general x4, matrix products, per_device(): lax.dot_general(ctx_own[:, cols], piece, dims_wgrad, preferred_element_ty...  42.2 us
    dot_general x4, matrix products, per_device(): lax.dot_general(ctx_q, piece, dims_wgrad, preferred_element_type=jnp.floa...  37.7 us
    ppermute x15, starting transfers between devices, per_device(): recv_cw = lax.ppermute(send_cw, 'chip', forward)  30.2 us
  transfers between devices with their start and end apart: 35, of which 17 were waited for; matrix products, arithmetic and copies ran while one was open for 31% of the time, Pallas kernels for 0%

profile of v6, /device:TPU:0, one launch (start us, length us, event | category | flops | bytes accessed | tf_op | source)
XLA Modules:
  0.0 928.6 jit_solution(15425049867033673594)
XLA Ops:
  7.2 4.1 convert_element_type.344
  11.3 8.6 copy.14
  19.9 3.8 broadcast_select_fusion.1
  23.7 11.3 %convolution_convert_fusion.3 = bf16[768,6144]{1,0:T(8,128)(2,1)} fusion(bf16[512,6144]{1,0:T(8,128)(2,1)} %param.11, bf16[512,3072]{0,1:T(8,128)(2,1)S(1)} %bitcast.97), kind=kOutput, calls=%fused_computation.19 | convolution fusion | flops 4836556800 | bytes 16515072 | tf_op jit(solution)/shard_map/dot_general | solution.py:45
  35.9 14.3 %collective-permute-done = bf16[768,6144]{1,0:T(8,128)(2,1)S(1)} collective-permute-done((bf16[768,6144]{1,0:T(8,128)(2,1)}, bf16[768,6144]{1,0:T(8,128)(2,1)S(1)}, u32[]{:S(2)}, u32[]{:S(2)}) %collective-permute-start) | collective-permute-done | bytes 9437216 | tf_op jit(solution)/shard_map/ppermute | solution.py:48
  50.2 10.3 %add_convert_fusion.3 = bf16[768,6144]{1,0:T(8,128)(2,1)} fusion(bf16[768,6144]{1,0:T(8,128)(2,1)S(1)} %collective-permute-done, bf16[512,6144]{1,0:T(8,128)(2,1)} %param.11, bf16[512,3072]{0,1:T(8,128)(2,1)S(1)} %bitcast.99), kind=kOutput, calls=%fused_computation.15 | convolution fusion | flops 4845993984 | bytes 25952256 | tf_op jit(solution)/shard_map/dot_general | solution.py:49
  60.5 8.1 convolution_convert_fusion.2
  69.0 14.3 %collective-permute-done.1 = bf16[768,6144]{1,0:T(8,128)(2,1)S(1)} collective-permute-done((bf16[768,6144]{1,0:T(8,128)(2,1)S(1)}, bf16[768,6144]{1,0:T(8,128)(2,1)S(1)}, u32[]{:S(2)}, u32[]{:S(2)}) %collective-permute-start.1) | collective-permute-done | bytes 9437216 | tf_op jit(solution)/shard_map/ppermute | solution.py:48
  83.3 11.2 %add_convert_fusion.2 = bf16[768,6144]{1,0:T(8,128)(2,1)} fusion(bf16[768,6144]{1,0:T(8,128)(2,1)S(1)} %collective-permute-done.1, bf16[512,6144]{1,0:T(8,128)(2,1)} %param.11, bf16[512,3072]{0,1:T(8,128)(2,1)S(1)} %bitcast.100), kind=kOutput, calls=%fused_computation.14 | convolution fusion | flops 4845993984 | bytes 25952256 | tf_op jit(solution)/shard_map/dot_general | solution.py:49
  94.6 8.0 convolution_convert_fusion.1
  103.1 14.3 %collective-permute-done.2 = bf16[768,6144]{1,0:T(8,128)(2,1)S(1)} collective-permute-done((bf16[768,6144]{1,0:T(8,128)(2,1)S(1)}, bf16[768,6144]{1,0:T(8,128)(2,1)S(1)}, u32[]{:S(2)}, u32[]{:S(2)}) %collective-permute-start.2) | collective-permute-done | bytes 9437216 | tf_op jit(solution)/shard_map/ppermute | solution.py:48
  117.4 10.6 %add_convert_fusion.1 = bf16[768,6144]{1,0:T(8,128)(2,1)} fusion(bf16[768,6144]{1,0:T(8,128)(2,1)S(1)} %collective-permute-done.2, bf16[512,6144]{1,0:T(8,128)(2,1)} %param.11, bf16[512,3072]{0,1:T(8,128)(2,1)S(1)} %bitcast.101), kind=kOutput, calls=%fused_computation.13 | convolution fusion | flops 4845993984 | bytes 25952256 | tf_op jit(solution)/shard_map/dot_general | solution.py:49
  128.0 10.2 %convolution_convert_fusion = bf16[768,6144]{1,0:T(8,128)(2,1)} fusion(bf16[512,768]{0,1:T(8,128)(2,1)S(1)} %get-tuple-element.34, bf16[512,6144]{1,0:T(8,128)(2,1)} %param.11), kind=kOutput, calls=%fused_computation.16 | convolution fusion | flops 4836556800 | bytes 16515072 | tf_op jit(solution)/shard_map/dot_general | solution.py:45
  154.2 10.0 %add_convert_fusion = bf16[768,6144]{1,0:T(8,128)(2,1)S(1)} fusion(bf16[768,6144]{1,0:T(8,128)(2,1)} %collective-permute-done.3, bf16[512,6144]{1,0:T(8,128)(2,1)} %param.11, bf16[512,3072]{0,1:T(8,128)(2,1)S(1)} %bitcast.102), kind=kOutput, calls=%fused_computation.12 | convolution fusion | flops 4845993984 | bytes 25952256 | tf_op jit(solution)/shard_map/dot_general | solution.py:49
  164.2 8.3 dynamic-slice_select_fusion.60
  172.5 3.4 collective-permute-start.14
  180.7 43.0 %collective-permute-done.14 = bf16[192,3072]{1,0:T(8,128)(2,1)S(1)} collective-permute-done((bf16[192,3072]{1,0:T(8,128)(2,1)S(1)}, bf16[192,3072]{1,0:T(8,128)(2,1)S(1)}, u32[]{:S(2)}, u32[]{:S(2)}) %collective-permute-start.14) | collective-permute-done | bytes 1179680 | tf_op jit(solution)/shard_map/ppermute | solution.py:94
  223.8 6.4 add_convert_fusion.23
  230.2 1.8 collective-permute-start.15
  232.0 5.6 collective-permute-start.5
  255.4 59.3 %collective-permute-done.15 = bf16[192,3072]{1,0:T(8,128)(2,1)S(1)} collective-permute-done((bf16[192,3072]{1,0:T(8,128)(2,1)S(1)}, bf16[192,3072]{1,0:T(8,128)(2,1)S(1)}, u32[]{:S(2)}, u32[]{:S(2)}) %collective-permute-start.15) | collective-permute-done | bytes 1179680 | tf_op jit(solution)/shard_map/ppermute | solution.py:94
  314.7 6.4 add_convert_fusion.22
  321.2 3.4 collective-permute-start.16
  324.6 2.0 collective-permute-start.6
  331.3 73.7 %collective-permute-done.16 = bf16[192,3072]{1,0:T(8,128)(2,1)} collective-permute-done((bf16[192,3072]{1,0:T(8,128)(2,1)S(1)}, bf16[192,3072]{1,0:T(8,128)(2,1)}, u32[]{:S(2)}, u32[]{:S(2)}) %collective-permute-start.16) | collective-permute-done | bytes 1179680 | tf_op jit(solution)/shard_map/ppermute | solution.py:94
  405.0 6.8 add_convert_fusion.21
  411.8 1.9 collective-permute-start.17
  419.0 71.5 %collective-permute-done.17 = bf16[192,3072]{1,0:T(8,128)(2,1)} collective-permute-done((bf16[192,3072]{1,0:T(8,128)(2,1)S(1)}, bf16[192,3072]{1,0:T(8,128)(2,1)}, u32[]{:S(2)}, u32[]{:S(2)}) %collective-permute-start.17) | collective-permute-done | bytes 1179680 | tf_op jit(solution)/shard_map/ppermute | solution.py:94
  490.5 6.8 add_convert_fusion.20
  497.4 4.8 collective-permute-start.8
  506.9 17.1 %collective-permute-done.18 = bf16[192,3072]{1,0:T(8,128)(2,1)} collective-permute-done((bf16[192,3072]{1,0:T(8,128)(2,1)S(1)}, bf16[192,3072]{1,0:T(8,128)(2,1)}, u32[]{:S(2)}, u32[]{:S(2)}) %collective-permute-start.18) | collective-permute-done | bytes 1179680 | tf_op jit(solution)/shard_map/ppermute | solution.py:94
  524.1 6.8 add_convert_fusion.19
  531.2 2.0 collective-permute-start.9
  538.2 18.6 %collective-permute-done.19 = bf16[192,3072]{1,0:T(8,128)(2,1)} collective-permute-done((bf16[192,3072]{1,0:T(8,128)(2,1)S(1)}, bf16[192,3072]{1,0:T(8,128)(2,1)}, u32[]{:S(2)}, u32[]{:S(2)}) %collective-permute-start.19) | collective-permute-done | bytes 1179680 | tf_op jit(solution)/shard_map/ppermute | solution.py:94
  557.2 6.8 add_convert_fusion.18
  571.0 17.8 %collective-permute-done.20 = bf16[192,3072]{1,0:T(8,128)(2,1)} collective-permute-done((bf16[192,3072]{1,0:T(8,128)(2,1)S(1)}, bf16[192,3072]{1,0:T(8,128)(2,1)}, u32[]{:S(2)}, u32[]{:S(2)}) %collective-permute-start.20) | collective-permute-done | bytes 1179680 | tf_op jit(solution)/shard_map/ppermute | solution.py:94
  589.0 6.8 add_convert_fusion.17
  602.8 16.8 %collective-permute-done.21 = bf16[192,3072]{1,0:T(8,128)(2,1)} collective-permute-done((bf16[192,3072]{1,0:T(8,128)(2,1)S(1)}, bf16[192,3072]{1,0:T(8,128)(2,1)}, u32[]{:S(2)}, u32[]{:S(2)}) %collective-permute-start.21) | collective-permute-done | bytes 1179680 | tf_op jit(solution)/shard_map/ppermute | solution.py:94
  619.7 6.8 add_convert_fusion.16
  626.8 1.8 collective-permute-start.12
  633.9 15.5 %collective-permute-done.22 = bf16[192,3072]{1,0:T(8,128)(2,1)} collective-permute-done((bf16[192,3072]{1,0:T(8,128)(2,1)S(1)}, bf16[192,3072]{1,0:T(8,128)(2,1)}, u32[]{:S(2)}, u32[]{:S(2)}) %collective-permute-start.22) | collective-permute-done | bytes 1179680 | tf_op jit(solution)/shard_map/ppermute | solution.py:94
  649.4 6.8 add_convert_fusion.15
  656.5 2.2 collective-permute-start.13
  689.9 7.9 add_convert_fusion.14
  697.7 19.9 %fusion.39 = bf16[512,2048]{0,1:T(8,128)(2,1)S(1)} fusion(bf16[512,6144]{1,0:T(8,128)(2,1)} %param.7, bf16[6144,6144]{1,0:T(8,128)(2,1)} %all-gather.2.cloned.1.call-done), kind=kOutput, calls=%fused_computation.39 | convolution fusion | flops 12885950464 | bytes 33554432 | tf_op jit(solution)/shard_map/dot_general | solution.py:79
  717.7 1.7 collective-permute-start.24
  719.9 20.8 %fusion.36 = bf16[512,2048]{0,1:T(8,128)(2,1)} fusion(bf16[512,6144]{1,0:T(8,128)(2,1)} %param.7, bf16[6144,6144]{1,0:T(8,128)(2,1)} %all-gather.2.cloned.1.call-done), kind=kOutput, calls=%fused_computation.38 | convolution fusion | flops 12885950464 | bytes 33554432 | tf_op jit(solution)/shard_map/dot_general | solution.py:79
  740.7 7.8 add_convert_fusion.12
  748.5 1.7 collective-permute-start.26
  750.7 20.8 %fusion.33 = bf16[512,2048]{0,1:T(8,128)(2,1)} fusion(bf16[512,6144]{1,0:T(8,128)(2,1)} %param.7, bf16[6144,6144]{1,0:T(8,128)(2,1)} %all-gather.2.cloned.1.call-done), kind=kOutput, calls=%fused_computation.37 | convolution fusion | flops 12885950464 | bytes 33554432 | tf_op jit(solution)/shard_map/dot_general | solution.py:79
  771.5 7.9 add_convert_fusion.10
  779.4 1.7 collective-permute-start.28
  781.8 20.7 %fusion.48 = bf16[512,2048]{0,1:T(8,128)(2,1)} fusion(bf16[512,6144]{1,0:T(8,128)(2,1)} %param.11, bf16[6144,6144]{1,0:T(8,128)(2,1)} %all-gather.2.cloned.1.call-done), kind=kOutput, calls=%fused_computation.42 | convolution fusion | flops 12885950464 | bytes 33554432 | tf_op jit(solution)/shard_map/dot_general | solution.py:83
  802.5 5.4 pad_maximum_fusion
  807.9 8.6 copy.15
  816.5 6.8 add_convert_fusion.8
  823.3 1.7 collective-permute-start.30
  825.5 20.7 %fusion.45 = bf16[512,2048]{0,1:T(8,128)(2,1)} fusion(bf16[512,6144]{1,0:T(8,128)(2,1)} %param.11, bf16[6144,6144]{1,0:T(8,128)(2,1)} %all-gather.2.cloned.1.call-done), kind=kOutput, calls=%fused_computation.41 | convolution fusion | flops 12885950464 | bytes 33554432 | tf_op jit(solution)/shard_map/dot_general | solution.py:83
  846.2 7.5 add_convert_fusion.6
  855.9 20.7 %fusion.42 = bf16[512,2048]{0,1:T(8,128)(2,1)} fusion(bf16[512,6144]{1,0:T(8,128)(2,1)} %param.11, bf16[6144,6144]{1,0:T(8,128)(2,1)} %all-gather.2.cloned.1.call-done), kind=kOutput, calls=%fused_computation.40 | convolution fusion | flops 12885950464 | bytes 33554432 | tf_op jit(solution)/shard_map/dot_general | solution.py:83
  877.6 7.2 add_convert_fusion.4
  884.9 17.8 %pad_maximum_fusion.1 = bf16[512,6144]{0,1:T(8,128)(2,1)} fusion(bf16[512,2048]{0,1:T(8,128)(2,1)S(1)} %copy-done.3, bf16[512,2048]{0,1:T(8,128)(2,1)S(1)} %copy-done.2, bf16[512,2048]{0,1:T(8,128)(2,1)S(1)} %copy-done.1), kind=kLoop, calls=%fused_computation.24 | loop fusion | flops 18874368 | bytes 12582912 | tf_op jit(solution)/shard_map/concatenate | solution.py:110
  902.7 8.6 copy.16
  911.3 10.1 %multiply_subtract_fusion = (f32[192,6144]{1,0:T(8,128)}, f32[192,6144]{1,0:T(8,128)}, f32[192,6144]{1,0:T(8,128)}) fusion(f32[192,6144]{1,0:T(8,128)} %param.8, bf16[192,3072]{1,0:T(8,128)(2,1)S(1)} %get-tuple-element.58, bf16[192,3072]{1,0:T(8,128)(2,1)S(1)} %get-tuple-element.57, f32[192,6144]{1,0:T(8,128)} %param.9, f32[192,6144]{1,0:T(8,128)} %param.10), kind=kLoop, calls=%fused_computation.28 | loop fusion | flops 23592960 | bytes 30670848 | tf_op jit(solution)/shard_map/sub | solution.py:121
  (65 shorter events, 15.8 us)
Async XLA Ops:
  7.2 690.6 %all-gather.2.cloned.1.call-start = ((), (), s32[]{:S(2)}) async-start(), calls=%async_computation | async-start | bytes 77856768 | tf_op jit(solution)/shard_map/all_gather | solution.py:37
  35.1 15.1 %collective-permute-start = (bf16[768,6144]{1,0:T(8,128)(2,1)}, bf16[768,6144]{1,0:T(8,128)(2,1)S(1)}, u32[]{:S(2)}, u32[]{:S(2)}) collective-permute-start(bf16[768,6144]{1,0:T(8,128)(2,1)} %convolution_convert_fusion.3), channel_id=1, source_target_pairs={{0,1},{1,0},{2,3},{3,2},{4,5},{5,4},{6,7},{7,6},{8,9},{9,8},{10,11... | collective-permute-start | bytes 28311560 | tf_op jit(solution)/shard_map/ppermute | solution.py:48
  68.6 14.7 %collective-permute-start.1 = (bf16[768,6144]{1,0:T(8,128)(2,1)S(1)}, bf16[768,6144]{1,0:T(8,128)(2,1)S(1)}, u32[]{:S(2)}, u32[]{:S(2)}) collective-permute-start(bf16[768,6144]{1,0:T(8,128)(2,1)S(1)} %convolution_convert_fusion.2), channel_id=1, source_target_pairs={{0,1},{1,0},{2,3},{3,2},{4,5},{5,4},{6,7},{7,6},{8,9},{9,8},{10,11... | collective-permute-start | bytes 28311560 | tf_op jit(solution)/shard_map/ppermute | solution.py:48
  102.6 14.8 %collective-permute-start.2 = (bf16[768,6144]{1,0:T(8,128)(2,1)S(1)}, bf16[768,6144]{1,0:T(8,128)(2,1)S(1)}, u32[]{:S(2)}, u32[]{:S(2)}) collective-permute-start(bf16[768,6144]{1,0:T(8,128)(2,1)S(1)} %convolution_convert_fusion.1), channel_id=1, source_target_pairs={{0,1},{1,0},{2,3},{3,2},{4,5},{5,4},{6,7},{7,6},{8,9},{9,8},{10,11... | collective-permute-start | bytes 28311560 | tf_op jit(solution)/shard_map/ppermute | solution.py:48
  128.0 10.6 %copy-start.7 = (s32[16]{0:T(128)S(1)}, s32[16]{0:T(128)}, u32[]{:S(2)}) copy-start(s32[16]{0:T(128)} %constant.674.clone) | copy-start | bytes 196
  128.0 20.5 %copy-start.6 = (s32[16]{0:T(128)S(1)}, s32[16]{0:T(128)}, u32[]{:S(2)}) copy-start(s32[16]{0:T(128)} %constant.673.clone) | copy-start | bytes 196
  138.2 16.0 %collective-permute-start.3 = (bf16[768,6144]{1,0:T(8,128)(2,1)}, bf16[768,6144]{1,0:T(8,128)(2,1)}, u32[]{:S(2)}, u32[]{:S(2)}) collective-permute-start(bf16[768,6144]{1,0:T(8,128)(2,1)} %convolution_convert_fusion), channel_id=1, source_target_pairs={{0,1},{1,0},{2,3},{3,2},{4,5},{5,4},{6,7},{7,6},{8,9},{9,8},{10,11... | collective-permute-start | bytes 28311560 | tf_op jit(solution)/shard_map/ppermute | solution.py:48
  164.2 8.3 copy-start
  172.5 51.3 %collective-permute-start.14 = (bf16[192,3072]{1,0:T(8,128)(2,1)S(1)}, bf16[192,3072]{1,0:T(8,128)(2,1)S(1)}, u32[]{:S(2)}, u32[]{:S(2)}) collective-permute-start(bf16[192,3072]{1,0:T(8,128)(2,1)S(1)} %get-tuple-element.102), channel_id=1, source_target_pairs={{8,0},{16,8},{24,16},{26,24},{18,26},{10,18},{2,10},{6,2},{14,6},{... | collective-permute-start | bytes 3538952 | tf_op jit(solution)/shard_map/ppermute | solution.py:94
  175.9 47.9 %collective-permute-start.4 = (bf16[192,3072]{1,0:T(8,128)(2,1)S(1)}, bf16[192,3072]{1,0:T(8,128)(2,1)}, u32[]{:S(2)}, u32[]{:S(2)}) collective-permute-start(bf16[192,3072]{1,0:T(8,128)(2,1)S(1)} %get-tuple-element.103), channel_id=1, source_target_pairs={{0,8},{8,16},{16,24},{24,26},{26,18},{18,10},{10,2},{2,6},{6,14},{... | collective-permute-start | bytes 3538952 | tf_op jit(solution)/shard_map/ppermute | solution.py:93
  230.2 84.5 %collective-permute-start.15 = (bf16[192,3072]{1,0:T(8,128)(2,1)S(1)}, bf16[192,3072]{1,0:T(8,128)(2,1)S(1)}, u32[]{:S(2)}, u32[]{:S(2)}) collective-permute-start(bf16[192,3072]{1,0:T(8,128)(2,1)S(1)} %get-tuple-element.100), channel_id=1, source_target_pairs={{8,0},{16,8},{24,16},{26,24},{18,26},{10,18},{2,10},{6,2},{14,6},{... | collective-permute-start | bytes 3538952 | tf_op jit(solution)/shard_map/ppermute | solution.py:94
  232.0 82.7 %collective-permute-start.5 = (bf16[192,3072]{1,0:T(8,128)(2,1)S(1)}, bf16[192,3072]{1,0:T(8,128)(2,1)}, u32[]{:S(2)}, u32[]{:S(2)}) collective-permute-start(bf16[192,3072]{1,0:T(8,128)(2,1)S(1)} %get-tuple-element.101), channel_id=1, source_target_pairs={{0,8},{8,16},{16,24},{24,26},{26,18},{18,10},{10,2},{2,6},{6,14},{... | collective-permute-start | bytes 3538952 | tf_op jit(solution)/shard_map/ppermute | solution.py:93
  321.2 83.8 %collective-permute-start.16 = (bf16[192,3072]{1,0:T(8,128)(2,1)S(1)}, bf16[192,3072]{1,0:T(8,128)(2,1)}, u32[]{:S(2)}, u32[]{:S(2)}) collective-permute-start(bf16[192,3072]{1,0:T(8,128)(2,1)S(1)} %get-tuple-element.98), channel_id=1, source_target_pairs={{8,0},{16,8},{24,16},{26,24},{18,26},{10,18},{2,10},{6,2},{14,6},{... | collective-permute-start | bytes 3538952 | tf_op jit(solution)/shard_map/ppermute | solution.py:94
  324.6 80.4 %collective-permute-start.6 = (bf16[192,3072]{1,0:T(8,128)(2,1)S(1)}, bf16[192,3072]{1,0:T(8,128)(2,1)}, u32[]{:S(2)}, u32[]{:S(2)}) collective-permute-start(bf16[192,3072]{1,0:T(8,128)(2,1)S(1)} %get-tuple-element.99), channel_id=1, source_target_pairs={{0,8},{8,16},{16,24},{24,26},{26,18},{18,10},{10,2},{2,6},{6,14},{... | collective-permute-start | bytes 3538952 | tf_op jit(solution)/shard_map/ppermute | solution.py:93
  411.8 78.7 %collective-permute-start.17 = (bf16[192,3072]{1,0:T(8,128)(2,1)S(1)}, bf16[192,3072]{1,0:T(8,128)(2,1)}, u32[]{:S(2)}, u32[]{:S(2)}) collective-permute-start(bf16[192,3072]{1,0:T(8,128)(2,1)S(1)} %get-tuple-element.96), channel_id=1, source_target_pairs={{8,0},{16,8},{24,16},{26,24},{18,26},{10,18},{2,10},{6,2},{14,6},{... | collective-permute-start | bytes 3538952 | tf_op jit(solution)/shard_map/ppermute | solution.py:94
  413.7 76.8 %collective-permute-start.7 = (bf16[192,3072]{1,0:T(8,128)(2,1)S(1)}, bf16[192,3072]{1,0:T(8,128)(2,1)}, u32[]{:S(2)}, u32[]{:S(2)}) collective-permute-start(bf16[192,3072]{1,0:T(8,128)(2,1)S(1)} %get-tuple-element.97), channel_id=1, source_target_pairs={{0,8},{8,16},{16,24},{24,26},{26,18},{18,10},{10,2},{2,6},{6,14},{... | collective-permute-start | bytes 3538952 | tf_op jit(solution)/shard_map/ppermute | solution.py:93
  497.3 26.7 %collective-permute-start.18 = (bf16[192,3072]{1,0:T(8,128)(2,1)S(1)}, bf16[192,3072]{1,0:T(8,128)(2,1)}, u32[]{:S(2)}, u32[]{:S(2)}) collective-permute-start(bf16[192,3072]{1,0:T(8,128)(2,1)S(1)} %get-tuple-element.94), channel_id=1, source_target_pairs={{8,0},{16,8},{24,16},{26,24},{18,26},{10,18},{2,10},{6,2},{14,6},{... | collective-permute-start | bytes 3538952 | tf_op jit(solution)/shard_map/ppermute | solution.py:94
  497.4 26.7 %collective-permute-start.8 = (bf16[192,3072]{1,0:T(8,128)(2,1)S(1)}, bf16[192,3072]{1,0:T(8,128)(2,1)}, u32[]{:S(2)}, u32[]{:S(2)}) collective-permute-start(bf16[192,3072]{1,0:T(8,128)(2,1)S(1)} %get-tuple-element.95), channel_id=1, source_target_pairs={{0,8},{8,16},{16,24},{24,26},{26,18},{18,10},{10,2},{2,6},{6,14},{... | collective-permute-start | bytes 3538952 | tf_op jit(solution)/shard_map/ppermute | solution.py:93
  530.9 25.8 %collective-permute-start.19 = (bf16[192,3072]{1,0:T(8,128)(2,1)S(1)}, bf16[192,3072]{1,0:T(8,128)(2,1)}, u32[]{:S(2)}, u32[]{:S(2)}) collective-permute-start(bf16[192,3072]{1,0:T(8,128)(2,1)S(1)} %get-tuple-element.92), channel_id=1, source_target_pairs={{8,0},{16,8},{24,16},{26,24},{18,26},{10,18},{2,10},{6,2},{14,6},{... | collective-permute-start | bytes 3538952 | tf_op jit(solution)/shard_map/ppermute | solution.py:94
  531.2 25.9 %collective-permute-start.9 = (bf16[192,3072]{1,0:T(8,128)(2,1)S(1)}, bf16[192,3072]{1,0:T(8,128)(2,1)}, u32[]{:S(2)}, u32[]{:S(2)}) collective-permute-start(bf16[192,3072]{1,0:T(8,128)(2,1)S(1)} %get-tuple-element.93), channel_id=1, source_target_pairs={{0,8},{8,16},{16,24},{24,26},{26,18},{18,10},{10,2},{2,6},{6,14},{... | collective-permute-start | bytes 3538952 | tf_op jit(solution)/shard_map/ppermute | solution.py:93
  564.0 24.9 %collective-permute-start.20 = (bf16[192,3072]{1,0:T(8,128)(2,1)S(1)}, bf16[192,3072]{1,0:T(8,128)(2,1)}, u32[]{:S(2)}, u32[]{:S(2)}) collective-permute-start(bf16[192,3072]{1,0:T(8,128)(2,1)S(1)} %get-tuple-element.90), channel_id=1, source_target_pairs={{8,0},{16,8},{24,16},{26,24},{18,26},{10,18},{2,10},{6,2},{14,6},{... | collective-permute-start | bytes 3538952 | tf_op jit(solution)/shard_map/ppermute | solution.py:94
  564.6 24.4 %collective-permute-start.10 = (bf16[192,3072]{1,0:T(8,128)(2,1)S(1)}, bf16[192,3072]{1,0:T(8,128)(2,1)}, u32[]{:S(2)}, u32[]{:S(2)}) collective-permute-start(bf16[192,3072]{1,0:T(8,128)(2,1)S(1)} %get-tuple-element.91), channel_id=1, source_target_pairs={{0,8},{8,16},{16,24},{24,26},{26,18},{18,10},{10,2},{2,6},{6,14},{... | collective-permute-start | bytes 3538952 | tf_op jit(solution)/shard_map/ppermute | solution.py:93
  595.8 23.9 %collective-permute-start.21 = (bf16[192,3072]{1,0:T(8,128)(2,1)S(1)}, bf16[192,3072]{1,0:T(8,128)(2,1)}, u32[]{:S(2)}, u32[]{:S(2)}) collective-permute-start(bf16[192,3072]{1,0:T(8,128)(2,1)S(1)} %get-tuple-element.88), channel_id=1, source_target_pairs={{8,0},{16,8},{24,16},{26,24},{18,26},{10,18},{2,10},{6,2},{14,6},{... | collective-permute-start | bytes 3538952 | tf_op jit(solution)/shard_map/ppermute | solution.py:94
  596.2 23.5 %collective-permute-start.11 = (bf16[192,3072]{1,0:T(8,128)(2,1)S(1)}, bf16[192,3072]{1,0:T(8,128)(2,1)}, u32[]{:S(2)}, u32[]{:S(2)}) collective-permute-start(bf16[192,3072]{1,0:T(8,128)(2,1)S(1)} %get-tuple-element.89), channel_id=1, source_target_pairs={{0,8},{8,16},{16,24},{24,26},{26,18},{18,10},{10,2},{2,6},{6,14},{... | collective-permute-start | bytes 3538952 | tf_op jit(solution)/shard_map/ppermute | solution.py:93
  626.5 22.9 %collective-permute-start.22 = (bf16[192,3072]{1,0:T(8,128)(2,1)S(1)}, bf16[192,3072]{1,0:T(8,128)(2,1)}, u32[]{:S(2)}, u32[]{:S(2)}) collective-permute-start(bf16[192,3072]{1,0:T(8,128)(2,1)S(1)} %get-tuple-element.86), channel_id=1, source_target_pairs={{8,0},{16,8},{24,16},{26,24},{18,26},{10,18},{2,10},{6,2},{14,6},{... | collective-permute-start | bytes 3538952 | tf_op jit(solution)/shard_map/ppermute | solution.py:94
  626.8 22.6 %collective-permute-start.12 = (bf16[192,3072]{1,0:T(8,128)(2,1)S(1)}, bf16[192,3072]{1,0:T(8,128)(2,1)}, u32[]{:S(2)}, u32[]{:S(2)}) collective-permute-start(bf16[192,3072]{1,0:T(8,128)(2,1)S(1)} %get-tuple-element.87), channel_id=1, source_target_pairs={{0,8},{8,16},{16,24},{24,26},{26,18},{18,10},{10,2},{2,6},{6,14},{... | collective-permute-start | bytes 3538952 | tf_op jit(solution)/shard_map/ppermute | solution.py:93
  656.2 33.6 %collective-permute-start.23 = (bf16[192,3072]{1,0:T(8,128)(2,1)S(1)}, bf16[192,3072]{1,0:T(8,128)(2,1)S(1)}, u32[]{:S(2)}, u32[]{:S(2)}) collective-permute-start(bf16[192,3072]{1,0:T(8,128)(2,1)S(1)} %get-tuple-element.84), channel_id=1, source_target_pairs={{8,0},{16,8},{24,16},{26,24},{18,26},{10,18},{2,10},{6,2},{14,6},{... | collective-permute-start | bytes 3538952 | tf_op jit(solution)/shard_map/ppermute | solution.py:94
  656.5 33.4 %collective-permute-start.13 = (bf16[192,3072]{1,0:T(8,128)(2,1)S(1)}, bf16[192,3072]{1,0:T(8,128)(2,1)}, u32[]{:S(2)}, u32[]{:S(2)}) collective-permute-start(bf16[192,3072]{1,0:T(8,128)(2,1)S(1)} %get-tuple-element.85), channel_id=1, source_target_pairs={{0,8},{8,16},{16,24},{24,26},{26,18},{18,10},{10,2},{2,6},{6,14},{... | collective-permute-start | bytes 3538952 | tf_op jit(solution)/shard_map/ppermute | solution.py:93
  697.7 19.9 %copy-start.4 = (bf16[192,3072]{1,0:T(8,128)(2,1)S(1)}, bf16[192,3072]{1,0:T(8,128)(2,1)}, u32[]{:S(2)}) copy-start(bf16[192,3072]{1,0:T(8,128)(2,1)} %get-tuple-element.37) | copy-start | bytes 3538948
  717.7 23.0 %collective-permute-start.24 = (bf16[192,3072]{1,0:T(8,128)(2,1)S(1)}, bf16[192,3072]{1,0:T(8,128)(2,1)}, u32[]{:S(2)}, u32[]{:S(2)}) collective-permute-start(bf16[192,3072]{1,0:T(8,128)(2,1)S(1)} %copy-done.4), channel_id=1, source_target_pairs={{0,8},{8,16},{16,24},{24,26},{26,18},{18,10},{10,2},{2,6},{6,14},{... | collective-permute-start | bytes 3538952 | tf_op jit(solution)/shard_map/ppermute | solution.py:93
  719.4 21.3 %collective-permute-start.25 = (bf16[192,3072]{1,0:T(8,128)(2,1)}, bf16[192,3072]{1,0:T(8,128)(2,1)}, u32[]{:S(2)}, u32[]{:S(2)}) collective-permute-start(bf16[192,3072]{1,0:T(8,128)(2,1)} %get-tuple-element.38), channel_id=1, source_target_pairs={{8,0},{16,8},{24,16},{26,24},{18,26},{10,18},{2,10},{6,2},{14,6},{... | collective-permute-start | bytes 3538952 | tf_op jit(solution)/shard_map/ppermute | solution.py:94
  748.5 23.0 %collective-permute-start.26 = (bf16[192,3072]{1,0:T(8,128)(2,1)S(1)}, bf16[192,3072]{1,0:T(8,128)(2,1)}, u32[]{:S(2)}, u32[]{:S(2)}) collective-permute-start(bf16[192,3072]{1,0:T(8,128)(2,1)S(1)} %get-tuple-element.41), channel_id=1, source_target_pairs={{0,8},{8,16},{16,24},{24,26},{26,18},{18,10},{10,2},{2,6},{6,14},{... | collective-permute-start | bytes 3538952 | tf_op jit(solution)/shard_map/ppermute | solution.py:93
  750.2 21.3 %collective-permute-start.27 = (bf16[192,3072]{1,0:T(8,128)(2,1)}, bf16[192,3072]{1,0:T(8,128)(2,1)}, u32[]{:S(2)}, u32[]{:S(2)}) collective-permute-start(bf16[192,3072]{1,0:T(8,128)(2,1)} %get-tuple-element.42), channel_id=1, source_target_pairs={{8,0},{16,8},{24,16},{26,24},{18,26},{10,18},{2,10},{6,2},{14,6},{... | collective-permute-start | bytes 3538952 | tf_op jit(solution)/shard_map/ppermute | solution.py:94
  779.4 37.1 %collective-permute-start.28 = (bf16[192,3072]{1,0:T(8,128)(2,1)S(1)}, bf16[192,3072]{1,0:T(8,128)(2,1)}, u32[]{:S(2)}, u32[]{:S(2)}) collective-permute-start(bf16[192,3072]{1,0:T(8,128)(2,1)S(1)} %get-tuple-element.45), channel_id=1, source_target_pairs={{0,8},{8,16},{16,24},{24,26},{26,18},{18,10},{10,2},{2,6},{6,14},{... | collective-permute-start | bytes 3538952 | tf_op jit(solution)/shard_map/ppermute | solution.py:93
  781.1 35.4 %collective-permute-start.29 = (bf16[192,3072]{1,0:T(8,128)(2,1)}, bf16[192,3072]{1,0:T(8,128)(2,1)}, u32[]{:S(2)}, u32[]{:S(2)}) collective-permute-start(bf16[192,3072]{1,0:T(8,128)(2,1)} %get-tuple-element.46), channel_id=1, source_target_pairs={{8,0},{16,8},{24,16},{26,24},{18,26},{10,18},{2,10},{6,2},{14,6},{... | collective-permute-start | bytes 3538952 | tf_op jit(solution)/shard_map/ppermute | solution.py:94
  823.3 22.9 %collective-permute-start.30 = (bf16[192,3072]{1,0:T(8,128)(2,1)S(1)}, bf16[192,3072]{1,0:T(8,128)(2,1)S(1)}, u32[]{:S(2)}, u32[]{:S(2)}) collective-permute-start(bf16[192,3072]{1,0:T(8,128)(2,1)S(1)} %get-tuple-element.49), channel_id=1, source_target_pairs={{0,8},{8,16},{16,24},{24,26},{26,18},{18,10},{10,2},{2,6},{6,14},{... | collective-permute-start | bytes 3538952 | tf_op jit(solution)/shard_map/ppermute | solution.py:93
  825.0 21.2 %collective-permute-start.31 = (bf16[192,3072]{1,0:T(8,128)(2,1)S(1)}, bf16[192,3072]{1,0:T(8,128)(2,1)}, u32[]{:S(2)}, u32[]{:S(2)}) collective-permute-start(bf16[192,3072]{1,0:T(8,128)(2,1)S(1)} %get-tuple-element.50), channel_id=1, source_target_pairs={{8,0},{16,8},{24,16},{26,24},{18,26},{10,18},{2,10},{6,2},{14,6},{... | collective-permute-start | bytes 3538952 | tf_op jit(solution)/shard_map/ppermute | solution.py:94
  853.7 24.0 %collective-permute-start.32 = (bf16[192,3072]{1,0:T(8,128)(2,1)S(1)}, bf16[192,3072]{1,0:T(8,128)(2,1)S(1)}, u32[]{:S(2)}, u32[]{:S(2)}) collective-permute-start(bf16[192,3072]{1,0:T(8,128)(2,1)S(1)} %get-tuple-element.53), channel_id=1, source_target_pairs={{0,8},{8,16},{16,24},{24,26},{26,18},{18,10},{10,2},{2,6},{6,14},{... | collective-permute-start | bytes 3538952 | tf_op jit(solution)/shard_map/ppermute | solution.py:93
  855.4 21.2 %collective-permute-start.33 = (bf16[192,3072]{1,0:T(8,128)(2,1)}, bf16[192,3072]{1,0:T(8,128)(2,1)S(1)}, u32[]{:S(2)}, u32[]{:S(2)}) collective-permute-start(bf16[192,3072]{1,0:T(8,128)(2,1)} %get-tuple-element.54), channel_id=1, source_target_pairs={{8,0},{16,8},{24,16},{26,24},{18,26},{10,18},{2,10},{6,2},{14,6},{... | collective-permute-start | bytes 3538952 | tf_op jit(solution)/shard_map/ppermute | solution.py:94
  876.6 8.3 copy-start.1
  876.6 8.3 copy-start.2
  876.6 8.3 copy-start.3
  876.6 1.0 copy-start.5
Sparse Core Ops, SparseCore 0:
  11.5 490.1 all-gather.1

commit v7 on v6

--- a/solution.py
+++ b/solution.py
@@ -88,7 +88,7 @@
     send_cw = own_block(order_arr[(pos - 1) % n])[:, :half].astype(jnp.bfloat16)
     send_ccw = own_block(order_arr[(pos + 1) % n])[:, half:].astype(jnp.bfloat16)
     products = []
-    first_piece = max(0, n - 1 - 2 * n_pieces)
+    first_piece = max(0, n - 3 - 2 * n_pieces)
     for step in range(n - 1):
         recv_cw = lax.ppermute(send_cw, "chip", forward)
         recv_ccw = lax.ppermute(send_ccw, "chip", backward)

time: 940 us -> 917 us (0.976)
  waiting for transfers between devices: 377 us -> 355 us
    ppermute x15, waiting for transfers between devices: 333 us -> 303 us  [per_device(): recv_ccw = lax.ppermute(send_ccw, 'chip', backward)]
    convert_element_type x0 -> x2, other arithmetic: none -> 14.8 us  [per_device(): send_cw = (recv_cw.astype(jnp.float32) + mine_cw).astype(jnp.bfloat16)]
    convert_element_type x15 -> x13, other arithmetic: 106 us -> 92.2 us  [per_device(): send_ccw = (recv_ccw.astype(jnp.float32) + mine_ccw).astype(jnp.bfloat16)]
    concatenate x1, other arithmetic: 17.8 us -> 5.46 us  [per_device(): d_context = jnp.concatenate(products[n_pieces:], axis=1)]
    concatenate x1, other arithmetic: 5.4 us -> 17.4 us  [per_device(): out = jnp.concatenate(products[:n_pieces], axis=1)]
    unnamed x19 -> x21, local copies, waits for them, and re-layouts: 26.9 us -> 27.1 us
  transfers between devices with their start and end apart: 35 -> 35, of which waited for: 17 -> 15; matrix products, arithmetic and copies ran while one was open for 31% -> 33% of each run, Pallas kernels for 0% -> 0%
where the time goes in v7:
time: 917 us; the launch traced here: 906 us
  waiting for transfers between devices  355 us (39%)
  matrix products  203 us (22%)
  other arithmetic  155 us (17%)
  between operations  116 us (13%)
  starting transfers between devices  47.4 us (5%)
  local copies, waits for them, and re-layouts  29.3 us (3%)
    ppermute x15, waiting for transfers between devices, per_device(): recv_ccw = lax.ppermute(send_ccw, 'chip', backward)  303 us
    convert_element_type x13, other arithmetic, per_device(): send_ccw = (recv_ccw.astype(jnp.float32) + mine_ccw).astype(jnp.bfloat16)  92.2 us
    dot_general x3, matrix products, product(): lax.dot_general(piece, w[k * d_rows:(k + 1) * d_rows], (((1,), (1,)), (()...  62.1 us
    dot_general x3, matrix products, product(): jnp.dot(context, w[:, j * out_cols:(j + 1) * out_cols], preferred_element...  61.4 us
    ppermute x4, waiting for transfers between devices, per_device(): grad_from_other = lax.ppermute(grad_for_other, 'core', swap)  42.9 us
    dot_general x4, matrix products, per_device(): lax.dot_general(ctx_own[:, cols], piece, dims_wgrad, preferred_element_ty...  42.1 us
    dot_general x4, matrix products, per_device(): lax.dot_general(ctx_q, piece, dims_wgrad, preferred_element_type=jnp.floa...  37.6 us
    unnamed x21, local copies, waits for them, and re-layouts  27.1 us
  transfers between devices with their start and end apart: 35, of which 15 were waited for; matrix products, arithmetic and copies ran while one was open for 33% of the time, Pallas kernels for 0%

profile of v7, /device:TPU:0, one launch (start us, length us, event | category | flops | bytes accessed | tf_op | source)
XLA Modules:
  0.0 905.6 jit_solution(10312552427805811395)
XLA Ops:
  7.2 4.1 convert_element_type.336
  11.3 8.6 copy.14
  19.9 3.8 broadcast_select_fusion.1
  23.7 11.3 %convolution_convert_fusion.3 = bf16[768,6144]{1,0:T(8,128)(2,1)} fusion(bf16[512,6144]{1,0:T(8,128)(2,1)} %param.11, bf16[512,3072]{0,1:T(8,128)(2,1)S(1)} %bitcast.99), kind=kOutput, calls=%fused_computation.19 | convolution fusion | flops 4836556800 | bytes 16515072 | tf_op jit(solution)/shard_map/dot_general | solution.py:45
  35.8 14.3 %collective-permute-done = bf16[768,6144]{1,0:T(8,128)(2,1)S(1)} collective-permute-done((bf16[768,6144]{1,0:T(8,128)(2,1)}, bf16[768,6144]{1,0:T(8,128)(2,1)S(1)}, u32[]{:S(2)}, u32[]{:S(2)}) %collective-permute-start) | collective-permute-done | bytes 9437216 | tf_op jit(solution)/shard_map/ppermute | solution.py:48
  50.2 10.3 %add_convert_fusion.3 = bf16[768,6144]{1,0:T(8,128)(2,1)} fusion(bf16[768,6144]{1,0:T(8,128)(2,1)S(1)} %collective-permute-done, bf16[512,6144]{1,0:T(8,128)(2,1)} %param.11, bf16[512,3072]{0,1:T(8,128)(2,1)S(1)} %bitcast.101), kind=kOutput, calls=%fused_computation.15 | convolution fusion | flops 4845993984 | bytes 25952256 | tf_op jit(solution)/shard_map/dot_general | solution.py:49
  60.5 8.1 convolution_convert_fusion.2
  69.0 14.3 %collective-permute-done.1 = bf16[768,6144]{1,0:T(8,128)(2,1)S(1)} collective-permute-done((bf16[768,6144]{1,0:T(8,128)(2,1)S(1)}, bf16[768,6144]{1,0:T(8,128)(2,1)S(1)}, u32[]{:S(2)}, u32[]{:S(2)}) %collective-permute-start.1) | collective-permute-done | bytes 9437216 | tf_op jit(solution)/shard_map/ppermute | solution.py:48
  83.3 11.2 %add_convert_fusion.2 = bf16[768,6144]{1,0:T(8,128)(2,1)} fusion(bf16[768,6144]{1,0:T(8,128)(2,1)S(1)} %collective-permute-done.1, bf16[512,6144]{1,0:T(8,128)(2,1)} %param.11, bf16[512,3072]{0,1:T(8,128)(2,1)S(1)} %bitcast.102), kind=kOutput, calls=%fused_computation.14 | convolution fusion | flops 4845993984 | bytes 25952256 | tf_op jit(solution)/shard_map/dot_general | solution.py:49
  94.5 8.0 convolution_convert_fusion.1
  103.1 14.3 %collective-permute-done.2 = bf16[768,6144]{1,0:T(8,128)(2,1)S(1)} collective-permute-done((bf16[768,6144]{1,0:T(8,128)(2,1)S(1)}, bf16[768,6144]{1,0:T(8,128)(2,1)S(1)}, u32[]{:S(2)}, u32[]{:S(2)}) %collective-permute-start.2) | collective-permute-done | bytes 9437216 | tf_op jit(solution)/shard_map/ppermute | solution.py:48
  117.4 10.6 %add_convert_fusion.1 = bf16[768,6144]{1,0:T(8,128)(2,1)} fusion(bf16[768,6144]{1,0:T(8,128)(2,1)S(1)} %collective-permute-done.2, bf16[512,6144]{1,0:T(8,128)(2,1)} %param.11, bf16[512,3072]{0,1:T(8,128)(2,1)S(1)} %bitcast.103), kind=kOutput, calls=%fused_computation.13 | convolution fusion | flops 4845993984 | bytes 25952256 | tf_op jit(solution)/shard_map/dot_general | solution.py:49
  128.0 10.2 %convolution_convert_fusion = bf16[768,6144]{1,0:T(8,128)(2,1)} fusion(bf16[512,768]{0,1:T(8,128)(2,1)S(1)} %get-tuple-element.34, bf16[512,6144]{1,0:T(8,128)(2,1)} %param.11), kind=kOutput, calls=%fused_computation.16 | convolution fusion | flops 4836556800 | bytes 16515072 | tf_op jit(solution)/shard_map/dot_general | solution.py:45
  154.2 10.0 %add_convert_fusion = bf16[768,6144]{1,0:T(8,128)(2,1)S(1)} fusion(bf16[768,6144]{1,0:T(8,128)(2,1)} %collective-permute-done.3, bf16[512,6144]{1,0:T(8,128)(2,1)} %param.11, bf16[512,3072]{0,1:T(8,128)(2,1)S(1)} %bitcast.104), kind=kOutput, calls=%fused_computation.12 | convolution fusion | flops 4845993984 | bytes 25952256 | tf_op jit(solution)/shard_map/dot_general | solution.py:49
  164.3 8.3 dynamic-slice_select_fusion.66
  172.5 3.4 collective-permute-start.12
  181.3 42.6 %collective-permute-done.12 = bf16[192,3072]{1,0:T(8,128)(2,1)S(1)} collective-permute-done((bf16[192,3072]{1,0:T(8,128)(2,1)S(1)}, bf16[192,3072]{1,0:T(8,128)(2,1)S(1)}, u32[]{:S(2)}, u32[]{:S(2)}) %collective-permute-start.12) | collective-permute-done | bytes 1179680 | tf_op jit(solution)/shard_map/ppermute | solution.py:94
  223.9 6.4 add_convert_fusion.25
  230.4 1.8 collective-permute-start.13
  232.2 5.6 collective-permute-start.5
  242.7 72.2 %collective-permute-done.13 = bf16[192,3072]{1,0:T(8,128)(2,1)S(1)} collective-permute-done((bf16[192,3072]{1,0:T(8,128)(2,1)S(1)}, bf16[192,3072]{1,0:T(8,128)(2,1)S(1)}, u32[]{:S(2)}, u32[]{:S(2)}) %collective-permute-start.13) | collective-permute-done | bytes 1179680 | tf_op jit(solution)/shard_map/ppermute | solution.py:94
  314.9 6.4 add_convert_fusion.24
  321.3 3.4 collective-permute-start.14
  324.7 1.9 collective-permute-start.6
  344.0 60.9 %collective-permute-done.14 = bf16[192,3072]{1,0:T(8,128)(2,1)S(1)} collective-permute-done((bf16[192,3072]{1,0:T(8,128)(2,1)S(1)}, bf16[192,3072]{1,0:T(8,128)(2,1)S(1)}, u32[]{:S(2)}, u32[]{:S(2)}) %collective-permute-start.14) | collective-permute-done | bytes 1179680 | tf_op jit(solution)/shard_map/ppermute | solution.py:94
  404.8 6.5 add_convert_fusion.23
  411.3 2.0 collective-permute-start.15
  418.2 72.0 %collective-permute-done.15 = bf16[192,3072]{1,0:T(8,128)(2,1)S(1)} collective-permute-done((bf16[192,3072]{1,0:T(8,128)(2,1)S(1)}, bf16[192,3072]{1,0:T(8,128)(2,1)S(1)}, u32[]{:S(2)}, u32[]{:S(2)}) %collective-permute-start.15) | collective-permute-done | bytes 1179680 | tf_op jit(solution)/shard_map/ppermute | solution.py:94
  490.2 6.4 add_convert_fusion.22
  496.7 4.9 collective-permute-start.8
  506.5 16.8 %collective-permute-done.16 = bf16[192,3072]{1,0:T(8,128)(2,1)S(1)} collective-permute-done((bf16[192,3072]{1,0:T(8,128)(2,1)S(1)}, bf16[192,3072]{1,0:T(8,128)(2,1)S(1)}, u32[]{:S(2)}, u32[]{:S(2)}) %collective-permute-start.16) | collective-permute-done | bytes 1179680 | tf_op jit(solution)/shard_map/ppermute | solution.py:94
  523.5 6.4 add_convert_fusion.21
  530.1 2.3 collective-permute-start.9
  537.5 18.2 %collective-permute-done.17 = bf16[192,3072]{1,0:T(8,128)(2,1)S(1)} collective-permute-done((bf16[192,3072]{1,0:T(8,128)(2,1)S(1)}, bf16[192,3072]{1,0:T(8,128)(2,1)S(1)}, u32[]{:S(2)}, u32[]{:S(2)}) %collective-permute-start.17) | collective-permute-done | bytes 1179680 | tf_op jit(solution)/shard_map/ppermute | solution.py:94
  556.3 6.4 add_convert_fusion.20
  569.8 17.9 %collective-permute-done.18 = bf16[192,3072]{1,0:T(8,128)(2,1)S(1)} collective-permute-done((bf16[192,3072]{1,0:T(8,128)(2,1)S(1)}, bf16[192,3072]{1,0:T(8,128)(2,1)S(1)}, u32[]{:S(2)}, u32[]{:S(2)}) %collective-permute-start.18) | collective-permute-done | bytes 1179680 | tf_op jit(solution)/shard_map/ppermute | solution.py:94
  587.9 6.4 add_convert_fusion.19
  594.4 2.2 collective-permute-start.19
  626.4 7.9 add_convert_fusion.18
  634.3 20.8 %fusion.39 = bf16[512,2048]{0,1:T(8,128)(2,1)} fusion(bf16[512,6144]{1,0:T(8,128)(2,1)} %param.7, bf16[6144,6144]{1,0:T(8,128)(2,1)} %all-gather.2.cloned.1.call-done), kind=kOutput, calls=%fused_computation.39 | convolution fusion | flops 12885950464 | bytes 33554432 | tf_op jit(solution)/shard_map/dot_general | solution.py:79
  657.3 19.8 %fusion.36 = bf16[512,2048]{0,1:T(8,128)(2,1)S(1)} fusion(bf16[512,6144]{1,0:T(8,128)(2,1)} %param.7, bf16[6144,6144]{1,0:T(8,128)(2,1)} %all-gather.2.cloned.1.call-done), kind=kOutput, calls=%fused_computation.38 | convolution fusion | flops 12885950464 | bytes 33554432 | tf_op jit(solution)/shard_map/dot_general | solution.py:79
  677.1 2.7 collective-permute-done.21
  679.8 7.9 add_convert_fusion.16
  688.4 1.5 collective-permute-start.23
  689.9 20.8 %fusion.33 = bf16[512,2048]{0,1:T(8,128)(2,1)} fusion(bf16[512,6144]{1,0:T(8,128)(2,1)} %param.7, bf16[6144,6144]{1,0:T(8,128)(2,1)} %all-gather.2.cloned.1.call-done), kind=kOutput, calls=%fused_computation.37 | convolution fusion | flops 12885950464 | bytes 33554432 | tf_op jit(solution)/shard_map/dot_general | solution.py:79
  710.6 7.9 add_convert_fusion.14
  719.3 1.7 collective-permute-start.25
  720.9 20.7 %fusion.48 = bf16[512,2048]{0,1:T(8,128)(2,1)} fusion(bf16[512,6144]{1,0:T(8,128)(2,1)} %param.11, bf16[6144,6144]{1,0:T(8,128)(2,1)} %all-gather.2.cloned.1.call-done), kind=kOutput, calls=%fused_computation.42 | convolution fusion | flops 12885950464 | bytes 33554432 | tf_op jit(solution)/shard_map/dot_general | solution.py:83
  741.7 7.9 add_convert_fusion.12
  750.3 1.4 collective-permute-start.27
  751.7 20.7 %fusion.45 = bf16[512,2048]{0,1:T(8,128)(2,1)} fusion(bf16[512,6144]{1,0:T(8,128)(2,1)} %param.11, bf16[6144,6144]{1,0:T(8,128)(2,1)} %all-gather.2.cloned.1.call-done), kind=kOutput, calls=%fused_computation.41 | convolution fusion | flops 12885950464 | bytes 33554432 | tf_op jit(solution)/shard_map/dot_general | solution.py:83
  773.4 7.8 add_convert_fusion.10
  781.9 1.5 collective-permute-start.29
  783.4 20.7 %fusion.42 = bf16[512,2048]{0,1:T(8,128)(2,1)} fusion(bf16[512,6144]{1,0:T(8,128)(2,1)} %param.11, bf16[6144,6144]{1,0:T(8,128)(2,1)} %all-gather.2.cloned.1.call-done), kind=kOutput, calls=%fused_computation.40 | convolution fusion | flops 12885950464 | bytes 33554432 | tf_op jit(solution)/shard_map/dot_general | solution.py:83
  804.1 7.8 add_convert_fusion.8
  824.5 7.5 collective-permute-done.30
  832.0 8.3 add_convert_fusion.7
  840.6 2.0 collective-permute-start.33
  842.6 17.4 %pad_maximum_fusion = bf16[512,6144]{0,1:T(8,128)(2,1)} fusion(bf16[512,2048]{0,1:T(8,128)(2,1)S(1)} %copy-done.2, bf16[512,2048]{0,1:T(8,128)(2,1)S(1)} %fusion.36, bf16[512,2048]{0,1:T(8,128)(2,1)S(1)} %copy-done.1), kind=kLoop, calls=%fused_computation.23 | loop fusion | flops 18874368 | bytes 12582912 | tf_op jit(solution)/shard_map/concatenate | solution.py:108
  860.0 8.8 copy.15
  868.7 5.5 pad_maximum_fusion.1
  874.2 8.7 copy.16
  882.9 6.6 add_convert_fusion.6
  889.5 8.8 multiply_subtract_fusion
  (68 shorter events, 16.3 us)
Async XLA Ops:
  7.2 627.1 %all-gather.2.cloned.1.call-start = ((), (), s32[]{:S(2)}) async-start(), calls=%async_computation | async-start | bytes 77856768 | tf_op jit(solution)/shard_map/all_gather | solution.py:37
  35.0 15.1 %collective-permute-start = (bf16[768,6144]{1,0:T(8,128)(2,1)}, bf16[768,6144]{1,0:T(8,128)(2,1)S(1)}, u32[]{:S(2)}, u32[]{:S(2)}) collective-permute-start(bf16[768,6144]{1,0:T(8,128)(2,1)} %convolution_convert_fusion.3), channel_id=1, source_target_pairs={{0,1},{1,0},{2,3},{3,2},{4,5},{5,4},{6,7},{7,6},{8,9},{9,8},{10,11... | collective-permute-start | bytes 28311560 | tf_op jit(solution)/shard_map/ppermute | solution.py:48
  68.6 14.7 %collective-permute-start.1 = (bf16[768,6144]{1,0:T(8,128)(2,1)S(1)}, bf16[768,6144]{1,0:T(8,128)(2,1)S(1)}, u32[]{:S(2)}, u32[]{:S(2)}) collective-permute-start(bf16[768,6144]{1,0:T(8,128)(2,1)S(1)} %convolution_convert_fusion.2), channel_id=1, source_target_pairs={{0,1},{1,0},{2,3},{3,2},{4,5},{5,4},{6,7},{7,6},{8,9},{9,8},{10,11... | collective-permute-start | bytes 28311560 | tf_op jit(solution)/shard_map/ppermute | solution.py:48
  102.6 14.8 %collective-permute-start.2 = (bf16[768,6144]{1,0:T(8,128)(2,1)S(1)}, bf16[768,6144]{1,0:T(8,128)(2,1)S(1)}, u32[]{:S(2)}, u32[]{:S(2)}) collective-permute-start(bf16[768,6144]{1,0:T(8,128)(2,1)S(1)} %convolution_convert_fusion.1), channel_id=1, source_target_pairs={{0,1},{1,0},{2,3},{3,2},{4,5},{5,4},{6,7},{7,6},{8,9},{9,8},{10,11... | collective-permute-start | bytes 28311560 | tf_op jit(solution)/shard_map/ppermute | solution.py:48
  128.0 10.6 %copy-start.6 = (s32[16]{0:T(128)S(1)}, s32[16]{0:T(128)}, u32[]{:S(2)}) copy-start(s32[16]{0:T(128)} %constant.674.clone) | copy-start | bytes 196
  128.0 20.5 %copy-start.5 = (s32[16]{0:T(128)S(1)}, s32[16]{0:T(128)}, u32[]{:S(2)}) copy-start(s32[16]{0:T(128)} %constant.673.clone) | copy-start | bytes 196
  138.2 16.1 %collective-permute-start.3 = (bf16[768,6144]{1,0:T(8,128)(2,1)}, bf16[768,6144]{1,0:T(8,128)(2,1)}, u32[]{:S(2)}, u32[]{:S(2)}) collective-permute-start(bf16[768,6144]{1,0:T(8,128)(2,1)} %convolution_convert_fusion), channel_id=1, source_target_pairs={{0,1},{1,0},{2,3},{3,2},{4,5},{5,4},{6,7},{7,6},{8,9},{9,8},{10,11... | collective-permute-start | bytes 28311560 | tf_op jit(solution)/shard_map/ppermute | solution.py:48
  164.3 8.3 copy-start
  172.5 51.4 %collective-permute-start.12 = (bf16[192,3072]{1,0:T(8,128)(2,1)S(1)}, bf16[192,3072]{1,0:T(8,128)(2,1)S(1)}, u32[]{:S(2)}, u32[]{:S(2)}) collective-permute-start(bf16[192,3072]{1,0:T(8,128)(2,1)S(1)} %get-tuple-element.102), channel_id=1, source_target_pairs={{8,0},{16,8},{24,16},{26,24},{18,26},{10,18},{2,10},{6,2},{14,6},{... | collective-permute-start | bytes 3538952 | tf_op jit(solution)/shard_map/ppermute | solution.py:94
  175.9 48.0 %collective-permute-start.4 = (bf16[192,3072]{1,0:T(8,128)(2,1)S(1)}, bf16[192,3072]{1,0:T(8,128)(2,1)}, u32[]{:S(2)}, u32[]{:S(2)}) collective-permute-start(bf16[192,3072]{1,0:T(8,128)(2,1)S(1)} %get-tuple-element.103), channel_id=1, source_target_pairs={{0,8},{8,16},{16,24},{24,26},{26,18},{18,10},{10,2},{2,6},{6,14},{... | collective-permute-start | bytes 3538952 | tf_op jit(solution)/shard_map/ppermute | solution.py:93
  230.4 84.5 %collective-permute-start.13 = (bf16[192,3072]{1,0:T(8,128)(2,1)S(1)}, bf16[192,3072]{1,0:T(8,128)(2,1)S(1)}, u32[]{:S(2)}, u32[]{:S(2)}) collective-permute-start(bf16[192,3072]{1,0:T(8,128)(2,1)S(1)} %get-tuple-element.100), channel_id=1, source_target_pairs={{8,0},{16,8},{24,16},{26,24},{18,26},{10,18},{2,10},{6,2},{14,6},{... | collective-permute-start | bytes 3538952 | tf_op jit(solution)/shard_map/ppermute | solution.py:94
  232.2 82.7 %collective-permute-start.5 = (bf16[192,3072]{1,0:T(8,128)(2,1)S(1)}, bf16[192,3072]{1,0:T(8,128)(2,1)}, u32[]{:S(2)}, u32[]{:S(2)}) collective-permute-start(bf16[192,3072]{1,0:T(8,128)(2,1)S(1)} %get-tuple-element.101), channel_id=1, source_target_pairs={{0,8},{8,16},{16,24},{24,26},{26,18},{18,10},{10,2},{2,6},{6,14},{... | collective-permute-start | bytes 3538952 | tf_op jit(solution)/shard_map/ppermute | solution.py:93
  321.3 83.5 %collective-permute-start.14 = (bf16[192,3072]{1,0:T(8,128)(2,1)S(1)}, bf16[192,3072]{1,0:T(8,128)(2,1)S(1)}, u32[]{:S(2)}, u32[]{:S(2)}) collective-permute-start(bf16[192,3072]{1,0:T(8,128)(2,1)S(1)} %get-tuple-element.98), channel_id=1, source_target_pairs={{8,0},{16,8},{24,16},{26,24},{18,26},{10,18},{2,10},{6,2},{14,6},{... | collective-permute-start | bytes 3538952 | tf_op jit(solution)/shard_map/ppermute | solution.py:94
  324.7 80.1 %collective-permute-start.6 = (bf16[192,3072]{1,0:T(8,128)(2,1)S(1)}, bf16[192,3072]{1,0:T(8,128)(2,1)}, u32[]{:S(2)}, u32[]{:S(2)}) collective-permute-start(bf16[192,3072]{1,0:T(8,128)(2,1)S(1)} %get-tuple-element.99), channel_id=1, source_target_pairs={{0,8},{8,16},{16,24},{24,26},{26,18},{18,10},{10,2},{2,6},{6,14},{... | collective-permute-start | bytes 3538952 | tf_op jit(solution)/shard_map/ppermute | solution.py:93
  411.3 78.9 %collective-permute-start.15 = (bf16[192,3072]{1,0:T(8,128)(2,1)S(1)}, bf16[192,3072]{1,0:T(8,128)(2,1)S(1)}, u32[]{:S(2)}, u32[]{:S(2)}) collective-permute-start(bf16[192,3072]{1,0:T(8,128)(2,1)S(1)} %get-tuple-element.96), channel_id=1, source_target_pairs={{8,0},{16,8},{24,16},{26,24},{18,26},{10,18},{2,10},{6,2},{14,6},{... | collective-permute-start | bytes 3538952 | tf_op jit(solution)/shard_map/ppermute | solution.py:94
  413.4 76.8 %collective-permute-start.7 = (bf16[192,3072]{1,0:T(8,128)(2,1)S(1)}, bf16[192,3072]{1,0:T(8,128)(2,1)}, u32[]{:S(2)}, u32[]{:S(2)}) collective-permute-start(bf16[192,3072]{1,0:T(8,128)(2,1)S(1)} %get-tuple-element.97), channel_id=1, source_target_pairs={{0,8},{8,16},{16,24},{24,26},{26,18},{18,10},{10,2},{2,6},{6,14},{... | collective-permute-start | bytes 3538952 | tf_op jit(solution)/shard_map/ppermute | solution.py:93
  496.7 26.6 %collective-permute-start.16 = (bf16[192,3072]{1,0:T(8,128)(2,1)S(1)}, bf16[192,3072]{1,0:T(8,128)(2,1)S(1)}, u32[]{:S(2)}, u32[]{:S(2)}) collective-permute-start(bf16[192,3072]{1,0:T(8,128)(2,1)S(1)} %get-tuple-element.94), channel_id=1, source_target_pairs={{8,0},{16,8},{24,16},{26,24},{18,26},{10,18},{2,10},{6,2},{14,6},{... | collective-permute-start | bytes 3538952 | tf_op jit(solution)/shard_map/ppermute | solution.py:94
  496.7 26.7 %collective-permute-start.8 = (bf16[192,3072]{1,0:T(8,128)(2,1)S(1)}, bf16[192,3072]{1,0:T(8,128)(2,1)}, u32[]{:S(2)}, u32[]{:S(2)}) collective-permute-start(bf16[192,3072]{1,0:T(8,128)(2,1)S(1)} %get-tuple-element.95), channel_id=1, source_target_pairs={{0,8},{8,16},{16,24},{24,26},{26,18},{18,10},{10,2},{2,6},{6,14},{... | collective-permute-start | bytes 3538952 | tf_op jit(solution)/shard_map/ppermute | solution.py:93
  529.9 25.7 %collective-permute-start.17 = (bf16[192,3072]{1,0:T(8,128)(2,1)S(1)}, bf16[192,3072]{1,0:T(8,128)(2,1)S(1)}, u32[]{:S(2)}, u32[]{:S(2)}) collective-permute-start(bf16[192,3072]{1,0:T(8,128)(2,1)S(1)} %get-tuple-element.92), channel_id=1, source_target_pairs={{8,0},{16,8},{24,16},{26,24},{18,26},{10,18},{2,10},{6,2},{14,6},{... | collective-permute-start | bytes 3538952 | tf_op jit(solution)/shard_map/ppermute | solution.py:94
  530.1 26.2 %collective-permute-start.9 = (bf16[192,3072]{1,0:T(8,128)(2,1)S(1)}, bf16[192,3072]{1,0:T(8,128)(2,1)}, u32[]{:S(2)}, u32[]{:S(2)}) collective-permute-start(bf16[192,3072]{1,0:T(8,128)(2,1)S(1)} %get-tuple-element.93), channel_id=1, source_target_pairs={{0,8},{8,16},{16,24},{24,26},{26,18},{18,10},{10,2},{2,6},{6,14},{... | collective-permute-start | bytes 3538952 | tf_op jit(solution)/shard_map/ppermute | solution.py:93
  562.8 24.9 %collective-permute-start.18 = (bf16[192,3072]{1,0:T(8,128)(2,1)S(1)}, bf16[192,3072]{1,0:T(8,128)(2,1)S(1)}, u32[]{:S(2)}, u32[]{:S(2)}) collective-permute-start(bf16[192,3072]{1,0:T(8,128)(2,1)S(1)} %get-tuple-element.90), channel_id=1, source_target_pairs={{8,0},{16,8},{24,16},{26,24},{18,26},{10,18},{2,10},{6,2},{14,6},{... | collective-permute-start | bytes 3538952 | tf_op jit(solution)/shard_map/ppermute | solution.py:94
  563.7 24.3 %collective-permute-start.10 = (bf16[192,3072]{1,0:T(8,128)(2,1)S(1)}, bf16[192,3072]{1,0:T(8,128)(2,1)}, u32[]{:S(2)}, u32[]{:S(2)}) collective-permute-start(bf16[192,3072]{1,0:T(8,128)(2,1)S(1)} %get-tuple-element.91), channel_id=1, source_target_pairs={{0,8},{8,16},{16,24},{24,26},{26,18},{18,10},{10,2},{2,6},{6,14},{... | collective-permute-start | bytes 3538952 | tf_op jit(solution)/shard_map/ppermute | solution.py:93
  594.4 32.1 %collective-permute-start.19 = (bf16[192,3072]{1,0:T(8,128)(2,1)S(1)}, bf16[192,3072]{1,0:T(8,128)(2,1)S(1)}, u32[]{:S(2)}, u32[]{:S(2)}) collective-permute-start(bf16[192,3072]{1,0:T(8,128)(2,1)S(1)} %get-tuple-element.88), channel_id=1, source_target_pairs={{8,0},{16,8},{24,16},{26,24},{18,26},{10,18},{2,10},{6,2},{14,6},{... | collective-permute-start | bytes 3538952 | tf_op jit(solution)/shard_map/ppermute | solution.py:94
  596.6 29.8 %collective-permute-start.11 = (bf16[192,3072]{1,0:T(8,128)(2,1)S(1)}, bf16[192,3072]{1,0:T(8,128)(2,1)}, u32[]{:S(2)}, u32[]{:S(2)}) collective-permute-start(bf16[192,3072]{1,0:T(8,128)(2,1)S(1)} %get-tuple-element.89), channel_id=1, source_target_pairs={{0,8},{8,16},{16,24},{24,26},{26,18},{18,10},{10,2},{2,6},{6,14},{... | collective-permute-start | bytes 3538952 | tf_op jit(solution)/shard_map/ppermute | solution.py:93
  655.1 24.7 %collective-permute-start.20 = (bf16[192,3072]{1,0:T(8,128)(2,1)}, bf16[192,3072]{1,0:T(8,128)(2,1)S(1)}, u32[]{:S(2)}, u32[]{:S(2)}) collective-permute-start(bf16[192,3072]{1,0:T(8,128)(2,1)} %get-tuple-element.37), channel_id=1, source_target_pairs={{0,8},{8,16},{16,24},{24,26},{26,18},{18,10},{10,2},{2,6},{6,14},{... | collective-permute-start | bytes 3538952 | tf_op jit(solution)/shard_map/ppermute | solution.py:93
  656.5 23.3 %collective-permute-start.21 = (bf16[192,3072]{1,0:T(8,128)(2,1)}, bf16[192,3072]{1,0:T(8,128)(2,1)}, u32[]{:S(2)}, u32[]{:S(2)}) collective-permute-start(bf16[192,3072]{1,0:T(8,128)(2,1)} %get-tuple-element.38), channel_id=1, source_target_pairs={{8,0},{16,8},{24,16},{26,24},{18,26},{10,18},{2,10},{6,2},{14,6},{... | collective-permute-start | bytes 3538952 | tf_op jit(solution)/shard_map/ppermute | solution.py:94
  687.6 23.0 %collective-permute-start.22 = (bf16[192,3072]{1,0:T(8,128)(2,1)}, bf16[192,3072]{1,0:T(8,128)(2,1)S(1)}, u32[]{:S(2)}, u32[]{:S(2)}) collective-permute-start(bf16[192,3072]{1,0:T(8,128)(2,1)} %get-tuple-element.41), channel_id=1, source_target_pairs={{0,8},{8,16},{16,24},{24,26},{26,18},{18,10},{10,2},{2,6},{6,14},{... | collective-permute-start | bytes 3538952 | tf_op jit(solution)/shard_map/ppermute | solution.py:93
  688.4 22.2 %collective-permute-start.23 = (bf16[192,3072]{1,0:T(8,128)(2,1)}, bf16[192,3072]{1,0:T(8,128)(2,1)}, u32[]{:S(2)}, u32[]{:S(2)}) collective-permute-start(bf16[192,3072]{1,0:T(8,128)(2,1)} %get-tuple-element.42), channel_id=1, source_target_pairs={{8,0},{16,8},{24,16},{26,24},{18,26},{10,18},{2,10},{6,2},{14,6},{... | collective-permute-start | bytes 3538952 | tf_op jit(solution)/shard_map/ppermute | solution.py:94
  718.5 23.1 %collective-permute-start.24 = (bf16[192,3072]{1,0:T(8,128)(2,1)}, bf16[192,3072]{1,0:T(8,128)(2,1)S(1)}, u32[]{:S(2)}, u32[]{:S(2)}) collective-permute-start(bf16[192,3072]{1,0:T(8,128)(2,1)} %get-tuple-element.45), channel_id=1, source_target_pairs={{0,8},{8,16},{16,24},{24,26},{26,18},{18,10},{10,2},{2,6},{6,14},{... | collective-permute-start | bytes 3538952 | tf_op jit(solution)/shard_map/ppermute | solution.py:93
  719.3 22.4 %collective-permute-start.25 = (bf16[192,3072]{1,0:T(8,128)(2,1)}, bf16[192,3072]{1,0:T(8,128)(2,1)}, u32[]{:S(2)}, u32[]{:S(2)}) collective-permute-start(bf16[192,3072]{1,0:T(8,128)(2,1)} %get-tuple-element.46), channel_id=1, source_target_pairs={{8,0},{16,8},{24,16},{26,24},{18,26},{10,18},{2,10},{6,2},{14,6},{... | collective-permute-start | bytes 3538952 | tf_op jit(solution)/shard_map/ppermute | solution.py:94
  749.5 23.9 %collective-permute-start.26 = (bf16[192,3072]{1,0:T(8,128)(2,1)}, bf16[192,3072]{1,0:T(8,128)(2,1)}, u32[]{:S(2)}, u32[]{:S(2)}) collective-permute-start(bf16[192,3072]{1,0:T(8,128)(2,1)} %get-tuple-element.49), channel_id=1, source_target_pairs={{0,8},{8,16},{16,24},{24,26},{26,18},{18,10},{10,2},{2,6},{6,14},{... | collective-permute-start | bytes 3538952 | tf_op jit(solution)/shard_map/ppermute | solution.py:93
  750.3 22.1 %collective-permute-start.27 = (bf16[192,3072]{1,0:T(8,128)(2,1)}, bf16[192,3072]{1,0:T(8,128)(2,1)S(1)}, u32[]{:S(2)}, u32[]{:S(2)}) collective-permute-start(bf16[192,3072]{1,0:T(8,128)(2,1)} %get-tuple-element.50), channel_id=1, source_target_pairs={{8,0},{16,8},{24,16},{26,24},{18,26},{10,18},{2,10},{6,2},{14,6},{... | collective-permute-start | bytes 3538952 | tf_op jit(solution)/shard_map/ppermute | solution.py:94
  772.4 1.0 copy-start.4
  781.2 22.9 %collective-permute-start.28 = (bf16[192,3072]{1,0:T(8,128)(2,1)S(1)}, bf16[192,3072]{1,0:T(8,128)(2,1)}, u32[]{:S(2)}, u32[]{:S(2)}) collective-permute-start(bf16[192,3072]{1,0:T(8,128)(2,1)S(1)} %get-tuple-element.53), channel_id=1, source_target_pairs={{0,8},{8,16},{16,24},{24,26},{26,18},{18,10},{10,2},{2,6},{6,14},{... | collective-permute-start | bytes 3538952 | tf_op jit(solution)/shard_map/ppermute | solution.py:93
  781.9 22.2 %collective-permute-start.29 = (bf16[192,3072]{1,0:T(8,128)(2,1)}, bf16[192,3072]{1,0:T(8,128)(2,1)}, u32[]{:S(2)}, u32[]{:S(2)}) collective-permute-start(bf16[192,3072]{1,0:T(8,128)(2,1)} %get-tuple-element.54), channel_id=1, source_target_pairs={{8,0},{16,8},{24,16},{26,24},{18,26},{10,18},{2,10},{6,2},{14,6},{... | collective-permute-start | bytes 3538952 | tf_op jit(solution)/shard_map/ppermute | solution.py:94
  811.9 20.1 %collective-permute-start.30 = (bf16[192,3072]{1,0:T(8,128)(2,1)}, bf16[192,3072]{1,0:T(8,128)(2,1)}, u32[]{:S(2)}, u32[]{:S(2)}) collective-permute-start(bf16[192,3072]{1,0:T(8,128)(2,1)} %get-tuple-element.57), channel_id=1, source_target_pairs={{0,8},{8,16},{16,24},{24,26},{26,18},{18,10},{10,2},{2,6},{6,14},{... | collective-permute-start | bytes 3538952 | tf_op jit(solution)/shard_map/ppermute | solution.py:93
  812.7 19.4 %collective-permute-start.32 = (bf16[192,3072]{1,0:T(8,128)(2,1)S(1)}, bf16[192,3072]{1,0:T(8,128)(2,1)}, u32[]{:S(2)}, u32[]{:S(2)}) collective-permute-start(bf16[192,3072]{1,0:T(8,128)(2,1)S(1)} %get-tuple-element.58), channel_id=1, source_target_pairs={{8,0},{16,8},{24,16},{26,24},{18,26},{10,18},{2,10},{6,2},{14,6},{... | collective-permute-start | bytes 3538952 | tf_op jit(solution)/shard_map/ppermute | solution.py:94
  824.5 18.1 %copy-start.1 = (bf16[512,2048]{0,1:T(8,128)(2,1)S(1)}, bf16[512,2048]{0,1:T(8,128)(2,1)}, u32[]{:S(2)}) copy-start(bf16[512,2048]{0,1:T(8,128)(2,1)} %fusion.39) | copy-start | bytes 6291460
  824.5 18.1 %copy-start.2 = (bf16[512,2048]{0,1:T(8,128)(2,1)S(1)}, bf16[512,2048]{0,1:T(8,128)(2,1)}, u32[]{:S(2)}) copy-start(bf16[512,2048]{0,1:T(8,128)(2,1)} %fusion.33) | copy-start | bytes 6291460
  840.3 42.6 %collective-permute-start.31 = (bf16[192,3072]{1,0:T(8,128)(2,1)}, bf16[192,3072]{1,0:T(8,128)(2,1)S(1)}, u32[]{:S(2)}, u32[]{:S(2)}) collective-permute-start(bf16[192,3072]{1,0:T(8,128)(2,1)} %get-tuple-element.74), channel_id=1, source_target_pairs={{0,8},{8,16},{16,24},{24,26},{26,18},{18,10},{10,2},{2,6},{6,14},{... | collective-permute-start | bytes 3538952 | tf_op jit(solution)/shard_map/ppermute | solution.py:93
  840.6 42.3 %collective-permute-start.33 = (bf16[192,3072]{1,0:T(8,128)(2,1)}, bf16[192,3072]{1,0:T(8,128)(2,1)}, u32[]{:S(2)}, u32[]{:S(2)}) collective-permute-start(bf16[192,3072]{1,0:T(8,128)(2,1)} %get-tuple-element.75), channel_id=1, source_target_pairs={{8,0},{16,8},{24,16},{26,24},{18,26},{10,18},{2,10},{6,2},{14,6},{... | collective-permute-start | bytes 3538952 | tf_op jit(solution)/shard_map/ppermute | solution.py:94
  860.0 8.8 copy-start.3
  874.2 15.3 %slice-start = ((s8[4718592]{0:T(1024)(128)(4,1)}), s8[524288]{0:T(1024)(128)(4,1)S(1)}, s32[]{:S(2)}) async-start(s8[4718592]{0:T(1024)(128)(4,1)} %bitcast.97), calls=%async_computation.1 | async-start | bytes 1048576
  882.9 6.6 slice-start.1
Sparse Core Ops, SparseCore 0:
  11.5 490.1 all-gather.1

commit v8 on v7

--- a/solution.py
+++ b/solution.py
@@ -35,18 +35,17 @@
     dims_wgrad = (((0,), (0,)), ((), ()))
 
     full_weight = lax.all_gather(weight_bf, DP, axis=0, tiled=True)
-    quarter = chips * rows // 4
+    quarter = width // 4
     sums = []
     for q in range(4):
-        cols = slice(q * quarter, (q + 1) * quarter)
-        ctx_q = ctx_other[:, cols]
+        piece_q = piece[:, q * quarter:(q + 1) * quarter]
         if sums:
-            ctx_q, _ = lax.optimization_barrier((ctx_q, sums[-1]))
+            piece_q, _ = lax.optimization_barrier((piece_q, sums[-1]))
         grad_for_other = lax.dot_general(
-            ctx_q, piece, dims_wgrad, preferred_element_type=jnp.float32
+            ctx_other, piece_q, dims_wgrad, preferred_element_type=jnp.float32
         ).astype(jnp.bfloat16)
         grad_from_other = lax.ppermute(grad_for_other, "core", swap)
-        grad_mine = lax.dot_general(ctx_own[:, cols], piece, dims_wgrad, preferred_element_type=jnp.float32)
+        grad_mine = lax.dot_general(ctx_own, piece_q, dims_wgrad, preferred_element_type=jnp.float32)
         sums.append((grad_mine + grad_from_other.astype(jnp.float32)).astype(jnp.bfloat16))
 
     n = chips
@@ -60,15 +59,10 @@
     pos = jnp.asarray(np.array(position, np.int32))[lax.axis_index("chip")]
     half = width // 2
 
-    per_quarter = quarter // rows
-
-    def own_block(block):
-        within = (block % per_quarter) * rows
-        which = block // per_quarter
-        picked = lax.dynamic_slice_in_dim(sums[0], within, rows, 0)
-        for q in range(1, 4):
-            picked = jnp.where(which == q, lax.dynamic_slice_in_dim(sums[q], within, rows, 0), picked)
-        return picked.astype(jnp.float32)
+    def own_block(block, first):
+        return jnp.concatenate(
+            [lax.dynamic_slice_in_dim(sums[q], block * rows, rows, 0) for q in (first, first + 1)], axis=1
+        ).astype(jnp.float32)
 
     n_pieces = 3
     out_cols = width // n_pieces
@@ -85,8 +79,8 @@
             preferred_element_type=jnp.float32,
         ).astype(jnp.bfloat16)
 
-    send_cw = own_block(order_arr[(pos - 1) % n])[:, :half].astype(jnp.bfloat16)
-    send_ccw = own_block(order_arr[(pos + 1) % n])[:, half:].astype(jnp.bfloat16)
+    send_cw = own_block(order_arr[(pos - 1) % n], 0).astype(jnp.bfloat16)
+    send_ccw = own_block(order_arr[(pos + 1) % n], 2).astype(jnp.bfloat16)
     products = []
     first_piece = max(0, n - 3 - 2 * n_pieces)
     for step in range(n - 1):
@@ -96,8 +90,8 @@
         if 0 <= j < 2 * n_pieces:
             w_now, _ = lax.optimization_barrier((full_weight, send_cw))
             products.append(product(j, w_now))
-        mine_cw = own_block(order_arr[(pos - step - 2) % n])[:, :half]
-        mine_ccw = own_block(order_arr[(pos + step + 2) % n])[:, half:]
+        mine_cw = own_block(order_arr[(pos - step - 2) % n], 0)
+        mine_ccw = own_block(order_arr[(pos + step + 2) % n], 2)
         send_cw = (recv_cw.astype(jnp.float32) + mine_cw).astype(jnp.bfloat16)
         send_ccw = (recv_ccw.astype(jnp.float32) + mine_ccw).astype(jnp.bfloat16)
         if 0 <= j < 2 * n_pieces:

time: 917 us -> 872 us (0.951)
  starting transfers between devices: 47.4 us -> 124 us
  between operations: 116 us -> 57.3 us
  other arithmetic: 155 us -> 97.5 us
  local copies, waits for them, and re-layouts: 29.3 us -> 52.1 us
  matrix products: 203 us -> 181 us
    ppermute x15, waiting for transfers between devices: 303 us -> 152 us  [per_device(): recv_ccw = lax.ppermute(send_ccw, 'chip', backward)]
    ppermute x15, waiting for transfers between devices: 8.69 us -> 154 us  [per_device(): recv_cw = lax.ppermute(send_cw, 'chip', forward)]
    ppermute x15, starting transfers between devices: 21.4 us -> 114 us  [per_device(): recv_cw = lax.ppermute(send_cw, 'chip', forward)]
    convert_element_type x13 -> x15, other arithmetic: 92.2 us -> 21.8 us  [per_device(): send_ccw = (recv_ccw.astype(jnp.float32) + mine_ccw).astype(jnp.bfloat16)]
    dot_general x8, matrix products: 79.8 us -> 56.5 us  [the longest x4 33.4 us: per_device(): lax.dot_general(ctx_own, piece_q, dims_wgrad, preferred_element_type=jnp....]
    dynamic_slice x2 -> x6, local copies, waits for them, and re-layouts: 1.48 us -> 22.4 us  [the longest x4 20.9 us: own_block(): lax.dynamic_slice_in_dim(sums[q], block * rows, rows, 0)]
    ppermute x15, starting transfers between devices: 24.1 us -> 8.64 us  [per_device(): recv_ccw = lax.ppermute(send_ccw, 'chip', backward)]
    concatenate x1, other arithmetic: 5.46 us -> 17.6 us  [per_device(): d_context = jnp.concatenate(products[n_pieces:], axis=1)]
  transfers between devices with their start and end apart: 35 -> 35, of which waited for: 15 -> 22; matrix products, arithmetic and copies ran while one was open for 33% -> 33% of each run, Pallas kernels for 0% -> 0%
where the time goes in v8:
time: 872 us; the launch traced here: 862 us
  waiting for transfers between devices  349 us (40%)
  matrix products  181 us (21%)
  starting transfers between devices  124 us (14%)
  other arithmetic  97.5 us (11%)
  between operations  57.3 us (7%)
  local copies, waits for them, and re-layouts  52.1 us (6%)
    ppermute x15, waiting for transfers between devices, per_device(): recv_cw = lax.ppermute(send_cw, 'chip', forward)  154 us
    ppermute x15, waiting for transfers between devices, per_device(): recv_ccw = lax.ppermute(send_ccw, 'chip', backward)  152 us
    ppermute x15, starting transfers between devices, per_device(): recv_cw = lax.ppermute(send_cw, 'chip', forward)  114 us
    dot_general x3, matrix products, product(): jnp.dot(context, w[:, j * out_cols:(j + 1) * out_cols], preferred_element...  62.3 us
    dot_general x3, matrix products, product(): lax.dot_general(piece, w[k * d_rows:(k + 1) * d_rows], (((1,), (1,)), (()...  62.3 us
    ppermute x4, waiting for transfers between devices, per_device(): grad_from_other = lax.ppermute(grad_for_other, 'core', swap)  42.6 us
    dot_general x4, matrix products, per_device(): lax.dot_general(ctx_own, piece_q, dims_wgrad, preferred_element_type=jnp....  33.4 us
    unnamed x129, local copies, waits for them, and re-layouts  28.7 us
  transfers between devices with their start and end apart: 35, of which 22 were waited for; matrix products, arithmetic and copies ran while one was open for 33% of the time, Pallas kernels for 0%

profile of v8, /device:TPU:0, one launch (start us, length us, event | category | flops | bytes accessed | tf_op | source)
XLA Modules:
  0.0 861.7 jit_solution(6236851447530516566)
XLA Ops:
  7.2 4.1 convert_element_type.412
  11.3 8.8 %copy.14 = bf16[512,6144]{0,1:T(8,128)(2,1)} copy(bf16[512,6144]{1,0:T(8,128)(2,1)} %param.7) | data formatting | bytes 12582912 | tf_op args[0]
  20.1 4.2 broadcast_select_fusion
  24.3 2.2 slice-done.4
  26.5 5.3 convolution_convert_fusion.3
  32.7 14.0 %collective-permute-done = bf16[3072,1536]{1,0:T(8,128)(2,1)} collective-permute-done((bf16[3072,1536]{1,0:T(8,128)(2,1)S(1)}, bf16[3072,1536]{1,0:T(8,128)(2,1)}, u32[]{:S(2)}, u32[]{:S(2)}) %collective-permute-start) | collective-permute-done | bytes 9437216 | tf_op jit(solution)/shard_map/ppermute | solution.py:47
  46.7 9.9 %add_convert_fusion.3 = bf16[3072,1536]{1,0:T(8,128)(2,1)} fusion(bf16[3072,1536]{1,0:T(8,128)(2,1)} %collective-permute-done, bf16[512,3072]{0,1:T(8,128)(2,1)S(1)} %bitcast.104, bf16[512,6144]{1,0:T(8,128)(2,1)S(1)} %bitcast.103), kind=kOutput, calls=%fused_computation.15 | convolution fusion | flops 4845993984 | bytes 23592960 | tf_op jit(solution)/shard_map/dot_general | solution.py:48
  56.6 5.2 convolution_convert_fusion.2
  62.3 14.3 %collective-permute-done.1 = bf16[3072,1536]{1,0:T(8,128)(2,1)S(1)} collective-permute-done((bf16[3072,1536]{1,0:T(8,128)(2,1)S(1)}, bf16[3072,1536]{1,0:T(8,128)(2,1)S(1)}, u32[]{:S(2)}, u32[]{:S(2)}) %collective-permute-start.1) | collective-permute-done | bytes 9437216 | tf_op jit(solution)/shard_map/ppermute | solution.py:47
  76.6 7.5 add_convert_fusion.2
  84.1 5.2 convolution_convert_fusion.1
  89.8 14.3 %collective-permute-done.10 = bf16[3072,1536]{1,0:T(8,128)(2,1)S(1)} collective-permute-done((bf16[3072,1536]{1,0:T(8,128)(2,1)S(1)}, bf16[3072,1536]{1,0:T(8,128)(2,1)S(1)}, u32[]{:S(2)}, u32[]{:S(2)}) %collective-permute-start.10) | collective-permute-done | bytes 9437216 | tf_op jit(solution)/shard_map/ppermute | solution.py:47
  104.1 7.8 add_convert_fusion.1
  111.9 7.4 convolution_convert_fusion
  163.8 7.5 constant_dynamic-slice_fusion.5
  171.2 6.9 constant_dynamic-slice_fusion.4
  179.3 2.8 collective-permute-start.2
  182.0 3.3 constant_dynamic-slice_fusion.1
  185.4 8.2 add_convert_fusion
  193.6 3.2 constant_dynamic-slice_fusion
  198.7 26.7 %collective-permute-done.2 = bf16[192,3072]{1,0:T(8,128)(2,1)} collective-permute-done((bf16[192,3072]{1,0:T(8,128)(2,1)}, bf16[192,3072]{1,0:T(8,128)(2,1)}, u32[]{:S(2)}, u32[]{:S(2)}) %collective-permute-start.2) | collective-permute-done | bytes 1179680 | tf_op jit(solution)/shard_map/ppermute | solution.py:87
  227.0 17.9 %collective-permute-start.3 = (bf16[192,3072]{1,0:T(8,128)(2,1)S(1)}, bf16[192,3072]{1,0:T(8,128)(2,1)S(1)}, u32[]{:S(2)}, u32[]{:S(2)}) collective-permute-start(bf16[192,3072]{1,0:T(8,128)(2,1)S(1)} %add_convert_fusion.33), channel_id=1, source_target_pairs={{0,8},{8,16},{16,24},{24,26},{26,18},{18,10},{10,2},{2,6},{6,14},{... | collective-permute-start | bytes 3538952 | tf_op jit(solution)/shard_map/ppermute | solution.py:87
  244.9 22.0 %collective-permute-done.12 = bf16[192,3072]{1,0:T(8,128)(2,1)S(1)} collective-permute-done((bf16[192,3072]{1,0:T(8,128)(2,1)S(1)}, bf16[192,3072]{1,0:T(8,128)(2,1)S(1)}, u32[]{:S(2)}, u32[]{:S(2)}) %collective-permute-start.12) | collective-permute-done | bytes 1179680 | tf_op jit(solution)/shard_map/ppermute | solution.py:88
  267.4 28.8 %collective-permute-done.3 = bf16[192,3072]{1,0:T(8,128)(2,1)S(1)} collective-permute-done((bf16[192,3072]{1,0:T(8,128)(2,1)S(1)}, bf16[192,3072]{1,0:T(8,128)(2,1)S(1)}, u32[]{:S(2)}, u32[]{:S(2)}) %collective-permute-start.3) | collective-permute-done | bytes 1179680 | tf_op jit(solution)/shard_map/ppermute | solution.py:87
  296.5 28.0 %collective-permute-start.4 = (bf16[192,3072]{1,0:T(8,128)(2,1)S(1)}, bf16[192,3072]{1,0:T(8,128)(2,1)S(1)}, u32[]{:S(2)}, u32[]{:S(2)}) collective-permute-start(bf16[192,3072]{1,0:T(8,128)(2,1)S(1)} %add_convert_fusion.32), channel_id=1, source_target_pairs={{0,8},{8,16},{16,24},{24,26},{26,18},{18,10},{10,2},{2,6},{6,14},{... | collective-permute-start | bytes 3538952 | tf_op jit(solution)/shard_map/ppermute | solution.py:87
  324.6 28.8 %collective-permute-done.13 = bf16[192,3072]{1,0:T(8,128)(2,1)S(1)} collective-permute-done((bf16[192,3072]{1,0:T(8,128)(2,1)S(1)}, bf16[192,3072]{1,0:T(8,128)(2,1)S(1)}, u32[]{:S(2)}, u32[]{:S(2)}) %collective-permute-start.13) | collective-permute-done | bytes 1179680 | tf_op jit(solution)/shard_map/ppermute | solution.py:88
  353.8 25.6 %collective-permute-done.4 = bf16[192,3072]{1,0:T(8,128)(2,1)S(1)} collective-permute-done((bf16[192,3072]{1,0:T(8,128)(2,1)S(1)}, bf16[192,3072]{1,0:T(8,128)(2,1)S(1)}, u32[]{:S(2)}, u32[]{:S(2)}) %collective-permute-start.4) | collective-permute-done | bytes 1179680 | tf_op jit(solution)/shard_map/ppermute | solution.py:87
  379.8 25.0 %collective-permute-start.5 = (bf16[192,3072]{1,0:T(8,128)(2,1)S(1)}, bf16[192,3072]{1,0:T(8,128)(2,1)S(1)}, u32[]{:S(2)}, u32[]{:S(2)}) collective-permute-start(bf16[192,3072]{1,0:T(8,128)(2,1)S(1)} %add_convert_fusion.31), channel_id=1, source_target_pairs={{0,8},{8,16},{16,24},{24,26},{26,18},{18,10},{10,2},{2,6},{6,14},{... | collective-permute-start | bytes 3538952 | tf_op jit(solution)/shard_map/ppermute | solution.py:87
  404.8 31.2 %collective-permute-done.14 = bf16[192,3072]{1,0:T(8,128)(2,1)S(1)} collective-permute-done((bf16[192,3072]{1,0:T(8,128)(2,1)S(1)}, bf16[192,3072]{1,0:T(8,128)(2,1)S(1)}, u32[]{:S(2)}, u32[]{:S(2)}) %collective-permute-start.14) | collective-permute-done | bytes 1179680 | tf_op jit(solution)/shard_map/ppermute | solution.py:88
  436.4 18.6 %collective-permute-done.5 = bf16[192,3072]{1,0:T(8,128)(2,1)S(1)} collective-permute-done((bf16[192,3072]{1,0:T(8,128)(2,1)S(1)}, bf16[192,3072]{1,0:T(8,128)(2,1)S(1)}, u32[]{:S(2)}, u32[]{:S(2)}) %collective-permute-start.5) | collective-permute-done | bytes 1179680 | tf_op jit(solution)/shard_map/ppermute | solution.py:87
  455.4 28.2 %collective-permute-start.6 = (bf16[192,3072]{1,0:T(8,128)(2,1)S(1)}, bf16[192,3072]{1,0:T(8,128)(2,1)S(1)}, u32[]{:S(2)}, u32[]{:S(2)}) collective-permute-start(bf16[192,3072]{1,0:T(8,128)(2,1)S(1)} %add_convert_fusion.30), channel_id=1, source_target_pairs={{0,8},{8,16},{16,24},{24,26},{26,18},{18,10},{10,2},{2,6},{6,14},{... | collective-permute-start | bytes 3538952 | tf_op jit(solution)/shard_map/ppermute | solution.py:87
  483.7 20.7 %collective-permute-done.15 = bf16[192,3072]{1,0:T(8,128)(2,1)S(1)} collective-permute-done((bf16[192,3072]{1,0:T(8,128)(2,1)S(1)}, bf16[192,3072]{1,0:T(8,128)(2,1)S(1)}, u32[]{:S(2)}, u32[]{:S(2)}) %collective-permute-start.15) | collective-permute-done | bytes 1179680 | tf_op jit(solution)/shard_map/ppermute | solution.py:88
  504.8 13.1 %collective-permute-done.6 = bf16[192,3072]{1,0:T(8,128)(2,1)S(1)} collective-permute-done((bf16[192,3072]{1,0:T(8,128)(2,1)S(1)}, bf16[192,3072]{1,0:T(8,128)(2,1)S(1)}, u32[]{:S(2)}, u32[]{:S(2)}) %collective-permute-start.6) | collective-permute-done | bytes 1179680 | tf_op jit(solution)/shard_map/ppermute | solution.py:87
  518.3 2.5 collective-permute-start.7
  520.8 10.9 %collective-permute-done.16 = bf16[192,3072]{1,0:T(8,128)(2,1)S(1)} collective-permute-done((bf16[192,3072]{1,0:T(8,128)(2,1)S(1)}, bf16[192,3072]{1,0:T(8,128)(2,1)S(1)}, u32[]{:S(2)}, u32[]{:S(2)}) %collective-permute-start.16) | collective-permute-done | bytes 1179680 | tf_op jit(solution)/shard_map/ppermute | solution.py:88
  532.5 14.3 %collective-permute-done.7 = bf16[192,3072]{1,0:T(8,128)(2,1)S(1)} collective-permute-done((bf16[192,3072]{1,0:T(8,128)(2,1)S(1)}, bf16[192,3072]{1,0:T(8,128)(2,1)S(1)}, u32[]{:S(2)}, u32[]{:S(2)}) %collective-permute-start.7) | collective-permute-done | bytes 1179680 | tf_op jit(solution)/shard_map/ppermute | solution.py:87
  547.2 11.0 %collective-permute-done.17 = bf16[192,3072]{1,0:T(8,128)(2,1)S(1)} collective-permute-done((bf16[192,3072]{1,0:T(8,128)(2,1)S(1)}, bf16[192,3072]{1,0:T(8,128)(2,1)S(1)}, u32[]{:S(2)}, u32[]{:S(2)}) %collective-permute-start.17) | collective-permute-done | bytes 1179680 | tf_op jit(solution)/shard_map/ppermute | solution.py:88
  559.2 14.5 %collective-permute-done.8 = bf16[192,3072]{1,0:T(8,128)(2,1)S(1)} collective-permute-done((bf16[192,3072]{1,0:T(8,128)(2,1)S(1)}, bf16[192,3072]{1,0:T(8,128)(2,1)S(1)}, u32[]{:S(2)}, u32[]{:S(2)}) %collective-permute-start.8) | collective-permute-done | bytes 1179680 | tf_op jit(solution)/shard_map/ppermute | solution.py:87
  574.4 12.2 %collective-permute-done.18 = bf16[192,3072]{1,0:T(8,128)(2,1)S(1)} collective-permute-done((bf16[192,3072]{1,0:T(8,128)(2,1)S(1)}, bf16[192,3072]{1,0:T(8,128)(2,1)S(1)}, u32[]{:S(2)}, u32[]{:S(2)}) %collective-permute-start.18) | collective-permute-done | bytes 1179680 | tf_op jit(solution)/shard_map/ppermute | solution.py:88
  587.1 12.7 %collective-permute-done.9 = bf16[192,3072]{1,0:T(8,128)(2,1)S(1)} collective-permute-done((bf16[192,3072]{1,0:T(8,128)(2,1)S(1)}, bf16[192,3072]{1,0:T(8,128)(2,1)S(1)}, u32[]{:S(2)}, u32[]{:S(2)}) %collective-permute-start.9) | collective-permute-done | bytes 1179680 | tf_op jit(solution)/shard_map/ppermute | solution.py:87
  601.2 11.8 %collective-permute-done.19 = bf16[192,3072]{1,0:T(8,128)(2,1)S(1)} collective-permute-done((bf16[192,3072]{1,0:T(8,128)(2,1)S(1)}, bf16[192,3072]{1,0:T(8,128)(2,1)S(1)}, u32[]{:S(2)}, u32[]{:S(2)}) %collective-permute-start.19) | collective-permute-done | bytes 1179680 | tf_op jit(solution)/shard_map/ppermute | solution.py:88
  614.3 20.8 %fusion.39 = bf16[512,2048]{0,1:T(8,128)(2,1)} fusion(bf16[512,6144]{1,0:T(8,128)(2,1)} %param.7, bf16[6144,6144]{1,0:T(8,128)(2,1)} %all-gather.2.cloned.1.call-done), kind=kOutput, calls=%fused_computation.39 | convolution fusion | flops 12885950464 | bytes 33554432 | tf_op jit(solution)/shard_map/dot_general | solution.py:73
  635.4 1.9 collective-permute-start.20
  637.3 20.8 %fusion.36 = bf16[512,2048]{0,1:T(8,128)(2,1)} fusion(bf16[512,6144]{1,0:T(8,128)(2,1)} %param.7, bf16[6144,6144]{1,0:T(8,128)(2,1)} %all-gather.2.cloned.1.call-done), kind=kOutput, calls=%fused_computation.38 | convolution fusion | flops 12885950464 | bytes 33554432 | tf_op jit(solution)/shard_map/dot_general | solution.py:73
  658.1 2.2 collective-permute-done.21
  660.3 3.0 add_convert_fusion.16
  663.3 2.6 add_convert_fusion.17
  668.2 20.8 %fusion.33 = bf16[512,2048]{0,1:T(8,128)(2,1)} fusion(bf16[512,6144]{1,0:T(8,128)(2,1)} %param.7, bf16[6144,6144]{1,0:T(8,128)(2,1)} %all-gather.2.cloned.1.call-done), kind=kOutput, calls=%fused_computation.37 | convolution fusion | flops 12885950464 | bytes 33554432 | tf_op jit(solution)/shard_map/dot_general | solution.py:73
  690.2 2.6 add_convert_fusion.14
  697.0 20.7 %fusion.48 = bf16[512,2048]{0,1:T(8,128)(2,1)} fusion(bf16[512,6144]{1,0:T(8,128)(2,1)} %param.11, bf16[6144,6144]{1,0:T(8,128)(2,1)} %all-gather.2.cloned.1.call-done), kind=kOutput, calls=%fused_computation.42 | convolution fusion | flops 12885950464 | bytes 33554432 | tf_op jit(solution)/shard_map/dot_general | solution.py:77
  717.9 2.7 add_convert_fusion.12
  724.5 20.7 %fusion.45 = bf16[512,2048]{0,1:T(8,128)(2,1)} fusion(bf16[512,6144]{1,0:T(8,128)(2,1)} %param.11, bf16[6144,6144]{1,0:T(8,128)(2,1)} %all-gather.2.cloned.1.call-done), kind=kOutput, calls=%fused_computation.41 | convolution fusion | flops 12885950464 | bytes 33554432 | tf_op jit(solution)/shard_map/dot_general | solution.py:77
  745.2 2.7 add_convert_fusion.10
  751.6 20.8 %fusion.42 = bf16[512,2048]{0,1:T(8,128)(2,1)} fusion(bf16[512,6144]{1,0:T(8,128)(2,1)} %param.11, bf16[6144,6144]{1,0:T(8,128)(2,1)} %all-gather.2.cloned.1.call-done), kind=kOutput, calls=%fused_computation.40 | convolution fusion | flops 12885950464 | bytes 33554432 | tf_op jit(solution)/shard_map/dot_general | solution.py:77
  772.5 2.8 add_convert_fusion.8
  775.3 2.8 add_convert_fusion.9
  780.4 17.6 %pad_maximum_fusion = bf16[512,6144]{0,1:T(8,128)(2,1)} fusion(bf16[512,2048]{0,1:T(8,128)(2,1)S(1)} %copy-done.52, bf16[512,2048]{0,1:T(8,128)(2,1)S(1)} %copy-done.50, bf16[512,2048]{0,1:T(8,128)(2,1)S(1)} %copy-done.49), kind=kLoop, calls=%fused_computation.23 | loop fusion | flops 18874368 | bytes 12582912 | tf_op jit(solution)/shard_map/concatenate | solution.py:102
  798.0 8.8 %copy.15 = bf16[512,6144]{1,0:T(8,128)(2,1)} copy(bf16[512,6144]{0,1:T(8,128)(2,1)} %pad_maximum_fusion) | data formatting | bytes 12582912
  806.8 2.8 add_convert_fusion.7
  810.3 2.6 add_convert_fusion.5
  814.5 17.6 %pad_maximum_fusion.1 = bf16[512,6144]{0,1:T(8,128)(2,1)} fusion(bf16[512,2048]{0,1:T(8,128)(2,1)S(1)} %copy-done.54, bf16[512,2048]{0,1:T(8,128)(2,1)S(1)} %copy-done.53, bf16[512,2048]{0,1:T(8,128)(2,1)S(1)} %copy-done.51), kind=kLoop, calls=%fused_computation.24 | loop fusion | flops 18874368 | bytes 12582912 | tf_op jit(solution)/shard_map/concatenate | solution.py:104
  832.2 8.7 %copy.16 = bf16[512,6144]{1,0:T(8,128)(2,1)} copy(bf16[512,6144]{0,1:T(8,128)(2,1)} %pad_maximum_fusion.1) | data formatting | bytes 12582912
  840.9 1.7 add_convert_fusion.6
  844.2 10.1 %multiply_subtract_fusion = (f32[192,6144]{1,0:T(8,128)}, f32[192,6144]{1,0:T(8,128)}, f32[192,6144]{1,0:T(8,128)}) fusion(f32[192,6144]{1,0:T(8,128)} %param.8, bf16[192,3072]{1,0:T(8,128)(2,1)S(1)} %add_convert_fusion.4, bf16[192,3072]{1,0:T(8,128)(2,1)S(1)} %add_convert_fusion.6, f32[192,6144]{1,0:T(8,128)} %param.9, f32[192,6144]{1,0:T(8,128)} %param.10), kind=kLoop, calls=%fused_computation.28 | loop fusion | flops 23592960 | bytes 30670848 | tf_op jit(solution)/shard_map/sub | solution.py:115
  (197 shorter events, 39.7 us)
Async XLA Ops:
  7.2 607.1 %all-gather.2.cloned.1.call-start = ((), (), s32[]{:S(2)}) async-start(), calls=%async_computation | async-start | bytes 77856768 | tf_op jit(solution)/shard_map/all_gather | solution.py:37
  24.3 79.8 %copy-start = (bf16[512,16,1,192]{0,3,2,1:T(8,128)(2,1)}, bf16[512,16,1,192]{0,3,2,1:T(8,128)(2,1)S(1)}, u32[]{:S(2)}) copy-start(bf16[512,16,1,192]{0,3,2,1:T(8,128)(2,1)S(1)} %get-tuple-element.140) | copy-start | bytes 9437188
  31.8 14.9 %collective-permute-start = (bf16[3072,1536]{1,0:T(8,128)(2,1)S(1)}, bf16[3072,1536]{1,0:T(8,128)(2,1)}, u32[]{:S(2)}, u32[]{:S(2)}) collective-permute-start(bf16[3072,1536]{1,0:T(8,128)(2,1)S(1)} %convolution_convert_fusion.3), channel_id=1, source_target_pairs={{0,1},{1,0},{2,3},{3,2},{4,5},{5,4},{6,7},{7,6},{8,9},{9,8},{10,11... | collective-permute-start | bytes 28311560 | tf_op jit(solution)/shard_map/ppermute | solution.py:47
  32.7 79.2 %copy-start.55 = (bf16[512,1536]{1,0:T(8,128)(2,1)}, bf16[512,1536]{1,0:T(8,128)(2,1)S(1)}, u32[]{:S(2)}) copy-start(bf16[512,1536]{1,0:T(8,128)(2,1)S(1)} %get-tuple-element.34) | copy-start | bytes 4718596
  61.9 14.7 %collective-permute-start.1 = (bf16[3072,1536]{1,0:T(8,128)(2,1)S(1)}, bf16[3072,1536]{1,0:T(8,128)(2,1)S(1)}, u32[]{:S(2)}, u32[]{:S(2)}) collective-permute-start(bf16[3072,1536]{1,0:T(8,128)(2,1)S(1)} %convolution_convert_fusion.2), channel_id=1, source_target_pairs={{0,1},{1,0},{2,3},{3,2},{4,5},{5,4},{6,7},{7,6},{8,9},{9,8},{10,11... | collective-permute-start | bytes 28311560 | tf_op jit(solution)/shard_map/ppermute | solution.py:47
  89.3 14.7 %collective-permute-start.10 = (bf16[3072,1536]{1,0:T(8,128)(2,1)S(1)}, bf16[3072,1536]{1,0:T(8,128)(2,1)S(1)}, u32[]{:S(2)}, u32[]{:S(2)}) collective-permute-start(bf16[3072,1536]{1,0:T(8,128)(2,1)S(1)} %convolution_convert_fusion.1), channel_id=1, source_target_pairs={{0,1},{1,0},{2,3},{3,2},{4,5},{5,4},{6,7},{7,6},{8,9},{9,8},{10,11... | collective-permute-start | bytes 28311560 | tf_op jit(solution)/shard_map/ppermute | solution.py:47
  119.2 66.1 %collective-permute-start.11 = (bf16[3072,1536]{1,0:T(8,128)(2,1)}, bf16[3072,1536]{1,0:T(8,128)(2,1)}, u32[]{:S(2)}, u32[]{:S(2)}) collective-permute-start(bf16[3072,1536]{1,0:T(8,128)(2,1)} %convolution_convert_fusion), channel_id=1, source_target_pairs={{0,1},{1,0},{2,3},{3,2},{4,5},{5,4},{6,7},{7,6},{8,9},{9,8},{10,11... | collective-permute-start | bytes 28311560 | tf_op jit(solution)/shard_map/ppermute | solution.py:47
  179.3 46.1 %collective-permute-start.2 = (bf16[192,3072]{1,0:T(8,128)(2,1)}, bf16[192,3072]{1,0:T(8,128)(2,1)}, u32[]{:S(2)}, u32[]{:S(2)}) collective-permute-start(bf16[192,3072]{1,0:T(8,128)(2,1)} %pad_maximum_fusion.3), channel_id=1, source_target_pairs={{0,8},{8,16},{16,24},{24,26},{26,18},{18,10},{10,2},{2,6},{6,14},{... | collective-permute-start | bytes 3538952 | tf_op jit(solution)/shard_map/ppermute | solution.py:87
  196.8 28.6 %copy-start.40 = (bf16[192,1536]{1,0:T(8,128)(2,1)S(1)}, bf16[192,1536]{1,0:T(8,128)(2,1)}, u32[]{:S(2)}) copy-start(bf16[192,1536]{1,0:T(8,128)(2,1)} %get-tuple-element.86) | copy-start | bytes 1769476
  196.8 28.6 %copy-start.43 = (bf16[192,1536]{1,0:T(8,128)(2,1)S(1)}, bf16[192,1536]{1,0:T(8,128)(2,1)}, u32[]{:S(2)}) copy-start(bf16[192,1536]{1,0:T(8,128)(2,1)} %get-tuple-element.102) | copy-start | bytes 1769476
  198.2 68.7 %copy-start.46 = (bf16[192,1536]{1,0:T(8,128)(2,1)S(1)}, bf16[192,1536]{1,0:T(8,128)(2,1)}, u32[]{:S(2)}) copy-start(bf16[192,1536]{1,0:T(8,128)(2,1)} %get-tuple-element.118) | copy-start | bytes 1769476
  198.2 68.7 %copy-start.48 = (bf16[192,1536]{1,0:T(8,128)(2,1)S(1)}, bf16[192,1536]{1,0:T(8,128)(2,1)}, u32[]{:S(2)}) copy-start(bf16[192,1536]{1,0:T(8,128)(2,1)} %get-tuple-element.134) | copy-start | bytes 1769476
  198.3 68.7 %collective-permute-start.12 = (bf16[192,3072]{1,0:T(8,128)(2,1)S(1)}, bf16[192,3072]{1,0:T(8,128)(2,1)S(1)}, u32[]{:S(2)}, u32[]{:S(2)}) collective-permute-start(bf16[192,3072]{1,0:T(8,128)(2,1)S(1)} %pad_maximum_fusion.4), channel_id=1, source_target_pairs={{8,0},{16,8},{24,16},{26,24},{18,26},{10,18},{2,10},{6,2},{14,6},{... | collective-permute-start | bytes 3538952 | tf_op jit(solution)/shard_map/ppermute | solution.py:88
  227.0 69.2 %copy-start.36 = (bf16[192,1536]{1,0:T(8,128)(2,1)S(1)}, bf16[192,1536]{1,0:T(8,128)(2,1)}, u32[]{:S(2)}) copy-start(bf16[192,1536]{1,0:T(8,128)(2,1)} %get-tuple-element.85) | copy-start | bytes 1769476
  227.0 69.2 %copy-start.39 = (bf16[192,1536]{1,0:T(8,128)(2,1)S(1)}, bf16[192,1536]{1,0:T(8,128)(2,1)}, u32[]{:S(2)}) copy-start(bf16[192,1536]{1,0:T(8,128)(2,1)} %get-tuple-element.101) | copy-start | bytes 1769476
  227.0 69.2 %collective-permute-start.3 = (bf16[192,3072]{1,0:T(8,128)(2,1)S(1)}, bf16[192,3072]{1,0:T(8,128)(2,1)S(1)}, u32[]{:S(2)}, u32[]{:S(2)}) collective-permute-start(bf16[192,3072]{1,0:T(8,128)(2,1)S(1)} %add_convert_fusion.33), channel_id=1, source_target_pairs={{0,8},{8,16},{16,24},{24,26},{26,18},{18,10},{10,2},{2,6},{6,14},{... | collective-permute-start | bytes 3538952 | tf_op jit(solution)/shard_map/ppermute | solution.py:87
  267.3 86.1 %copy-start.44 = (bf16[192,1536]{1,0:T(8,128)(2,1)S(1)}, bf16[192,1536]{1,0:T(8,128)(2,1)}, u32[]{:S(2)}) copy-start(bf16[192,1536]{1,0:T(8,128)(2,1)} %get-tuple-element.117) | copy-start | bytes 1769476
  267.3 86.1 %copy-start.47 = (bf16[192,1536]{1,0:T(8,128)(2,1)S(1)}, bf16[192,1536]{1,0:T(8,128)(2,1)}, u32[]{:S(2)}) copy-start(bf16[192,1536]{1,0:T(8,128)(2,1)} %get-tuple-element.133) | copy-start | bytes 1769476
  267.3 86.1 %collective-permute-start.13 = (bf16[192,3072]{1,0:T(8,128)(2,1)S(1)}, bf16[192,3072]{1,0:T(8,128)(2,1)S(1)}, u32[]{:S(2)}, u32[]{:S(2)}) collective-permute-start(bf16[192,3072]{1,0:T(8,128)(2,1)S(1)} %add_convert_fusion.25), channel_id=1, source_target_pairs={{8,0},{16,8},{24,16},{26,24},{18,26},{10,18},{2,10},{6,2},{14,6},{... | collective-permute-start | bytes 3538952 | tf_op jit(solution)/shard_map/ppermute | solution.py:88
  296.5 82.9 %copy-start.33 = (bf16[192,1536]{1,0:T(8,128)(2,1)S(1)}, bf16[192,1536]{1,0:T(8,128)(2,1)}, u32[]{:S(2)}) copy-start(bf16[192,1536]{1,0:T(8,128)(2,1)} %get-tuple-element.84) | copy-start | bytes 1769476
  296.5 82.9 %copy-start.35 = (bf16[192,1536]{1,0:T(8,128)(2,1)S(1)}, bf16[192,1536]{1,0:T(8,128)(2,1)}, u32[]{:S(2)}) copy-start(bf16[192,1536]{1,0:T(8,128)(2,1)} %get-tuple-element.100) | copy-start | bytes 1769476
  296.5 82.9 %collective-permute-start.4 = (bf16[192,3072]{1,0:T(8,128)(2,1)S(1)}, bf16[192,3072]{1,0:T(8,128)(2,1)S(1)}, u32[]{:S(2)}, u32[]{:S(2)}) collective-permute-start(bf16[192,3072]{1,0:T(8,128)(2,1)S(1)} %add_convert_fusion.32), channel_id=1, source_target_pairs={{0,8},{8,16},{16,24},{24,26},{26,18},{18,10},{10,2},{2,6},{6,14},{... | collective-permute-start | bytes 3538952 | tf_op jit(solution)/shard_map/ppermute | solution.py:87
  353.7 82.2 %copy-start.41 = (bf16[192,1536]{1,0:T(8,128)(2,1)S(1)}, bf16[192,1536]{1,0:T(8,128)(2,1)}, u32[]{:S(2)}) copy-start(bf16[192,1536]{1,0:T(8,128)(2,1)} %get-tuple-element.116) | copy-start | bytes 1769476
  353.7 82.2 %copy-start.45 = (bf16[192,1536]{1,0:T(8,128)(2,1)S(1)}, bf16[192,1536]{1,0:T(8,128)(2,1)}, u32[]{:S(2)}) copy-start(bf16[192,1536]{1,0:T(8,128)(2,1)} %get-tuple-element.132) | copy-start | bytes 1769476
  353.8 82.2 %collective-permute-start.14 = (bf16[192,3072]{1,0:T(8,128)(2,1)S(1)}, bf16[192,3072]{1,0:T(8,128)(2,1)S(1)}, u32[]{:S(2)}, u32[]{:S(2)}) collective-permute-start(bf16[192,3072]{1,0:T(8,128)(2,1)S(1)} %add_convert_fusion.24), channel_id=1, source_target_pairs={{8,0},{16,8},{24,16},{26,24},{18,26},{10,18},{2,10},{6,2},{14,6},{... | collective-permute-start | bytes 3538952 | tf_op jit(solution)/shard_map/ppermute | solution.py:88
  379.8 75.3 %copy-start.30 = (bf16[192,1536]{1,0:T(8,128)(2,1)S(1)}, bf16[192,1536]{1,0:T(8,128)(2,1)}, u32[]{:S(2)}) copy-start(bf16[192,1536]{1,0:T(8,128)(2,1)} %get-tuple-element.83) | copy-start | bytes 1769476
  379.8 75.3 %copy-start.32 = (bf16[192,1536]{1,0:T(8,128)(2,1)S(1)}, bf16[192,1536]{1,0:T(8,128)(2,1)}, u32[]{:S(2)}) copy-start(bf16[192,1536]{1,0:T(8,128)(2,1)} %get-tuple-element.99) | copy-start | bytes 1769476
  379.8 75.3 %collective-permute-start.5 = (bf16[192,3072]{1,0:T(8,128)(2,1)S(1)}, bf16[192,3072]{1,0:T(8,128)(2,1)S(1)}, u32[]{:S(2)}, u32[]{:S(2)}) collective-permute-start(bf16[192,3072]{1,0:T(8,128)(2,1)S(1)} %add_convert_fusion.31), channel_id=1, source_target_pairs={{0,8},{8,16},{16,24},{24,26},{26,18},{18,10},{10,2},{2,6},{6,14},{... | collective-permute-start | bytes 3538952 | tf_op jit(solution)/shard_map/ppermute | solution.py:87
  436.3 68.0 %copy-start.37 = (bf16[192,1536]{1,0:T(8,128)(2,1)S(1)}, bf16[192,1536]{1,0:T(8,128)(2,1)}, u32[]{:S(2)}) copy-start(bf16[192,1536]{1,0:T(8,128)(2,1)} %get-tuple-element.115) | copy-start | bytes 1769476
  436.3 68.0 %copy-start.42 = (bf16[192,1536]{1,0:T(8,128)(2,1)S(1)}, bf16[192,1536]{1,0:T(8,128)(2,1)}, u32[]{:S(2)}) copy-start(bf16[192,1536]{1,0:T(8,128)(2,1)} %get-tuple-element.131) | copy-start | bytes 1769476
  436.4 68.0 %collective-permute-start.15 = (bf16[192,3072]{1,0:T(8,128)(2,1)S(1)}, bf16[192,3072]{1,0:T(8,128)(2,1)S(1)}, u32[]{:S(2)}, u32[]{:S(2)}) collective-permute-start(bf16[192,3072]{1,0:T(8,128)(2,1)S(1)} %add_convert_fusion.23), channel_id=1, source_target_pairs={{8,0},{16,8},{24,16},{26,24},{18,26},{10,18},{2,10},{6,2},{14,6},{... | collective-permute-start | bytes 3538952 | tf_op jit(solution)/shard_map/ppermute | solution.py:88
  455.4 62.5 %copy-start.27 = (bf16[192,1536]{1,0:T(8,128)(2,1)S(1)}, bf16[192,1536]{1,0:T(8,128)(2,1)}, u32[]{:S(2)}) copy-start(bf16[192,1536]{1,0:T(8,128)(2,1)} %get-tuple-element.82) | copy-start | bytes 1769476
  455.4 62.5 %copy-start.29 = (bf16[192,1536]{1,0:T(8,128)(2,1)S(1)}, bf16[192,1536]{1,0:T(8,128)(2,1)}, u32[]{:S(2)}) copy-start(bf16[192,1536]{1,0:T(8,128)(2,1)} %get-tuple-element.98) | copy-start | bytes 1769476
  455.4 62.5 %collective-permute-start.6 = (bf16[192,3072]{1,0:T(8,128)(2,1)S(1)}, bf16[192,3072]{1,0:T(8,128)(2,1)S(1)}, u32[]{:S(2)}, u32[]{:S(2)}) collective-permute-start(bf16[192,3072]{1,0:T(8,128)(2,1)S(1)} %add_convert_fusion.30), channel_id=1, source_target_pairs={{0,8},{8,16},{16,24},{24,26},{26,18},{18,10},{10,2},{2,6},{6,14},{... | collective-permute-start | bytes 3538952 | tf_op jit(solution)/shard_map/ppermute | solution.py:87
  504.7 27.1 %copy-start.34 = (bf16[192,1536]{1,0:T(8,128)(2,1)S(1)}, bf16[192,1536]{1,0:T(8,128)(2,1)}, u32[]{:S(2)}) copy-start(bf16[192,1536]{1,0:T(8,128)(2,1)} %get-tuple-element.114) | copy-start | bytes 1769476
  504.7 27.1 %copy-start.38 = (bf16[192,1536]{1,0:T(8,128)(2,1)S(1)}, bf16[192,1536]{1,0:T(8,128)(2,1)}, u32[]{:S(2)}) copy-start(bf16[192,1536]{1,0:T(8,128)(2,1)} %get-tuple-element.130) | copy-start | bytes 1769476
  504.7 27.1 %collective-permute-start.16 = (bf16[192,3072]{1,0:T(8,128)(2,1)S(1)}, bf16[192,3072]{1,0:T(8,128)(2,1)S(1)}, u32[]{:S(2)}, u32[]{:S(2)}) collective-permute-start(bf16[192,3072]{1,0:T(8,128)(2,1)S(1)} %add_convert_fusion.22), channel_id=1, source_target_pairs={{8,0},{16,8},{24,16},{26,24},{18,26},{10,18},{2,10},{6,2},{14,6},{... | collective-permute-start | bytes 3538952 | tf_op jit(solution)/shard_map/ppermute | solution.py:88
  518.3 28.5 %copy-start.24 = (bf16[192,1536]{1,0:T(8,128)(2,1)S(1)}, bf16[192,1536]{1,0:T(8,128)(2,1)}, u32[]{:S(2)}) copy-start(bf16[192,1536]{1,0:T(8,128)(2,1)} %get-tuple-element.81) | copy-start | bytes 1769476
  518.3 28.5 %copy-start.26 = (bf16[192,1536]{1,0:T(8,128)(2,1)S(1)}, bf16[192,1536]{1,0:T(8,128)(2,1)}, u32[]{:S(2)}) copy-start(bf16[192,1536]{1,0:T(8,128)(2,1)} %get-tuple-element.97) | copy-start | bytes 1769476
  518.3 28.5 %collective-permute-start.7 = (bf16[192,3072]{1,0:T(8,128)(2,1)S(1)}, bf16[192,3072]{1,0:T(8,128)(2,1)S(1)}, u32[]{:S(2)}, u32[]{:S(2)}) collective-permute-start(bf16[192,3072]{1,0:T(8,128)(2,1)S(1)} %add_convert_fusion.29), channel_id=1, source_target_pairs={{0,8},{8,16},{16,24},{24,26},{26,18},{18,10},{10,2},{2,6},{6,14},{... | collective-permute-start | bytes 3538952 | tf_op jit(solution)/shard_map/ppermute | solution.py:87
  532.1 26.1 %copy-start.31 = (bf16[192,1536]{1,0:T(8,128)(2,1)S(1)}, bf16[192,1536]{1,0:T(8,128)(2,1)}, u32[]{:S(2)}) copy-start(bf16[192,1536]{1,0:T(8,128)(2,1)} %get-tuple-element.113) | copy-start | bytes 1769476
  532.1 26.1 %collective-permute-start.17 = (bf16[192,3072]{1,0:T(8,128)(2,1)S(1)}, bf16[192,3072]{1,0:T(8,128)(2,1)S(1)}, u32[]{:S(2)}, u32[]{:S(2)}) collective-permute-start(bf16[192,3072]{1,0:T(8,128)(2,1)S(1)} %add_convert_fusion.21), channel_id=1, source_target_pairs={{8,0},{16,8},{24,16},{26,24},{18,26},{10,18},{2,10},{6,2},{14,6},{... | collective-permute-start | bytes 3538952 | tf_op jit(solution)/shard_map/ppermute | solution.py:88
  547.1 26.6 %copy-start.21 = (bf16[192,1536]{1,0:T(8,128)(2,1)S(1)}, bf16[192,1536]{1,0:T(8,128)(2,1)}, u32[]{:S(2)}) copy-start(bf16[192,1536]{1,0:T(8,128)(2,1)} %get-tuple-element.80) | copy-start | bytes 1769476
  547.1 26.6 %copy-start.23 = (bf16[192,1536]{1,0:T(8,128)(2,1)S(1)}, bf16[192,1536]{1,0:T(8,128)(2,1)}, u32[]{:S(2)}) copy-start(bf16[192,1536]{1,0:T(8,128)(2,1)} %get-tuple-element.96) | copy-start | bytes 1769476
  547.1 26.6 %collective-permute-start.8 = (bf16[192,3072]{1,0:T(8,128)(2,1)S(1)}, bf16[192,3072]{1,0:T(8,128)(2,1)S(1)}, u32[]{:S(2)}, u32[]{:S(2)}) collective-permute-start(bf16[192,3072]{1,0:T(8,128)(2,1)S(1)} %add_convert_fusion.28), channel_id=1, source_target_pairs={{0,8},{8,16},{16,24},{24,26},{26,18},{18,10},{10,2},{2,6},{6,14},{... | collective-permute-start | bytes 3538952 | tf_op jit(solution)/shard_map/ppermute | solution.py:87
  558.6 28.1 %copy-start.28 = (bf16[192,1536]{1,0:T(8,128)(2,1)S(1)}, bf16[192,1536]{1,0:T(8,128)(2,1)}, u32[]{:S(2)}) copy-start(bf16[192,1536]{1,0:T(8,128)(2,1)} %get-tuple-element.112) | copy-start | bytes 1769476
  558.6 28.1 %collective-permute-start.18 = (bf16[192,3072]{1,0:T(8,128)(2,1)S(1)}, bf16[192,3072]{1,0:T(8,128)(2,1)S(1)}, u32[]{:S(2)}, u32[]{:S(2)}) collective-permute-start(bf16[192,3072]{1,0:T(8,128)(2,1)S(1)} %add_convert_fusion.20), channel_id=1, source_target_pairs={{8,0},{16,8},{24,16},{26,24},{18,26},{10,18},{2,10},{6,2},{14,6},{... | collective-permute-start | bytes 3538952 | tf_op jit(solution)/shard_map/ppermute | solution.py:88
  574.1 25.7 %collective-permute-start.9 = (bf16[192,3072]{1,0:T(8,128)(2,1)S(1)}, bf16[192,3072]{1,0:T(8,128)(2,1)S(1)}, u32[]{:S(2)}, u32[]{:S(2)}) collective-permute-start(bf16[192,3072]{1,0:T(8,128)(2,1)S(1)} %add_convert_fusion.27), channel_id=1, source_target_pairs={{0,8},{8,16},{16,24},{24,26},{26,18},{18,10},{10,2},{2,6},{6,14},{... | collective-permute-start | bytes 3538952 | tf_op jit(solution)/shard_map/ppermute | solution.py:87
  587.1 25.9 %collective-permute-start.19 = (bf16[192,3072]{1,0:T(8,128)(2,1)S(1)}, bf16[192,3072]{1,0:T(8,128)(2,1)S(1)}, u32[]{:S(2)}, u32[]{:S(2)}) collective-permute-start(bf16[192,3072]{1,0:T(8,128)(2,1)S(1)} %add_convert_fusion.19), channel_id=1, source_target_pairs={{8,0},{16,8},{24,16},{26,24},{18,26},{10,18},{2,10},{6,2},{14,6},{... | collective-permute-start | bytes 3538952 | tf_op jit(solution)/shard_map/ppermute | solution.py:88
  635.1 25.2 %collective-permute-start.21 = (bf16[192,3072]{1,0:T(8,128)(2,1)}, bf16[192,3072]{1,0:T(8,128)(2,1)}, u32[]{:S(2)}, u32[]{:S(2)}) collective-permute-start(bf16[192,3072]{1,0:T(8,128)(2,1)} %add_convert_fusion.18), channel_id=1, source_target_pairs={{8,0},{16,8},{24,16},{26,24},{18,26},{10,18},{2,10},{6,2},{14,6},{... | collective-permute-start | bytes 3538952 | tf_op jit(solution)/shard_map/ppermute | solution.py:88
  635.4 27.9 %collective-permute-start.20 = (bf16[192,3072]{1,0:T(8,128)(2,1)}, bf16[192,3072]{1,0:T(8,128)(2,1)}, u32[]{:S(2)}, u32[]{:S(2)}) collective-permute-start(bf16[192,3072]{1,0:T(8,128)(2,1)} %add_convert_fusion.26), channel_id=1, source_target_pairs={{0,8},{8,16},{16,24},{24,26},{26,18},{18,10},{10,2},{2,6},{6,14},{... | collective-permute-start | bytes 3538952 | tf_op jit(solution)/shard_map/ppermute | solution.py:87
  665.9 24.3 %collective-permute-start.23 = (bf16[192,3072]{1,0:T(8,128)(2,1)}, bf16[192,3072]{1,0:T(8,128)(2,1)}, u32[]{:S(2)}, u32[]{:S(2)}) collective-permute-start(bf16[192,3072]{1,0:T(8,128)(2,1)} %add_convert_fusion.16), channel_id=1, source_target_pairs={{8,0},{16,8},{24,16},{26,24},{18,26},{10,18},{2,10},{6,2},{14,6},{... | collective-permute-start | bytes 3538952 | tf_op jit(solution)/shard_map/ppermute | solution.py:88
  666.5 26.4 %collective-permute-start.22 = (bf16[192,3072]{1,0:T(8,128)(2,1)}, bf16[192,3072]{1,0:T(8,128)(2,1)}, u32[]{:S(2)}, u32[]{:S(2)}) collective-permute-start(bf16[192,3072]{1,0:T(8,128)(2,1)} %add_convert_fusion.17), channel_id=1, source_target_pairs={{0,8},{8,16},{16,24},{24,26},{26,18},{18,10},{10,2},{2,6},{6,14},{... | collective-permute-start | bytes 3538952 | tf_op jit(solution)/shard_map/ppermute | solution.py:87
  694.5 23.4 %collective-permute-start.25 = (bf16[192,3072]{1,0:T(8,128)(2,1)}, bf16[192,3072]{1,0:T(8,128)(2,1)}, u32[]{:S(2)}, u32[]{:S(2)}) collective-permute-start(bf16[192,3072]{1,0:T(8,128)(2,1)} %add_convert_fusion.14), channel_id=1, source_target_pairs={{8,0},{16,8},{24,16},{26,24},{18,26},{10,18},{2,10},{6,2},{14,6},{... | collective-permute-start | bytes 3538952 | tf_op jit(solution)/shard_map/ppermute | solution.py:88
  695.4 25.2 %collective-permute-start.24 = (bf16[192,3072]{1,0:T(8,128)(2,1)S(1)}, bf16[192,3072]{1,0:T(8,128)(2,1)}, u32[]{:S(2)}, u32[]{:S(2)}) collective-permute-start(bf16[192,3072]{1,0:T(8,128)(2,1)S(1)} %add_convert_fusion.15), channel_id=1, source_target_pairs={{0,8},{8,16},{16,24},{24,26},{26,18},{18,10},{10,2},{2,6},{6,14},{... | collective-permute-start | bytes 3538952 | tf_op jit(solution)/shard_map/ppermute | solution.py:87
  722.3 22.9 %collective-permute-start.27 = (bf16[192,3072]{1,0:T(8,128)(2,1)}, bf16[192,3072]{1,0:T(8,128)(2,1)}, u32[]{:S(2)}, u32[]{:S(2)}) collective-permute-start(bf16[192,3072]{1,0:T(8,128)(2,1)} %add_convert_fusion.12), channel_id=1, source_target_pairs={{8,0},{16,8},{24,16},{26,24},{18,26},{10,18},{2,10},{6,2},{14,6},{... | collective-permute-start | bytes 3538952 | tf_op jit(solution)/shard_map/ppermute | solution.py:88
  723.4 24.6 %collective-permute-start.26 = (bf16[192,3072]{1,0:T(8,128)(2,1)S(1)}, bf16[192,3072]{1,0:T(8,128)(2,1)S(1)}, u32[]{:S(2)}, u32[]{:S(2)}) collective-permute-start(bf16[192,3072]{1,0:T(8,128)(2,1)S(1)} %add_convert_fusion.13), channel_id=1, source_target_pairs={{0,8},{8,16},{16,24},{24,26},{26,18},{18,10},{10,2},{2,6},{6,14},{... | collective-permute-start | bytes 3538952 | tf_op jit(solution)/shard_map/ppermute | solution.py:87
  749.3 23.1 %collective-permute-start.29 = (bf16[192,3072]{1,0:T(8,128)(2,1)}, bf16[192,3072]{1,0:T(8,128)(2,1)}, u32[]{:S(2)}, u32[]{:S(2)}) collective-permute-start(bf16[192,3072]{1,0:T(8,128)(2,1)} %add_convert_fusion.10), channel_id=1, source_target_pairs={{8,0},{16,8},{24,16},{26,24},{18,26},{10,18},{2,10},{6,2},{14,6},{... | collective-permute-start | bytes 3538952 | tf_op jit(solution)/shard_map/ppermute | solution.py:88
  750.4 24.8 %collective-permute-start.28 = (bf16[192,3072]{1,0:T(8,128)(2,1)}, bf16[192,3072]{1,0:T(8,128)(2,1)}, u32[]{:S(2)}, u32[]{:S(2)}) collective-permute-start(bf16[192,3072]{1,0:T(8,128)(2,1)} %add_convert_fusion.11), channel_id=1, source_target_pairs={{0,8},{8,16},{16,24},{24,26},{26,18},{18,10},{10,2},{2,6},{6,14},{... | collective-permute-start | bytes 3538952 | tf_op jit(solution)/shard_map/ppermute | solution.py:87
  751.6 28.8 %copy-start.52 = (bf16[512,2048]{0,1:T(8,128)(2,1)S(1)}, bf16[512,2048]{0,1:T(8,128)(2,1)}, u32[]{:S(2)}) copy-start(bf16[512,2048]{0,1:T(8,128)(2,1)} %fusion.33) | copy-start | bytes 6291460
  778.1 28.7 %collective-permute-start.30 = (bf16[192,3072]{1,0:T(8,128)(2,1)}, bf16[192,3072]{1,0:T(8,128)(2,1)}, u32[]{:S(2)}, u32[]{:S(2)}) collective-permute-start(bf16[192,3072]{1,0:T(8,128)(2,1)} %add_convert_fusion.9), channel_id=1, source_target_pairs={{0,8},{8,16},{16,24},{24,26},{26,18},{18,10},{10,2},{2,6},{6,14},{... | collective-permute-start | bytes 3538952 | tf_op jit(solution)/shard_map/ppermute | solution.py:87
  778.9 31.5 %collective-permute-start.32 = (bf16[192,3072]{1,0:T(8,128)(2,1)}, bf16[192,3072]{1,0:T(8,128)(2,1)}, u32[]{:S(2)}, u32[]{:S(2)}) collective-permute-start(bf16[192,3072]{1,0:T(8,128)(2,1)} %add_convert_fusion.8), channel_id=1, source_target_pairs={{8,0},{16,8},{24,16},{26,24},{18,26},{10,18},{2,10},{6,2},{14,6},{... | collective-permute-start | bytes 3538952 | tf_op jit(solution)/shard_map/ppermute | solution.py:88
  809.6 31.3 %collective-permute-start.31 = (bf16[192,3072]{1,0:T(8,128)(2,1)}, bf16[192,3072]{1,0:T(8,128)(2,1)}, u32[]{:S(2)}, u32[]{:S(2)}) collective-permute-start(bf16[192,3072]{1,0:T(8,128)(2,1)} %add_convert_fusion.7), channel_id=1, source_target_pairs={{0,8},{8,16},{16,24},{24,26},{26,18},{18,10},{10,2},{2,6},{6,14},{... | collective-permute-start | bytes 3538952 | tf_op jit(solution)/shard_map/ppermute | solution.py:87
  813.0 29.6 %collective-permute-start.33 = (bf16[192,3072]{1,0:T(8,128)(2,1)}, bf16[192,3072]{1,0:T(8,128)(2,1)}, u32[]{:S(2)}, u32[]{:S(2)}) collective-permute-start(bf16[192,3072]{1,0:T(8,128)(2,1)} %add_convert_fusion.5), channel_id=1, source_target_pairs={{8,0},{16,8},{24,16},{26,24},{18,26},{10,18},{2,10},{6,2},{14,6},{... | collective-permute-start | bytes 3538952 | tf_op jit(solution)/shard_map/ppermute | solution.py:88
  (34 other events, 371.8 us)
Sparse Core Ops, SparseCore 0:
  11.5 496.6 all-gather.1

commit v9 on v8

--- a/solution.py
+++ b/solution.py
@@ -82,7 +82,7 @@
     send_cw = own_block(order_arr[(pos - 1) % n], 0).astype(jnp.bfloat16)
     send_ccw = own_block(order_arr[(pos + 1) % n], 2).astype(jnp.bfloat16)
     products = []
-    first_piece = max(0, n - 3 - 2 * n_pieces)
+    first_piece = max(0, n - 4 - 2 * n_pieces)
     for step in range(n - 1):
         recv_cw = lax.ppermute(send_cw, "chip", forward)
         recv_ccw = lax.ppermute(send_ccw, "chip", backward)

time: 872 us -> 875 us (level)
    unnamed x129 -> x127, local copies, waits for them, and re-layouts: 28.7 us -> 28.7 us
  transfers between devices with their start and end apart: 35 -> 35, of which waited for: 22 -> 22; matrix products, arithmetic and copies ran while one was open for 33% -> 32% of each run, Pallas kernels for 0% -> 0%
where the time goes in v9:
time: 875 us; the launch traced here: 866 us
  waiting for transfers between devices  352 us (40%)
  matrix products  179 us (20%)
  starting transfers between devices  125 us (14%)
  other arithmetic  99.6 us (11%)
  between operations  57.3 us (7%)
  local copies, waits for them, and re-layouts  52 us (6%)
    ppermute x15, waiting for transfers between devices, per_device(): recv_cw = lax.ppermute(send_cw, 'chip', forward)  162 us
    ppermute x15, waiting for transfers between devices, per_device(): recv_ccw = lax.ppermute(send_ccw, 'chip', backward)  147 us
    ppermute x15, starting transfers between devices, per_device(): recv_cw = lax.ppermute(send_cw, 'chip', forward)  115 us
    dot_general x3, matrix products, product(): jnp.dot(context, w[:, j * out_cols:(j + 1) * out_cols], preferred_element...  62.3 us
    dot_general x3, matrix products, product(): lax.dot_general(piece, w[k * d_rows:(k + 1) * d_rows], (((1,), (1,)), (()...  60.3 us
    ppermute x4, waiting for transfers between devices, per_device(): grad_from_other = lax.ppermute(grad_for_other, 'core', swap)  42.6 us
    dot_general x4, matrix products, per_device(): lax.dot_general(ctx_own, piece_q, dims_wgrad, preferred_element_type=jnp....  33.5 us
    unnamed x127, local copies, waits for them, and re-layouts  28.7 us
  transfers between devices with their start and end apart: 35, of which 22 were waited for; matrix products, arithmetic and copies ran while one was open for 32% of the time, Pallas kernels for 0%

profile of v9, /device:TPU:0, one launch (start us, length us, event | category | flops | bytes accessed | tf_op | source)
XLA Modules:
  0.0 866.0 jit_solution(11937150636327363642)
XLA Ops:
  7.2 4.1 convert_element_type.406
  11.3 8.8 %copy.14 = bf16[512,6144]{0,1:T(8,128)(2,1)} copy(bf16[512,6144]{1,0:T(8,128)(2,1)} %param.7) | data formatting | bytes 12582912 | tf_op args[0]
  20.1 4.2 broadcast_select_fusion
  24.3 2.2 slice-done.4
  26.5 5.3 convolution_convert_fusion.3
  32.7 14.0 %collective-permute-done = bf16[3072,1536]{1,0:T(8,128)(2,1)} collective-permute-done((bf16[3072,1536]{1,0:T(8,128)(2,1)S(1)}, bf16[3072,1536]{1,0:T(8,128)(2,1)}, u32[]{:S(2)}, u32[]{:S(2)}) %collective-permute-start) | collective-permute-done | bytes 9437216 | tf_op jit(solution)/shard_map/ppermute | solution.py:47
  46.7 9.9 %add_convert_fusion.3 = bf16[3072,1536]{1,0:T(8,128)(2,1)} fusion(bf16[3072,1536]{1,0:T(8,128)(2,1)} %collective-permute-done, bf16[512,3072]{0,1:T(8,128)(2,1)S(1)} %bitcast.104, bf16[512,6144]{1,0:T(8,128)(2,1)S(1)} %bitcast.103), kind=kOutput, calls=%fused_computation.15 | convolution fusion | flops 4845993984 | bytes 23592960 | tf_op jit(solution)/shard_map/dot_general | solution.py:48
  56.7 5.2 convolution_convert_fusion.2
  62.3 14.3 %collective-permute-done.1 = bf16[3072,1536]{1,0:T(8,128)(2,1)S(1)} collective-permute-done((bf16[3072,1536]{1,0:T(8,128)(2,1)S(1)}, bf16[3072,1536]{1,0:T(8,128)(2,1)S(1)}, u32[]{:S(2)}, u32[]{:S(2)}) %collective-permute-start.1) | collective-permute-done | bytes 9437216 | tf_op jit(solution)/shard_map/ppermute | solution.py:47
  76.6 7.5 add_convert_fusion.2
  84.1 5.2 convolution_convert_fusion.1
  89.8 14.3 %collective-permute-done.9 = bf16[3072,1536]{1,0:T(8,128)(2,1)S(1)} collective-permute-done((bf16[3072,1536]{1,0:T(8,128)(2,1)S(1)}, bf16[3072,1536]{1,0:T(8,128)(2,1)S(1)}, u32[]{:S(2)}, u32[]{:S(2)}) %collective-permute-start.9) | collective-permute-done | bytes 9437216 | tf_op jit(solution)/shard_map/ppermute | solution.py:47
  104.1 7.9 add_convert_fusion.1
  112.0 7.4 convolution_convert_fusion
  164.0 7.5 constant_dynamic-slice_fusion.7
  171.4 6.7 constant_dynamic-slice_fusion.6
  179.3 2.7 collective-permute-start.2
  182.0 3.5 constant_dynamic-slice_fusion.1
  185.6 8.2 add_convert_fusion
  193.8 3.2 constant_dynamic-slice_fusion
  198.8 26.6 %collective-permute-done.2 = bf16[192,3072]{1,0:T(8,128)(2,1)} collective-permute-done((bf16[192,3072]{1,0:T(8,128)(2,1)}, bf16[192,3072]{1,0:T(8,128)(2,1)}, u32[]{:S(2)}, u32[]{:S(2)}) %collective-permute-start.2) | collective-permute-done | bytes 1179680 | tf_op jit(solution)/shard_map/ppermute | solution.py:87
  227.0 17.9 %collective-permute-start.3 = (bf16[192,3072]{1,0:T(8,128)(2,1)S(1)}, bf16[192,3072]{1,0:T(8,128)(2,1)S(1)}, u32[]{:S(2)}, u32[]{:S(2)}) collective-permute-start(bf16[192,3072]{1,0:T(8,128)(2,1)S(1)} %add_convert_fusion.33), channel_id=1, source_target_pairs={{0,8},{8,16},{16,24},{24,26},{26,18},{18,10},{10,2},{2,6},{6,14},{... | collective-permute-start | bytes 3538952 | tf_op jit(solution)/shard_map/ppermute | solution.py:87
  245.0 22.5 %collective-permute-done.11 = bf16[192,3072]{1,0:T(8,128)(2,1)S(1)} collective-permute-done((bf16[192,3072]{1,0:T(8,128)(2,1)S(1)}, bf16[192,3072]{1,0:T(8,128)(2,1)S(1)}, u32[]{:S(2)}, u32[]{:S(2)}) %collective-permute-start.11) | collective-permute-done | bytes 1179680 | tf_op jit(solution)/shard_map/ppermute | solution.py:88
  267.9 28.4 %collective-permute-done.3 = bf16[192,3072]{1,0:T(8,128)(2,1)S(1)} collective-permute-done((bf16[192,3072]{1,0:T(8,128)(2,1)S(1)}, bf16[192,3072]{1,0:T(8,128)(2,1)S(1)}, u32[]{:S(2)}, u32[]{:S(2)}) %collective-permute-start.3) | collective-permute-done | bytes 1179680 | tf_op jit(solution)/shard_map/ppermute | solution.py:87
  296.6 28.0 %collective-permute-start.4 = (bf16[192,3072]{1,0:T(8,128)(2,1)S(1)}, bf16[192,3072]{1,0:T(8,128)(2,1)S(1)}, u32[]{:S(2)}, u32[]{:S(2)}) collective-permute-start(bf16[192,3072]{1,0:T(8,128)(2,1)S(1)} %add_convert_fusion.32), channel_id=1, source_target_pairs={{0,8},{8,16},{16,24},{24,26},{26,18},{18,10},{10,2},{2,6},{6,14},{... | collective-permute-start | bytes 3538952 | tf_op jit(solution)/shard_map/ppermute | solution.py:87
  324.6 29.3 %collective-permute-done.12 = bf16[192,3072]{1,0:T(8,128)(2,1)S(1)} collective-permute-done((bf16[192,3072]{1,0:T(8,128)(2,1)S(1)}, bf16[192,3072]{1,0:T(8,128)(2,1)S(1)}, u32[]{:S(2)}, u32[]{:S(2)}) %collective-permute-start.12) | collective-permute-done | bytes 1179680 | tf_op jit(solution)/shard_map/ppermute | solution.py:88
  354.3 25.1 %collective-permute-done.4 = bf16[192,3072]{1,0:T(8,128)(2,1)S(1)} collective-permute-done((bf16[192,3072]{1,0:T(8,128)(2,1)S(1)}, bf16[192,3072]{1,0:T(8,128)(2,1)S(1)}, u32[]{:S(2)}, u32[]{:S(2)}) %collective-permute-start.4) | collective-permute-done | bytes 1179680 | tf_op jit(solution)/shard_map/ppermute | solution.py:87
  379.8 24.9 %collective-permute-start.5 = (bf16[192,3072]{1,0:T(8,128)(2,1)S(1)}, bf16[192,3072]{1,0:T(8,128)(2,1)S(1)}, u32[]{:S(2)}, u32[]{:S(2)}) collective-permute-start(bf16[192,3072]{1,0:T(8,128)(2,1)S(1)} %add_convert_fusion.31), channel_id=1, source_target_pairs={{0,8},{8,16},{16,24},{24,26},{26,18},{18,10},{10,2},{2,6},{6,14},{... | collective-permute-start | bytes 3538952 | tf_op jit(solution)/shard_map/ppermute | solution.py:87
  404.8 31.7 %collective-permute-done.13 = bf16[192,3072]{1,0:T(8,128)(2,1)S(1)} collective-permute-done((bf16[192,3072]{1,0:T(8,128)(2,1)S(1)}, bf16[192,3072]{1,0:T(8,128)(2,1)S(1)}, u32[]{:S(2)}, u32[]{:S(2)}) %collective-permute-start.13) | collective-permute-done | bytes 1179680 | tf_op jit(solution)/shard_map/ppermute | solution.py:88
  436.9 18.2 %collective-permute-done.5 = bf16[192,3072]{1,0:T(8,128)(2,1)S(1)} collective-permute-done((bf16[192,3072]{1,0:T(8,128)(2,1)S(1)}, bf16[192,3072]{1,0:T(8,128)(2,1)S(1)}, u32[]{:S(2)}, u32[]{:S(2)}) %collective-permute-start.5) | collective-permute-done | bytes 1179680 | tf_op jit(solution)/shard_map/ppermute | solution.py:87
  455.4 28.2 %collective-permute-start.6 = (bf16[192,3072]{1,0:T(8,128)(2,1)S(1)}, bf16[192,3072]{1,0:T(8,128)(2,1)S(1)}, u32[]{:S(2)}, u32[]{:S(2)}) collective-permute-start(bf16[192,3072]{1,0:T(8,128)(2,1)S(1)} %add_convert_fusion.30), channel_id=1, source_target_pairs={{0,8},{8,16},{16,24},{24,26},{26,18},{18,10},{10,2},{2,6},{6,14},{... | collective-permute-start | bytes 3538952 | tf_op jit(solution)/shard_map/ppermute | solution.py:87
  483.7 20.8 %collective-permute-done.14 = bf16[192,3072]{1,0:T(8,128)(2,1)S(1)} collective-permute-done((bf16[192,3072]{1,0:T(8,128)(2,1)S(1)}, bf16[192,3072]{1,0:T(8,128)(2,1)S(1)}, u32[]{:S(2)}, u32[]{:S(2)}) %collective-permute-start.14) | collective-permute-done | bytes 1179680 | tf_op jit(solution)/shard_map/ppermute | solution.py:88
  504.9 13.0 %collective-permute-done.6 = bf16[192,3072]{1,0:T(8,128)(2,1)S(1)} collective-permute-done((bf16[192,3072]{1,0:T(8,128)(2,1)S(1)}, bf16[192,3072]{1,0:T(8,128)(2,1)S(1)}, u32[]{:S(2)}, u32[]{:S(2)}) %collective-permute-start.6) | collective-permute-done | bytes 1179680 | tf_op jit(solution)/shard_map/ppermute | solution.py:87
  518.3 2.5 collective-permute-start.7
  520.8 11.0 %collective-permute-done.15 = bf16[192,3072]{1,0:T(8,128)(2,1)S(1)} collective-permute-done((bf16[192,3072]{1,0:T(8,128)(2,1)S(1)}, bf16[192,3072]{1,0:T(8,128)(2,1)S(1)}, u32[]{:S(2)}, u32[]{:S(2)}) %collective-permute-start.15) | collective-permute-done | bytes 1179680 | tf_op jit(solution)/shard_map/ppermute | solution.py:88
  532.5 14.2 %collective-permute-done.7 = bf16[192,3072]{1,0:T(8,128)(2,1)S(1)} collective-permute-done((bf16[192,3072]{1,0:T(8,128)(2,1)S(1)}, bf16[192,3072]{1,0:T(8,128)(2,1)S(1)}, u32[]{:S(2)}, u32[]{:S(2)}) %collective-permute-start.7) | collective-permute-done | bytes 1179680 | tf_op jit(solution)/shard_map/ppermute | solution.py:87
  547.1 11.1 %collective-permute-done.16 = bf16[192,3072]{1,0:T(8,128)(2,1)S(1)} collective-permute-done((bf16[192,3072]{1,0:T(8,128)(2,1)S(1)}, bf16[192,3072]{1,0:T(8,128)(2,1)S(1)}, u32[]{:S(2)}, u32[]{:S(2)}) %collective-permute-start.16) | collective-permute-done | bytes 1179680 | tf_op jit(solution)/shard_map/ppermute | solution.py:88
  559.2 14.5 %collective-permute-done.8 = bf16[192,3072]{1,0:T(8,128)(2,1)S(1)} collective-permute-done((bf16[192,3072]{1,0:T(8,128)(2,1)S(1)}, bf16[192,3072]{1,0:T(8,128)(2,1)S(1)}, u32[]{:S(2)}, u32[]{:S(2)}) %collective-permute-start.8) | collective-permute-done | bytes 1179680 | tf_op jit(solution)/shard_map/ppermute | solution.py:87
  575.0 11.8 %collective-permute-done.17 = bf16[192,3072]{1,0:T(8,128)(2,1)S(1)} collective-permute-done((bf16[192,3072]{1,0:T(8,128)(2,1)S(1)}, bf16[192,3072]{1,0:T(8,128)(2,1)S(1)}, u32[]{:S(2)}, u32[]{:S(2)}) %collective-permute-start.17) | collective-permute-done | bytes 1179680 | tf_op jit(solution)/shard_map/ppermute | solution.py:88
  588.3 20.8 %fusion.39 = bf16[512,2048]{0,1:T(8,128)(2,1)} fusion(bf16[512,6144]{1,0:T(8,128)(2,1)} %param.7, bf16[6144,6144]{1,0:T(8,128)(2,1)} %all-gather.2.cloned.1.call-done), kind=kOutput, calls=%fused_computation.39 | convolution fusion | flops 12885950464 | bytes 33554432 | tf_op jit(solution)/shard_map/dot_general | solution.py:73
  609.0 2.2 collective-permute-start.18
  611.2 20.8 %fusion.36 = bf16[512,2048]{0,1:T(8,128)(2,1)} fusion(bf16[512,6144]{1,0:T(8,128)(2,1)} %param.7, bf16[6144,6144]{1,0:T(8,128)(2,1)} %all-gather.2.cloned.1.call-done), kind=kOutput, calls=%fused_computation.38 | convolution fusion | flops 12885950464 | bytes 33554432 | tf_op jit(solution)/shard_map/dot_general | solution.py:73
  632.0 3.2 collective-permute-done.19
  635.2 3.0 add_convert_fusion.18
  638.2 2.6 add_convert_fusion.19
  641.1 2.1 collective-permute-start.20
  643.2 20.8 %fusion.33 = bf16[512,2048]{0,1:T(8,128)(2,1)} fusion(bf16[512,6144]{1,0:T(8,128)(2,1)} %param.7, bf16[6144,6144]{1,0:T(8,128)(2,1)} %all-gather.2.cloned.1.call-done), kind=kOutput, calls=%fused_computation.37 | convolution fusion | flops 12885950464 | bytes 33554432 | tf_op jit(solution)/shard_map/dot_general | solution.py:73
  666.0 2.6 add_convert_fusion.16
  672.5 20.7 %fusion.48 = bf16[512,2048]{0,1:T(8,128)(2,1)} fusion(bf16[512,6144]{1,0:T(8,128)(2,1)} %param.11, bf16[6144,6144]{1,0:T(8,128)(2,1)} %all-gather.2.cloned.1.call-done), kind=kOutput, calls=%fused_computation.42 | convolution fusion | flops 12885950464 | bytes 33554432 | tf_op jit(solution)/shard_map/dot_general | solution.py:77
  694.6 2.6 add_convert_fusion.14
  697.2 2.6 add_convert_fusion.15
  701.9 18.9 %fusion.45 = bf16[512,2048]{0,1:T(8,128)(2,1)S(1)} fusion(bf16[512,6144]{1,0:T(8,128)(2,1)} %param.11, bf16[6144,6144]{1,0:T(8,128)(2,1)} %all-gather.2.cloned.1.call-done), kind=kOutput, calls=%fused_computation.41 | convolution fusion | flops 12885950464 | bytes 33554432 | tf_op jit(solution)/shard_map/dot_general | solution.py:77
  720.8 2.4 collective-permute-done.25
  723.3 2.6 add_convert_fusion.12
  725.9 2.6 add_convert_fusion.13
  730.8 20.7 %fusion.42 = bf16[512,2048]{0,1:T(8,128)(2,1)} fusion(bf16[512,6144]{1,0:T(8,128)(2,1)} %param.11, bf16[6144,6144]{1,0:T(8,128)(2,1)} %all-gather.2.cloned.1.call-done), kind=kOutput, calls=%fused_computation.40 | convolution fusion | flops 12885950464 | bytes 33554432 | tf_op jit(solution)/shard_map/dot_general | solution.py:77
  757.2 22.5 %collective-permute-done.28 = bf16[192,3072]{1,0:T(8,128)(2,1)S(1)} collective-permute-done((bf16[192,3072]{1,0:T(8,128)(2,1)S(1)}, bf16[192,3072]{1,0:T(8,128)(2,1)S(1)}, u32[]{:S(2)}, u32[]{:S(2)}) %collective-permute-start.28) | collective-permute-done | bytes 1179680 | tf_op jit(solution)/shard_map/ppermute | solution.py:87
  784.7 17.7 %pad_maximum_fusion = bf16[512,6144]{0,1:T(8,128)(2,1)} fusion(bf16[512,2048]{0,1:T(8,128)(2,1)S(1)} %copy-done.52, bf16[512,2048]{0,1:T(8,128)(2,1)S(1)} %copy-done.50, bf16[512,2048]{0,1:T(8,128)(2,1)S(1)} %copy-done.49), kind=kLoop, calls=%fused_computation.23 | loop fusion | flops 18874368 | bytes 12582912 | tf_op jit(solution)/shard_map/concatenate | solution.py:102
  802.4 8.7 %copy.15 = bf16[512,6144]{1,0:T(8,128)(2,1)} copy(bf16[512,6144]{0,1:T(8,128)(2,1)} %pad_maximum_fusion) | data formatting | bytes 12582912
  811.1 2.8 add_convert_fusion.8
  814.6 2.6 add_convert_fusion.5
  818.9 17.6 %pad_maximum_fusion.1 = bf16[512,6144]{0,1:T(8,128)(2,1)} fusion(bf16[512,2048]{0,1:T(8,128)(2,1)S(1)} %copy-done.53, bf16[512,2048]{0,1:T(8,128)(2,1)S(1)} %fusion.45, bf16[512,2048]{0,1:T(8,128)(2,1)S(1)} %copy-done.51), kind=kLoop, calls=%fused_computation.24 | loop fusion | flops 18874368 | bytes 12582912 | tf_op jit(solution)/shard_map/concatenate | solution.py:104
  836.4 8.7 %copy.16 = bf16[512,6144]{1,0:T(8,128)(2,1)} copy(bf16[512,6144]{0,1:T(8,128)(2,1)} %pad_maximum_fusion.1) | data formatting | bytes 12582912
  848.5 10.1 %multiply_subtract_fusion = (f32[192,6144]{1,0:T(8,128)}, f32[192,6144]{1,0:T(8,128)}, f32[192,6144]{1,0:T(8,128)}) fusion(f32[192,6144]{1,0:T(8,128)} %param.8, bf16[192,3072]{1,0:T(8,128)(2,1)S(1)} %add_convert_fusion.4, bf16[192,3072]{1,0:T(8,128)(2,1)S(1)} %add_convert_fusion.7, f32[192,6144]{1,0:T(8,128)} %param.9, f32[192,6144]{1,0:T(8,128)} %param.10), kind=kLoop, calls=%fused_computation.28 | loop fusion | flops 23592960 | bytes 30670848 | tf_op jit(solution)/shard_map/sub | solution.py:115
  (195 shorter events, 44.8 us)
Async XLA Ops:
  7.2 581.1 %all-gather.2.cloned.1.call-start = ((), (), s32[]{:S(2)}) async-start(), calls=%async_computation | async-start | bytes 77856768 | tf_op jit(solution)/shard_map/all_gather | solution.py:37
  24.3 79.8 %copy-start = (bf16[512,16,1,192]{0,3,2,1:T(8,128)(2,1)}, bf16[512,16,1,192]{0,3,2,1:T(8,128)(2,1)S(1)}, u32[]{:S(2)}) copy-start(bf16[512,16,1,192]{0,3,2,1:T(8,128)(2,1)S(1)} %get-tuple-element.140) | copy-start | bytes 9437188
  31.8 14.9 %collective-permute-start = (bf16[3072,1536]{1,0:T(8,128)(2,1)S(1)}, bf16[3072,1536]{1,0:T(8,128)(2,1)}, u32[]{:S(2)}, u32[]{:S(2)}) collective-permute-start(bf16[3072,1536]{1,0:T(8,128)(2,1)S(1)} %convolution_convert_fusion.3), channel_id=1, source_target_pairs={{0,1},{1,0},{2,3},{3,2},{4,5},{5,4},{6,7},{7,6},{8,9},{9,8},{10,11... | collective-permute-start | bytes 28311560 | tf_op jit(solution)/shard_map/ppermute | solution.py:47
  32.7 79.3 %copy-start.54 = (bf16[512,1536]{1,0:T(8,128)(2,1)}, bf16[512,1536]{1,0:T(8,128)(2,1)S(1)}, u32[]{:S(2)}) copy-start(bf16[512,1536]{1,0:T(8,128)(2,1)S(1)} %get-tuple-element.34) | copy-start | bytes 4718596
  61.9 14.7 %collective-permute-start.1 = (bf16[3072,1536]{1,0:T(8,128)(2,1)S(1)}, bf16[3072,1536]{1,0:T(8,128)(2,1)S(1)}, u32[]{:S(2)}, u32[]{:S(2)}) collective-permute-start(bf16[3072,1536]{1,0:T(8,128)(2,1)S(1)} %convolution_convert_fusion.2), channel_id=1, source_target_pairs={{0,1},{1,0},{2,3},{3,2},{4,5},{5,4},{6,7},{7,6},{8,9},{9,8},{10,11... | collective-permute-start | bytes 28311560 | tf_op jit(solution)/shard_map/ppermute | solution.py:47
  89.4 14.7 %collective-permute-start.9 = (bf16[3072,1536]{1,0:T(8,128)(2,1)S(1)}, bf16[3072,1536]{1,0:T(8,128)(2,1)S(1)}, u32[]{:S(2)}, u32[]{:S(2)}) collective-permute-start(bf16[3072,1536]{1,0:T(8,128)(2,1)S(1)} %convolution_convert_fusion.1), channel_id=1, source_target_pairs={{0,1},{1,0},{2,3},{3,2},{4,5},{5,4},{6,7},{7,6},{8,9},{9,8},{10,11... | collective-permute-start | bytes 28311560 | tf_op jit(solution)/shard_map/ppermute | solution.py:47
  119.4 66.2 %collective-permute-start.10 = (bf16[3072,1536]{1,0:T(8,128)(2,1)}, bf16[3072,1536]{1,0:T(8,128)(2,1)}, u32[]{:S(2)}, u32[]{:S(2)}) collective-permute-start(bf16[3072,1536]{1,0:T(8,128)(2,1)} %convolution_convert_fusion), channel_id=1, source_target_pairs={{0,1},{1,0},{2,3},{3,2},{4,5},{5,4},{6,7},{7,6},{8,9},{9,8},{10,11... | collective-permute-start | bytes 28311560 | tf_op jit(solution)/shard_map/ppermute | solution.py:47
  179.3 46.1 %collective-permute-start.2 = (bf16[192,3072]{1,0:T(8,128)(2,1)}, bf16[192,3072]{1,0:T(8,128)(2,1)}, u32[]{:S(2)}, u32[]{:S(2)}) collective-permute-start(bf16[192,3072]{1,0:T(8,128)(2,1)} %pad_maximum_fusion.3), channel_id=1, source_target_pairs={{0,8},{8,16},{16,24},{24,26},{26,18},{18,10},{10,2},{2,6},{6,14},{... | collective-permute-start | bytes 3538952 | tf_op jit(solution)/shard_map/ppermute | solution.py:87
  196.9 28.5 %copy-start.40 = (bf16[192,1536]{1,0:T(8,128)(2,1)S(1)}, bf16[192,1536]{1,0:T(8,128)(2,1)}, u32[]{:S(2)}) copy-start(bf16[192,1536]{1,0:T(8,128)(2,1)} %get-tuple-element.86) | copy-start | bytes 1769476
  196.9 28.5 %copy-start.43 = (bf16[192,1536]{1,0:T(8,128)(2,1)S(1)}, bf16[192,1536]{1,0:T(8,128)(2,1)}, u32[]{:S(2)}) copy-start(bf16[192,1536]{1,0:T(8,128)(2,1)} %get-tuple-element.102) | copy-start | bytes 1769476
  198.4 69.0 %copy-start.46 = (bf16[192,1536]{1,0:T(8,128)(2,1)S(1)}, bf16[192,1536]{1,0:T(8,128)(2,1)}, u32[]{:S(2)}) copy-start(bf16[192,1536]{1,0:T(8,128)(2,1)} %get-tuple-element.118) | copy-start | bytes 1769476
  198.4 69.0 %copy-start.48 = (bf16[192,1536]{1,0:T(8,128)(2,1)S(1)}, bf16[192,1536]{1,0:T(8,128)(2,1)}, u32[]{:S(2)}) copy-start(bf16[192,1536]{1,0:T(8,128)(2,1)} %get-tuple-element.134) | copy-start | bytes 1769476
  198.4 69.0 %collective-permute-start.11 = (bf16[192,3072]{1,0:T(8,128)(2,1)S(1)}, bf16[192,3072]{1,0:T(8,128)(2,1)S(1)}, u32[]{:S(2)}, u32[]{:S(2)}) collective-permute-start(bf16[192,3072]{1,0:T(8,128)(2,1)S(1)} %pad_maximum_fusion.4), channel_id=1, source_target_pairs={{8,0},{16,8},{24,16},{26,24},{18,26},{10,18},{2,10},{6,2},{14,6},{... | collective-permute-start | bytes 3538952 | tf_op jit(solution)/shard_map/ppermute | solution.py:88
  227.0 69.2 %copy-start.37 = (bf16[192,1536]{1,0:T(8,128)(2,1)S(1)}, bf16[192,1536]{1,0:T(8,128)(2,1)}, u32[]{:S(2)}) copy-start(bf16[192,1536]{1,0:T(8,128)(2,1)} %get-tuple-element.85) | copy-start | bytes 1769476
  227.0 69.2 %copy-start.39 = (bf16[192,1536]{1,0:T(8,128)(2,1)S(1)}, bf16[192,1536]{1,0:T(8,128)(2,1)}, u32[]{:S(2)}) copy-start(bf16[192,1536]{1,0:T(8,128)(2,1)} %get-tuple-element.101) | copy-start | bytes 1769476
  227.0 69.2 %collective-permute-start.3 = (bf16[192,3072]{1,0:T(8,128)(2,1)S(1)}, bf16[192,3072]{1,0:T(8,128)(2,1)S(1)}, u32[]{:S(2)}, u32[]{:S(2)}) collective-permute-start(bf16[192,3072]{1,0:T(8,128)(2,1)S(1)} %add_convert_fusion.33), channel_id=1, source_target_pairs={{0,8},{8,16},{16,24},{24,26},{26,18},{18,10},{10,2},{2,6},{6,14},{... | collective-permute-start | bytes 3538952 | tf_op jit(solution)/shard_map/ppermute | solution.py:87
  267.8 86.1 %copy-start.44 = (bf16[192,1536]{1,0:T(8,128)(2,1)S(1)}, bf16[192,1536]{1,0:T(8,128)(2,1)}, u32[]{:S(2)}) copy-start(bf16[192,1536]{1,0:T(8,128)(2,1)} %get-tuple-element.117) | copy-start | bytes 1769476
  267.8 86.1 %copy-start.47 = (bf16[192,1536]{1,0:T(8,128)(2,1)S(1)}, bf16[192,1536]{1,0:T(8,128)(2,1)}, u32[]{:S(2)}) copy-start(bf16[192,1536]{1,0:T(8,128)(2,1)} %get-tuple-element.133) | copy-start | bytes 1769476
  267.8 86.1 %collective-permute-start.12 = (bf16[192,3072]{1,0:T(8,128)(2,1)S(1)}, bf16[192,3072]{1,0:T(8,128)(2,1)S(1)}, u32[]{:S(2)}, u32[]{:S(2)}) collective-permute-start(bf16[192,3072]{1,0:T(8,128)(2,1)S(1)} %add_convert_fusion.26), channel_id=1, source_target_pairs={{8,0},{16,8},{24,16},{26,24},{18,26},{10,18},{2,10},{6,2},{14,6},{... | collective-permute-start | bytes 3538952 | tf_op jit(solution)/shard_map/ppermute | solution.py:88
  296.6 82.9 %copy-start.34 = (bf16[192,1536]{1,0:T(8,128)(2,1)S(1)}, bf16[192,1536]{1,0:T(8,128)(2,1)}, u32[]{:S(2)}) copy-start(bf16[192,1536]{1,0:T(8,128)(2,1)} %get-tuple-element.84) | copy-start | bytes 1769476
  296.6 82.9 %copy-start.36 = (bf16[192,1536]{1,0:T(8,128)(2,1)S(1)}, bf16[192,1536]{1,0:T(8,128)(2,1)}, u32[]{:S(2)}) copy-start(bf16[192,1536]{1,0:T(8,128)(2,1)} %get-tuple-element.100) | copy-start | bytes 1769476
  296.6 82.9 %collective-permute-start.4 = (bf16[192,3072]{1,0:T(8,128)(2,1)S(1)}, bf16[192,3072]{1,0:T(8,128)(2,1)S(1)}, u32[]{:S(2)}, u32[]{:S(2)}) collective-permute-start(bf16[192,3072]{1,0:T(8,128)(2,1)S(1)} %add_convert_fusion.32), channel_id=1, source_target_pairs={{0,8},{8,16},{16,24},{24,26},{26,18},{18,10},{10,2},{2,6},{6,14},{... | collective-permute-start | bytes 3538952 | tf_op jit(solution)/shard_map/ppermute | solution.py:87
  354.2 82.2 %copy-start.41 = (bf16[192,1536]{1,0:T(8,128)(2,1)S(1)}, bf16[192,1536]{1,0:T(8,128)(2,1)}, u32[]{:S(2)}) copy-start(bf16[192,1536]{1,0:T(8,128)(2,1)} %get-tuple-element.116) | copy-start | bytes 1769476
  354.2 82.2 %copy-start.45 = (bf16[192,1536]{1,0:T(8,128)(2,1)S(1)}, bf16[192,1536]{1,0:T(8,128)(2,1)}, u32[]{:S(2)}) copy-start(bf16[192,1536]{1,0:T(8,128)(2,1)} %get-tuple-element.132) | copy-start | bytes 1769476
  354.2 82.2 %collective-permute-start.13 = (bf16[192,3072]{1,0:T(8,128)(2,1)S(1)}, bf16[192,3072]{1,0:T(8,128)(2,1)S(1)}, u32[]{:S(2)}, u32[]{:S(2)}) collective-permute-start(bf16[192,3072]{1,0:T(8,128)(2,1)S(1)} %add_convert_fusion.25), channel_id=1, source_target_pairs={{8,0},{16,8},{24,16},{26,24},{18,26},{10,18},{2,10},{6,2},{14,6},{... | collective-permute-start | bytes 3538952 | tf_op jit(solution)/shard_map/ppermute | solution.py:88
  379.8 75.3 %copy-start.31 = (bf16[192,1536]{1,0:T(8,128)(2,1)S(1)}, bf16[192,1536]{1,0:T(8,128)(2,1)}, u32[]{:S(2)}) copy-start(bf16[192,1536]{1,0:T(8,128)(2,1)} %get-tuple-element.83) | copy-start | bytes 1769476
  379.8 75.3 %copy-start.33 = (bf16[192,1536]{1,0:T(8,128)(2,1)S(1)}, bf16[192,1536]{1,0:T(8,128)(2,1)}, u32[]{:S(2)}) copy-start(bf16[192,1536]{1,0:T(8,128)(2,1)} %get-tuple-element.99) | copy-start | bytes 1769476
  379.8 75.2 %collective-permute-start.5 = (bf16[192,3072]{1,0:T(8,128)(2,1)S(1)}, bf16[192,3072]{1,0:T(8,128)(2,1)S(1)}, u32[]{:S(2)}, u32[]{:S(2)}) collective-permute-start(bf16[192,3072]{1,0:T(8,128)(2,1)S(1)} %add_convert_fusion.31), channel_id=1, source_target_pairs={{0,8},{8,16},{16,24},{24,26},{26,18},{18,10},{10,2},{2,6},{6,14},{... | collective-permute-start | bytes 3538952 | tf_op jit(solution)/shard_map/ppermute | solution.py:87
  436.8 67.7 %copy-start.38 = (bf16[192,1536]{1,0:T(8,128)(2,1)S(1)}, bf16[192,1536]{1,0:T(8,128)(2,1)}, u32[]{:S(2)}) copy-start(bf16[192,1536]{1,0:T(8,128)(2,1)} %get-tuple-element.115) | copy-start | bytes 1769476
  436.8 67.7 %copy-start.42 = (bf16[192,1536]{1,0:T(8,128)(2,1)S(1)}, bf16[192,1536]{1,0:T(8,128)(2,1)}, u32[]{:S(2)}) copy-start(bf16[192,1536]{1,0:T(8,128)(2,1)} %get-tuple-element.131) | copy-start | bytes 1769476
  436.8 67.7 %collective-permute-start.14 = (bf16[192,3072]{1,0:T(8,128)(2,1)S(1)}, bf16[192,3072]{1,0:T(8,128)(2,1)S(1)}, u32[]{:S(2)}, u32[]{:S(2)}) collective-permute-start(bf16[192,3072]{1,0:T(8,128)(2,1)S(1)} %add_convert_fusion.24), channel_id=1, source_target_pairs={{8,0},{16,8},{24,16},{26,24},{18,26},{10,18},{2,10},{6,2},{14,6},{... | collective-permute-start | bytes 3538952 | tf_op jit(solution)/shard_map/ppermute | solution.py:88
  455.4 62.5 %copy-start.28 = (bf16[192,1536]{1,0:T(8,128)(2,1)S(1)}, bf16[192,1536]{1,0:T(8,128)(2,1)}, u32[]{:S(2)}) copy-start(bf16[192,1536]{1,0:T(8,128)(2,1)} %get-tuple-element.82) | copy-start | bytes 1769476
  455.4 62.5 %copy-start.30 = (bf16[192,1536]{1,0:T(8,128)(2,1)S(1)}, bf16[192,1536]{1,0:T(8,128)(2,1)}, u32[]{:S(2)}) copy-start(bf16[192,1536]{1,0:T(8,128)(2,1)} %get-tuple-element.98) | copy-start | bytes 1769476
  455.4 62.5 %collective-permute-start.6 = (bf16[192,3072]{1,0:T(8,128)(2,1)S(1)}, bf16[192,3072]{1,0:T(8,128)(2,1)S(1)}, u32[]{:S(2)}, u32[]{:S(2)}) collective-permute-start(bf16[192,3072]{1,0:T(8,128)(2,1)S(1)} %add_convert_fusion.30), channel_id=1, source_target_pairs={{0,8},{8,16},{16,24},{24,26},{26,18},{18,10},{10,2},{2,6},{6,14},{... | collective-permute-start | bytes 3538952 | tf_op jit(solution)/shard_map/ppermute | solution.py:87
  504.8 27.0 %copy-start.35 = (bf16[192,1536]{1,0:T(8,128)(2,1)S(1)}, bf16[192,1536]{1,0:T(8,128)(2,1)}, u32[]{:S(2)}) copy-start(bf16[192,1536]{1,0:T(8,128)(2,1)} %get-tuple-element.114) | copy-start | bytes 1769476
  504.9 27.0 %collective-permute-start.15 = (bf16[192,3072]{1,0:T(8,128)(2,1)S(1)}, bf16[192,3072]{1,0:T(8,128)(2,1)S(1)}, u32[]{:S(2)}, u32[]{:S(2)}) collective-permute-start(bf16[192,3072]{1,0:T(8,128)(2,1)S(1)} %add_convert_fusion.23), channel_id=1, source_target_pairs={{8,0},{16,8},{24,16},{26,24},{18,26},{10,18},{2,10},{6,2},{14,6},{... | collective-permute-start | bytes 3538952 | tf_op jit(solution)/shard_map/ppermute | solution.py:88
  518.3 28.5 %copy-start.25 = (bf16[192,1536]{1,0:T(8,128)(2,1)S(1)}, bf16[192,1536]{1,0:T(8,128)(2,1)}, u32[]{:S(2)}) copy-start(bf16[192,1536]{1,0:T(8,128)(2,1)} %get-tuple-element.81) | copy-start | bytes 1769476
  518.3 28.5 %copy-start.27 = (bf16[192,1536]{1,0:T(8,128)(2,1)S(1)}, bf16[192,1536]{1,0:T(8,128)(2,1)}, u32[]{:S(2)}) copy-start(bf16[192,1536]{1,0:T(8,128)(2,1)} %get-tuple-element.97) | copy-start | bytes 1769476
  518.3 28.5 %collective-permute-start.7 = (bf16[192,3072]{1,0:T(8,128)(2,1)S(1)}, bf16[192,3072]{1,0:T(8,128)(2,1)S(1)}, u32[]{:S(2)}, u32[]{:S(2)}) collective-permute-start(bf16[192,3072]{1,0:T(8,128)(2,1)S(1)} %add_convert_fusion.29), channel_id=1, source_target_pairs={{0,8},{8,16},{16,24},{24,26},{26,18},{18,10},{10,2},{2,6},{6,14},{... | collective-permute-start | bytes 3538952 | tf_op jit(solution)/shard_map/ppermute | solution.py:87
  532.2 26.0 %collective-permute-start.16 = (bf16[192,3072]{1,0:T(8,128)(2,1)S(1)}, bf16[192,3072]{1,0:T(8,128)(2,1)S(1)}, u32[]{:S(2)}, u32[]{:S(2)}) collective-permute-start(bf16[192,3072]{1,0:T(8,128)(2,1)S(1)} %add_convert_fusion.22), channel_id=1, source_target_pairs={{8,0},{16,8},{24,16},{26,24},{18,26},{10,18},{2,10},{6,2},{14,6},{... | collective-permute-start | bytes 3538952 | tf_op jit(solution)/shard_map/ppermute | solution.py:88
  547.1 26.6 %collective-permute-start.8 = (bf16[192,3072]{1,0:T(8,128)(2,1)S(1)}, bf16[192,3072]{1,0:T(8,128)(2,1)S(1)}, u32[]{:S(2)}, u32[]{:S(2)}) collective-permute-start(bf16[192,3072]{1,0:T(8,128)(2,1)S(1)} %add_convert_fusion.28), channel_id=1, source_target_pairs={{0,8},{8,16},{16,24},{24,26},{26,18},{18,10},{10,2},{2,6},{6,14},{... | collective-permute-start | bytes 3538952 | tf_op jit(solution)/shard_map/ppermute | solution.py:87
  558.6 28.3 %copy-start.29 = (bf16[192,1536]{1,0:T(8,128)(2,1)S(1)}, bf16[192,1536]{1,0:T(8,128)(2,1)}, u32[]{:S(2)}) copy-start(bf16[192,1536]{1,0:T(8,128)(2,1)} %get-tuple-element.112) | copy-start | bytes 1769476
  558.6 28.3 %collective-permute-start.17 = (bf16[192,3072]{1,0:T(8,128)(2,1)S(1)}, bf16[192,3072]{1,0:T(8,128)(2,1)S(1)}, u32[]{:S(2)}, u32[]{:S(2)}) collective-permute-start(bf16[192,3072]{1,0:T(8,128)(2,1)S(1)} %add_convert_fusion.21), channel_id=1, source_target_pairs={{8,0},{16,8},{24,16},{26,24},{18,26},{10,18},{2,10},{6,2},{14,6},{... | collective-permute-start | bytes 3538952 | tf_op jit(solution)/shard_map/ppermute | solution.py:88
  609.0 26.1 %collective-permute-start.19 = (bf16[192,3072]{1,0:T(8,128)(2,1)}, bf16[192,3072]{1,0:T(8,128)(2,1)}, u32[]{:S(2)}, u32[]{:S(2)}) collective-permute-start(bf16[192,3072]{1,0:T(8,128)(2,1)} %add_convert_fusion.20), channel_id=1, source_target_pairs={{8,0},{16,8},{24,16},{26,24},{18,26},{10,18},{2,10},{6,2},{14,6},{... | collective-permute-start | bytes 3538952 | tf_op jit(solution)/shard_map/ppermute | solution.py:88
  609.0 29.1 %collective-permute-start.18 = (bf16[192,3072]{1,0:T(8,128)(2,1)}, bf16[192,3072]{1,0:T(8,128)(2,1)}, u32[]{:S(2)}, u32[]{:S(2)}) collective-permute-start(bf16[192,3072]{1,0:T(8,128)(2,1)} %add_convert_fusion.27), channel_id=1, source_target_pairs={{0,8},{8,16},{16,24},{24,26},{26,18},{18,10},{10,2},{2,6},{6,14},{... | collective-permute-start | bytes 3538952 | tf_op jit(solution)/shard_map/ppermute | solution.py:87
  640.8 25.2 %collective-permute-start.21 = (bf16[192,3072]{1,0:T(8,128)(2,1)}, bf16[192,3072]{1,0:T(8,128)(2,1)}, u32[]{:S(2)}, u32[]{:S(2)}) collective-permute-start(bf16[192,3072]{1,0:T(8,128)(2,1)} %add_convert_fusion.18), channel_id=1, source_target_pairs={{8,0},{16,8},{24,16},{26,24},{18,26},{10,18},{2,10},{6,2},{14,6},{... | collective-permute-start | bytes 3538952 | tf_op jit(solution)/shard_map/ppermute | solution.py:88
  641.1 27.6 %collective-permute-start.20 = (bf16[192,3072]{1,0:T(8,128)(2,1)}, bf16[192,3072]{1,0:T(8,128)(2,1)}, u32[]{:S(2)}, u32[]{:S(2)}) collective-permute-start(bf16[192,3072]{1,0:T(8,128)(2,1)} %add_convert_fusion.19), channel_id=1, source_target_pairs={{0,8},{8,16},{16,24},{24,26},{26,18},{18,10},{10,2},{2,6},{6,14},{... | collective-permute-start | bytes 3538952 | tf_op jit(solution)/shard_map/ppermute | solution.py:87
  670.3 24.4 %collective-permute-start.23 = (bf16[192,3072]{1,0:T(8,128)(2,1)}, bf16[192,3072]{1,0:T(8,128)(2,1)}, u32[]{:S(2)}, u32[]{:S(2)}) collective-permute-start(bf16[192,3072]{1,0:T(8,128)(2,1)} %add_convert_fusion.16), channel_id=1, source_target_pairs={{8,0},{16,8},{24,16},{26,24},{18,26},{10,18},{2,10},{6,2},{14,6},{... | collective-permute-start | bytes 3538952 | tf_op jit(solution)/shard_map/ppermute | solution.py:88
  670.9 26.4 %collective-permute-start.22 = (bf16[192,3072]{1,0:T(8,128)(2,1)S(1)}, bf16[192,3072]{1,0:T(8,128)(2,1)}, u32[]{:S(2)}, u32[]{:S(2)}) collective-permute-start(bf16[192,3072]{1,0:T(8,128)(2,1)S(1)} %add_convert_fusion.17), channel_id=1, source_target_pairs={{0,8},{8,16},{16,24},{24,26},{26,18},{18,10},{10,2},{2,6},{6,14},{... | collective-permute-start | bytes 3538952 | tf_op jit(solution)/shard_map/ppermute | solution.py:87
  699.9 23.4 %collective-permute-start.25 = (bf16[192,3072]{1,0:T(8,128)(2,1)}, bf16[192,3072]{1,0:T(8,128)(2,1)}, u32[]{:S(2)}, u32[]{:S(2)}) collective-permute-start(bf16[192,3072]{1,0:T(8,128)(2,1)} %add_convert_fusion.14), channel_id=1, source_target_pairs={{8,0},{16,8},{24,16},{26,24},{18,26},{10,18},{2,10},{6,2},{14,6},{... | collective-permute-start | bytes 3538952 | tf_op jit(solution)/shard_map/ppermute | solution.py:88
  700.7 25.2 %collective-permute-start.24 = (bf16[192,3072]{1,0:T(8,128)(2,1)}, bf16[192,3072]{1,0:T(8,128)(2,1)}, u32[]{:S(2)}, u32[]{:S(2)}) collective-permute-start(bf16[192,3072]{1,0:T(8,128)(2,1)} %add_convert_fusion.15), channel_id=1, source_target_pairs={{0,8},{8,16},{16,24},{24,26},{26,18},{18,10},{10,2},{2,6},{6,14},{... | collective-permute-start | bytes 3538952 | tf_op jit(solution)/shard_map/ppermute | solution.py:87
  728.6 22.9 %collective-permute-start.27 = (bf16[192,3072]{1,0:T(8,128)(2,1)}, bf16[192,3072]{1,0:T(8,128)(2,1)}, u32[]{:S(2)}, u32[]{:S(2)}) collective-permute-start(bf16[192,3072]{1,0:T(8,128)(2,1)} %add_convert_fusion.12), channel_id=1, source_target_pairs={{8,0},{16,8},{24,16},{26,24},{18,26},{10,18},{2,10},{6,2},{14,6},{... | collective-permute-start | bytes 3538952 | tf_op jit(solution)/shard_map/ppermute | solution.py:88
  729.7 23.6 %collective-permute-start.26 = (bf16[192,3072]{1,0:T(8,128)(2,1)}, bf16[192,3072]{1,0:T(8,128)(2,1)}, u32[]{:S(2)}, u32[]{:S(2)}) collective-permute-start(bf16[192,3072]{1,0:T(8,128)(2,1)} %add_convert_fusion.13), channel_id=1, source_target_pairs={{0,8},{8,16},{16,24},{24,26},{26,18},{18,10},{10,2},{2,6},{6,14},{... | collective-permute-start | bytes 3538952 | tf_op jit(solution)/shard_map/ppermute | solution.py:87
  753.2 26.4 %copy-start.7 = (bf16[192,1536]{1,0:T(8,128)(2,1)S(1)}, bf16[192,1536]{1,0:T(8,128)(2,1)}, u32[]{:S(2)}) copy-start(bf16[192,1536]{1,0:T(8,128)(2,1)} %get-tuple-element.74) | copy-start | bytes 1769476
  753.2 26.4 %copy-start.10 = (bf16[192,1536]{1,0:T(8,128)(2,1)S(1)}, bf16[192,1536]{1,0:T(8,128)(2,1)}, u32[]{:S(2)}) copy-start(bf16[192,1536]{1,0:T(8,128)(2,1)} %get-tuple-element.90) | copy-start | bytes 1769476
  753.3 31.4 %copy-start.52 = (bf16[512,2048]{0,1:T(8,128)(2,1)S(1)}, bf16[512,2048]{0,1:T(8,128)(2,1)}, u32[]{:S(2)}) copy-start(bf16[512,2048]{0,1:T(8,128)(2,1)} %fusion.33) | copy-start | bytes 6291460
  755.1 26.7 %copy-start.15 = (bf16[192,1536]{1,0:T(8,128)(2,1)S(1)}, bf16[192,1536]{1,0:T(8,128)(2,1)}, u32[]{:S(2)}) copy-start(bf16[192,1536]{1,0:T(8,128)(2,1)} %get-tuple-element.106) | copy-start | bytes 1769476
  755.1 26.7 %copy-start.18 = (bf16[192,1536]{1,0:T(8,128)(2,1)S(1)}, bf16[192,1536]{1,0:T(8,128)(2,1)}, u32[]{:S(2)}) copy-start(bf16[192,1536]{1,0:T(8,128)(2,1)} %get-tuple-element.122) | copy-start | bytes 1769476
  755.1 24.5 %collective-permute-start.28 = (bf16[192,3072]{1,0:T(8,128)(2,1)S(1)}, bf16[192,3072]{1,0:T(8,128)(2,1)S(1)}, u32[]{:S(2)}, u32[]{:S(2)}) collective-permute-start(bf16[192,3072]{1,0:T(8,128)(2,1)S(1)} %add_convert_fusion.11), channel_id=1, source_target_pairs={{0,8},{8,16},{16,24},{24,26},{26,18},{18,10},{10,2},{2,6},{6,14},{... | collective-permute-start | bytes 3538952 | tf_op jit(solution)/shard_map/ppermute | solution.py:87
  755.8 25.9 %collective-permute-start.31 = (bf16[192,3072]{1,0:T(8,128)(2,1)S(1)}, bf16[192,3072]{1,0:T(8,128)(2,1)S(1)}, u32[]{:S(2)}, u32[]{:S(2)}) collective-permute-start(bf16[192,3072]{1,0:T(8,128)(2,1)S(1)} %add_convert_fusion.10), channel_id=1, source_target_pairs={{8,0},{16,8},{24,16},{26,24},{18,26},{10,18},{2,10},{6,2},{14,6},{... | collective-permute-start | bytes 3538952 | tf_op jit(solution)/shard_map/ppermute | solution.py:88
  781.0 30.1 %collective-permute-start.29 = (bf16[192,3072]{1,0:T(8,128)(2,1)}, bf16[192,3072]{1,0:T(8,128)(2,1)}, u32[]{:S(2)}, u32[]{:S(2)}) collective-permute-start(bf16[192,3072]{1,0:T(8,128)(2,1)} %add_convert_fusion.9), channel_id=1, source_target_pairs={{0,8},{8,16},{16,24},{24,26},{26,18},{18,10},{10,2},{2,6},{6,14},{... | collective-permute-start | bytes 3538952 | tf_op jit(solution)/shard_map/ppermute | solution.py:87
  783.1 31.5 %collective-permute-start.32 = (bf16[192,3072]{1,0:T(8,128)(2,1)}, bf16[192,3072]{1,0:T(8,128)(2,1)}, u32[]{:S(2)}, u32[]{:S(2)}) collective-permute-start(bf16[192,3072]{1,0:T(8,128)(2,1)} %add_convert_fusion.6), channel_id=1, source_target_pairs={{8,0},{16,8},{24,16},{26,24},{18,26},{10,18},{2,10},{6,2},{14,6},{... | collective-permute-start | bytes 3538952 | tf_op jit(solution)/shard_map/ppermute | solution.py:88
  813.9 31.2 %collective-permute-start.30 = (bf16[192,3072]{1,0:T(8,128)(2,1)}, bf16[192,3072]{1,0:T(8,128)(2,1)}, u32[]{:S(2)}, u32[]{:S(2)}) collective-permute-start(bf16[192,3072]{1,0:T(8,128)(2,1)} %add_convert_fusion.8), channel_id=1, source_target_pairs={{0,8},{8,16},{16,24},{24,26},{26,18},{18,10},{10,2},{2,6},{6,14},{... | collective-permute-start | bytes 3538952 | tf_op jit(solution)/shard_map/ppermute | solution.py:87
  817.3 29.6 %collective-permute-start.33 = (bf16[192,3072]{1,0:T(8,128)(2,1)}, bf16[192,3072]{1,0:T(8,128)(2,1)}, u32[]{:S(2)}, u32[]{:S(2)}) collective-permute-start(bf16[192,3072]{1,0:T(8,128)(2,1)} %add_convert_fusion.5), channel_id=1, source_target_pairs={{8,0},{16,8},{24,16},{26,24},{18,26},{10,18},{2,10},{6,2},{14,6},{... | collective-permute-start | bytes 3538952 | tf_op jit(solution)/shard_map/ppermute | solution.py:88
  (33 other events, 378.7 us)
Sparse Core Ops, SparseCore 0:
  11.5 496.6 all-gather.1

commit v10 on v8

--- a/solution.py
+++ b/solution.py
@@ -64,7 +64,7 @@
             [lax.dynamic_slice_in_dim(sums[q], block * rows, rows, 0) for q in (first, first + 1)], axis=1
         ).astype(jnp.float32)
 
-    n_pieces = 3
+    n_pieces = 1
     out_cols = width // n_pieces
     d_rows = local_cols // n_pieces
 

time: 872 us -> 893 us (1.024)
  waiting for transfers between devices: 349 us -> 466 us
  other arithmetic: 97.5 us -> 37.3 us
  matrix products: 181 us -> 152 us
    ppermute x15, waiting for transfers between devices: 154 us -> 218 us  [per_device(): recv_cw = lax.ppermute(send_cw, 'chip', forward)]
    ppermute x15, waiting for transfers between devices: 152 us -> 205 us  [per_device(): recv_ccw = lax.ppermute(send_ccw, 'chip', backward)]
    concatenate x2 -> x0, other arithmetic: 35.2 us -> none  [the longest x1 17.6 us: per_device(): out = jnp.concatenate(products[:n_pieces], axis=1)]
    dot_general x3 -> x1, matrix products: 62.3 us -> 47.4 us  [product(): lax.dot_general(piece, w[k * d_rows:(k + 1) * d_rows], (((1,), (1,)), (()...]
    dot_general x3 -> x1, matrix products: 62.3 us -> 47.6 us  [product(): jnp.dot(context, w[:, j * out_cols:(j + 1) * out_cols], preferred_element...]
    convert_element_type x15, other arithmetic: 21.8 us -> 8.67 us  [per_device(): send_ccw = (recv_ccw.astype(jnp.float32) + mine_ccw).astype(jnp.bfloat16)]
    convert_element_type x15, other arithmetic: 19.5 us -> 7.71 us  [per_device(): send_cw = (recv_cw.astype(jnp.float32) + mine_cw).astype(jnp.bfloat16)]
    unnamed x129 -> x121, local copies, waits for them, and re-layouts: 28.7 us -> 29.4 us
  transfers between devices with their start and end apart: 35 -> 35, of which waited for: 22 -> 28; matrix products, arithmetic and copies ran while one was open for 33% -> 20% of each run, Pallas kernels for 0% -> 0%
where the time goes in v10:
time: 893 us; the launch traced here: 883 us
  waiting for transfers between devices  466 us (52%)
  matrix products  152 us (17%)
  starting transfers between devices  118 us (13%)
  between operations  57.5 us (6%)
  local copies, waits for them, and re-layouts  52.9 us (6%)
  other arithmetic  37.3 us (4%)
    ppermute x15, waiting for transfers between devices, per_device(): recv_cw = lax.ppermute(send_cw, 'chip', forward)  218 us
    ppermute x15, waiting for transfers between devices, per_device(): recv_ccw = lax.ppermute(send_ccw, 'chip', backward)  205 us
    ppermute x15, starting transfers between devices, per_device(): recv_cw = lax.ppermute(send_cw, 'chip', forward)  111 us
    dot_general x1, matrix products, product(): jnp.dot(context, w[:, j * out_cols:(j + 1) * out_cols], preferred_element...  47.6 us
    dot_general x1, matrix products, product(): lax.dot_general(piece, w[k * d_rows:(k + 1) * d_rows], (((1,), (1,)), (()...  47.4 us
    ppermute x4, waiting for transfers between devices, per_device(): grad_from_other = lax.ppermute(grad_for_other, 'core', swap)  42.6 us
    dot_general x4, matrix products, per_device(): lax.dot_general(ctx_own, piece_q, dims_wgrad, preferred_element_type=jnp....  33.5 us
    unnamed x121, local copies, waits for them, and re-layouts  29.4 us
  transfers between devices with their start and end apart: 35, of which 28 were waited for; matrix products, arithmetic and copies ran while one was open for 20% of the time, Pallas kernels for 0%

profile of v10, /device:TPU:0, one launch (start us, length us, event | category | flops | bytes accessed | tf_op | source)
XLA Modules:
  0.0 882.8 jit_solution(8990211437485045632)
XLA Ops:
  7.2 4.1 convert_element_type.412
  11.3 8.8 copy.14
  20.1 4.2 broadcast_select_fusion
  24.3 2.2 slice-done.4
  26.5 5.3 convolution_convert_fusion.3
  32.7 14.0 %collective-permute-done = bf16[3072,1536]{1,0:T(8,128)(2,1)} collective-permute-done((bf16[3072,1536]{1,0:T(8,128)(2,1)S(1)}, bf16[3072,1536]{1,0:T(8,128)(2,1)}, u32[]{:S(2)}, u32[]{:S(2)}) %collective-permute-start) | collective-permute-done | bytes 9437216 | tf_op jit(solution)/shard_map/ppermute | solution.py:47
  46.7 9.9 %add_convert_fusion.3 = bf16[3072,1536]{1,0:T(8,128)(2,1)} fusion(bf16[3072,1536]{1,0:T(8,128)(2,1)} %collective-permute-done, bf16[512,3072]{0,1:T(8,128)(2,1)S(1)} %bitcast.94, bf16[512,6144]{1,0:T(8,128)(2,1)S(1)} %bitcast.93), kind=kOutput, calls=%fused_computation.3 | convolution fusion | flops 4845993984 | bytes 23592960 | tf_op jit(solution)/shard_map/dot_general | solution.py:48
  56.6 5.2 convolution_convert_fusion.2
  62.3 14.3 %collective-permute-done.1 = bf16[3072,1536]{1,0:T(8,128)(2,1)S(1)} collective-permute-done((bf16[3072,1536]{1,0:T(8,128)(2,1)S(1)}, bf16[3072,1536]{1,0:T(8,128)(2,1)S(1)}, u32[]{:S(2)}, u32[]{:S(2)}) %collective-permute-start.1) | collective-permute-done | bytes 9437216 | tf_op jit(solution)/shard_map/ppermute | solution.py:47
  76.6 7.5 add_convert_fusion.2
  84.1 5.2 convolution_convert_fusion.1
  89.8 14.3 %collective-permute-done.14 = bf16[3072,1536]{1,0:T(8,128)(2,1)S(1)} collective-permute-done((bf16[3072,1536]{1,0:T(8,128)(2,1)S(1)}, bf16[3072,1536]{1,0:T(8,128)(2,1)S(1)}, u32[]{:S(2)}, u32[]{:S(2)}) %collective-permute-start.14) | collective-permute-done | bytes 9437216 | tf_op jit(solution)/shard_map/ppermute | solution.py:47
  104.1 7.9 add_convert_fusion.1
  112.0 7.4 convolution_convert_fusion
  164.1 7.2 constant_dynamic-slice_fusion.5
  171.3 7.0 constant_dynamic-slice_fusion.4
  179.4 2.7 collective-permute-start.2
  182.2 3.6 constant_dynamic-slice_fusion.1
  185.7 8.2 add_convert_fusion
  193.9 3.2 constant_dynamic-slice_fusion
  197.2 1.4 pad_maximum_fusion.2
  199.0 26.6 %collective-permute-done.2 = bf16[192,3072]{1,0:T(8,128)(2,1)} collective-permute-done((bf16[192,3072]{1,0:T(8,128)(2,1)}, bf16[192,3072]{1,0:T(8,128)(2,1)}, u32[]{:S(2)}, u32[]{:S(2)}) %collective-permute-start.2) | collective-permute-done | bytes 1179680 | tf_op jit(solution)/shard_map/ppermute | solution.py:87
  225.5 1.6 add_convert_fusion.33
  227.2 17.9 %collective-permute-start.3 = (bf16[192,3072]{1,0:T(8,128)(2,1)S(1)}, bf16[192,3072]{1,0:T(8,128)(2,1)S(1)}, u32[]{:S(2)}, u32[]{:S(2)}) collective-permute-start(bf16[192,3072]{1,0:T(8,128)(2,1)S(1)} %add_convert_fusion.33), channel_id=1, source_target_pairs={{0,8},{8,16},{16,24},{24,26},{26,18},{18,10},{10,2},{2,6},{6,14},{... | collective-permute-start | bytes 3538952 | tf_op jit(solution)/shard_map/ppermute | solution.py:87
  245.1 23.0 %collective-permute-done.16 = bf16[192,3072]{1,0:T(8,128)(2,1)S(1)} collective-permute-done((bf16[192,3072]{1,0:T(8,128)(2,1)S(1)}, bf16[192,3072]{1,0:T(8,128)(2,1)S(1)}, u32[]{:S(2)}, u32[]{:S(2)}) %collective-permute-start.16) | collective-permute-done | bytes 1179680 | tf_op jit(solution)/shard_map/ppermute | solution.py:88
  268.6 27.8 %collective-permute-done.3 = bf16[192,3072]{1,0:T(8,128)(2,1)S(1)} collective-permute-done((bf16[192,3072]{1,0:T(8,128)(2,1)S(1)}, bf16[192,3072]{1,0:T(8,128)(2,1)S(1)}, u32[]{:S(2)}, u32[]{:S(2)}) %collective-permute-start.3) | collective-permute-done | bytes 1179680 | tf_op jit(solution)/shard_map/ppermute | solution.py:87
  296.7 28.0 %collective-permute-start.4 = (bf16[192,3072]{1,0:T(8,128)(2,1)S(1)}, bf16[192,3072]{1,0:T(8,128)(2,1)S(1)}, u32[]{:S(2)}, u32[]{:S(2)}) collective-permute-start(bf16[192,3072]{1,0:T(8,128)(2,1)S(1)} %add_convert_fusion.32), channel_id=1, source_target_pairs={{0,8},{8,16},{16,24},{24,26},{26,18},{18,10},{10,2},{2,6},{6,14},{... | collective-permute-start | bytes 3538952 | tf_op jit(solution)/shard_map/ppermute | solution.py:87
  324.7 29.7 %collective-permute-done.17 = bf16[192,3072]{1,0:T(8,128)(2,1)S(1)} collective-permute-done((bf16[192,3072]{1,0:T(8,128)(2,1)S(1)}, bf16[192,3072]{1,0:T(8,128)(2,1)S(1)}, u32[]{:S(2)}, u32[]{:S(2)}) %collective-permute-start.17) | collective-permute-done | bytes 1179680 | tf_op jit(solution)/shard_map/ppermute | solution.py:88
  354.9 24.7 %collective-permute-done.4 = bf16[192,3072]{1,0:T(8,128)(2,1)S(1)} collective-permute-done((bf16[192,3072]{1,0:T(8,128)(2,1)S(1)}, bf16[192,3072]{1,0:T(8,128)(2,1)S(1)}, u32[]{:S(2)}, u32[]{:S(2)}) %collective-permute-start.4) | collective-permute-done | bytes 1179680 | tf_op jit(solution)/shard_map/ppermute | solution.py:87
  380.0 24.8 %collective-permute-start.5 = (bf16[192,3072]{1,0:T(8,128)(2,1)S(1)}, bf16[192,3072]{1,0:T(8,128)(2,1)S(1)}, u32[]{:S(2)}, u32[]{:S(2)}) collective-permute-start(bf16[192,3072]{1,0:T(8,128)(2,1)S(1)} %add_convert_fusion.31), channel_id=1, source_target_pairs={{0,8},{8,16},{16,24},{24,26},{26,18},{18,10},{10,2},{2,6},{6,14},{... | collective-permute-start | bytes 3538952 | tf_op jit(solution)/shard_map/ppermute | solution.py:87
  404.8 32.2 %collective-permute-done.18 = bf16[192,3072]{1,0:T(8,128)(2,1)S(1)} collective-permute-done((bf16[192,3072]{1,0:T(8,128)(2,1)S(1)}, bf16[192,3072]{1,0:T(8,128)(2,1)S(1)}, u32[]{:S(2)}, u32[]{:S(2)}) %collective-permute-start.18) | collective-permute-done | bytes 1179680 | tf_op jit(solution)/shard_map/ppermute | solution.py:88
  437.3 17.7 %collective-permute-done.5 = bf16[192,3072]{1,0:T(8,128)(2,1)S(1)} collective-permute-done((bf16[192,3072]{1,0:T(8,128)(2,1)S(1)}, bf16[192,3072]{1,0:T(8,128)(2,1)S(1)}, u32[]{:S(2)}, u32[]{:S(2)}) %collective-permute-start.5) | collective-permute-done | bytes 1179680 | tf_op jit(solution)/shard_map/ppermute | solution.py:87
  455.4 28.2 %collective-permute-start.6 = (bf16[192,3072]{1,0:T(8,128)(2,1)S(1)}, bf16[192,3072]{1,0:T(8,128)(2,1)S(1)}, u32[]{:S(2)}, u32[]{:S(2)}) collective-permute-start(bf16[192,3072]{1,0:T(8,128)(2,1)S(1)} %add_convert_fusion.30), channel_id=1, source_target_pairs={{0,8},{8,16},{16,24},{24,26},{26,18},{18,10},{10,2},{2,6},{6,14},{... | collective-permute-start | bytes 3538952 | tf_op jit(solution)/shard_map/ppermute | solution.py:87
  483.7 21.0 %collective-permute-done.19 = bf16[192,3072]{1,0:T(8,128)(2,1)S(1)} collective-permute-done((bf16[192,3072]{1,0:T(8,128)(2,1)S(1)}, bf16[192,3072]{1,0:T(8,128)(2,1)S(1)}, u32[]{:S(2)}, u32[]{:S(2)}) %collective-permute-start.19) | collective-permute-done | bytes 1179680 | tf_op jit(solution)/shard_map/ppermute | solution.py:88
  505.1 12.8 %collective-permute-done.6 = bf16[192,3072]{1,0:T(8,128)(2,1)S(1)} collective-permute-done((bf16[192,3072]{1,0:T(8,128)(2,1)S(1)}, bf16[192,3072]{1,0:T(8,128)(2,1)S(1)}, u32[]{:S(2)}, u32[]{:S(2)}) %collective-permute-start.6) | collective-permute-done | bytes 1179680 | tf_op jit(solution)/shard_map/ppermute | solution.py:87
  518.3 2.5 collective-permute-start.7
  520.8 11.1 %collective-permute-done.20 = bf16[192,3072]{1,0:T(8,128)(2,1)S(1)} collective-permute-done((bf16[192,3072]{1,0:T(8,128)(2,1)S(1)}, bf16[192,3072]{1,0:T(8,128)(2,1)S(1)}, u32[]{:S(2)}, u32[]{:S(2)}) %collective-permute-start.20) | collective-permute-done | bytes 1179680 | tf_op jit(solution)/shard_map/ppermute | solution.py:88
  532.6 14.1 %collective-permute-done.7 = bf16[192,3072]{1,0:T(8,128)(2,1)S(1)} collective-permute-done((bf16[192,3072]{1,0:T(8,128)(2,1)S(1)}, bf16[192,3072]{1,0:T(8,128)(2,1)S(1)}, u32[]{:S(2)}, u32[]{:S(2)}) %collective-permute-start.7) | collective-permute-done | bytes 1179680 | tf_op jit(solution)/shard_map/ppermute | solution.py:87
  547.2 11.1 %collective-permute-done.21 = bf16[192,3072]{1,0:T(8,128)(2,1)S(1)} collective-permute-done((bf16[192,3072]{1,0:T(8,128)(2,1)S(1)}, bf16[192,3072]{1,0:T(8,128)(2,1)S(1)}, u32[]{:S(2)}, u32[]{:S(2)}) %collective-permute-start.21) | collective-permute-done | bytes 1179680 | tf_op jit(solution)/shard_map/ppermute | solution.py:88
  559.2 14.4 %collective-permute-done.8 = bf16[192,3072]{1,0:T(8,128)(2,1)S(1)} collective-permute-done((bf16[192,3072]{1,0:T(8,128)(2,1)S(1)}, bf16[192,3072]{1,0:T(8,128)(2,1)S(1)}, u32[]{:S(2)}, u32[]{:S(2)}) %collective-permute-start.8) | collective-permute-done | bytes 1179680 | tf_op jit(solution)/shard_map/ppermute | solution.py:87
  574.3 12.8 %collective-permute-done.22 = bf16[192,3072]{1,0:T(8,128)(2,1)S(1)} collective-permute-done((bf16[192,3072]{1,0:T(8,128)(2,1)S(1)}, bf16[192,3072]{1,0:T(8,128)(2,1)S(1)}, u32[]{:S(2)}, u32[]{:S(2)}) %collective-permute-start.22) | collective-permute-done | bytes 1179680 | tf_op jit(solution)/shard_map/ppermute | solution.py:88
  587.5 12.2 %collective-permute-done.9 = bf16[192,3072]{1,0:T(8,128)(2,1)S(1)} collective-permute-done((bf16[192,3072]{1,0:T(8,128)(2,1)S(1)}, bf16[192,3072]{1,0:T(8,128)(2,1)S(1)}, u32[]{:S(2)}, u32[]{:S(2)}) %collective-permute-start.9) | collective-permute-done | bytes 1179680 | tf_op jit(solution)/shard_map/ppermute | solution.py:87
  600.5 12.8 %collective-permute-done.23 = bf16[192,3072]{1,0:T(8,128)(2,1)S(1)} collective-permute-done((bf16[192,3072]{1,0:T(8,128)(2,1)S(1)}, bf16[192,3072]{1,0:T(8,128)(2,1)S(1)}, u32[]{:S(2)}, u32[]{:S(2)}) %collective-permute-start.23) | collective-permute-done | bytes 1179680 | tf_op jit(solution)/shard_map/ppermute | solution.py:88
  614.0 11.9 %collective-permute-done.10 = bf16[192,3072]{1,0:T(8,128)(2,1)S(1)} collective-permute-done((bf16[192,3072]{1,0:T(8,128)(2,1)S(1)}, bf16[192,3072]{1,0:T(8,128)(2,1)S(1)}, u32[]{:S(2)}, u32[]{:S(2)}) %collective-permute-start.10) | collective-permute-done | bytes 1179680 | tf_op jit(solution)/shard_map/ppermute | solution.py:87
  626.6 12.8 %collective-permute-done.24 = bf16[192,3072]{1,0:T(8,128)(2,1)S(1)} collective-permute-done((bf16[192,3072]{1,0:T(8,128)(2,1)S(1)}, bf16[192,3072]{1,0:T(8,128)(2,1)S(1)}, u32[]{:S(2)}, u32[]{:S(2)}) %collective-permute-start.24) | collective-permute-done | bytes 1179680 | tf_op jit(solution)/shard_map/ppermute | solution.py:88
  640.1 11.9 %collective-permute-done.11 = bf16[192,3072]{1,0:T(8,128)(2,1)S(1)} collective-permute-done((bf16[192,3072]{1,0:T(8,128)(2,1)S(1)}, bf16[192,3072]{1,0:T(8,128)(2,1)S(1)}, u32[]{:S(2)}, u32[]{:S(2)}) %collective-permute-start.11) | collective-permute-done | bytes 1179680 | tf_op jit(solution)/shard_map/ppermute | solution.py:87
  652.8 12.8 %collective-permute-done.25 = bf16[192,3072]{1,0:T(8,128)(2,1)S(1)} collective-permute-done((bf16[192,3072]{1,0:T(8,128)(2,1)S(1)}, bf16[192,3072]{1,0:T(8,128)(2,1)S(1)}, u32[]{:S(2)}, u32[]{:S(2)}) %collective-permute-start.25) | collective-permute-done | bytes 1179680 | tf_op jit(solution)/shard_map/ppermute | solution.py:88
  666.2 11.9 %collective-permute-done.12 = bf16[192,3072]{1,0:T(8,128)(2,1)S(1)} collective-permute-done((bf16[192,3072]{1,0:T(8,128)(2,1)S(1)}, bf16[192,3072]{1,0:T(8,128)(2,1)S(1)}, u32[]{:S(2)}, u32[]{:S(2)}) %collective-permute-start.12) | collective-permute-done | bytes 1179680 | tf_op jit(solution)/shard_map/ppermute | solution.py:87
  678.9 12.6 %collective-permute-done.26 = bf16[192,3072]{1,0:T(8,128)(2,1)S(1)} collective-permute-done((bf16[192,3072]{1,0:T(8,128)(2,1)S(1)}, bf16[192,3072]{1,0:T(8,128)(2,1)S(1)}, u32[]{:S(2)}, u32[]{:S(2)}) %collective-permute-start.26) | collective-permute-done | bytes 1179680 | tf_op jit(solution)/shard_map/ppermute | solution.py:88
  692.4 8.3 collective-permute-done.13
  701.0 13.4 %collective-permute-done.27 = bf16[192,3072]{1,0:T(8,128)(2,1)S(1)} collective-permute-done((bf16[192,3072]{1,0:T(8,128)(2,1)S(1)}, bf16[192,3072]{1,0:T(8,128)(2,1)S(1)}, u32[]{:S(2)}, u32[]{:S(2)}) %collective-permute-start.27) | collective-permute-done | bytes 1179680 | tf_op jit(solution)/shard_map/ppermute | solution.py:88
  714.8 47.6 %fusion = bf16[512,6144]{0,1:T(8,128)(2,1)} fusion(bf16[6144,6144]{1,0:T(8,128)(2,1)} %all-gather.2.cloned.1.call-done, bf16[512,6144]{1,0:T(8,128)(2,1)} %param.7), kind=kOutput, calls=%fused_computation.10 | convolution fusion | flops 38657851392 | bytes 88080384 | tf_op jit(solution)/shard_map/dot_general | solution.py:73
  763.0 1.7 collective-permute-start.28
  764.7 47.4 %fusion.1 = bf16[512,6144]{0,1:T(8,128)(2,1)} fusion(bf16[6144,6144]{1,0:T(8,128)(2,1)} %all-gather.2.cloned.1.call-done, bf16[512,6144]{1,0:T(8,128)(2,1)} %param.11), kind=kOutput, calls=%fused_computation.11 | convolution fusion | flops 38657851392 | bytes 88080384 | tf_op jit(solution)/shard_map/dot_general | solution.py:77
  812.2 1.7 add_convert_fusion.8
  813.9 1.7 add_convert_fusion.9
  815.7 1.5 collective-permute-start.30
  817.7 23.7 %collective-permute-done.30 = bf16[192,3072]{1,0:T(8,128)(2,1)S(1)} collective-permute-done((bf16[192,3072]{1,0:T(8,128)(2,1)S(1)}, bf16[192,3072]{1,0:T(8,128)(2,1)S(1)}, u32[]{:S(2)}, u32[]{:S(2)}) %collective-permute-start.30) | collective-permute-done | bytes 1179680 | tf_op jit(solution)/shard_map/ppermute | solution.py:87
  841.8 1.5 collective-permute-start.31
  843.3 1.4 add_convert_fusion.5
  845.2 8.6 copy.15
  853.9 8.7 copy.16
  863.8 1.6 add_convert_fusion.4
  865.4 10.1 %multiply_subtract_fusion = (f32[192,6144]{1,0:T(8,128)}, f32[192,6144]{1,0:T(8,128)}, f32[192,6144]{1,0:T(8,128)}) fusion(f32[192,6144]{1,0:T(8,128)} %param.8, bf16[192,3072]{1,0:T(8,128)(2,1)S(1)} %add_convert_fusion.4, bf16[192,3072]{1,0:T(8,128)(2,1)S(1)} %add_convert_fusion.6, f32[192,6144]{1,0:T(8,128)} %param.9, f32[192,6144]{1,0:T(8,128)} %param.10), kind=kLoop, calls=%fused_computation.18 | loop fusion | flops 23592960 | bytes 30670848 | tf_op jit(solution)/shard_map/sub | solution.py:115
  (183 shorter events, 22.0 us)
Async XLA Ops:
  7.2 707.6 %all-gather.2.cloned.1.call-start = ((), (), s32[]{:S(2)}) async-start(), calls=%async_computation | async-start | bytes 77856768 | tf_op jit(solution)/shard_map/all_gather | solution.py:37
  24.3 79.8 %copy-start = (bf16[512,16,1,192]{0,3,2,1:T(8,128)(2,1)}, bf16[512,16,1,192]{0,3,2,1:T(8,128)(2,1)S(1)}, u32[]{:S(2)}) copy-start(bf16[512,16,1,192]{0,3,2,1:T(8,128)(2,1)S(1)} %get-tuple-element.108) | copy-start | bytes 9437188
  31.8 14.9 %collective-permute-start = (bf16[3072,1536]{1,0:T(8,128)(2,1)S(1)}, bf16[3072,1536]{1,0:T(8,128)(2,1)}, u32[]{:S(2)}, u32[]{:S(2)}) collective-permute-start(bf16[3072,1536]{1,0:T(8,128)(2,1)S(1)} %convolution_convert_fusion.3), channel_id=1, source_target_pairs={{0,1},{1,0},{2,3},{3,2},{4,5},{5,4},{6,7},{7,6},{8,9},{9,8},{10,11... | collective-permute-start | bytes 28311560 | tf_op jit(solution)/shard_map/ppermute | solution.py:47
  32.7 79.3 %copy-start.51 = (bf16[512,1536]{1,0:T(8,128)(2,1)}, bf16[512,1536]{1,0:T(8,128)(2,1)S(1)}, u32[]{:S(2)}) copy-start(bf16[512,1536]{1,0:T(8,128)(2,1)S(1)} %get-tuple-element.18) | copy-start | bytes 4718596
  61.9 14.7 %collective-permute-start.1 = (bf16[3072,1536]{1,0:T(8,128)(2,1)S(1)}, bf16[3072,1536]{1,0:T(8,128)(2,1)S(1)}, u32[]{:S(2)}, u32[]{:S(2)}) collective-permute-start(bf16[3072,1536]{1,0:T(8,128)(2,1)S(1)} %convolution_convert_fusion.2), channel_id=1, source_target_pairs={{0,1},{1,0},{2,3},{3,2},{4,5},{5,4},{6,7},{7,6},{8,9},{9,8},{10,11... | collective-permute-start | bytes 28311560 | tf_op jit(solution)/shard_map/ppermute | solution.py:47
  89.4 14.7 %collective-permute-start.14 = (bf16[3072,1536]{1,0:T(8,128)(2,1)S(1)}, bf16[3072,1536]{1,0:T(8,128)(2,1)S(1)}, u32[]{:S(2)}, u32[]{:S(2)}) collective-permute-start(bf16[3072,1536]{1,0:T(8,128)(2,1)S(1)} %convolution_convert_fusion.1), channel_id=1, source_target_pairs={{0,1},{1,0},{2,3},{3,2},{4,5},{5,4},{6,7},{7,6},{8,9},{9,8},{10,11... | collective-permute-start | bytes 28311560 | tf_op jit(solution)/shard_map/ppermute | solution.py:47
  119.4 66.4 %collective-permute-start.15 = (bf16[3072,1536]{1,0:T(8,128)(2,1)}, bf16[3072,1536]{1,0:T(8,128)(2,1)}, u32[]{:S(2)}, u32[]{:S(2)}) collective-permute-start(bf16[3072,1536]{1,0:T(8,128)(2,1)} %convolution_convert_fusion), channel_id=1, source_target_pairs={{0,1},{1,0},{2,3},{3,2},{4,5},{5,4},{6,7},{7,6},{8,9},{9,8},{10,11... | collective-permute-start | bytes 28311560 | tf_op jit(solution)/shard_map/ppermute | solution.py:47
  179.4 46.1 %collective-permute-start.2 = (bf16[192,3072]{1,0:T(8,128)(2,1)}, bf16[192,3072]{1,0:T(8,128)(2,1)}, u32[]{:S(2)}, u32[]{:S(2)}) collective-permute-start(bf16[192,3072]{1,0:T(8,128)(2,1)} %pad_maximum_fusion.1), channel_id=1, source_target_pairs={{0,8},{8,16},{16,24},{24,26},{26,18},{18,10},{10,2},{2,6},{6,14},{... | collective-permute-start | bytes 3538952 | tf_op jit(solution)/shard_map/ppermute | solution.py:87
  197.2 28.4 %copy-start.42 = (bf16[192,1536]{1,0:T(8,128)(2,1)S(1)}, bf16[192,1536]{1,0:T(8,128)(2,1)}, u32[]{:S(2)}) copy-start(bf16[192,1536]{1,0:T(8,128)(2,1)} %get-tuple-element.54) | copy-start | bytes 1769476
  197.2 28.4 %copy-start.45 = (bf16[192,1536]{1,0:T(8,128)(2,1)S(1)}, bf16[192,1536]{1,0:T(8,128)(2,1)}, u32[]{:S(2)}) copy-start(bf16[192,1536]{1,0:T(8,128)(2,1)} %get-tuple-element.70) | copy-start | bytes 1769476
  198.6 69.5 %copy-start.48 = (bf16[192,1536]{1,0:T(8,128)(2,1)S(1)}, bf16[192,1536]{1,0:T(8,128)(2,1)}, u32[]{:S(2)}) copy-start(bf16[192,1536]{1,0:T(8,128)(2,1)} %get-tuple-element.86) | copy-start | bytes 1769476
  198.6 69.5 %copy-start.50 = (bf16[192,1536]{1,0:T(8,128)(2,1)S(1)}, bf16[192,1536]{1,0:T(8,128)(2,1)}, u32[]{:S(2)}) copy-start(bf16[192,1536]{1,0:T(8,128)(2,1)} %get-tuple-element.102) | copy-start | bytes 1769476
  198.6 69.5 %collective-permute-start.16 = (bf16[192,3072]{1,0:T(8,128)(2,1)S(1)}, bf16[192,3072]{1,0:T(8,128)(2,1)S(1)}, u32[]{:S(2)}, u32[]{:S(2)}) collective-permute-start(bf16[192,3072]{1,0:T(8,128)(2,1)S(1)} %pad_maximum_fusion.2), channel_id=1, source_target_pairs={{8,0},{16,8},{24,16},{26,24},{18,26},{10,18},{2,10},{6,2},{14,6},{... | collective-permute-start | bytes 3538952 | tf_op jit(solution)/shard_map/ppermute | solution.py:88
  227.2 69.2 %copy-start.38 = (bf16[192,1536]{1,0:T(8,128)(2,1)S(1)}, bf16[192,1536]{1,0:T(8,128)(2,1)}, u32[]{:S(2)}) copy-start(bf16[192,1536]{1,0:T(8,128)(2,1)} %get-tuple-element.53) | copy-start | bytes 1769476
  227.2 69.2 %copy-start.41 = (bf16[192,1536]{1,0:T(8,128)(2,1)S(1)}, bf16[192,1536]{1,0:T(8,128)(2,1)}, u32[]{:S(2)}) copy-start(bf16[192,1536]{1,0:T(8,128)(2,1)} %get-tuple-element.69) | copy-start | bytes 1769476
  227.2 69.2 %collective-permute-start.3 = (bf16[192,3072]{1,0:T(8,128)(2,1)S(1)}, bf16[192,3072]{1,0:T(8,128)(2,1)S(1)}, u32[]{:S(2)}, u32[]{:S(2)}) collective-permute-start(bf16[192,3072]{1,0:T(8,128)(2,1)S(1)} %add_convert_fusion.33), channel_id=1, source_target_pairs={{0,8},{8,16},{16,24},{24,26},{26,18},{18,10},{10,2},{2,6},{6,14},{... | collective-permute-start | bytes 3538952 | tf_op jit(solution)/shard_map/ppermute | solution.py:87
  268.5 86.0 %copy-start.46 = (bf16[192,1536]{1,0:T(8,128)(2,1)S(1)}, bf16[192,1536]{1,0:T(8,128)(2,1)}, u32[]{:S(2)}) copy-start(bf16[192,1536]{1,0:T(8,128)(2,1)} %get-tuple-element.85) | copy-start | bytes 1769476
  268.5 85.9 %copy-start.49 = (bf16[192,1536]{1,0:T(8,128)(2,1)S(1)}, bf16[192,1536]{1,0:T(8,128)(2,1)}, u32[]{:S(2)}) copy-start(bf16[192,1536]{1,0:T(8,128)(2,1)} %get-tuple-element.101) | copy-start | bytes 1769476
  268.5 85.9 %collective-permute-start.17 = (bf16[192,3072]{1,0:T(8,128)(2,1)S(1)}, bf16[192,3072]{1,0:T(8,128)(2,1)S(1)}, u32[]{:S(2)}, u32[]{:S(2)}) collective-permute-start(bf16[192,3072]{1,0:T(8,128)(2,1)S(1)} %add_convert_fusion.21), channel_id=1, source_target_pairs={{8,0},{16,8},{24,16},{26,24},{18,26},{10,18},{2,10},{6,2},{14,6},{... | collective-permute-start | bytes 3538952 | tf_op jit(solution)/shard_map/ppermute | solution.py:88
  296.7 82.9 %copy-start.34 = (bf16[192,1536]{1,0:T(8,128)(2,1)S(1)}, bf16[192,1536]{1,0:T(8,128)(2,1)}, u32[]{:S(2)}) copy-start(bf16[192,1536]{1,0:T(8,128)(2,1)} %get-tuple-element.52) | copy-start | bytes 1769476
  296.7 82.9 %copy-start.37 = (bf16[192,1536]{1,0:T(8,128)(2,1)S(1)}, bf16[192,1536]{1,0:T(8,128)(2,1)}, u32[]{:S(2)}) copy-start(bf16[192,1536]{1,0:T(8,128)(2,1)} %get-tuple-element.68) | copy-start | bytes 1769476
  296.7 82.9 %collective-permute-start.4 = (bf16[192,3072]{1,0:T(8,128)(2,1)S(1)}, bf16[192,3072]{1,0:T(8,128)(2,1)S(1)}, u32[]{:S(2)}, u32[]{:S(2)}) collective-permute-start(bf16[192,3072]{1,0:T(8,128)(2,1)S(1)} %add_convert_fusion.32), channel_id=1, source_target_pairs={{0,8},{8,16},{16,24},{24,26},{26,18},{18,10},{10,2},{2,6},{6,14},{... | collective-permute-start | bytes 3538952 | tf_op jit(solution)/shard_map/ppermute | solution.py:87
  354.8 82.1 %copy-start.43 = (bf16[192,1536]{1,0:T(8,128)(2,1)S(1)}, bf16[192,1536]{1,0:T(8,128)(2,1)}, u32[]{:S(2)}) copy-start(bf16[192,1536]{1,0:T(8,128)(2,1)} %get-tuple-element.84) | copy-start | bytes 1769476
  354.8 82.1 %copy-start.47 = (bf16[192,1536]{1,0:T(8,128)(2,1)S(1)}, bf16[192,1536]{1,0:T(8,128)(2,1)}, u32[]{:S(2)}) copy-start(bf16[192,1536]{1,0:T(8,128)(2,1)} %get-tuple-element.100) | copy-start | bytes 1769476
  354.8 82.1 %collective-permute-start.18 = (bf16[192,3072]{1,0:T(8,128)(2,1)S(1)}, bf16[192,3072]{1,0:T(8,128)(2,1)S(1)}, u32[]{:S(2)}, u32[]{:S(2)}) collective-permute-start(bf16[192,3072]{1,0:T(8,128)(2,1)S(1)} %add_convert_fusion.20), channel_id=1, source_target_pairs={{8,0},{16,8},{24,16},{26,24},{18,26},{10,18},{2,10},{6,2},{14,6},{... | collective-permute-start | bytes 3538952 | tf_op jit(solution)/shard_map/ppermute | solution.py:88
  379.9 75.1 %copy-start.30 = (bf16[192,1536]{1,0:T(8,128)(2,1)S(1)}, bf16[192,1536]{1,0:T(8,128)(2,1)}, u32[]{:S(2)}) copy-start(bf16[192,1536]{1,0:T(8,128)(2,1)} %get-tuple-element.51) | copy-start | bytes 1769476
  379.9 75.1 %copy-start.33 = (bf16[192,1536]{1,0:T(8,128)(2,1)S(1)}, bf16[192,1536]{1,0:T(8,128)(2,1)}, u32[]{:S(2)}) copy-start(bf16[192,1536]{1,0:T(8,128)(2,1)} %get-tuple-element.67) | copy-start | bytes 1769476
  380.0 75.1 %collective-permute-start.5 = (bf16[192,3072]{1,0:T(8,128)(2,1)S(1)}, bf16[192,3072]{1,0:T(8,128)(2,1)S(1)}, u32[]{:S(2)}, u32[]{:S(2)}) collective-permute-start(bf16[192,3072]{1,0:T(8,128)(2,1)S(1)} %add_convert_fusion.31), channel_id=1, source_target_pairs={{0,8},{8,16},{16,24},{24,26},{26,18},{18,10},{10,2},{2,6},{6,14},{... | collective-permute-start | bytes 3538952 | tf_op jit(solution)/shard_map/ppermute | solution.py:87
  437.3 67.4 %copy-start.39 = (bf16[192,1536]{1,0:T(8,128)(2,1)S(1)}, bf16[192,1536]{1,0:T(8,128)(2,1)}, u32[]{:S(2)}) copy-start(bf16[192,1536]{1,0:T(8,128)(2,1)} %get-tuple-element.83) | copy-start | bytes 1769476
  437.3 67.4 %copy-start.44 = (bf16[192,1536]{1,0:T(8,128)(2,1)S(1)}, bf16[192,1536]{1,0:T(8,128)(2,1)}, u32[]{:S(2)}) copy-start(bf16[192,1536]{1,0:T(8,128)(2,1)} %get-tuple-element.99) | copy-start | bytes 1769476
  437.3 67.4 %collective-permute-start.19 = (bf16[192,3072]{1,0:T(8,128)(2,1)S(1)}, bf16[192,3072]{1,0:T(8,128)(2,1)S(1)}, u32[]{:S(2)}, u32[]{:S(2)}) collective-permute-start(bf16[192,3072]{1,0:T(8,128)(2,1)S(1)} %add_convert_fusion.19), channel_id=1, source_target_pairs={{8,0},{16,8},{24,16},{26,24},{18,26},{10,18},{2,10},{6,2},{14,6},{... | collective-permute-start | bytes 3538952 | tf_op jit(solution)/shard_map/ppermute | solution.py:88
  455.4 62.5 %copy-start.26 = (bf16[192,1536]{1,0:T(8,128)(2,1)S(1)}, bf16[192,1536]{1,0:T(8,128)(2,1)}, u32[]{:S(2)}) copy-start(bf16[192,1536]{1,0:T(8,128)(2,1)} %get-tuple-element.50) | copy-start | bytes 1769476
  455.4 62.5 %copy-start.29 = (bf16[192,1536]{1,0:T(8,128)(2,1)S(1)}, bf16[192,1536]{1,0:T(8,128)(2,1)}, u32[]{:S(2)}) copy-start(bf16[192,1536]{1,0:T(8,128)(2,1)} %get-tuple-element.66) | copy-start | bytes 1769476
  455.4 62.5 %collective-permute-start.6 = (bf16[192,3072]{1,0:T(8,128)(2,1)S(1)}, bf16[192,3072]{1,0:T(8,128)(2,1)S(1)}, u32[]{:S(2)}, u32[]{:S(2)}) collective-permute-start(bf16[192,3072]{1,0:T(8,128)(2,1)S(1)} %add_convert_fusion.30), channel_id=1, source_target_pairs={{0,8},{8,16},{16,24},{24,26},{26,18},{18,10},{10,2},{2,6},{6,14},{... | collective-permute-start | bytes 3538952 | tf_op jit(solution)/shard_map/ppermute | solution.py:87
  505.1 26.9 %collective-permute-start.20 = (bf16[192,3072]{1,0:T(8,128)(2,1)S(1)}, bf16[192,3072]{1,0:T(8,128)(2,1)S(1)}, u32[]{:S(2)}, u32[]{:S(2)}) collective-permute-start(bf16[192,3072]{1,0:T(8,128)(2,1)S(1)} %add_convert_fusion.18), channel_id=1, source_target_pairs={{8,0},{16,8},{24,16},{26,24},{18,26},{10,18},{2,10},{6,2},{14,6},{... | collective-permute-start | bytes 3538952 | tf_op jit(solution)/shard_map/ppermute | solution.py:88
  518.3 28.4 %copy-start.22 = (bf16[192,1536]{1,0:T(8,128)(2,1)S(1)}, bf16[192,1536]{1,0:T(8,128)(2,1)}, u32[]{:S(2)}) copy-start(bf16[192,1536]{1,0:T(8,128)(2,1)} %get-tuple-element.49) | copy-start | bytes 1769476
  518.3 28.4 %copy-start.25 = (bf16[192,1536]{1,0:T(8,128)(2,1)S(1)}, bf16[192,1536]{1,0:T(8,128)(2,1)}, u32[]{:S(2)}) copy-start(bf16[192,1536]{1,0:T(8,128)(2,1)} %get-tuple-element.65) | copy-start | bytes 1769476
  518.3 28.4 %collective-permute-start.7 = (bf16[192,3072]{1,0:T(8,128)(2,1)S(1)}, bf16[192,3072]{1,0:T(8,128)(2,1)S(1)}, u32[]{:S(2)}, u32[]{:S(2)}) collective-permute-start(bf16[192,3072]{1,0:T(8,128)(2,1)S(1)} %add_convert_fusion.29), channel_id=1, source_target_pairs={{0,8},{8,16},{16,24},{24,26},{26,18},{18,10},{10,2},{2,6},{6,14},{... | collective-permute-start | bytes 3538952 | tf_op jit(solution)/shard_map/ppermute | solution.py:87
  532.3 25.9 %collective-permute-start.21 = (bf16[192,3072]{1,0:T(8,128)(2,1)S(1)}, bf16[192,3072]{1,0:T(8,128)(2,1)S(1)}, u32[]{:S(2)}, u32[]{:S(2)}) collective-permute-start(bf16[192,3072]{1,0:T(8,128)(2,1)S(1)} %add_convert_fusion.17), channel_id=1, source_target_pairs={{8,0},{16,8},{24,16},{26,24},{18,26},{10,18},{2,10},{6,2},{14,6},{... | collective-permute-start | bytes 3538952 | tf_op jit(solution)/shard_map/ppermute | solution.py:88
  547.1 26.5 %collective-permute-start.8 = (bf16[192,3072]{1,0:T(8,128)(2,1)S(1)}, bf16[192,3072]{1,0:T(8,128)(2,1)S(1)}, u32[]{:S(2)}, u32[]{:S(2)}) collective-permute-start(bf16[192,3072]{1,0:T(8,128)(2,1)S(1)} %add_convert_fusion.28), channel_id=1, source_target_pairs={{0,8},{8,16},{16,24},{24,26},{26,18},{18,10},{10,2},{2,6},{6,14},{... | collective-permute-start | bytes 3538952 | tf_op jit(solution)/shard_map/ppermute | solution.py:87
  558.6 28.5 %copy-start.27 = (bf16[192,1536]{1,0:T(8,128)(2,1)S(1)}, bf16[192,1536]{1,0:T(8,128)(2,1)}, u32[]{:S(2)}) copy-start(bf16[192,1536]{1,0:T(8,128)(2,1)} %get-tuple-element.80) | copy-start | bytes 1769476
  558.6 28.5 %copy-start.32 = (bf16[192,1536]{1,0:T(8,128)(2,1)S(1)}, bf16[192,1536]{1,0:T(8,128)(2,1)}, u32[]{:S(2)}) copy-start(bf16[192,1536]{1,0:T(8,128)(2,1)} %get-tuple-element.96) | copy-start | bytes 1769476
  558.6 28.5 %collective-permute-start.22 = (bf16[192,3072]{1,0:T(8,128)(2,1)S(1)}, bf16[192,3072]{1,0:T(8,128)(2,1)S(1)}, u32[]{:S(2)}, u32[]{:S(2)}) collective-permute-start(bf16[192,3072]{1,0:T(8,128)(2,1)S(1)} %add_convert_fusion.16), channel_id=1, source_target_pairs={{8,0},{16,8},{24,16},{26,24},{18,26},{10,18},{2,10},{6,2},{14,6},{... | collective-permute-start | bytes 3538952 | tf_op jit(solution)/shard_map/ppermute | solution.py:88
  573.9 25.8 %collective-permute-start.9 = (bf16[192,3072]{1,0:T(8,128)(2,1)S(1)}, bf16[192,3072]{1,0:T(8,128)(2,1)S(1)}, u32[]{:S(2)}, u32[]{:S(2)}) collective-permute-start(bf16[192,3072]{1,0:T(8,128)(2,1)S(1)} %add_convert_fusion.27), channel_id=1, source_target_pairs={{0,8},{8,16},{16,24},{24,26},{26,18},{18,10},{10,2},{2,6},{6,14},{... | collective-permute-start | bytes 3538952 | tf_op jit(solution)/shard_map/ppermute | solution.py:87
  587.4 25.9 %collective-permute-start.23 = (bf16[192,3072]{1,0:T(8,128)(2,1)S(1)}, bf16[192,3072]{1,0:T(8,128)(2,1)S(1)}, u32[]{:S(2)}, u32[]{:S(2)}) collective-permute-start(bf16[192,3072]{1,0:T(8,128)(2,1)S(1)} %add_convert_fusion.15), channel_id=1, source_target_pairs={{8,0},{16,8},{24,16},{26,24},{18,26},{10,18},{2,10},{6,2},{14,6},{... | collective-permute-start | bytes 3538952 | tf_op jit(solution)/shard_map/ppermute | solution.py:88
  600.1 25.8 %collective-permute-start.10 = (bf16[192,3072]{1,0:T(8,128)(2,1)S(1)}, bf16[192,3072]{1,0:T(8,128)(2,1)S(1)}, u32[]{:S(2)}, u32[]{:S(2)}) collective-permute-start(bf16[192,3072]{1,0:T(8,128)(2,1)S(1)} %add_convert_fusion.26), channel_id=1, source_target_pairs={{0,8},{8,16},{16,24},{24,26},{26,18},{18,10},{10,2},{2,6},{6,14},{... | collective-permute-start | bytes 3538952 | tf_op jit(solution)/shard_map/ppermute | solution.py:87
  613.6 25.8 %collective-permute-start.24 = (bf16[192,3072]{1,0:T(8,128)(2,1)S(1)}, bf16[192,3072]{1,0:T(8,128)(2,1)S(1)}, u32[]{:S(2)}, u32[]{:S(2)}) collective-permute-start(bf16[192,3072]{1,0:T(8,128)(2,1)S(1)} %add_convert_fusion.14), channel_id=1, source_target_pairs={{8,0},{16,8},{24,16},{26,24},{18,26},{10,18},{2,10},{6,2},{14,6},{... | collective-permute-start | bytes 3538952 | tf_op jit(solution)/shard_map/ppermute | solution.py:88
  626.2 25.8 %collective-permute-start.11 = (bf16[192,3072]{1,0:T(8,128)(2,1)S(1)}, bf16[192,3072]{1,0:T(8,128)(2,1)S(1)}, u32[]{:S(2)}, u32[]{:S(2)}) collective-permute-start(bf16[192,3072]{1,0:T(8,128)(2,1)S(1)} %add_convert_fusion.25), channel_id=1, source_target_pairs={{0,8},{8,16},{16,24},{24,26},{26,18},{18,10},{10,2},{2,6},{6,14},{... | collective-permute-start | bytes 3538952 | tf_op jit(solution)/shard_map/ppermute | solution.py:87
  639.8 25.8 %collective-permute-start.25 = (bf16[192,3072]{1,0:T(8,128)(2,1)S(1)}, bf16[192,3072]{1,0:T(8,128)(2,1)S(1)}, u32[]{:S(2)}, u32[]{:S(2)}) collective-permute-start(bf16[192,3072]{1,0:T(8,128)(2,1)S(1)} %add_convert_fusion.13), channel_id=1, source_target_pairs={{8,0},{16,8},{24,16},{26,24},{18,26},{10,18},{2,10},{6,2},{14,6},{... | collective-permute-start | bytes 3538952 | tf_op jit(solution)/shard_map/ppermute | solution.py:88
  652.4 25.8 %collective-permute-start.12 = (bf16[192,3072]{1,0:T(8,128)(2,1)S(1)}, bf16[192,3072]{1,0:T(8,128)(2,1)S(1)}, u32[]{:S(2)}, u32[]{:S(2)}) collective-permute-start(bf16[192,3072]{1,0:T(8,128)(2,1)S(1)} %add_convert_fusion.24), channel_id=1, source_target_pairs={{0,8},{8,16},{16,24},{24,26},{26,18},{18,10},{10,2},{2,6},{6,14},{... | collective-permute-start | bytes 3538952 | tf_op jit(solution)/shard_map/ppermute | solution.py:87
  665.9 25.6 %collective-permute-start.26 = (bf16[192,3072]{1,0:T(8,128)(2,1)S(1)}, bf16[192,3072]{1,0:T(8,128)(2,1)S(1)}, u32[]{:S(2)}, u32[]{:S(2)}) collective-permute-start(bf16[192,3072]{1,0:T(8,128)(2,1)S(1)} %add_convert_fusion.12), channel_id=1, source_target_pairs={{8,0},{16,8},{24,16},{26,24},{18,26},{10,18},{2,10},{6,2},{14,6},{... | collective-permute-start | bytes 3538952 | tf_op jit(solution)/shard_map/ppermute | solution.py:88
  678.5 22.2 %collective-permute-start.13 = (bf16[192,3072]{1,0:T(8,128)(2,1)S(1)}, bf16[192,3072]{1,0:T(8,128)(2,1)S(1)}, u32[]{:S(2)}, u32[]{:S(2)}) collective-permute-start(bf16[192,3072]{1,0:T(8,128)(2,1)S(1)} %add_convert_fusion.23), channel_id=1, source_target_pairs={{0,8},{8,16},{16,24},{24,26},{26,18},{18,10},{10,2},{2,6},{6,14},{... | collective-permute-start | bytes 3538952 | tf_op jit(solution)/shard_map/ppermute | solution.py:87
  691.8 22.6 %collective-permute-start.27 = (bf16[192,3072]{1,0:T(8,128)(2,1)S(1)}, bf16[192,3072]{1,0:T(8,128)(2,1)S(1)}, u32[]{:S(2)}, u32[]{:S(2)}) collective-permute-start(bf16[192,3072]{1,0:T(8,128)(2,1)S(1)} %add_convert_fusion.11), channel_id=1, source_target_pairs={{8,0},{16,8},{24,16},{26,24},{18,26},{10,18},{2,10},{6,2},{14,6},{... | collective-permute-start | bytes 3538952 | tf_op jit(solution)/shard_map/ppermute | solution.py:88
  762.4 49.7 %copy-start.12 = (bf16[192,1536]{1,0:T(8,128)(2,1)S(1)}, bf16[192,1536]{1,0:T(8,128)(2,1)}, u32[]{:S(2)}) copy-start(bf16[192,1536]{1,0:T(8,128)(2,1)} %get-tuple-element.74) | copy-start | bytes 1769476
  762.4 49.7 %copy-start.13 = (bf16[192,1536]{1,0:T(8,128)(2,1)S(1)}, bf16[192,1536]{1,0:T(8,128)(2,1)}, u32[]{:S(2)}) copy-start(bf16[192,1536]{1,0:T(8,128)(2,1)} %get-tuple-element.90) | copy-start | bytes 1769476
  762.4 49.7 %collective-permute-start.29 = (bf16[192,3072]{1,0:T(8,128)(2,1)S(1)}, bf16[192,3072]{1,0:T(8,128)(2,1)}, u32[]{:S(2)}, u32[]{:S(2)}) collective-permute-start(bf16[192,3072]{1,0:T(8,128)(2,1)S(1)} %add_convert_fusion.10), channel_id=1, source_target_pairs={{8,0},{16,8},{24,16},{26,24},{18,26},{10,18},{2,10},{6,2},{14,6},{... | collective-permute-start | bytes 3538952 | tf_op jit(solution)/shard_map/ppermute | solution.py:88
  763.0 50.9 %collective-permute-start.28 = (bf16[192,3072]{1,0:T(8,128)(2,1)S(1)}, bf16[192,3072]{1,0:T(8,128)(2,1)}, u32[]{:S(2)}, u32[]{:S(2)}) collective-permute-start(bf16[192,3072]{1,0:T(8,128)(2,1)S(1)} %add_convert_fusion.22), channel_id=1, source_target_pairs={{0,8},{8,16},{16,24},{24,26},{26,18},{18,10},{10,2},{2,6},{6,14},{... | collective-permute-start | bytes 3538952 | tf_op jit(solution)/shard_map/ppermute | solution.py:87
  813.9 27.6 %copy-start.4 = (bf16[192,1536]{1,0:T(8,128)(2,1)S(1)}, bf16[192,1536]{1,0:T(8,128)(2,1)}, u32[]{:S(2)}) copy-start(bf16[192,1536]{1,0:T(8,128)(2,1)} %get-tuple-element.41) | copy-start | bytes 1769476
  815.6 27.7 %copy-start.10 = (bf16[192,1536]{1,0:T(8,128)(2,1)S(1)}, bf16[192,1536]{1,0:T(8,128)(2,1)}, u32[]{:S(2)}) copy-start(bf16[192,1536]{1,0:T(8,128)(2,1)} %get-tuple-element.73) | copy-start | bytes 1769476
  815.6 27.6 %copy-start.11 = (bf16[192,1536]{1,0:T(8,128)(2,1)S(1)}, bf16[192,1536]{1,0:T(8,128)(2,1)}, u32[]{:S(2)}) copy-start(bf16[192,1536]{1,0:T(8,128)(2,1)} %get-tuple-element.89) | copy-start | bytes 1769476
  815.7 25.8 %collective-permute-start.30 = (bf16[192,3072]{1,0:T(8,128)(2,1)S(1)}, bf16[192,3072]{1,0:T(8,128)(2,1)S(1)}, u32[]{:S(2)}, u32[]{:S(2)}) collective-permute-start(bf16[192,3072]{1,0:T(8,128)(2,1)S(1)} %add_convert_fusion.9), channel_id=1, source_target_pairs={{0,8},{8,16},{16,24},{24,26},{26,18},{18,10},{10,2},{2,6},{6,14},{... | collective-permute-start | bytes 3538952 | tf_op jit(solution)/shard_map/ppermute | solution.py:87
  817.1 26.1 %collective-permute-start.32 = (bf16[192,3072]{1,0:T(8,128)(2,1)S(1)}, bf16[192,3072]{1,0:T(8,128)(2,1)S(1)}, u32[]{:S(2)}, u32[]{:S(2)}) collective-permute-start(bf16[192,3072]{1,0:T(8,128)(2,1)S(1)} %add_convert_fusion.8), channel_id=1, source_target_pairs={{8,0},{16,8},{24,16},{26,24},{18,26},{10,18},{2,10},{6,2},{14,6},{... | collective-permute-start | bytes 3538952 | tf_op jit(solution)/shard_map/ppermute | solution.py:88
  841.8 20.8 %collective-permute-start.31 = (bf16[192,3072]{1,0:T(8,128)(2,1)S(1)}, bf16[192,3072]{1,0:T(8,128)(2,1)S(1)}, u32[]{:S(2)}, u32[]{:S(2)}) collective-permute-start(bf16[192,3072]{1,0:T(8,128)(2,1)S(1)} %add_convert_fusion.7), channel_id=1, source_target_pairs={{0,8},{8,16},{16,24},{24,26},{26,18},{18,10},{10,2},{2,6},{6,14},{... | collective-permute-start | bytes 3538952 | tf_op jit(solution)/shard_map/ppermute | solution.py:87
  844.6 18.3 %collective-permute-start.33 = (bf16[192,3072]{1,0:T(8,128)(2,1)}, bf16[192,3072]{1,0:T(8,128)(2,1)}, u32[]{:S(2)}, u32[]{:S(2)}) collective-permute-start(bf16[192,3072]{1,0:T(8,128)(2,1)} %add_convert_fusion.5), channel_id=1, source_target_pairs={{8,0},{16,8},{24,16},{26,24},{18,26},{10,18},{2,10},{6,2},{14,6},{... | collective-permute-start | bytes 3538952 | tf_op jit(solution)/shard_map/ppermute | solution.py:88
  (30 other events, 542.8 us)
Sparse Core Ops, SparseCore 0:
  11.5 496.9 all-gather.1

commit v11 on v10

--- a/solution.py
+++ b/solution.py
@@ -64,7 +64,7 @@
             [lax.dynamic_slice_in_dim(sums[q], block * rows, rows, 0) for q in (first, first + 1)], axis=1
         ).astype(jnp.float32)
 
-    n_pieces = 1
+    n_pieces = 4
     out_cols = width // n_pieces
     d_rows = local_cols // n_pieces
 

time: 893 us -> 851 us (0.953)
  waiting for transfers between devices: 466 us -> 333 us
  matrix products: 152 us -> 189 us
  other arithmetic: 37.3 us -> 72.7 us
  starting transfers between devices: 118 us -> 134 us
    ppermute x15, waiting for transfers between devices: 218 us -> 142 us  [per_device(): recv_cw = lax.ppermute(send_cw, 'chip', forward)]
    ppermute x15, waiting for transfers between devices: 205 us -> 148 us  [per_device(): recv_ccw = lax.ppermute(send_ccw, 'chip', backward)]
    dot_general x1 -> x4, matrix products: 47.6 us -> 66.6 us  [product(): jnp.dot(context, w[:, j * out_cols:(j + 1) * out_cols], preferred_element...]
    dot_general x1 -> x4, matrix products: 47.4 us -> 65.6 us  [product(): lax.dot_general(piece, w[k * d_rows:(k + 1) * d_rows], (((1,), (1,)), (()...]
    convert_element_type x15, other arithmetic: 8.67 us -> 23.1 us  [per_device(): send_ccw = (recv_ccw.astype(jnp.float32) + mine_ccw).astype(jnp.bfloat16)]
    convert_element_type x15, other arithmetic: 7.71 us -> 22 us  [per_device(): send_cw = (recv_cw.astype(jnp.float32) + mine_cw).astype(jnp.bfloat16)]
    ppermute x15, starting transfers between devices: 111 us -> 124 us  [per_device(): recv_cw = lax.ppermute(send_cw, 'chip', forward)]
    unnamed x121 -> x129, local copies, waits for them, and re-layouts: 29.4 us -> 31.7 us
  transfers between devices with their start and end apart: 35 -> 35, of which waited for: 28 -> 24; matrix products, arithmetic and copies ran while one was open for 20% -> 32% of each run, Pallas kernels for 0% -> 0%
where the time goes in v11:
time: 851 us; the launch traced here: 840 us
  waiting for transfers between devices  333 us (39%)
  matrix products  189 us (22%)
  starting transfers between devices  134 us (16%)
  other arithmetic  72.7 us (9%)
  between operations  57.1 us (7%)
  local copies, waits for them, and re-layouts  55 us (6%)
    ppermute x15, waiting for transfers between devices, per_device(): recv_ccw = lax.ppermute(send_ccw, 'chip', backward)  148 us
    ppermute x15, waiting for transfers between devices, per_device(): recv_cw = lax.ppermute(send_cw, 'chip', forward)  142 us
    ppermute x15, starting transfers between devices, per_device(): recv_cw = lax.ppermute(send_cw, 'chip', forward)  124 us
    dot_general x4, matrix products, product(): jnp.dot(context, w[:, j * out_cols:(j + 1) * out_cols], preferred_element...  66.6 us
    dot_general x4, matrix products, product(): lax.dot_general(piece, w[k * d_rows:(k + 1) * d_rows], (((1,), (1,)), (()...  65.6 us
    ppermute x4, waiting for transfers between devices, per_device(): grad_from_other = lax.ppermute(grad_for_other, 'core', swap)  42.6 us
    dot_general x4, matrix products, per_device(): lax.dot_general(ctx_own, piece_q, dims_wgrad, preferred_element_type=jnp....  33.2 us
    unnamed x129, local copies, waits for them, and re-layouts  31.7 us
  transfers between devices with their start and end apart: 35, of which 24 were waited for; matrix products, arithmetic and copies ran while one was open for 32% of the time, Pallas kernels for 0%

profile of v11, /device:TPU:0, one launch (start us, length us, event | category | flops | bytes accessed | tf_op | source)
XLA Modules:
  0.0 839.6 jit_solution(12032046684114093389)
XLA Ops:
  7.2 4.1 convert_element_type.412
  11.3 8.8 %copy.14 = bf16[512,6144]{0,1:T(8,128)(2,1)} copy(bf16[512,6144]{1,0:T(8,128)(2,1)} %param.7) | data formatting | bytes 12582912 | tf_op args[0]
  20.1 4.2 broadcast_select_fusion
  26.5 5.3 convolution_convert_fusion.3
  32.7 14.0 %collective-permute-done = bf16[3072,1536]{1,0:T(8,128)(2,1)} collective-permute-done((bf16[3072,1536]{1,0:T(8,128)(2,1)S(1)}, bf16[3072,1536]{1,0:T(8,128)(2,1)}, u32[]{:S(2)}, u32[]{:S(2)}) %collective-permute-start) | collective-permute-done | bytes 9437216 | tf_op jit(solution)/shard_map/ppermute | solution.py:47
  46.7 9.9 %add_convert_fusion.3 = bf16[3072,1536]{1,0:T(8,128)(2,1)} fusion(bf16[3072,1536]{1,0:T(8,128)(2,1)} %collective-permute-done, bf16[512,3072]{0,1:T(8,128)(2,1)S(1)} %bitcast.110, bf16[512,6144]{1,0:T(8,128)(2,1)S(1)} %bitcast.109), kind=kOutput, calls=%fused_computation.19 | convolution fusion | flops 4845993984 | bytes 23592960 | tf_op jit(solution)/shard_map/dot_general | solution.py:48
  56.6 5.2 convolution_convert_fusion.2
  62.3 14.3 %collective-permute-done.1 = bf16[3072,1536]{1,0:T(8,128)(2,1)S(1)} collective-permute-done((bf16[3072,1536]{1,0:T(8,128)(2,1)S(1)}, bf16[3072,1536]{1,0:T(8,128)(2,1)S(1)}, u32[]{:S(2)}, u32[]{:S(2)}) %collective-permute-start.1) | collective-permute-done | bytes 9437216 | tf_op jit(solution)/shard_map/ppermute | solution.py:47
  76.6 7.5 add_convert_fusion.2
  84.1 5.2 convolution_convert_fusion.1
  89.8 14.3 %collective-permute-done.8 = bf16[3072,1536]{1,0:T(8,128)(2,1)S(1)} collective-permute-done((bf16[3072,1536]{1,0:T(8,128)(2,1)S(1)}, bf16[3072,1536]{1,0:T(8,128)(2,1)S(1)}, u32[]{:S(2)}, u32[]{:S(2)}) %collective-permute-start.8) | collective-permute-done | bytes 9437216 | tf_op jit(solution)/shard_map/ppermute | solution.py:47
  104.1 7.6 add_convert_fusion.1
  111.7 7.4 convolution_convert_fusion
  163.6 7.2 constant_dynamic-slice_fusion.5
  170.8 6.8 constant_dynamic-slice_fusion.4
  178.7 2.7 collective-permute-start.2
  181.5 3.7 constant_dynamic-slice_fusion.1
  185.2 8.2 add_convert_fusion
  193.4 3.2 constant_dynamic-slice_fusion
  198.4 26.4 %collective-permute-done.2 = bf16[192,3072]{1,0:T(8,128)(2,1)} collective-permute-done((bf16[192,3072]{1,0:T(8,128)(2,1)}, bf16[192,3072]{1,0:T(8,128)(2,1)}, u32[]{:S(2)}, u32[]{:S(2)}) %collective-permute-start.2) | collective-permute-done | bytes 1179680 | tf_op jit(solution)/shard_map/ppermute | solution.py:87
  226.4 17.9 %collective-permute-start.3 = (bf16[192,3072]{1,0:T(8,128)(2,1)S(1)}, bf16[192,3072]{1,0:T(8,128)(2,1)S(1)}, u32[]{:S(2)}, u32[]{:S(2)}) collective-permute-start(bf16[192,3072]{1,0:T(8,128)(2,1)S(1)} %add_convert_fusion.33), channel_id=1, source_target_pairs={{0,8},{8,16},{16,24},{24,26},{26,18},{18,10},{10,2},{2,6},{6,14},{... | collective-permute-start | bytes 3538952 | tf_op jit(solution)/shard_map/ppermute | solution.py:87
  244.4 21.7 %collective-permute-done.10 = bf16[192,3072]{1,0:T(8,128)(2,1)S(1)} collective-permute-done((bf16[192,3072]{1,0:T(8,128)(2,1)S(1)}, bf16[192,3072]{1,0:T(8,128)(2,1)S(1)}, u32[]{:S(2)}, u32[]{:S(2)}) %collective-permute-start.10) | collective-permute-done | bytes 1179680 | tf_op jit(solution)/shard_map/ppermute | solution.py:88
  266.5 29.1 %collective-permute-done.3 = bf16[192,3072]{1,0:T(8,128)(2,1)S(1)} collective-permute-done((bf16[192,3072]{1,0:T(8,128)(2,1)S(1)}, bf16[192,3072]{1,0:T(8,128)(2,1)S(1)}, u32[]{:S(2)}, u32[]{:S(2)}) %collective-permute-start.3) | collective-permute-done | bytes 1179680 | tf_op jit(solution)/shard_map/ppermute | solution.py:87
  296.0 28.1 %collective-permute-start.4 = (bf16[192,3072]{1,0:T(8,128)(2,1)S(1)}, bf16[192,3072]{1,0:T(8,128)(2,1)S(1)}, u32[]{:S(2)}, u32[]{:S(2)}) collective-permute-start(bf16[192,3072]{1,0:T(8,128)(2,1)S(1)} %add_convert_fusion.32), channel_id=1, source_target_pairs={{0,8},{8,16},{16,24},{24,26},{26,18},{18,10},{10,2},{2,6},{6,14},{... | collective-permute-start | bytes 3538952 | tf_op jit(solution)/shard_map/ppermute | solution.py:87
  324.0 26.8 %collective-permute-done.11 = bf16[192,3072]{1,0:T(8,128)(2,1)S(1)} collective-permute-done((bf16[192,3072]{1,0:T(8,128)(2,1)S(1)}, bf16[192,3072]{1,0:T(8,128)(2,1)S(1)}, u32[]{:S(2)}, u32[]{:S(2)}) %collective-permute-start.11) | collective-permute-done | bytes 1179680 | tf_op jit(solution)/shard_map/ppermute | solution.py:88
  351.3 23.7 %collective-permute-done.4 = bf16[192,3072]{1,0:T(8,128)(2,1)S(1)} collective-permute-done((bf16[192,3072]{1,0:T(8,128)(2,1)S(1)}, bf16[192,3072]{1,0:T(8,128)(2,1)S(1)}, u32[]{:S(2)}, u32[]{:S(2)}) %collective-permute-start.4) | collective-permute-done | bytes 1179680 | tf_op jit(solution)/shard_map/ppermute | solution.py:87
  375.4 29.5 %collective-permute-start.5 = (bf16[192,3072]{1,0:T(8,128)(2,1)S(1)}, bf16[192,3072]{1,0:T(8,128)(2,1)S(1)}, u32[]{:S(2)}, u32[]{:S(2)}) collective-permute-start(bf16[192,3072]{1,0:T(8,128)(2,1)S(1)} %add_convert_fusion.31), channel_id=1, source_target_pairs={{0,8},{8,16},{16,24},{24,26},{26,18},{18,10},{10,2},{2,6},{6,14},{... | collective-permute-start | bytes 3538952 | tf_op jit(solution)/shard_map/ppermute | solution.py:87
  404.9 27.5 %collective-permute-done.12 = bf16[192,3072]{1,0:T(8,128)(2,1)S(1)} collective-permute-done((bf16[192,3072]{1,0:T(8,128)(2,1)S(1)}, bf16[192,3072]{1,0:T(8,128)(2,1)S(1)}, u32[]{:S(2)}, u32[]{:S(2)}) %collective-permute-start.12) | collective-permute-done | bytes 1179680 | tf_op jit(solution)/shard_map/ppermute | solution.py:88
  432.8 22.4 %collective-permute-done.5 = bf16[192,3072]{1,0:T(8,128)(2,1)S(1)} collective-permute-done((bf16[192,3072]{1,0:T(8,128)(2,1)S(1)}, bf16[192,3072]{1,0:T(8,128)(2,1)S(1)}, u32[]{:S(2)}, u32[]{:S(2)}) %collective-permute-start.5) | collective-permute-done | bytes 1179680 | tf_op jit(solution)/shard_map/ppermute | solution.py:87
  455.5 28.8 %collective-permute-start.6 = (bf16[192,3072]{1,0:T(8,128)(2,1)S(1)}, bf16[192,3072]{1,0:T(8,128)(2,1)S(1)}, u32[]{:S(2)}, u32[]{:S(2)}) collective-permute-start(bf16[192,3072]{1,0:T(8,128)(2,1)S(1)} %add_convert_fusion.30), channel_id=1, source_target_pairs={{0,8},{8,16},{16,24},{24,26},{26,18},{18,10},{10,2},{2,6},{6,14},{... | collective-permute-start | bytes 3538952 | tf_op jit(solution)/shard_map/ppermute | solution.py:87
  484.3 20.1 %collective-permute-done.13 = bf16[192,3072]{1,0:T(8,128)(2,1)S(1)} collective-permute-done((bf16[192,3072]{1,0:T(8,128)(2,1)S(1)}, bf16[192,3072]{1,0:T(8,128)(2,1)S(1)}, u32[]{:S(2)}, u32[]{:S(2)}) %collective-permute-start.13) | collective-permute-done | bytes 1179680 | tf_op jit(solution)/shard_map/ppermute | solution.py:88
  504.9 13.0 %collective-permute-done.6 = bf16[192,3072]{1,0:T(8,128)(2,1)S(1)} collective-permute-done((bf16[192,3072]{1,0:T(8,128)(2,1)S(1)}, bf16[192,3072]{1,0:T(8,128)(2,1)S(1)}, u32[]{:S(2)}, u32[]{:S(2)}) %collective-permute-start.6) | collective-permute-done | bytes 1179680 | tf_op jit(solution)/shard_map/ppermute | solution.py:87
  520.8 9.8 %collective-permute-done.14 = bf16[192,3072]{1,0:T(8,128)(2,1)S(1)} collective-permute-done((bf16[192,3072]{1,0:T(8,128)(2,1)S(1)}, bf16[192,3072]{1,0:T(8,128)(2,1)S(1)}, u32[]{:S(2)}, u32[]{:S(2)}) %collective-permute-start.14) | collective-permute-done | bytes 1179680 | tf_op jit(solution)/shard_map/ppermute | solution.py:88
  531.4 15.8 %collective-permute-done.7 = bf16[192,3072]{1,0:T(8,128)(2,1)S(1)} collective-permute-done((bf16[192,3072]{1,0:T(8,128)(2,1)S(1)}, bf16[192,3072]{1,0:T(8,128)(2,1)S(1)}, u32[]{:S(2)}, u32[]{:S(2)}) %collective-permute-start.7) | collective-permute-done | bytes 1179680 | tf_op jit(solution)/shard_map/ppermute | solution.py:87
  548.6 7.2 collective-permute-done.15
  557.2 16.6 %fusion.52 = bf16[512,1536]{0,1:T(8,128)(2,1)} fusion(bf16[512,6144]{1,0:T(8,128)(2,1)} %param.7, bf16[6144,6144]{1,0:T(8,128)(2,1)} %all-gather.2.cloned.1.call-done), kind=kOutput, calls=%fused_computation.46 | convolution fusion | flops 9664462848 | bytes 26738688 | tf_op jit(solution)/shard_map/dot_general | solution.py:73
  578.0 16.7 %fusion.49 = bf16[512,1536]{0,1:T(8,128)(2,1)} fusion(bf16[512,6144]{1,0:T(8,128)(2,1)} %param.7, bf16[6144,6144]{1,0:T(8,128)(2,1)} %all-gather.2.cloned.1.call-done), kind=kOutput, calls=%fused_computation.45 | convolution fusion | flops 9664462848 | bytes 26738688 | tf_op jit(solution)/shard_map/dot_general | solution.py:73
  594.7 7.3 collective-permute-done.17
  602.1 2.8 add_convert_fusion.20
  608.6 16.6 %fusion.46 = bf16[512,1536]{0,1:T(8,128)(2,1)} fusion(bf16[512,6144]{1,0:T(8,128)(2,1)} %param.7, bf16[6144,6144]{1,0:T(8,128)(2,1)} %all-gather.2.cloned.1.call-done), kind=kOutput, calls=%fused_computation.44 | convolution fusion | flops 9664462848 | bytes 26738688 | tf_op jit(solution)/shard_map/dot_general | solution.py:73
  625.2 7.0 collective-permute-done.19
  632.2 2.8 add_convert_fusion.18
  638.9 16.6 %fusion.43 = bf16[512,1536]{0,1:T(8,128)(2,1)} fusion(bf16[512,6144]{1,0:T(8,128)(2,1)} %param.7, bf16[6144,6144]{1,0:T(8,128)(2,1)} %all-gather.2.cloned.1.call-done), kind=kOutput, calls=%fused_computation.43 | convolution fusion | flops 9664462848 | bytes 26738688 | tf_op jit(solution)/shard_map/dot_general | solution.py:73
  655.5 5.8 collective-permute-done.21
  666.5 15.7 %fusion.64 = bf16[512,1536]{0,1:T(8,128)(2,1)S(1)} fusion(bf16[512,6144]{1,0:T(8,128)(2,1)} %param.11, bf16[6144,6144]{1,0:T(8,128)(2,1)} %all-gather.2.cloned.1.call-done), kind=kOutput, calls=%fused_computation.50 | convolution fusion | flops 9664462848 | bytes 26738688 | tf_op jit(solution)/shard_map/dot_general | solution.py:77
  682.2 5.9 collective-permute-done.23
  689.9 2.6 add_convert_fusion.15
  694.7 16.6 %fusion.61 = bf16[512,1536]{0,1:T(8,128)(2,1)} fusion(bf16[512,6144]{1,0:T(8,128)(2,1)} %param.11, bf16[6144,6144]{1,0:T(8,128)(2,1)} %all-gather.2.cloned.1.call-done), kind=kOutput, calls=%fused_computation.49 | convolution fusion | flops 9664462848 | bytes 26738688 | tf_op jit(solution)/shard_map/dot_general | solution.py:77
  711.4 3.8 collective-permute-done.25
  721.7 16.7 %fusion.58 = bf16[512,1536]{0,1:T(8,128)(2,1)} fusion(bf16[512,6144]{1,0:T(8,128)(2,1)} %param.11, bf16[6144,6144]{1,0:T(8,128)(2,1)} %all-gather.2.cloned.1.call-done), kind=kOutput, calls=%fused_computation.48 | convolution fusion | flops 9664462848 | bytes 26738688 | tf_op jit(solution)/shard_map/dot_general | solution.py:77
  738.4 3.0 collective-permute-done.27
  743.2 2.7 add_convert_fusion.11
  748.2 16.6 %fusion.55 = bf16[512,1536]{0,1:T(8,128)(2,1)} fusion(bf16[512,6144]{1,0:T(8,128)(2,1)} %param.11, bf16[6144,6144]{1,0:T(8,128)(2,1)} %all-gather.2.cloned.1.call-done), kind=kOutput, calls=%fused_computation.47 | convolution fusion | flops 9664462848 | bytes 26738688 | tf_op jit(solution)/shard_map/dot_general | solution.py:77
  767.6 3.0 add_convert_fusion.8
  770.6 2.8 add_convert_fusion.9
  775.5 3.2 pad_maximum_fusion
  778.8 8.7 %copy.15 = bf16[512,6144]{1,0:T(8,128)(2,1)} copy(bf16[512,6144]{0,1:T(8,128)(2,1)} %pad_maximum_fusion) | data formatting | bytes 12582912
  787.5 9.4 %collective-permute-done.30 = bf16[192,3072]{1,0:T(8,128)(2,1)} collective-permute-done((bf16[192,3072]{1,0:T(8,128)(2,1)}, bf16[192,3072]{1,0:T(8,128)(2,1)}, u32[]{:S(2)}, u32[]{:S(2)}) %collective-permute-start.30) | collective-permute-done | bytes 1179680 | tf_op jit(solution)/shard_map/ppermute | solution.py:87
  796.9 2.7 add_convert_fusion.7
  800.6 2.6 add_convert_fusion.5
  804.3 3.4 pad_maximum_fusion.1
  807.7 8.7 %copy.16 = bf16[512,6144]{1,0:T(8,128)(2,1)} copy(bf16[512,6144]{0,1:T(8,128)(2,1)} %pad_maximum_fusion.1) | data formatting | bytes 12582912
  816.4 2.5 collective-permute-done.31
  822.2 10.1 %multiply_subtract_fusion = (f32[192,6144]{1,0:T(8,128)}, f32[192,6144]{1,0:T(8,128)}, f32[192,6144]{1,0:T(8,128)}) fusion(f32[192,6144]{1,0:T(8,128)} %param.8, bf16[192,3072]{1,0:T(8,128)(2,1)S(1)} %add_convert_fusion.4, bf16[192,3072]{1,0:T(8,128)(2,1)S(1)} %add_convert_fusion.6, f32[192,6144]{1,0:T(8,128)} %param.9, f32[192,6144]{1,0:T(8,128)} %param.10), kind=kLoop, calls=%fused_computation.32 | loop fusion | flops 23592960 | bytes 30670848 | tf_op jit(solution)/shard_map/sub | solution.py:115
  (199 shorter events, 61.9 us)
Async XLA Ops:
  7.2 550.0 %all-gather.2.cloned.1.call-start = ((), (), s32[]{:S(2)}) async-start(), calls=%async_computation | async-start | bytes 77856768 | tf_op jit(solution)/shard_map/all_gather | solution.py:37
  24.3 79.8 %copy-start = (bf16[512,16,1,192]{0,3,2,1:T(8,128)(2,1)}, bf16[512,16,1,192]{0,3,2,1:T(8,128)(2,1)S(1)}, u32[]{:S(2)}) copy-start(bf16[512,16,1,192]{0,3,2,1:T(8,128)(2,1)S(1)} %get-tuple-element.156) | copy-start | bytes 9437188
  31.8 14.9 %collective-permute-start = (bf16[3072,1536]{1,0:T(8,128)(2,1)S(1)}, bf16[3072,1536]{1,0:T(8,128)(2,1)}, u32[]{:S(2)}, u32[]{:S(2)}) collective-permute-start(bf16[3072,1536]{1,0:T(8,128)(2,1)S(1)} %convolution_convert_fusion.3), channel_id=1, source_target_pairs={{0,1},{1,0},{2,3},{3,2},{4,5},{5,4},{6,7},{7,6},{8,9},{9,8},{10,11... | collective-permute-start | bytes 28311560 | tf_op jit(solution)/shard_map/ppermute | solution.py:47
  32.7 79.0 %copy-start.44 = (bf16[512,1536]{1,0:T(8,128)(2,1)}, bf16[512,1536]{1,0:T(8,128)(2,1)S(1)}, u32[]{:S(2)}) copy-start(bf16[512,1536]{1,0:T(8,128)(2,1)S(1)} %get-tuple-element.42) | copy-start | bytes 4718596
  61.9 14.7 %collective-permute-start.1 = (bf16[3072,1536]{1,0:T(8,128)(2,1)S(1)}, bf16[3072,1536]{1,0:T(8,128)(2,1)S(1)}, u32[]{:S(2)}, u32[]{:S(2)}) collective-permute-start(bf16[3072,1536]{1,0:T(8,128)(2,1)S(1)} %convolution_convert_fusion.2), channel_id=1, source_target_pairs={{0,1},{1,0},{2,3},{3,2},{4,5},{5,4},{6,7},{7,6},{8,9},{9,8},{10,11... | collective-permute-start | bytes 28311560 | tf_op jit(solution)/shard_map/ppermute | solution.py:47
  89.3 14.7 %collective-permute-start.8 = (bf16[3072,1536]{1,0:T(8,128)(2,1)S(1)}, bf16[3072,1536]{1,0:T(8,128)(2,1)S(1)}, u32[]{:S(2)}, u32[]{:S(2)}) collective-permute-start(bf16[3072,1536]{1,0:T(8,128)(2,1)S(1)} %convolution_convert_fusion.1), channel_id=1, source_target_pairs={{0,1},{1,0},{2,3},{3,2},{4,5},{5,4},{6,7},{7,6},{8,9},{9,8},{10,11... | collective-permute-start | bytes 28311560 | tf_op jit(solution)/shard_map/ppermute | solution.py:47
  119.1 66.1 %collective-permute-start.9 = (bf16[3072,1536]{1,0:T(8,128)(2,1)}, bf16[3072,1536]{1,0:T(8,128)(2,1)}, u32[]{:S(2)}, u32[]{:S(2)}) collective-permute-start(bf16[3072,1536]{1,0:T(8,128)(2,1)} %convolution_convert_fusion), channel_id=1, source_target_pairs={{0,1},{1,0},{2,3},{3,2},{4,5},{5,4},{6,7},{7,6},{8,9},{9,8},{10,11... | collective-permute-start | bytes 28311560 | tf_op jit(solution)/shard_map/ppermute | solution.py:47
  178.7 46.1 %collective-permute-start.2 = (bf16[192,3072]{1,0:T(8,128)(2,1)}, bf16[192,3072]{1,0:T(8,128)(2,1)}, u32[]{:S(2)}, u32[]{:S(2)}) collective-permute-start(bf16[192,3072]{1,0:T(8,128)(2,1)} %pad_maximum_fusion.3), channel_id=1, source_target_pairs={{0,8},{8,16},{16,24},{24,26},{26,18},{18,10},{10,2},{2,6},{6,14},{... | collective-permute-start | bytes 3538952 | tf_op jit(solution)/shard_map/ppermute | solution.py:87
  196.6 28.2 %copy-start.36 = (bf16[192,1536]{1,0:T(8,128)(2,1)S(1)}, bf16[192,1536]{1,0:T(8,128)(2,1)}, u32[]{:S(2)}) copy-start(bf16[192,1536]{1,0:T(8,128)(2,1)} %get-tuple-element.102) | copy-start | bytes 1769476
  196.6 28.2 %copy-start.38 = (bf16[192,1536]{1,0:T(8,128)(2,1)S(1)}, bf16[192,1536]{1,0:T(8,128)(2,1)}, u32[]{:S(2)}) copy-start(bf16[192,1536]{1,0:T(8,128)(2,1)} %get-tuple-element.118) | copy-start | bytes 1769476
  198.0 68.1 %copy-start.41 = (bf16[192,1536]{1,0:T(8,128)(2,1)S(1)}, bf16[192,1536]{1,0:T(8,128)(2,1)}, u32[]{:S(2)}) copy-start(bf16[192,1536]{1,0:T(8,128)(2,1)} %get-tuple-element.134) | copy-start | bytes 1769476
  198.1 68.1 %copy-start.43 = (bf16[192,1536]{1,0:T(8,128)(2,1)S(1)}, bf16[192,1536]{1,0:T(8,128)(2,1)}, u32[]{:S(2)}) copy-start(bf16[192,1536]{1,0:T(8,128)(2,1)} %get-tuple-element.150) | copy-start | bytes 1769476
  198.1 68.0 %collective-permute-start.10 = (bf16[192,3072]{1,0:T(8,128)(2,1)S(1)}, bf16[192,3072]{1,0:T(8,128)(2,1)S(1)}, u32[]{:S(2)}, u32[]{:S(2)}) collective-permute-start(bf16[192,3072]{1,0:T(8,128)(2,1)S(1)} %pad_maximum_fusion.4), channel_id=1, source_target_pairs={{8,0},{16,8},{24,16},{26,24},{18,26},{10,18},{2,10},{6,2},{14,6},{... | collective-permute-start | bytes 3538952 | tf_op jit(solution)/shard_map/ppermute | solution.py:88
  226.4 69.2 %copy-start.33 = (bf16[192,1536]{1,0:T(8,128)(2,1)S(1)}, bf16[192,1536]{1,0:T(8,128)(2,1)}, u32[]{:S(2)}) copy-start(bf16[192,1536]{1,0:T(8,128)(2,1)} %get-tuple-element.101) | copy-start | bytes 1769476
  226.4 69.2 %copy-start.35 = (bf16[192,1536]{1,0:T(8,128)(2,1)S(1)}, bf16[192,1536]{1,0:T(8,128)(2,1)}, u32[]{:S(2)}) copy-start(bf16[192,1536]{1,0:T(8,128)(2,1)} %get-tuple-element.117) | copy-start | bytes 1769476
  226.4 69.2 %collective-permute-start.3 = (bf16[192,3072]{1,0:T(8,128)(2,1)S(1)}, bf16[192,3072]{1,0:T(8,128)(2,1)S(1)}, u32[]{:S(2)}, u32[]{:S(2)}) collective-permute-start(bf16[192,3072]{1,0:T(8,128)(2,1)S(1)} %add_convert_fusion.33), channel_id=1, source_target_pairs={{0,8},{8,16},{16,24},{24,26},{26,18},{18,10},{10,2},{2,6},{6,14},{... | collective-permute-start | bytes 3538952 | tf_op jit(solution)/shard_map/ppermute | solution.py:87
  266.5 84.4 %copy-start.39 = (bf16[192,1536]{1,0:T(8,128)(2,1)S(1)}, bf16[192,1536]{1,0:T(8,128)(2,1)}, u32[]{:S(2)}) copy-start(bf16[192,1536]{1,0:T(8,128)(2,1)} %get-tuple-element.133) | copy-start | bytes 1769476
  266.5 84.4 %copy-start.42 = (bf16[192,1536]{1,0:T(8,128)(2,1)S(1)}, bf16[192,1536]{1,0:T(8,128)(2,1)}, u32[]{:S(2)}) copy-start(bf16[192,1536]{1,0:T(8,128)(2,1)} %get-tuple-element.149) | copy-start | bytes 1769476
  266.5 84.4 %collective-permute-start.11 = (bf16[192,3072]{1,0:T(8,128)(2,1)S(1)}, bf16[192,3072]{1,0:T(8,128)(2,1)S(1)}, u32[]{:S(2)}, u32[]{:S(2)}) collective-permute-start(bf16[192,3072]{1,0:T(8,128)(2,1)S(1)} %add_convert_fusion.27), channel_id=1, source_target_pairs={{8,0},{16,8},{24,16},{26,24},{18,26},{10,18},{2,10},{6,2},{14,6},{... | collective-permute-start | bytes 3538952 | tf_op jit(solution)/shard_map/ppermute | solution.py:88
  296.0 79.0 %copy-start.30 = (bf16[192,1536]{1,0:T(8,128)(2,1)S(1)}, bf16[192,1536]{1,0:T(8,128)(2,1)}, u32[]{:S(2)}) copy-start(bf16[192,1536]{1,0:T(8,128)(2,1)} %get-tuple-element.100) | copy-start | bytes 1769476
  296.0 79.0 %copy-start.32 = (bf16[192,1536]{1,0:T(8,128)(2,1)S(1)}, bf16[192,1536]{1,0:T(8,128)(2,1)}, u32[]{:S(2)}) copy-start(bf16[192,1536]{1,0:T(8,128)(2,1)} %get-tuple-element.116) | copy-start | bytes 1769476
  296.0 79.0 %collective-permute-start.4 = (bf16[192,3072]{1,0:T(8,128)(2,1)S(1)}, bf16[192,3072]{1,0:T(8,128)(2,1)S(1)}, u32[]{:S(2)}, u32[]{:S(2)}) collective-permute-start(bf16[192,3072]{1,0:T(8,128)(2,1)S(1)} %add_convert_fusion.32), channel_id=1, source_target_pairs={{0,8},{8,16},{16,24},{24,26},{26,18},{18,10},{10,2},{2,6},{6,14},{... | collective-permute-start | bytes 3538952 | tf_op jit(solution)/shard_map/ppermute | solution.py:87
  351.2 81.2 %copy-start.37 = (bf16[192,1536]{1,0:T(8,128)(2,1)S(1)}, bf16[192,1536]{1,0:T(8,128)(2,1)}, u32[]{:S(2)}) copy-start(bf16[192,1536]{1,0:T(8,128)(2,1)} %get-tuple-element.132) | copy-start | bytes 1769476
  351.2 81.2 %copy-start.40 = (bf16[192,1536]{1,0:T(8,128)(2,1)S(1)}, bf16[192,1536]{1,0:T(8,128)(2,1)}, u32[]{:S(2)}) copy-start(bf16[192,1536]{1,0:T(8,128)(2,1)} %get-tuple-element.148) | copy-start | bytes 1769476
  351.2 81.2 %collective-permute-start.12 = (bf16[192,3072]{1,0:T(8,128)(2,1)S(1)}, bf16[192,3072]{1,0:T(8,128)(2,1)S(1)}, u32[]{:S(2)}, u32[]{:S(2)}) collective-permute-start(bf16[192,3072]{1,0:T(8,128)(2,1)S(1)} %add_convert_fusion.26), channel_id=1, source_target_pairs={{8,0},{16,8},{24,16},{26,24},{18,26},{10,18},{2,10},{6,2},{14,6},{... | collective-permute-start | bytes 3538952 | tf_op jit(solution)/shard_map/ppermute | solution.py:88
  375.4 79.8 %copy-start.27 = (bf16[192,1536]{1,0:T(8,128)(2,1)S(1)}, bf16[192,1536]{1,0:T(8,128)(2,1)}, u32[]{:S(2)}) copy-start(bf16[192,1536]{1,0:T(8,128)(2,1)} %get-tuple-element.99) | copy-start | bytes 1769476
  375.4 79.8 %copy-start.29 = (bf16[192,1536]{1,0:T(8,128)(2,1)S(1)}, bf16[192,1536]{1,0:T(8,128)(2,1)}, u32[]{:S(2)}) copy-start(bf16[192,1536]{1,0:T(8,128)(2,1)} %get-tuple-element.115) | copy-start | bytes 1769476
  375.4 79.8 %collective-permute-start.5 = (bf16[192,3072]{1,0:T(8,128)(2,1)S(1)}, bf16[192,3072]{1,0:T(8,128)(2,1)S(1)}, u32[]{:S(2)}, u32[]{:S(2)}) collective-permute-start(bf16[192,3072]{1,0:T(8,128)(2,1)S(1)} %add_convert_fusion.31), channel_id=1, source_target_pairs={{0,8},{8,16},{16,24},{24,26},{26,18},{18,10},{10,2},{2,6},{6,14},{... | collective-permute-start | bytes 3538952 | tf_op jit(solution)/shard_map/ppermute | solution.py:87
  432.7 71.7 %copy-start.34 = (bf16[192,1536]{1,0:T(8,128)(2,1)S(1)}, bf16[192,1536]{1,0:T(8,128)(2,1)}, u32[]{:S(2)}) copy-start(bf16[192,1536]{1,0:T(8,128)(2,1)} %get-tuple-element.131) | copy-start | bytes 1769476
  432.7 71.7 %collective-permute-start.13 = (bf16[192,3072]{1,0:T(8,128)(2,1)S(1)}, bf16[192,3072]{1,0:T(8,128)(2,1)S(1)}, u32[]{:S(2)}, u32[]{:S(2)}) collective-permute-start(bf16[192,3072]{1,0:T(8,128)(2,1)S(1)} %add_convert_fusion.25), channel_id=1, source_target_pairs={{8,0},{16,8},{24,16},{26,24},{18,26},{10,18},{2,10},{6,2},{14,6},{... | collective-permute-start | bytes 3538952 | tf_op jit(solution)/shard_map/ppermute | solution.py:88
  455.5 62.4 %copy-start.24 = (bf16[192,1536]{1,0:T(8,128)(2,1)S(1)}, bf16[192,1536]{1,0:T(8,128)(2,1)}, u32[]{:S(2)}) copy-start(bf16[192,1536]{1,0:T(8,128)(2,1)} %get-tuple-element.98) | copy-start | bytes 1769476
  455.5 62.4 %copy-start.26 = (bf16[192,1536]{1,0:T(8,128)(2,1)S(1)}, bf16[192,1536]{1,0:T(8,128)(2,1)}, u32[]{:S(2)}) copy-start(bf16[192,1536]{1,0:T(8,128)(2,1)} %get-tuple-element.114) | copy-start | bytes 1769476
  455.5 62.4 %collective-permute-start.6 = (bf16[192,3072]{1,0:T(8,128)(2,1)S(1)}, bf16[192,3072]{1,0:T(8,128)(2,1)S(1)}, u32[]{:S(2)}, u32[]{:S(2)}) collective-permute-start(bf16[192,3072]{1,0:T(8,128)(2,1)S(1)} %add_convert_fusion.30), channel_id=1, source_target_pairs={{0,8},{8,16},{16,24},{24,26},{26,18},{18,10},{10,2},{2,6},{6,14},{... | collective-permute-start | bytes 3538952 | tf_op jit(solution)/shard_map/ppermute | solution.py:87
  504.8 25.8 %copy-start.31 = (bf16[192,1536]{1,0:T(8,128)(2,1)S(1)}, bf16[192,1536]{1,0:T(8,128)(2,1)}, u32[]{:S(2)}) copy-start(bf16[192,1536]{1,0:T(8,128)(2,1)} %get-tuple-element.130) | copy-start | bytes 1769476
  504.8 25.8 %collective-permute-start.14 = (bf16[192,3072]{1,0:T(8,128)(2,1)S(1)}, bf16[192,3072]{1,0:T(8,128)(2,1)S(1)}, u32[]{:S(2)}, u32[]{:S(2)}) collective-permute-start(bf16[192,3072]{1,0:T(8,128)(2,1)S(1)} %add_convert_fusion.24), channel_id=1, source_target_pairs={{8,0},{16,8},{24,16},{26,24},{18,26},{10,18},{2,10},{6,2},{14,6},{... | collective-permute-start | bytes 3538952 | tf_op jit(solution)/shard_map/ppermute | solution.py:88
  518.3 29.0 %collective-permute-start.7 = (bf16[192,3072]{1,0:T(8,128)(2,1)S(1)}, bf16[192,3072]{1,0:T(8,128)(2,1)S(1)}, u32[]{:S(2)}, u32[]{:S(2)}) collective-permute-start(bf16[192,3072]{1,0:T(8,128)(2,1)S(1)} %add_convert_fusion.29), channel_id=1, source_target_pairs={{0,8},{8,16},{16,24},{24,26},{26,18},{18,10},{10,2},{2,6},{6,14},{... | collective-permute-start | bytes 3538952 | tf_op jit(solution)/shard_map/ppermute | solution.py:87
  530.9 24.9 %copy-start.28 = (bf16[192,1536]{1,0:T(8,128)(2,1)S(1)}, bf16[192,1536]{1,0:T(8,128)(2,1)}, u32[]{:S(2)}) copy-start(bf16[192,1536]{1,0:T(8,128)(2,1)} %get-tuple-element.129) | copy-start | bytes 1769476
  531.0 24.9 %collective-permute-start.15 = (bf16[192,3072]{1,0:T(8,128)(2,1)S(1)}, bf16[192,3072]{1,0:T(8,128)(2,1)S(1)}, u32[]{:S(2)}, u32[]{:S(2)}) collective-permute-start(bf16[192,3072]{1,0:T(8,128)(2,1)S(1)} %add_convert_fusion.23), channel_id=1, source_target_pairs={{8,0},{16,8},{24,16},{26,24},{18,26},{10,18},{2,10},{6,2},{14,6},{... | collective-permute-start | bytes 3538952 | tf_op jit(solution)/shard_map/ppermute | solution.py:88
  573.8 28.2 %collective-permute-start.17 = (bf16[192,3072]{1,0:T(8,128)(2,1)}, bf16[192,3072]{1,0:T(8,128)(2,1)}, u32[]{:S(2)}, u32[]{:S(2)}) collective-permute-start(bf16[192,3072]{1,0:T(8,128)(2,1)} %add_convert_fusion.22), channel_id=1, source_target_pairs={{8,0},{16,8},{24,16},{26,24},{18,26},{10,18},{2,10},{6,2},{14,6},{... | collective-permute-start | bytes 3538952 | tf_op jit(solution)/shard_map/ppermute | solution.py:88
  576.3 28.6 %collective-permute-start.16 = (bf16[192,3072]{1,0:T(8,128)(2,1)S(1)}, bf16[192,3072]{1,0:T(8,128)(2,1)}, u32[]{:S(2)}, u32[]{:S(2)}) collective-permute-start(bf16[192,3072]{1,0:T(8,128)(2,1)S(1)} %copy-done.52), channel_id=1, source_target_pairs={{0,8},{8,16},{16,24},{24,26},{26,18},{18,10},{10,2},{2,6},{6,14},{... | collective-permute-start | bytes 3538952 | tf_op jit(solution)/shard_map/ppermute | solution.py:87
  578.0 24.1 %copy-start.25 = (bf16[192,1536]{1,0:T(8,128)(2,1)S(1)}, bf16[192,1536]{1,0:T(8,128)(2,1)}, u32[]{:S(2)}) copy-start(bf16[192,1536]{1,0:T(8,128)(2,1)} %get-tuple-element.128) | copy-start | bytes 1769476
  578.0 26.9 %copy-start.20 = (bf16[192,1536]{1,0:T(8,128)(2,1)S(1)}, bf16[192,1536]{1,0:T(8,128)(2,1)}, u32[]{:S(2)}) copy-start(bf16[192,1536]{1,0:T(8,128)(2,1)} %get-tuple-element.96) | copy-start | bytes 1769476
  578.0 26.9 %copy-start.21 = (bf16[192,1536]{1,0:T(8,128)(2,1)S(1)}, bf16[192,1536]{1,0:T(8,128)(2,1)}, u32[]{:S(2)}) copy-start(bf16[192,1536]{1,0:T(8,128)(2,1)} %get-tuple-element.112) | copy-start | bytes 1769476
  606.5 25.7 %collective-permute-start.19 = (bf16[192,3072]{1,0:T(8,128)(2,1)}, bf16[192,3072]{1,0:T(8,128)(2,1)}, u32[]{:S(2)}, u32[]{:S(2)}) collective-permute-start(bf16[192,3072]{1,0:T(8,128)(2,1)} %add_convert_fusion.20), channel_id=1, source_target_pairs={{8,0},{16,8},{24,16},{26,24},{18,26},{10,18},{2,10},{6,2},{14,6},{... | collective-permute-start | bytes 3538952 | tf_op jit(solution)/shard_map/ppermute | solution.py:88
  607.1 27.9 %collective-permute-start.18 = (bf16[192,3072]{1,0:T(8,128)(2,1)S(1)}, bf16[192,3072]{1,0:T(8,128)(2,1)}, u32[]{:S(2)}, u32[]{:S(2)}) collective-permute-start(bf16[192,3072]{1,0:T(8,128)(2,1)S(1)} %add_convert_fusion.21), channel_id=1, source_target_pairs={{0,8},{8,16},{16,24},{24,26},{26,18},{18,10},{10,2},{2,6},{6,14},{... | collective-permute-start | bytes 3538952 | tf_op jit(solution)/shard_map/ppermute | solution.py:87
  608.6 23.6 %copy-start.23 = (bf16[192,1536]{1,0:T(8,128)(2,1)S(1)}, bf16[192,1536]{1,0:T(8,128)(2,1)}, u32[]{:S(2)}) copy-start(bf16[192,1536]{1,0:T(8,128)(2,1)} %get-tuple-element.127) | copy-start | bytes 1769476
  636.6 24.6 %collective-permute-start.21 = (bf16[192,3072]{1,0:T(8,128)(2,1)}, bf16[192,3072]{1,0:T(8,128)(2,1)S(1)}, u32[]{:S(2)}, u32[]{:S(2)}) collective-permute-start(bf16[192,3072]{1,0:T(8,128)(2,1)} %add_convert_fusion.18), channel_id=1, source_target_pairs={{8,0},{16,8},{24,16},{26,24},{18,26},{10,18},{2,10},{6,2},{14,6},{... | collective-permute-start | bytes 3538952 | tf_op jit(solution)/shard_map/ppermute | solution.py:88
  637.0 27.1 %collective-permute-start.20 = (bf16[192,3072]{1,0:T(8,128)(2,1)S(1)}, bf16[192,3072]{1,0:T(8,128)(2,1)S(1)}, u32[]{:S(2)}, u32[]{:S(2)}) collective-permute-start(bf16[192,3072]{1,0:T(8,128)(2,1)S(1)} %add_convert_fusion.19), channel_id=1, source_target_pairs={{0,8},{8,16},{16,24},{24,26},{26,18},{18,10},{10,2},{2,6},{6,14},{... | collective-permute-start | bytes 3538952 | tf_op jit(solution)/shard_map/ppermute | solution.py:87
  638.8 23.4 %copy-start.22 = (bf16[192,1536]{1,0:T(8,128)(2,1)S(1)}, bf16[192,1536]{1,0:T(8,128)(2,1)}, u32[]{:S(2)}) copy-start(bf16[192,1536]{1,0:T(8,128)(2,1)} %get-tuple-element.126) | copy-start | bytes 1769476
  664.4 23.6 %collective-permute-start.23 = (bf16[192,3072]{1,0:T(8,128)(2,1)S(1)}, bf16[192,3072]{1,0:T(8,128)(2,1)}, u32[]{:S(2)}, u32[]{:S(2)}) collective-permute-start(bf16[192,3072]{1,0:T(8,128)(2,1)S(1)} %add_convert_fusion.16), channel_id=1, source_target_pairs={{8,0},{16,8},{24,16},{26,24},{18,26},{10,18},{2,10},{6,2},{14,6},{... | collective-permute-start | bytes 3538952 | tf_op jit(solution)/shard_map/ppermute | solution.py:88
  664.8 25.1 %collective-permute-start.22 = (bf16[192,3072]{1,0:T(8,128)(2,1)S(1)}, bf16[192,3072]{1,0:T(8,128)(2,1)}, u32[]{:S(2)}, u32[]{:S(2)}) collective-permute-start(bf16[192,3072]{1,0:T(8,128)(2,1)S(1)} %add_convert_fusion.17), channel_id=1, source_target_pairs={{0,8},{8,16},{16,24},{24,26},{26,18},{18,10},{10,2},{2,6},{6,14},{... | collective-permute-start | bytes 3538952 | tf_op jit(solution)/shard_map/ppermute | solution.py:87
  692.5 22.6 %collective-permute-start.25 = (bf16[192,3072]{1,0:T(8,128)(2,1)S(1)}, bf16[192,3072]{1,0:T(8,128)(2,1)}, u32[]{:S(2)}, u32[]{:S(2)}) collective-permute-start(bf16[192,3072]{1,0:T(8,128)(2,1)S(1)} %add_convert_fusion.14), channel_id=1, source_target_pairs={{8,0},{16,8},{24,16},{26,24},{18,26},{10,18},{2,10},{6,2},{14,6},{... | collective-permute-start | bytes 3538952 | tf_op jit(solution)/shard_map/ppermute | solution.py:88
  692.8 24.2 %collective-permute-start.24 = (bf16[192,3072]{1,0:T(8,128)(2,1)}, bf16[192,3072]{1,0:T(8,128)(2,1)S(1)}, u32[]{:S(2)}, u32[]{:S(2)}) collective-permute-start(bf16[192,3072]{1,0:T(8,128)(2,1)} %add_convert_fusion.15), channel_id=1, source_target_pairs={{0,8},{8,16},{16,24},{24,26},{26,18},{18,10},{10,2},{2,6},{6,14},{... | collective-permute-start | bytes 3538952 | tf_op jit(solution)/shard_map/ppermute | solution.py:87
  694.7 23.3 %copy-start.13 = (bf16[192,1536]{1,0:T(8,128)(2,1)S(1)}, bf16[192,1536]{1,0:T(8,128)(2,1)}, u32[]{:S(2)}) copy-start(bf16[192,1536]{1,0:T(8,128)(2,1)} %get-tuple-element.92) | copy-start | bytes 1769476
  694.7 23.3 %copy-start.15 = (bf16[192,1536]{1,0:T(8,128)(2,1)S(1)}, bf16[192,1536]{1,0:T(8,128)(2,1)}, u32[]{:S(2)}) copy-start(bf16[192,1536]{1,0:T(8,128)(2,1)} %get-tuple-element.108) | copy-start | bytes 1769476
  719.6 21.8 %collective-permute-start.27 = (bf16[192,3072]{1,0:T(8,128)(2,1)S(1)}, bf16[192,3072]{1,0:T(8,128)(2,1)}, u32[]{:S(2)}, u32[]{:S(2)}) collective-permute-start(bf16[192,3072]{1,0:T(8,128)(2,1)S(1)} %add_convert_fusion.12), channel_id=1, source_target_pairs={{8,0},{16,8},{24,16},{26,24},{18,26},{10,18},{2,10},{6,2},{14,6},{... | collective-permute-start | bytes 3538952 | tf_op jit(solution)/shard_map/ppermute | solution.py:88
  720.0 23.2 %collective-permute-start.26 = (bf16[192,3072]{1,0:T(8,128)(2,1)S(1)}, bf16[192,3072]{1,0:T(8,128)(2,1)}, u32[]{:S(2)}, u32[]{:S(2)}) collective-permute-start(bf16[192,3072]{1,0:T(8,128)(2,1)S(1)} %add_convert_fusion.13), channel_id=1, source_target_pairs={{0,8},{8,16},{16,24},{24,26},{26,18},{18,10},{10,2},{2,6},{6,14},{... | collective-permute-start | bytes 3538952 | tf_op jit(solution)/shard_map/ppermute | solution.py:87
  745.9 20.7 %collective-permute-start.29 = (bf16[192,3072]{1,0:T(8,128)(2,1)S(1)}, bf16[192,3072]{1,0:T(8,128)(2,1)S(1)}, u32[]{:S(2)}, u32[]{:S(2)}) collective-permute-start(bf16[192,3072]{1,0:T(8,128)(2,1)S(1)} %add_convert_fusion.10), channel_id=1, source_target_pairs={{8,0},{16,8},{24,16},{26,24},{18,26},{10,18},{2,10},{6,2},{14,6},{... | collective-permute-start | bytes 3538952 | tf_op jit(solution)/shard_map/ppermute | solution.py:88
  746.2 24.4 %collective-permute-start.28 = (bf16[192,3072]{1,0:T(8,128)(2,1)}, bf16[192,3072]{1,0:T(8,128)(2,1)}, u32[]{:S(2)}, u32[]{:S(2)}) collective-permute-start(bf16[192,3072]{1,0:T(8,128)(2,1)} %add_convert_fusion.11), channel_id=1, source_target_pairs={{0,8},{8,16},{16,24},{24,26},{26,18},{18,10},{10,2},{2,6},{6,14},{... | collective-permute-start | bytes 3538952 | tf_op jit(solution)/shard_map/ppermute | solution.py:87
  748.2 22.5 %copy-start.8 = (bf16[192,1536]{1,0:T(8,128)(2,1)S(1)}, bf16[192,1536]{1,0:T(8,128)(2,1)}, u32[]{:S(2)}) copy-start(bf16[192,1536]{1,0:T(8,128)(2,1)} %get-tuple-element.106) | copy-start | bytes 1769476
  773.5 23.4 %collective-permute-start.30 = (bf16[192,3072]{1,0:T(8,128)(2,1)}, bf16[192,3072]{1,0:T(8,128)(2,1)}, u32[]{:S(2)}, u32[]{:S(2)}) collective-permute-start(bf16[192,3072]{1,0:T(8,128)(2,1)} %add_convert_fusion.9), channel_id=1, source_target_pairs={{0,8},{8,16},{16,24},{24,26},{26,18},{18,10},{10,2},{2,6},{6,14},{... | collective-permute-start | bytes 3538952 | tf_op jit(solution)/shard_map/ppermute | solution.py:87
  774.4 26.1 %collective-permute-start.32 = (bf16[192,3072]{1,0:T(8,128)(2,1)}, bf16[192,3072]{1,0:T(8,128)(2,1)}, u32[]{:S(2)}, u32[]{:S(2)}) collective-permute-start(bf16[192,3072]{1,0:T(8,128)(2,1)} %add_convert_fusion.8), channel_id=1, source_target_pairs={{8,0},{16,8},{24,16},{26,24},{18,26},{10,18},{2,10},{6,2},{14,6},{... | collective-permute-start | bytes 3538952 | tf_op jit(solution)/shard_map/ppermute | solution.py:88
  799.6 19.3 %collective-permute-start.31 = (bf16[192,3072]{1,0:T(8,128)(2,1)}, bf16[192,3072]{1,0:T(8,128)(2,1)}, u32[]{:S(2)}, u32[]{:S(2)}) collective-permute-start(bf16[192,3072]{1,0:T(8,128)(2,1)} %add_convert_fusion.7), channel_id=1, source_target_pairs={{0,8},{8,16},{16,24},{24,26},{26,18},{18,10},{10,2},{2,6},{6,14},{... | collective-permute-start | bytes 3538952 | tf_op jit(solution)/shard_map/ppermute | solution.py:87
  803.2 17.3 %collective-permute-start.33 = (bf16[192,3072]{1,0:T(8,128)(2,1)}, bf16[192,3072]{1,0:T(8,128)(2,1)}, u32[]{:S(2)}, u32[]{:S(2)}) collective-permute-start(bf16[192,3072]{1,0:T(8,128)(2,1)} %add_convert_fusion.5), channel_id=1, source_target_pairs={{8,0},{16,8},{24,16},{26,24},{18,26},{10,18},{2,10},{6,2},{14,6},{... | collective-permute-start | bytes 3538952 | tf_op jit(solution)/shard_map/ppermute | solution.py:88
  (34 other events, 405.1 us)
Sparse Core Ops, SparseCore 0:
  11.5 498.4 all-gather.1
